TPU v7x, 32 devices: a whole 2x2x4 slice. The times are simulated.
32 devices in a mesh: left: 4 (over y, x), right: 8 (over z, core).
Axes of the slice: x: 2, y: 2, z: 4, core: 2. Of those that a mesh axis runs over, the one named last changes fastest.
Arguments:
- state: float32 [32, 1024, 1024], P(('left', 'right')), may hold values from -20 to 20
- left_env: bfloat16 [2, 32, 1024, 1024], P(None, ('left', 'right')), may hold values from -0.5 to 2.5
- right_env: bfloat16 [2, 32, 1024, 1024], P(None, ('left', 'right')), may hold values from -0.5 to 2.5
- site_ops: float32 [2, 4, 4], replicated, may hold values from -3 to 3
- left_live: int32 [8], replicated, may hold values from 1 to 4
- right_live: int32 [10], replicated, may hold values from 1 to 4
Outputs:
- next_vector: float32 [32, 1024, 1024], P(('left', 'right'))
- coefficients: float32 [2], replicated
All inputs are finite; a program needn't handle non-finite values.
Results may differ from a plain program's by a relative error of at most 0.0047.
Values may be sent and summed in bfloat16 or wider, within the bound.
No kernel may reach another device: no remote copies, remote signals or barrier semaphores. Data moves between devices by JAX's collectives and lax.ppermute only.
A program may use at most 64 MiB of HBM per device.

v0:
```python
import jax
import jax.numpy as jnp
from jax import lax
from jax.sharding import PartitionSpec as P

BLOCK = 256


def from_behind(block, axis, distance):
    devices = range(lax.axis_size(axis))
    route = [(i - distance, i) for i in devices if i - distance in devices]
    return lax.ppermute(block, axis, route)


def small_lookup(table, index):
    places = jnp.arange(table.shape[0], dtype=jnp.int32)
    return jnp.sum(jnp.where(places == index, table, jnp.zeros_like(table)))


def table_entry(table, row, column):
    rows = jnp.arange(table.shape[0], dtype=jnp.int32)[:, None]
    columns = jnp.arange(table.shape[1], dtype=jnp.int32)[None, :]
    return jnp.sum(jnp.where((rows == row) & (columns == column), table, jnp.zeros_like(table)))


def per_device(state, left_env, right_env, site_ops, left_live, right_live):
    pairs = site_ops.shape[1]
    sec_size = state.shape[1]
    block_size = BLOCK
    block_index = lax.axis_index("left") * lax.axis_size("right") + lax.axis_index("right")
    own_pair = block_index % pairs
    sector = block_index // pairs
    steps = (jnp.arange(pairs, dtype=jnp.int32) + 1) // 2
    own_step = small_lookup(steps, own_pair)
    positions = jnp.arange(sec_size, dtype=jnp.int32)
    row_mask = (positions < small_lookup(left_live, sector) * block_size).astype(jnp.float32)
    col_mask = (positions < small_lookup(right_live, sector + own_step) * block_size).astype(
        jnp.float32
    )
    live = row_mask[:, None] * col_mask[None, :]
    entries = float(
        state.shape[0] * sec_size * sec_size * lax.axis_size("left") * lax.axis_size("right")
    )
    masked = state[0] * live
    start_sum = lax.psum(jnp.sum(masked * masked), ("left", "right"))
    start_mean = start_sum / entries
    vector = masked / jnp.sqrt(start_mean + 1e-06)
    rounded = vector.astype(jnp.bfloat16)
    far_two = from_behind(rounded, ("left", "right"), 2)
    far_three = from_behind(rounded, ("left", "right"), 3)
    weights = []
    for offset in (2, 3):
        source_pair = (own_pair - offset) % pairs
        valid = block_index >= offset
        weights.append(
            jnp.where(
                valid, table_entry(site_ops[0], own_pair, source_pair), jnp.zeros((), jnp.float32)
            )
        )
    source = (
        weights[0] * far_two.astype(jnp.float32) + weights[1] * far_three.astype(jnp.float32)
    ).astype(jnp.bfloat16)
    part_zero = jnp.dot(source, right_env[0, 0], preferred_element_type=jnp.float32).astype(
        jnp.bfloat16
    )
    part_one = jnp.dot(rounded, right_env[1, 0], preferred_element_type=jnp.float32).astype(
        jnp.bfloat16
    )
    diag_weight = table_entry(site_ops[1], own_pair, own_pair)
    image = jnp.dot(left_env[0, 0], part_zero, preferred_element_type=jnp.float32)
    image = image + diag_weight * jnp.dot(
        left_env[1, 0], part_one, preferred_element_type=jnp.float32
    )
    image = image * live
    cross_sum, image_sum = lax.psum(
        (jnp.sum(vector * image), jnp.sum(image * image)), ("left", "right")
    )
    alpha_value = cross_sum / entries
    vector_mean = start_mean / (start_mean + 1e-06)
    residual_mean = image_sum / entries - alpha_value * alpha_value * (2.0 - vector_mean)
    residual = image - alpha_value * vector
    beta_value = jnp.sqrt(residual_mean + 1e-06)
    next_vector = residual / beta_value
    return (next_vector[None], jnp.stack([alpha_value, beta_value]))


def solution(mesh):
    in_specs = (
        P(("left", "right"), None, None),
        P(None, ("left", "right"), None, None),
        P(None, ("left", "right"), None, None),
        P(),
        P(),
        P(),
    )
    out_specs = (P(("left", "right"), None, None), P())
    return jax.shard_map(
        per_device, mesh=mesh, in_specs=in_specs, out_specs=out_specs, check_vma=False
    )
```

profile of v0, /device:TPU:0, one launch (start us, length us, event | category | flops | bytes accessed | tf_op | source)
XLA Modules:
  0.0 256.7 jit_solution(7007591481380401742)
XLA Ops:
  0.6 0.6 select_reduce_fusion
  1.9 1.3 fusion.36
  3.2 1.3 fusion.37
  5.8 5.3 %copy.8 = f32[1,1024,1024]{1,2,0:T(8,128)} copy(f32[1,1024,1024]{2,1,0:T(8,128)} %param.6) | data formatting | bytes 8388608 | tf_op args[0]
  11.2 4.1 %multiply_reduce_fusion.2 = f32[]{:T(128)} fusion(f32[1,1024,1024]{1,2,0:T(8,128)} %copy.8, f32[1024]{0:T(1024)S(1)} %get-tuple-element.13, f32[1024]{0:T(1024)S(1)} %get-tuple-element.12), kind=kLoop, calls=%fused_computation.7 | loop fusion | flops 4194303 | bytes 4202500 | tf_op jit(solution)/shard_map/reduce_sum | solution.py:45
  15.3 0.0 copy-start
  15.3 42.2 %psum.21 = f32[]{:T(128)} all-reduce(f32[]{:T(128)} %multiply_reduce_fusion.2), channel_id=1, replica_groups=mesh['left'=4,'right'=8] {'left','right'}, use_global_device_ids=true, to_apply=%region_5.6 | all-reduce | flops 1 | bytes 8 | tf_op jit(solution)/shard_map/psum | solution.py:45
  58.2 2.7 %fusion.38 = bf16[1024,1024]{0,1:T(8,128)(2,1)S(1)} fusion(f32[]{:T(128)S(6)} %sqrt.6, f32[1024]{0:T(1024)S(1)} %get-tuple-element.13, f32[1024]{0:T(1024)S(1)} %get-tuple-element.12, f32[1,1024,1024]{1,2,0:T(8,128)} %copy.8), kind=kLoop, calls=%fused_computation.50 | loop fusion | flops 4194304 | bytes 6299652 | tf_op jit(solution)/shard_map/convert_element_type | solution.py:48
  60.9 3.6 %collective-permute-start.1 = (bf16[1024,1024]{0,1:T(8,128)(2,1)S(1)}, bf16[1024,1024]{0,1:T(8,128)(2,1)}, u32[]{:S(2)}, u32[]{:S(2)}) collective-permute-start(bf16[1024,1024]{0,1:T(8,128)(2,1)S(1)} %fusion.38), channel_id=1, source_target_pairs={{0,3},{1,4},{2,5},{3,6},{4,7},{5,8},{6,9},{7,10},{8,11},{9,12},{10... | collective-permute-start | bytes 6291464 | tf_op jit(solution)/shard_map/ppermute | solution.py:12
  64.5 4.6 %collective-permute-start = (bf16[1024,1024]{0,1:T(8,128)(2,1)S(1)}, bf16[1024,1024]{0,1:T(8,128)(2,1)}, u32[]{:S(2)}, u32[]{:S(2)}) collective-permute-start(bf16[1024,1024]{0,1:T(8,128)(2,1)S(1)} %fusion.38), channel_id=1, source_target_pairs={{0,2},{1,3},{2,4},{3,5},{4,6},{5,7},{6,8},{7,9},{8,10},{9,11},{10,... | collective-permute-start | bytes 6291464 | tf_op jit(solution)/shard_map/ppermute | solution.py:12
  69.2 0.0 copy-done
  69.2 0.8 fusion.33
  71.2 36.4 %collective-permute-done.1 = bf16[1024,1024]{0,1:T(8,128)(2,1)} collective-permute-done((bf16[1024,1024]{0,1:T(8,128)(2,1)S(1)}, bf16[1024,1024]{0,1:T(8,128)(2,1)}, u32[]{:S(2)}, u32[]{:S(2)}) %collective-permute-start.1) | collective-permute-done | bytes 2097184 | tf_op jit(solution)/shard_map/ppermute | solution.py:12
  107.7 44.9 %collective-permute-done = bf16[1024,1024]{0,1:T(8,128)(2,1)} collective-permute-done((bf16[1024,1024]{0,1:T(8,128)(2,1)S(1)}, bf16[1024,1024]{0,1:T(8,128)(2,1)}, u32[]{:S(2)}, u32[]{:S(2)}) %collective-permute-start) | collective-permute-done | bytes 2097184 | tf_op jit(solution)/shard_map/ppermute | solution.py:12
  152.6 10.0 %fusion.6 = f32[1024,1024]{1,0:T(8,128)} fusion(bf16[2,1,1024,1024]{3,2,1,0:T(8,128)(2,1)} %param.7, bf16[1024,1024]{0,1:T(8,128)(2,1)} %collective-permute-done.1, bf16[1024,1024]{0,1:T(8,128)(2,1)} %collective-permute-done, bf16[2,1,1024,1024]{3,2,1,0:T(8,128)(2,1)} %param.8, f32[]{:T(128)S(6)} %select_n.63, f32[]{:T(128)S(6)} %select_n.55), kind=kOutput, calls=%fused_computation.14 | convolution fusion | flops 4302307328 | bytes 12582920 | tf_op jit(solution)/shard_map/dot_general | solution.py:70
  162.6 13.4 %multiply_reduce_fusion.1 = (f32[]{:T(128)}, f32[]{:T(128)}, f32[1024,1024]{0,1:T(8,128)}) fusion(f32[]{:T(128)S(6)} %sqrt.6, f32[1024]{0:T(1024)S(1)} %get-tuple-element.13, f32[1024]{0:T(1024)S(1)} %get-tuple-element.12, f32[1,1024,1024]{1,2,0:T(8,128)} %copy.8, f32[1024,1024]{1,0:T(8,128)} %fusion.6, bf16[2,1,1024,1024]{3,2,1,0:T(8,128)(2,1)} %param.7, ...), kind=kOutput, calls=%fused_computation.4 | convolution fusion | flops 4310695936 | bytes 20989448 | tf_op jit(solution)/shard_map/dot_general | solution.py:71
  176.0 65.5 %all-reduce = (f32[]{:T(128)}, f32[]{:T(128)}) all-reduce(f32[]{:T(128)} %get-tuple-element.5, f32[]{:T(128)} %get-tuple-element.4), channel_id=1, replica_groups=mesh['left'=4,'right'=8] {'left','right'}, use_global_device_ids=true, to_apply=%region_11.12 | all-reduce | flops 2 | bytes 16 | tf_op jit(solution)/shard_map/psum | solution.py:75
  244.4 6.4 %divide_bitcast_fusion = f32[1,1024,1024]{1,2,0:T(8,128)} fusion(f32[1024,1024]{0,1:T(8,128)} %get-tuple-element.11, f32[]{:T(128)} %sqrt.7, f32[]{:T(128)} %div.58, f32[]{:T(128)S(6)} %sqrt.6, f32[1024]{0:T(1024)S(1)} %get-tuple-element.13, f32[1024]{0:T(1024)S(1)} %get-tuple-element.12, f32[1,1024,1024]{1,2,0:T(8,128)} %copy.8), kind=kLoop, calls=%fused_computation.2 | loop fusion | flops 6291456 | bytes 12591116 | tf_op jit(solution)/shard_map/broadcast_in_dim | solution.py:84
  250.7 5.3 %copy.9 = f32[1,1024,1024]{2,1,0:T(8,128)} copy(f32[1,1024,1024]{1,2,0:T(8,128)} %divide_bitcast_fusion) | data formatting | bytes 8388608
  256.1 0.6 pad_maximum_fusion
  (3 shorter events, 0.0 us)
Async XLA Ops:
  15.3 53.9 %copy-start = (f32[2,4,4]{2,1,0:T(4,128)S(1)}, f32[2,4,4]{2,1,0:T(4,128)}, u32[]{:S(2)}) copy-start(f32[2,4,4]{2,1,0:T(4,128)} %param.9) | copy-start | bytes 388
  60.9 46.7 %collective-permute-start.1 = (bf16[1024,1024]{0,1:T(8,128)(2,1)S(1)}, bf16[1024,1024]{0,1:T(8,128)(2,1)}, u32[]{:S(2)}, u32[]{:S(2)}) collective-permute-start(bf16[1024,1024]{0,1:T(8,128)(2,1)S(1)} %fusion.38), channel_id=1, source_target_pairs={{0,3},{1,4},{2,5},{3,6},{4,7},{5,8},{6,9},{7,10},{8,11},{9,12},{10... | collective-permute-start | bytes 6291464 | tf_op jit(solution)/shard_map/ppermute | solution.py:12
  64.5 88.1 %collective-permute-start = (bf16[1024,1024]{0,1:T(8,128)(2,1)S(1)}, bf16[1024,1024]{0,1:T(8,128)(2,1)}, u32[]{:S(2)}, u32[]{:S(2)}) collective-permute-start(bf16[1024,1024]{0,1:T(8,128)(2,1)S(1)} %fusion.38), channel_id=1, source_target_pairs={{0,2},{1,3},{2,4},{3,5},{4,6},{5,7},{6,8},{7,9},{8,10},{9,11},{10,... | collective-permute-start | bytes 6291464 | tf_op jit(solution)/shard_map/ppermute | solution.py:12
where the time goes:
time: 258 us; the launch traced here: 257 us
  blocking collectives  108 us (42%)
  waiting for transfers between devices  81.4 us (32%)
  matrix products  23.4 us (9%)
  other arithmetic  17.8 us (7%)
  local copies, waits for them, and re-layouts  10.7 us (4%)
  starting transfers between devices  8.19 us (3%)
  between operations  7.42 us (3%)
    ppermute x2, waiting for transfers between devices, from_behind(): return lax.ppermute(block, axis, route)  81.4 us
    psum x1, blocking collectives, per_device(): lax.psum((jnp.sum(vector * image), jnp.sum(image * image)), ('left', 'rig...  65.5 us
    psum x1, blocking collectives, per_device(): start_sum = lax.psum(jnp.sum(masked * masked), ('left', 'right'))  42.2 us
    dot_general x1, matrix products, per_device(): jnp.dot(left_env[1, 0], part_one, preferred_element_type=jnp.float32)  13.4 us
    unnamed x4, local copies, waits for them, and re-layouts  10.7 us
    dot_general x1, matrix products, per_device(): jnp.dot(left_env[0, 0], part_zero, preferred_element_type=jnp.float32)  9.99 us
    ppermute x2, starting transfers between devices, from_behind(): return lax.ppermute(block, axis, route)  8.19 us
    broadcast_in_dim x1, other arithmetic, per_device(): return (next_vector[None], jnp.stack([alpha_value, beta_value]))  6.39 us
  transfers between devices with their start and end apart: 2, of which 2 were waited for; matrix products, arithmetic and copies ran while one was open for 0% of the time, Pallas kernels for 0%

commit v1 on v0

v1 whole, which is shorter than its diff:
```python
import jax
import jax.numpy as jnp
from jax import lax
from jax.sharding import PartitionSpec as P

BLOCK = 256
AXES = ("left", "right")
CHUNKS = 4


def shift_up(block, distance):
    devices = range(lax.axis_size(AXES))
    route = [(i - distance, i) for i in devices if i - distance in devices]
    return lax.ppermute(block, AXES, route)


def butterfly_sum(values):
    count = lax.axis_size(AXES)
    bit = 1
    while bit < count:
        route = [(i, i ^ bit) for i in range(count) if (i ^ bit) < count]
        values = values + lax.ppermute(values, AXES, route)
        bit *= 2
    return values


def small_lookup(table, index):
    places = jnp.arange(table.shape[0], dtype=jnp.int32)
    return jnp.sum(jnp.where(places == index, table, jnp.zeros_like(table)))


def table_entry(table, row, column):
    rows = jnp.arange(table.shape[0], dtype=jnp.int32)[:, None]
    columns = jnp.arange(table.shape[1], dtype=jnp.int32)[None, :]
    return jnp.sum(jnp.where((rows == row) & (columns == column), table, jnp.zeros_like(table)))


def per_device(state, left_env, right_env, site_ops, left_live, right_live):
    pairs = site_ops.shape[1]
    sec_size = state.shape[1]
    block_index = lax.axis_index("left") * lax.axis_size("right") + lax.axis_index("right")
    own_pair = block_index % pairs
    sector = block_index // pairs
    steps = (jnp.arange(pairs, dtype=jnp.int32) + 1) // 2
    own_step = small_lookup(steps, own_pair)
    positions = jnp.arange(sec_size, dtype=jnp.int32)
    row_mask = (positions < small_lookup(left_live, sector) * BLOCK).astype(jnp.float32)
    col_mask = (positions < small_lookup(right_live, sector + own_step) * BLOCK).astype(jnp.float32)
    live = row_mask[:, None] * col_mask[None, :]
    entries = float(state.shape[0] * sec_size * sec_size * lax.axis_size(AXES))

    masked = state[0] * live
    start_sum = butterfly_sum(jnp.sum(masked * masked))
    start_mean = start_sum / entries
    vector = masked / jnp.sqrt(start_mean + 1e-06)
    rounded = vector.astype(jnp.bfloat16)

    weights = []
    for offset in (2, 3):
        source_pair = (own_pair - offset) % pairs
        valid = block_index >= offset
        weights.append(
            jnp.where(
                valid, table_entry(site_ops[0], own_pair, source_pair), jnp.zeros((), jnp.float32)
            )
        )

    part_one = jnp.dot(rounded, right_env[1, 0], preferred_element_type=jnp.float32).astype(
        jnp.bfloat16
    )
    diag_weight = table_entry(site_ops[1], own_pair, own_pair)
    image = diag_weight * jnp.dot(left_env[1, 0], part_one, preferred_element_type=jnp.float32)

    rows = sec_size // CHUNKS
    for c in range(CHUNKS):
        piece = rounded[c * rows:(c + 1) * rows]
        far_two = shift_up(piece, 2)
        far_three = shift_up(far_two, 1)
        source = (
            weights[0] * far_two.astype(jnp.float32) + weights[1] * far_three.astype(jnp.float32)
        ).astype(jnp.bfloat16)
        part_zero = jnp.dot(source, right_env[0, 0], preferred_element_type=jnp.float32).astype(
            jnp.bfloat16
        )
        image = image + jnp.dot(
            left_env[0, 0][:, c * rows:(c + 1) * rows], part_zero, preferred_element_type=jnp.float32
        )
    image = image * live

    sums = butterfly_sum(jnp.stack([jnp.sum(vector * image), jnp.sum(image * image)]))
    alpha_value = sums[0] / entries
    vector_mean = start_mean / (start_mean + 1e-06)
    residual_mean = sums[1] / entries - alpha_value * alpha_value * (2.0 - vector_mean)
    residual = image - alpha_value * vector
    beta_value = jnp.sqrt(residual_mean + 1e-06)
    next_vector = residual / beta_value
    return (next_vector[None], jnp.stack([alpha_value, beta_value]))


def solution(mesh):
    in_specs = (
        P(AXES, None, None),
        P(None, AXES, None, None),
        P(None, AXES, None, None),
        P(),
        P(),
        P(),
    )
    out_specs = (P(AXES, None, None), P())
    return jax.shard_map(
        per_device, mesh=mesh, in_specs=in_specs, out_specs=out_specs, check_vma=False
    )
```

time: 258 us -> 176 us (0.68)
  blocking collectives: 108 us -> 0 us
  starting transfers between devices: 8.19 us -> 56.9 us
  waiting for transfers between devices: 81.4 us -> 34.1 us
  matrix products: 23.4 us -> 37.6 us
  other arithmetic: 17.8 us -> 21.8 us
  local copies, waits for them, and re-layouts: 10.7 us -> 14.3 us
  between operations: 7.42 us -> 10.9 us
    psum x2 -> x0, blocking collectives: 108 us -> none  [the longest x1 65.5 us: per_device(): lax.psum((jnp.sum(vector * image), jnp.sum(image * image)), ('left', 'rig...]
    ppermute x2 -> x18, starting transfers between devices: 8.19 us -> 56.9 us  [the longest x10 33.9 us: butterfly_sum(): values = values + lax.ppermute(values, AXES, route)]
    ppermute x2 -> x18, waiting for transfers between devices: 81.4 us -> 34.1 us  [the longest x8 25.2 us: shift_up(): return lax.ppermute(block, AXES, route)]
    dot_general x1 -> x4, matrix products: 9.99 us -> 20.9 us  [per_device(): jnp.dot(left_env[0, 0][:, c * rows:(c + 1) * rows], part_zero, preferred_...]
    dot_general x1, matrix products: 13.4 us -> 16.7 us  [per_device(): jnp.dot(left_env[1, 0], part_one, preferred_element_type=jnp.float32)]
    add x0 -> x5, other arithmetic: none -> 2.65 us  [butterfly_sum(): values = values + lax.ppermute(values, AXES, route)]
  transfers between devices with their start and end apart: 2 -> 18, of which waited for: 2 -> 14; matrix products, arithmetic and copies ran while one was open for 0% -> 10% of each run, Pallas kernels for 0% -> 0%
where the time goes in v1:
time: 176 us
  starting transfers between devices  56.9 us (32%)
  matrix products  37.6 us (21%)
  waiting for transfers between devices  34.1 us (19%)
  other arithmetic  21.8 us (12%)
  local copies, waits for them, and re-layouts  14.3 us (8%)
  between operations  10.9 us (6%)
    ppermute x10, starting transfers between devices, butterfly_sum(): values = values + lax.ppermute(values, AXES, route)  33.9 us
    ppermute x8, waiting for transfers between devices, shift_up(): return lax.ppermute(block, AXES, route)  25.2 us
    ppermute x8, starting transfers between devices, shift_up(): return lax.ppermute(block, AXES, route)  23 us
    dot_general x4, matrix products, per_device(): jnp.dot(left_env[0, 0][:, c * rows:(c + 1) * rows], part_zero, preferred_...  20.9 us
    dot_general x1, matrix products, per_device(): jnp.dot(left_env[1, 0], part_one, preferred_element_type=jnp.float32)  16.7 us
    unnamed x4, local copies, waits for them, and re-layouts  10.7 us
    ppermute x10, waiting for transfers between devices, butterfly_sum(): values = values + lax.ppermute(values, AXES, route)  8.92 us
    broadcast_in_dim x1, other arithmetic, per_device(): return (next_vector[None], jnp.stack([alpha_value, beta_value]))  6.34 us
  transfers between devices with their start and end apart: 18, of which 14 were waited for; matrix products, arithmetic and copies ran while one was open for 10% of the time, Pallas kernels for 0%

profile of v1, /device:TPU:0, one launch (start us, length us, event | category | flops | bytes accessed | tf_op | source)
XLA Modules:
  0.0 175.5 jit_solution(14689439851938538136)
XLA Ops:
  5.8 5.3 %copy.8 = f32[1,1024,1024]{1,2,0:T(8,128)} copy(f32[1,1024,1024]{2,1,0:T(8,128)} %param.6) | data formatting | bytes 8388608 | tf_op args[0]
  11.2 4.1 %multiply_reduce_fusion.2 = f32[]{:T(128)} fusion(f32[1,1024,1024]{1,2,0:T(8,128)} %copy.8, f32[1024]{0:T(1024)S(1)} %get-tuple-element.17, f32[1024]{0:T(1024)S(1)} %get-tuple-element.16), kind=kLoop, calls=%fused_computation.6 | loop fusion | flops 4194303 | bytes 4202500 | tf_op jit(solution)/shard_map/reduce_sum | solution.py:53
  18.1 4.2 %collective-permute-start.1 = (f32[]{:T(128)}, f32[]{:T(128)}, u32[]{:S(2)}, u32[]{:S(2)}) collective-permute-start(f32[]{:T(128)} %add.93), channel_id=1, source_target_pairs={{0,2},{1,3},{2,0},{3,1},{4,6},{5,7},{6,4},{7,5},{8,10},{9,11},{10,... | collective-permute-start | bytes 20 | tf_op jit(solution)/shard_map/ppermute | solution.py:22
  23.1 4.4 %collective-permute-start.2 = (f32[]{:T(128)}, f32[]{:T(128)}, u32[]{:S(2)}, u32[]{:S(2)}) collective-permute-start(f32[]{:T(128)} %add.94), channel_id=1, source_target_pairs={{0,4},{1,5},{2,6},{3,7},{4,0},{5,1},{6,2},{7,3},{8,12},{9,13},{10,... | collective-permute-start | bytes 20 | tf_op jit(solution)/shard_map/ppermute | solution.py:22
  28.4 3.2 %collective-permute-start.3 = (f32[]{:T(128)}, f32[]{:T(128)}, u32[]{:S(2)}, u32[]{:S(2)}) collective-permute-start(f32[]{:T(128)} %add.95), channel_id=1, source_target_pairs={{0,8},{1,9},{2,10},{3,11},{4,12},{5,13},{6,14},{7,15},{8,0},{9,1},... | collective-permute-start | bytes 20 | tf_op jit(solution)/shard_map/ppermute | solution.py:22
  32.7 3.2 %collective-permute-start.4 = (f32[]{:T(128)}, f32[]{:T(128)}, u32[]{:S(2)}, u32[]{:S(2)}) collective-permute-start(f32[]{:T(128)} %add.96), channel_id=1, source_target_pairs={{0,16},{1,17},{2,18},{3,19},{4,20},{5,21},{6,22},{7,23},{8,24},{9,... | collective-permute-start | bytes 20 | tf_op jit(solution)/shard_map/ppermute | solution.py:22
  37.0 2.7 %fusion.81 = bf16[1024,1024]{0,1:T(8,128)(2,1)S(1)} fusion(f32[]{:T(128)S(6)} %sqrt.6, f32[1024]{0:T(1024)S(1)} %get-tuple-element.17, f32[1024]{0:T(1024)S(1)} %get-tuple-element.16, f32[1,1024,1024]{1,2,0:T(8,128)} %copy.8), kind=kLoop, calls=%fused_computation.78 | loop fusion | flops 4194304 | bytes 6299652 | tf_op jit(solution)/shard_map/convert_element_type | solution.py:56
  40.9 3.8 %collective-permute-start.7 = (bf16[256,1024]{0,1:T(8,128)(2,1)S(1)}, bf16[256,1024]{0,1:T(8,128)(2,1)S(1)}, u32[]{:S(2)}, u32[]{:S(2)}) collective-permute-start(bf16[256,1024]{0,1:T(8,128)(2,1)S(1)} %get-tuple-element.12), channel_id=1, source_target_pairs={{0,2},{1,3},{2,4},{3,5},{4,6},{5,7},{6,8},{7,9},{8,10},{9,11},{10,... | collective-permute-start | bytes 1572872 | tf_op jit(solution)/shard_map/ppermute | solution.py:14
  44.8 4.3 %collective-permute-start.9 = (bf16[256,1024]{0,1:T(8,128)(2,1)}, bf16[256,1024]{0,1:T(8,128)(2,1)}, u32[]{:S(2)}, u32[]{:S(2)}) collective-permute-start(bf16[256,1024]{0,1:T(8,128)(2,1)} %get-tuple-element.11), channel_id=1, source_target_pairs={{0,2},{1,3},{2,4},{3,5},{4,6},{5,7},{6,8},{7,9},{8,10},{9,11},{10,... | collective-permute-start | bytes 1572872 | tf_op jit(solution)/shard_map/ppermute | solution.py:14
  51.8 3.9 %collective-permute-start.11 = (bf16[256,1024]{0,1:T(8,128)(2,1)}, bf16[256,1024]{0,1:T(8,128)(2,1)}, u32[]{:S(2)}, u32[]{:S(2)}) collective-permute-start(bf16[256,1024]{0,1:T(8,128)(2,1)} %get-tuple-element.10), channel_id=1, source_target_pairs={{0,2},{1,3},{2,4},{3,5},{4,6},{5,7},{6,8},{7,9},{8,10},{9,11},{10,... | collective-permute-start | bytes 1572872 | tf_op jit(solution)/shard_map/ppermute | solution.py:14
  61.0 7.5 %collective-permute-done.9 = bf16[256,1024]{0,1:T(8,128)(2,1)} collective-permute-done((bf16[256,1024]{0,1:T(8,128)(2,1)}, bf16[256,1024]{0,1:T(8,128)(2,1)}, u32[]{:S(2)}, u32[]{:S(2)}) %collective-permute-start.9) | collective-permute-done | bytes 524320 | tf_op jit(solution)/shard_map/ppermute | solution.py:14
  72.6 7.1 %collective-permute-done.5 = bf16[256,1024]{0,1:T(8,128)(2,1)S(1)} collective-permute-done((bf16[256,1024]{0,1:T(8,128)(2,1)}, bf16[256,1024]{0,1:T(8,128)(2,1)S(1)}, u32[]{:S(2)}, u32[]{:S(2)}) %collective-permute-start.5) | collective-permute-done | bytes 524320 | tf_op jit(solution)/shard_map/ppermute | solution.py:14
  81.8 9.2 %collective-permute-done.11 = bf16[256,1024]{0,1:T(8,128)(2,1)} collective-permute-done((bf16[256,1024]{0,1:T(8,128)(2,1)}, bf16[256,1024]{0,1:T(8,128)(2,1)}, u32[]{:S(2)}, u32[]{:S(2)}) %collective-permute-start.11) | collective-permute-done | bytes 524320 | tf_op jit(solution)/shard_map/ppermute | solution.py:14
  93.0 5.1 %fusion.49 = f32[1024,1024]{1,0:T(8,128)} fusion(bf16[2,1,1024,1024]{3,2,1,0:T(8,128)(2,1)} %param.8, bf16[256,1024]{0,1:T(8,128)(2,1)} %collective-permute-done.8, bf16[256,1024]{0,1:T(8,128)(2,1)S(1)} %collective-permute-done.7, bf16[1024,1024]{1,0:T(8,128)(2,1)S(1)} %slice_bitcast_fusion, f32[]{:T(128)S(6)} %select_n.64, f32[]{:T(128)S(6)} %select_n.61), kind=kOutput, calls=%fused_computation.36 | convolution fusion | flops 1075576832 | bytes 7864328 | tf_op jit(solution)/shard_map/dot_general | solution.py:85
  98.1 5.3 %fusion.46 = f32[1024,1024]{1,0:T(8,128)} fusion(bf16[2,1,1024,1024]{3,2,1,0:T(8,128)(2,1)} %param.8, bf16[256,1024]{0,1:T(8,128)(2,1)} %collective-permute-done.10, bf16[256,1024]{0,1:T(8,128)(2,1)} %collective-permute-done.9, bf16[1024,1024]{1,0:T(8,128)(2,1)S(1)} %slice_bitcast_fusion, f32[]{:T(128)S(6)} %select_n.64, f32[]{:T(128)S(6)} %select_n.61), kind=kOutput, calls=%fused_computation.35 | convolution fusion | flops 1075576832 | bytes 7864328 | tf_op jit(solution)/shard_map/dot_general | solution.py:85
  103.4 5.3 %fusion.43 = f32[1024,1024]{1,0:T(8,128)} fusion(bf16[2,1,1024,1024]{3,2,1,0:T(8,128)(2,1)} %param.8, bf16[256,1024]{0,1:T(8,128)(2,1)} %collective-permute-done.12, bf16[256,1024]{0,1:T(8,128)(2,1)} %collective-permute-done.11, bf16[1024,1024]{1,0:T(8,128)(2,1)S(1)} %slice_bitcast_fusion, f32[]{:T(128)S(6)} %select_n.64, f32[]{:T(128)S(6)} %select_n.61), kind=kOutput, calls=%fused_computation.34 | convolution fusion | flops 1075576832 | bytes 7864328 | tf_op jit(solution)/shard_map/dot_general | solution.py:85
  108.7 5.2 %fusion.52 = f32[1024,1024]{1,0:T(8,128)} fusion(bf16[2,1,1024,1024]{3,2,1,0:T(8,128)(2,1)} %param.8, bf16[256,1024]{0,1:T(8,128)(2,1)} %collective-permute-done.6, bf16[256,1024]{0,1:T(8,128)(2,1)S(1)} %collective-permute-done.5, bf16[1024,1024]{1,0:T(8,128)(2,1)S(1)} %slice_bitcast_fusion, f32[]{:T(128)S(6)} %select_n.64, f32[]{:T(128)S(6)} %select_n.61), kind=kOutput, calls=%fused_computation.37 | convolution fusion | flops 1075576832 | bytes 7864328 | tf_op jit(solution)/shard_map/dot_general | solution.py:85
  113.9 16.7 %multiply_reduce_fusion.1 = (f32[]{:T(128)}, f32[]{:T(128)}, f32[1024,1024]{0,1:T(8,128)}) fusion(f32[]{:T(128)S(6)} %sqrt.6, f32[1024]{0:T(1024)S(1)} %get-tuple-element.17, f32[1024]{0:T(1024)S(1)} %get-tuple-element.16, f32[1,1024,1024]{1,2,0:T(8,128)} %copy.8, f32[1024,1024]{1,0:T(8,128)} %fusion.43, f32[1024,1024]{1,0:T(8,128)} %fusion.46, ...), kind=kOutput, calls=%fused_computation.4 | convolution fusion | flops 4313841664 | bytes 33572360 | tf_op jit(solution)/shard_map/dot_general | solution.py:72
  131.9 5.3 %collective-permute-start.13 = (f32[2]{0:T(128)S(1)}, f32[2]{0:T(128)S(1)}, u32[]{:S(2)}, u32[]{:S(2)}) collective-permute-start(f32[2]{0:T(128)S(1)} %pad_maximum_fusion), channel_id=1, source_target_pairs={{0,1},{1,0},{2,3},{3,2},{4,5},{5,4},{6,7},{7,6},{8,9},{9,8},{10,11... | collective-permute-start | bytes 32 | tf_op jit(solution)/shard_map/ppermute | solution.py:22
  144.8 3.0 %collective-permute-start.15 = (f32[2]{0:T(128)S(1)}, f32[2]{0:T(128)S(1)}, u32[]{:S(2)}, u32[]{:S(2)}) collective-permute-start(f32[2]{0:T(128)S(1)} %fusion.89), channel_id=1, source_target_pairs={{0,4},{1,5},{2,6},{3,7},{4,0},{5,1},{6,2},{7,3},{8,12},{9,13},{10,... | collective-permute-start | bytes 32 | tf_op jit(solution)/shard_map/ppermute | solution.py:22
  149.4 4.5 %collective-permute-start.16 = (f32[2]{0:T(128)S(1)}, f32[2]{0:T(128)S(1)}, u32[]{:S(2)}, u32[]{:S(2)}) collective-permute-start(f32[2]{0:T(128)S(1)} %add.112), channel_id=1, source_target_pairs={{0,8},{1,9},{2,10},{3,11},{4,12},{5,13},{6,14},{7,15},{8,0},{9,1},... | collective-permute-start | bytes 32 | tf_op jit(solution)/shard_map/ppermute | solution.py:22
  155.4 3.0 %collective-permute-start.17 = (f32[2]{0:T(128)S(1)}, f32[2]{0:T(128)S(1)}, u32[]{:S(2)}, u32[]{:S(2)}) collective-permute-start(f32[2]{0:T(128)S(1)} %add.113), channel_id=1, source_target_pairs={{0,16},{1,17},{2,18},{3,19},{4,20},{5,21},{6,22},{7,23},{8,24},{9,... | collective-permute-start | bytes 32 | tf_op jit(solution)/shard_map/ppermute | solution.py:22
  163.3 6.3 %divide_bitcast_fusion = f32[1,1024,1024]{1,2,0:T(8,128)} fusion(f32[1024,1024]{0,1:T(8,128)} %get-tuple-element.15, f32[]{:T(128)} %sqrt.7, f32[]{:T(128)} %bitcast.11, f32[]{:T(128)S(6)} %sqrt.6, f32[1024]{0:T(1024)S(1)} %get-tuple-element.17, f32[1024]{0:T(1024)S(1)} %get-tuple-element.16, f32[1,1024,1024]{1,2,0:T(8,128)} %copy.8), kind=kLoop, calls=%fused_computation.2 | loop fusion | flops 6291456 | bytes 12591116 | tf_op jit(solution)/shard_map/broadcast_in_dim | solution.py:97
  169.6 5.3 %copy.9 = f32[1,1024,1024]{2,1,0:T(8,128)} copy(f32[1,1024,1024]{1,2,0:T(8,128)} %divide_bitcast_fusion) | data formatting | bytes 8388608
  (41 shorter events, 36.6 us)
Async XLA Ops:
  15.3 1.4 collective-permute-start
  18.1 4.4 %collective-permute-start.1 = (f32[]{:T(128)}, f32[]{:T(128)}, u32[]{:S(2)}, u32[]{:S(2)}) collective-permute-start(f32[]{:T(128)} %add.93), channel_id=1, source_target_pairs={{0,2},{1,3},{2,0},{3,1},{4,6},{5,7},{6,4},{7,5},{8,10},{9,11},{10,... | collective-permute-start | bytes 20 | tf_op jit(solution)/shard_map/ppermute | solution.py:22
  23.1 4.6 %collective-permute-start.2 = (f32[]{:T(128)}, f32[]{:T(128)}, u32[]{:S(2)}, u32[]{:S(2)}) collective-permute-start(f32[]{:T(128)} %add.94), channel_id=1, source_target_pairs={{0,4},{1,5},{2,6},{3,7},{4,0},{5,1},{6,2},{7,3},{8,12},{9,13},{10,... | collective-permute-start | bytes 20 | tf_op jit(solution)/shard_map/ppermute | solution.py:22
  28.4 3.6 %collective-permute-start.3 = (f32[]{:T(128)}, f32[]{:T(128)}, u32[]{:S(2)}, u32[]{:S(2)}) collective-permute-start(f32[]{:T(128)} %add.95), channel_id=1, source_target_pairs={{0,8},{1,9},{2,10},{3,11},{4,12},{5,13},{6,14},{7,15},{8,0},{9,1},... | collective-permute-start | bytes 20 | tf_op jit(solution)/shard_map/ppermute | solution.py:22
  32.7 3.6 %collective-permute-start.4 = (f32[]{:T(128)}, f32[]{:T(128)}, u32[]{:S(2)}, u32[]{:S(2)}) collective-permute-start(f32[]{:T(128)} %add.96), channel_id=1, source_target_pairs={{0,16},{1,17},{2,18},{3,19},{4,20},{5,21},{6,22},{7,23},{8,24},{9,... | collective-permute-start | bytes 20 | tf_op jit(solution)/shard_map/ppermute | solution.py:22
  39.7 30.8 %copy-start = (f32[2,4,4]{2,1,0:T(4,128)S(1)}, f32[2,4,4]{2,1,0:T(4,128)}, u32[]{:S(2)}) copy-start(f32[2,4,4]{2,1,0:T(4,128)} %param.9) | copy-start | bytes 388
  40.9 16.2 %collective-permute-start.7 = (bf16[256,1024]{0,1:T(8,128)(2,1)S(1)}, bf16[256,1024]{0,1:T(8,128)(2,1)S(1)}, u32[]{:S(2)}, u32[]{:S(2)}) collective-permute-start(bf16[256,1024]{0,1:T(8,128)(2,1)S(1)} %get-tuple-element.12), channel_id=1, source_target_pairs={{0,2},{1,3},{2,4},{3,5},{4,6},{5,7},{6,8},{7,9},{8,10},{9,11},{10,... | collective-permute-start | bytes 1572872 | tf_op jit(solution)/shard_map/ppermute | solution.py:14
  44.8 23.6 %collective-permute-start.9 = (bf16[256,1024]{0,1:T(8,128)(2,1)}, bf16[256,1024]{0,1:T(8,128)(2,1)}, u32[]{:S(2)}, u32[]{:S(2)}) collective-permute-start(bf16[256,1024]{0,1:T(8,128)(2,1)} %get-tuple-element.11), channel_id=1, source_target_pairs={{0,2},{1,3},{2,4},{3,5},{4,6},{5,7},{6,8},{7,9},{8,10},{9,11},{10,... | collective-permute-start | bytes 1572872 | tf_op jit(solution)/shard_map/ppermute | solution.py:14
  49.2 30.5 %collective-permute-start.5 = (bf16[256,1024]{0,1:T(8,128)(2,1)}, bf16[256,1024]{0,1:T(8,128)(2,1)S(1)}, u32[]{:S(2)}, u32[]{:S(2)}) collective-permute-start(bf16[256,1024]{0,1:T(8,128)(2,1)} %get-tuple-element.9), channel_id=1, source_target_pairs={{0,2},{1,3},{2,4},{3,5},{4,6},{5,7},{6,8},{7,9},{8,10},{9,11},{10,... | collective-permute-start | bytes 1572872 | tf_op jit(solution)/shard_map/ppermute | solution.py:14
  51.8 39.1 %collective-permute-start.11 = (bf16[256,1024]{0,1:T(8,128)(2,1)}, bf16[256,1024]{0,1:T(8,128)(2,1)}, u32[]{:S(2)}, u32[]{:S(2)}) collective-permute-start(bf16[256,1024]{0,1:T(8,128)(2,1)} %get-tuple-element.10), channel_id=1, source_target_pairs={{0,2},{1,3},{2,4},{3,5},{4,6},{5,7},{6,8},{7,9},{8,10},{9,11},{10,... | collective-permute-start | bytes 1572872 | tf_op jit(solution)/shard_map/ppermute | solution.py:14
  57.1 35.9 %collective-permute-start.8 = (bf16[256,1024]{0,1:T(8,128)(2,1)S(1)}, bf16[256,1024]{0,1:T(8,128)(2,1)}, u32[]{:S(2)}, u32[]{:S(2)}) collective-permute-start(bf16[256,1024]{0,1:T(8,128)(2,1)S(1)} %collective-permute-done.7), channel_id=1, source_target_pairs={{0,1},{1,2},{2,3},{3,4},{4,5},{5,6},{6,7},{7,8},{8,9},{9,10},{10,1... | collective-permute-start | bytes 1572872 | tf_op jit(solution)/shard_map/ppermute | solution.py:14
  68.4 29.7 %collective-permute-start.10 = (bf16[256,1024]{0,1:T(8,128)(2,1)}, bf16[256,1024]{0,1:T(8,128)(2,1)}, u32[]{:S(2)}, u32[]{:S(2)}) collective-permute-start(bf16[256,1024]{0,1:T(8,128)(2,1)} %collective-permute-done.9), channel_id=1, source_target_pairs={{0,1},{1,2},{2,3},{3,4},{4,5},{5,6},{6,7},{7,8},{8,9},{9,10},{10,1... | collective-permute-start | bytes 1572872 | tf_op jit(solution)/shard_map/ppermute | solution.py:14
  79.7 29.1 %collective-permute-start.6 = (bf16[256,1024]{0,1:T(8,128)(2,1)S(1)}, bf16[256,1024]{0,1:T(8,128)(2,1)}, u32[]{:S(2)}, u32[]{:S(2)}) collective-permute-start(bf16[256,1024]{0,1:T(8,128)(2,1)S(1)} %collective-permute-done.5), channel_id=1, source_target_pairs={{0,1},{1,2},{2,3},{3,4},{4,5},{5,6},{6,7},{7,8},{8,9},{9,10},{10,1... | collective-permute-start | bytes 1572872 | tf_op jit(solution)/shard_map/ppermute | solution.py:14
  90.9 12.5 %collective-permute-start.12 = (bf16[256,1024]{0,1:T(8,128)(2,1)}, bf16[256,1024]{0,1:T(8,128)(2,1)}, u32[]{:S(2)}, u32[]{:S(2)}) collective-permute-start(bf16[256,1024]{0,1:T(8,128)(2,1)} %collective-permute-done.11), channel_id=1, source_target_pairs={{0,1},{1,2},{2,3},{3,4},{4,5},{5,6},{6,7},{7,8},{8,9},{9,10},{10,1... | collective-permute-start | bytes 1572872 | tf_op jit(solution)/shard_map/ppermute | solution.py:14
  131.9 6.1 %collective-permute-start.13 = (f32[2]{0:T(128)S(1)}, f32[2]{0:T(128)S(1)}, u32[]{:S(2)}, u32[]{:S(2)}) collective-permute-start(f32[2]{0:T(128)S(1)} %pad_maximum_fusion), channel_id=1, source_target_pairs={{0,1},{1,0},{2,3},{3,2},{4,5},{5,4},{6,7},{7,6},{8,9},{9,8},{10,11... | collective-permute-start | bytes 32 | tf_op jit(solution)/shard_map/ppermute | solution.py:22
  139.3 4.2 %collective-permute-start.14 = (f32[2]{0:T(128)S(1)}, f32[2]{0:T(128)S(1)}, u32[]{:S(2)}, u32[]{:S(2)}) collective-permute-start(f32[2]{0:T(128)S(1)} %fusion.88), channel_id=1, source_target_pairs={{0,2},{1,3},{2,0},{3,1},{4,6},{5,7},{6,4},{7,5},{8,10},{9,11},{10,... | collective-permute-start | bytes 32 | tf_op jit(solution)/shard_map/ppermute | solution.py:22
  144.8 4.6 %collective-permute-start.15 = (f32[2]{0:T(128)S(1)}, f32[2]{0:T(128)S(1)}, u32[]{:S(2)}, u32[]{:S(2)}) collective-permute-start(f32[2]{0:T(128)S(1)} %fusion.89), channel_id=1, source_target_pairs={{0,4},{1,5},{2,6},{3,7},{4,0},{5,1},{6,2},{7,3},{8,12},{9,13},{10,... | collective-permute-start | bytes 32 | tf_op jit(solution)/shard_map/ppermute | solution.py:22
  149.4 6.0 %collective-permute-start.16 = (f32[2]{0:T(128)S(1)}, f32[2]{0:T(128)S(1)}, u32[]{:S(2)}, u32[]{:S(2)}) collective-permute-start(f32[2]{0:T(128)S(1)} %add.112), channel_id=1, source_target_pairs={{0,8},{1,9},{2,10},{3,11},{4,12},{5,13},{6,14},{7,15},{8,0},{9,1},... | collective-permute-start | bytes 32 | tf_op jit(solution)/shard_map/ppermute | solution.py:22
  155.4 4.5 %collective-permute-start.17 = (f32[2]{0:T(128)S(1)}, f32[2]{0:T(128)S(1)}, u32[]{:S(2)}, u32[]{:S(2)}) collective-permute-start(f32[2]{0:T(128)S(1)} %add.113), channel_id=1, source_target_pairs={{0,16},{1,17},{2,18},{3,19},{4,20},{5,21},{6,22},{7,23},{8,24},{9,... | collective-permute-start | bytes 32 | tf_op jit(solution)/shard_map/ppermute | solution.py:22

commit v2 on v1

--- a/solution.py
+++ b/solution.py
@@ -2,6 +2,7 @@
 import jax.numpy as jnp
 from jax import lax
 from jax.sharding import PartitionSpec as P
+from jax.experimental.layout import Layout, with_layout_constraint
 
 BLOCK = 256
 AXES = ("left", "right")
@@ -22,6 +23,10 @@
         values = values + lax.ppermute(values, AXES, route)
         bit *= 2
     return values
+
+
+def row_major(array):
+    return with_layout_constraint(array, Layout(major_to_minor=tuple(range(array.ndim))))
 
 
 def small_lookup(table, index):
@@ -53,7 +58,7 @@
     start_sum = butterfly_sum(jnp.sum(masked * masked))
     start_mean = start_sum / entries
     vector = masked / jnp.sqrt(start_mean + 1e-06)
-    rounded = vector.astype(jnp.bfloat16)
+    rounded = row_major(vector.astype(jnp.bfloat16))
 
     weights = []
     for offset in (2, 3):
@@ -69,12 +74,14 @@
         jnp.bfloat16
     )
     diag_weight = table_entry(site_ops[1], own_pair, own_pair)
-    image = diag_weight * jnp.dot(left_env[1, 0], part_one, preferred_element_type=jnp.float32)
+    image_one = diag_weight * jnp.dot(left_env[1, 0], part_one, preferred_element_type=jnp.float32)
 
     rows = sec_size // CHUNKS
+    pieces = [rounded[c * rows:(c + 1) * rows] for c in range(CHUNKS)]
+    image_one, pieces[-1] = lax.optimization_barrier((image_one, pieces[-1]))
+    image = image_one
     for c in range(CHUNKS):
-        piece = rounded[c * rows:(c + 1) * rows]
-        far_two = shift_up(piece, 2)
+        far_two = shift_up(pieces[c], 2)
         far_three = shift_up(far_two, 1)
         source = (
             weights[0] * far_two.astype(jnp.float32) + weights[1] * far_three.astype(jnp.float32)
@@ -85,7 +92,7 @@
         image = image + jnp.dot(
             left_env[0, 0][:, c * rows:(c + 1) * rows], part_zero, preferred_element_type=jnp.float32
         )
-    image = image * live
+    image = row_major(image * live)
 
     sums = butterfly_sum(jnp.stack([jnp.sum(vector * image), jnp.sum(image * image)]))
     alpha_value = sums[0] / entries

time: 176 us -> 152 us (0.86)
  local copies, waits for them, and re-layouts: 14.3 us -> 3.7 us
  waiting for transfers between devices: 34.1 us -> 24.6 us
  starting transfers between devices: 56.9 us -> 55 us
    unnamed x4 -> x2, local copies, waits for them, and re-layouts: 10.7 us -> 0.01 us
    ppermute x8, waiting for transfers between devices: 25.2 us -> 15 us  [shift_up(): return lax.ppermute(block, AXES, route)]
    dot_general x1, matrix products: 16.7 us -> 9.28 us  [per_device(): jnp.dot(left_env[1, 0], part_one, preferred_element_type=jnp.float32)]
    ppermute x10, starting transfers between devices: 33.9 us -> 27.5 us  [butterfly_sum(): values = values + lax.ppermute(values, AXES, route)]
    dot_general x4, matrix products: 20.9 us -> 26.7 us  [per_device(): jnp.dot(left_env[0, 0][:, c * rows:(c + 1) * rows], part_zero, preferred_...]
    ppermute x8, starting transfers between devices: 23 us -> 27.5 us  [shift_up(): return lax.ppermute(block, AXES, route)]
  transfers between devices with their start and end apart: 18 -> 18, of which waited for: 14 -> 11; matrix products, arithmetic and copies ran while one was open for 10% -> 18% of each run, Pallas kernels for 0% -> 0%
where the time goes in v2:
time: 152 us
  starting transfers between devices  55 us (36%)
  matrix products  36 us (24%)
  waiting for transfers between devices  24.6 us (16%)
  other arithmetic  21.7 us (14%)
  between operations  10.7 us (7%)
  local copies, waits for them, and re-layouts  3.7 us (2%)
    ppermute x10, starting transfers between devices, butterfly_sum(): values = values + lax.ppermute(values, AXES, route)  27.5 us
    ppermute x8, starting transfers between devices, shift_up(): return lax.ppermute(block, AXES, route)  27.5 us
    dot_general x4, matrix products, per_device(): jnp.dot(left_env[0, 0][:, c * rows:(c + 1) * rows], part_zero, preferred_...  26.7 us
    ppermute x8, waiting for transfers between devices, shift_up(): return lax.ppermute(block, AXES, route)  15 us
    ppermute x10, waiting for transfers between devices, butterfly_sum(): values = values + lax.ppermute(values, AXES, route)  9.55 us
    dot_general x1, matrix products, per_device(): jnp.dot(left_env[1, 0], part_one, preferred_element_type=jnp.float32)  9.28 us
    broadcast_in_dim x1, other arithmetic, per_device(): return (next_vector[None], jnp.stack([alpha_value, beta_value]))  6.43 us
    reduce_sum x1, other arithmetic, per_device(): start_sum = butterfly_sum(jnp.sum(masked * masked))  4.14 us
  transfers between devices with their start and end apart: 18, of which 11 were waited for; matrix products, arithmetic and copies ran while one was open for 18% of the time, Pallas kernels for 0%

profile of v2, /device:TPU:0, one launch (start us, length us, event | category | flops | bytes accessed | tf_op | source)
XLA Modules:
  0.0 151.7 jit_solution(9762064491482846518)
XLA Ops:
  5.8 4.1 %multiply_reduce_fusion.2 = f32[]{:T(128)} fusion(f32[1,1024,1024]{2,1,0:T(8,128)} %param.6, f32[1024]{0:T(1024)S(1)} %get-tuple-element.19, f32[1024]{0:T(1024)S(1)} %get-tuple-element.18), kind=kLoop, calls=%fused_computation.10 | loop fusion | flops 4194303 | bytes 4202500 | tf_op jit(solution)/shard_map/reduce_sum | solution.py:58
  12.7 4.2 %collective-permute-start.1 = (f32[]{:T(128)}, f32[]{:T(128)}, u32[]{:S(2)}, u32[]{:S(2)}) collective-permute-start(f32[]{:T(128)} %add.88), channel_id=1, source_target_pairs={{0,2},{1,3},{2,0},{3,1},{4,6},{5,7},{6,4},{7,5},{8,10},{9,11},{10,... | collective-permute-start | bytes 20 | tf_op jit(solution)/shard_map/ppermute | solution.py:23
  17.8 4.4 %collective-permute-start.2 = (f32[]{:T(128)}, f32[]{:T(128)}, u32[]{:S(2)}, u32[]{:S(2)}) collective-permute-start(f32[]{:T(128)} %add.89), channel_id=1, source_target_pairs={{0,4},{1,5},{2,6},{3,7},{4,0},{5,1},{6,2},{7,3},{8,12},{9,13},{10,... | collective-permute-start | bytes 20 | tf_op jit(solution)/shard_map/ppermute | solution.py:23
  23.1 3.2 %collective-permute-start.3 = (f32[]{:T(128)}, f32[]{:T(128)}, u32[]{:S(2)}, u32[]{:S(2)}) collective-permute-start(f32[]{:T(128)} %add.90), channel_id=1, source_target_pairs={{0,8},{1,9},{2,10},{3,11},{4,12},{5,13},{6,14},{7,15},{8,0},{9,1},... | collective-permute-start | bytes 20 | tf_op jit(solution)/shard_map/ppermute | solution.py:23
  27.3 3.2 %collective-permute-start.4 = (f32[]{:T(128)}, f32[]{:T(128)}, u32[]{:S(2)}, u32[]{:S(2)}) collective-permute-start(f32[]{:T(128)} %add.91), channel_id=1, source_target_pairs={{0,16},{1,17},{2,18},{3,19},{4,20},{5,21},{6,22},{7,23},{8,24},{9,... | collective-permute-start | bytes 20 | tf_op jit(solution)/shard_map/ppermute | solution.py:23
  31.6 2.7 %fusion.73 = bf16[1024,1024]{1,0:T(8,128)(2,1)S(1)} fusion(f32[]{:T(128)S(6)} %sqrt.6, f32[1024]{0:T(1024)S(1)} %get-tuple-element.19, f32[1024]{0:T(1024)S(1)} %get-tuple-element.18, f32[1,1024,1024]{2,1,0:T(8,128)} %param.6), kind=kLoop, calls=%fused_computation.78 | loop fusion | flops 4194304 | bytes 6299652 | tf_op jit(solution)/shard_map/convert_element_type | solution.py:61
  35.7 3.8 %collective-permute-start.5 = (bf16[256,1024]{1,0:T(8,128)(2,1)}, bf16[256,1024]{1,0:T(8,128)(2,1)S(1)}, u32[]{:S(2)}, u32[]{:S(2)}) collective-permute-start(bf16[256,1024]{1,0:T(8,128)(2,1)} %get-tuple-element.11), channel_id=1, source_target_pairs={{0,2},{1,3},{2,4},{3,5},{4,6},{5,7},{6,8},{7,9},{8,10},{9,11},{10,... | collective-permute-start | bytes 1572872 | tf_op jit(solution)/shard_map/ppermute | solution.py:15
  39.6 3.5 %collective-permute-start.7 = (bf16[256,1024]{1,0:T(8,128)(2,1)}, bf16[256,1024]{1,0:T(8,128)(2,1)S(1)}, u32[]{:S(2)}, u32[]{:S(2)}) collective-permute-start(bf16[256,1024]{1,0:T(8,128)(2,1)} %get-tuple-element.12), channel_id=1, source_target_pairs={{0,2},{1,3},{2,4},{3,5},{4,6},{5,7},{6,8},{7,9},{8,10},{9,11},{10,... | collective-permute-start | bytes 1572872 | tf_op jit(solution)/shard_map/ppermute | solution.py:15
  43.1 4.3 %collective-permute-start.9 = (bf16[256,1024]{1,0:T(8,128)(2,1)}, bf16[256,1024]{1,0:T(8,128)(2,1)}, u32[]{:S(2)}, u32[]{:S(2)}) collective-permute-start(bf16[256,1024]{1,0:T(8,128)(2,1)} %get-tuple-element.14), channel_id=1, source_target_pairs={{0,2},{1,3},{2,4},{3,5},{4,6},{5,7},{6,8},{7,9},{8,10},{9,11},{10,... | collective-permute-start | bytes 1572872 | tf_op jit(solution)/shard_map/ppermute | solution.py:15
  47.3 9.3 %multiply_bitcast_fusion = f32[1024,1024]{1,0:T(8,128)} fusion(bf16[2,1,1024,1024]{3,2,1,0:T(8,128)(2,1)} %param.7, f32[]{:T(128)} %get-tuple-element.8, bf16[1024,1024]{1,0:T(8,128)(2,1)S(1)} %fusion.73, bf16[2,1,1024,1024]{3,2,1,0:T(8,128)(2,1)} %param.8), kind=kOutput, calls=%fused_computation.9 | convolution fusion | flops 4297064448 | bytes 10486272 | tf_op jit(solution)/shard_map/dot_general | solution.py:77
  56.6 3.1 %collective-permute-start.11 = (bf16[256,1024]{1,0:T(8,128)(2,1)}, bf16[256,1024]{1,0:T(8,128)(2,1)}, u32[]{:S(2)}, u32[]{:S(2)}) collective-permute-start(bf16[256,1024]{1,0:T(8,128)(2,1)} %get-tuple-element.5), channel_id=1, source_target_pairs={{0,2},{1,3},{2,4},{3,5},{4,6},{5,7},{6,8},{7,9},{8,10},{9,11},{10,... | collective-permute-start | bytes 1572872 | tf_op jit(solution)/shard_map/ppermute | solution.py:15
  59.7 15.0 %collective-permute-done.9 = bf16[256,1024]{1,0:T(8,128)(2,1)} collective-permute-done((bf16[256,1024]{1,0:T(8,128)(2,1)}, bf16[256,1024]{1,0:T(8,128)(2,1)}, u32[]{:S(2)}, u32[]{:S(2)}) %collective-permute-start.9) | collective-permute-done | bytes 524320 | tf_op jit(solution)/shard_map/ppermute | solution.py:15
  74.7 2.1 %collective-permute-start.10 = (bf16[256,1024]{1,0:T(8,128)(2,1)}, bf16[256,1024]{1,0:T(8,128)(2,1)}, u32[]{:S(2)}, u32[]{:S(2)}) collective-permute-start(bf16[256,1024]{1,0:T(8,128)(2,1)} %collective-permute-done.9), channel_id=1, source_target_pairs={{0,1},{1,2},{2,3},{3,4},{4,5},{5,6},{6,7},{7,8},{8,9},{9,10},{10,1... | collective-permute-start | bytes 1572872 | tf_op jit(solution)/shard_map/ppermute | solution.py:15
  76.8 5.2 %collective-permute-start.8 = (bf16[256,1024]{1,0:T(8,128)(2,1)S(1)}, bf16[256,1024]{1,0:T(8,128)(2,1)}, u32[]{:S(2)}, u32[]{:S(2)}) collective-permute-start(bf16[256,1024]{1,0:T(8,128)(2,1)S(1)} %collective-permute-done.7), channel_id=1, source_target_pairs={{0,1},{1,2},{2,3},{3,4},{4,5},{5,6},{6,7},{7,8},{8,9},{9,10},{10,1... | collective-permute-start | bytes 1572872 | tf_op jit(solution)/shard_map/ppermute | solution.py:15
  87.1 3.5 %collective-permute-start.12 = (bf16[256,1024]{1,0:T(8,128)(2,1)}, bf16[256,1024]{1,0:T(8,128)(2,1)}, u32[]{:S(2)}, u32[]{:S(2)}) collective-permute-start(bf16[256,1024]{1,0:T(8,128)(2,1)} %collective-permute-done.11), channel_id=1, source_target_pairs={{0,1},{1,2},{2,3},{3,4},{4,5},{5,6},{6,7},{7,8},{8,9},{9,10},{10,1... | collective-permute-start | bytes 1572872 | tf_op jit(solution)/shard_map/ppermute | solution.py:15
  90.5 5.2 %fusion.32 = f32[1024,1024]{0,1:T(8,128)} fusion(bf16[2,1,1024,1024]{3,2,1,0:T(8,128)(2,1)} %param.8, bf16[256,1024]{1,0:T(8,128)(2,1)} %collective-permute-done.10, bf16[256,1024]{1,0:T(8,128)(2,1)} %collective-permute-done.9, bf16[1024,1024]{1,0:T(8,128)(2,1)S(1)} %slice_bitcast_fusion, f32[]{:T(128)S(6)} %select_n.64, f32[]{:T(128)S(6)} %select_n.61), kind=kOutput, calls=%fused_computation.35 | convolution fusion | flops 1075576832 | bytes 7864328 | tf_op jit(solution)/shard_map/dot_general | solution.py:92
  95.8 5.0 %fusion.35 = f32[1024,1024]{0,1:T(8,128)} fusion(bf16[2,1,1024,1024]{3,2,1,0:T(8,128)(2,1)} %param.8, bf16[256,1024]{1,0:T(8,128)(2,1)} %collective-permute-done.8, bf16[256,1024]{1,0:T(8,128)(2,1)S(1)} %collective-permute-done.7, bf16[1024,1024]{1,0:T(8,128)(2,1)S(1)} %slice_bitcast_fusion, f32[]{:T(128)S(6)} %select_n.64, f32[]{:T(128)S(6)} %select_n.61), kind=kOutput, calls=%fused_computation.36 | convolution fusion | flops 1075576832 | bytes 7864328 | tf_op jit(solution)/shard_map/dot_general | solution.py:92
  100.8 5.0 %fusion.38 = f32[1024,1024]{0,1:T(8,128)} fusion(bf16[2,1,1024,1024]{3,2,1,0:T(8,128)(2,1)} %param.8, bf16[256,1024]{1,0:T(8,128)(2,1)} %collective-permute-done.6, bf16[256,1024]{1,0:T(8,128)(2,1)S(1)} %collective-permute-done.5, bf16[1024,1024]{1,0:T(8,128)(2,1)S(1)} %slice_bitcast_fusion, f32[]{:T(128)S(6)} %select_n.64, f32[]{:T(128)S(6)} %select_n.61), kind=kOutput, calls=%fused_computation.37 | convolution fusion | flops 1075576832 | bytes 7864328 | tf_op jit(solution)/shard_map/dot_general | solution.py:92
  105.8 11.5 %multiply_reduce_fusion.1 = (f32[]{:T(128)}, f32[]{:T(128)}, f32[1024,1024]{1,0:T(8,128)}) fusion(f32[]{:T(128)S(6)} %sqrt.6, f32[1024]{0:T(1024)S(1)} %get-tuple-element.19, f32[1024]{0:T(1024)S(1)} %get-tuple-element.18, f32[1,1024,1024]{2,1,0:T(8,128)} %param.6, bf16[2,1,1024,1024]{3,2,1,0:T(8,128)(2,1)} %param.8, ...), kind=kOutput, calls=%fused_computation.8 | convolution fusion | flops 1088159744 | bytes 28844052 | tf_op jit(solution)/shard_map/dot_general | solution.py:92
  121.9 2.6 %collective-permute-done.14 = f32[2]{0:T(128)S(1)} collective-permute-done((f32[2]{0:T(128)S(1)}, f32[2]{0:T(128)S(1)}, u32[]{:S(2)}, u32[]{:S(2)}) %collective-permute-start.14) | collective-permute-done | bytes 40 | tf_op jit(solution)/shard_map/ppermute | solution.py:23
  125.8 4.2 %collective-permute-start.15 = (f32[2]{0:T(128)S(1)}, f32[2]{0:T(128)S(1)}, u32[]{:S(2)}, u32[]{:S(2)}) collective-permute-start(f32[2]{0:T(128)S(1)} %fusion.80), channel_id=1, source_target_pairs={{0,4},{1,5},{2,6},{3,7},{4,0},{5,1},{6,2},{7,3},{8,12},{9,13},{10,... | collective-permute-start | bytes 32 | tf_op jit(solution)/shard_map/ppermute | solution.py:23
  131.5 3.1 %collective-permute-start.16 = (f32[2]{0:T(128)S(1)}, f32[2]{0:T(128)S(1)}, u32[]{:S(2)}, u32[]{:S(2)}) collective-permute-start(f32[2]{0:T(128)S(1)} %add.106), channel_id=1, source_target_pairs={{0,8},{1,9},{2,10},{3,11},{4,12},{5,13},{6,14},{7,15},{8,0},{9,1},... | collective-permute-start | bytes 32 | tf_op jit(solution)/shard_map/ppermute | solution.py:23
  136.1 3.8 %collective-permute-start.17 = (f32[2]{0:T(128)S(1)}, f32[2]{0:T(128)S(1)}, u32[]{:S(2)}, u32[]{:S(2)}) collective-permute-start(f32[2]{0:T(128)S(1)} %add.107), channel_id=1, source_target_pairs={{0,16},{1,17},{2,18},{3,19},{4,20},{5,21},{6,22},{7,23},{8,24},{9,... | collective-permute-start | bytes 32 | tf_op jit(solution)/shard_map/ppermute | solution.py:23
  145.2 6.4 %divide_bitcast_fusion = f32[1,1024,1024]{2,1,0:T(8,128)} fusion(f32[1024,1024]{1,0:T(8,128)} %get-tuple-element.17, f32[]{:T(128)} %sqrt.7, f32[]{:T(128)} %bitcast.14, f32[]{:T(128)S(6)} %sqrt.6, f32[1024]{0:T(1024)S(1)} %get-tuple-element.19, f32[1024]{0:T(1024)S(1)} %get-tuple-element.18, f32[1,1024,1024]{2,1,0:T(8,128)} %param.6), kind=kLoop, calls=%fused_computation.6 | loop fusion | flops 6291456 | bytes 12591116 | tf_op jit(solution)/shard_map/broadcast_in_dim | solution.py:104
  (39 shorter events, 22.6 us)
Async XLA Ops:
  0.6 9.8 %copy-start = (f32[2,4,4]{2,1,0:T(4,128)S(1)}, f32[2,4,4]{2,1,0:T(4,128)}, u32[]{:S(2)}) copy-start(f32[2,4,4]{2,1,0:T(4,128)} %param.9) | copy-start | bytes 388
  10.0 1.4 collective-permute-start
  12.7 4.4 %collective-permute-start.1 = (f32[]{:T(128)}, f32[]{:T(128)}, u32[]{:S(2)}, u32[]{:S(2)}) collective-permute-start(f32[]{:T(128)} %add.88), channel_id=1, source_target_pairs={{0,2},{1,3},{2,0},{3,1},{4,6},{5,7},{6,4},{7,5},{8,10},{9,11},{10,... | collective-permute-start | bytes 20 | tf_op jit(solution)/shard_map/ppermute | solution.py:23
  17.8 4.6 %collective-permute-start.2 = (f32[]{:T(128)}, f32[]{:T(128)}, u32[]{:S(2)}, u32[]{:S(2)}) collective-permute-start(f32[]{:T(128)} %add.89), channel_id=1, source_target_pairs={{0,4},{1,5},{2,6},{3,7},{4,0},{5,1},{6,2},{7,3},{8,12},{9,13},{10,... | collective-permute-start | bytes 20 | tf_op jit(solution)/shard_map/ppermute | solution.py:23
  23.1 3.6 %collective-permute-start.3 = (f32[]{:T(128)}, f32[]{:T(128)}, u32[]{:S(2)}, u32[]{:S(2)}) collective-permute-start(f32[]{:T(128)} %add.90), channel_id=1, source_target_pairs={{0,8},{1,9},{2,10},{3,11},{4,12},{5,13},{6,14},{7,15},{8,0},{9,1},... | collective-permute-start | bytes 20 | tf_op jit(solution)/shard_map/ppermute | solution.py:23
  27.3 3.6 %collective-permute-start.4 = (f32[]{:T(128)}, f32[]{:T(128)}, u32[]{:S(2)}, u32[]{:S(2)}) collective-permute-start(f32[]{:T(128)} %add.91), channel_id=1, source_target_pairs={{0,16},{1,17},{2,18},{3,19},{4,20},{5,21},{6,22},{7,23},{8,24},{9,... | collective-permute-start | bytes 20 | tf_op jit(solution)/shard_map/ppermute | solution.py:23
  35.7 49.3 %collective-permute-start.5 = (bf16[256,1024]{1,0:T(8,128)(2,1)}, bf16[256,1024]{1,0:T(8,128)(2,1)S(1)}, u32[]{:S(2)}, u32[]{:S(2)}) collective-permute-start(bf16[256,1024]{1,0:T(8,128)(2,1)} %get-tuple-element.11), channel_id=1, source_target_pairs={{0,2},{1,3},{2,4},{3,5},{4,6},{5,7},{6,8},{7,9},{8,10},{9,11},{10,... | collective-permute-start | bytes 1572872 | tf_op jit(solution)/shard_map/ppermute | solution.py:15
  39.6 37.2 %collective-permute-start.7 = (bf16[256,1024]{1,0:T(8,128)(2,1)}, bf16[256,1024]{1,0:T(8,128)(2,1)S(1)}, u32[]{:S(2)}, u32[]{:S(2)}) collective-permute-start(bf16[256,1024]{1,0:T(8,128)(2,1)} %get-tuple-element.12), channel_id=1, source_target_pairs={{0,2},{1,3},{2,4},{3,5},{4,6},{5,7},{6,8},{7,9},{8,10},{9,11},{10,... | collective-permute-start | bytes 1572872 | tf_op jit(solution)/shard_map/ppermute | solution.py:15
  43.1 31.6 %collective-permute-start.9 = (bf16[256,1024]{1,0:T(8,128)(2,1)}, bf16[256,1024]{1,0:T(8,128)(2,1)}, u32[]{:S(2)}, u32[]{:S(2)}) collective-permute-start(bf16[256,1024]{1,0:T(8,128)(2,1)} %get-tuple-element.14), channel_id=1, source_target_pairs={{0,2},{1,3},{2,4},{3,5},{4,6},{5,7},{6,8},{7,9},{8,10},{9,11},{10,... | collective-permute-start | bytes 1572872 | tf_op jit(solution)/shard_map/ppermute | solution.py:15
  56.6 30.5 %collective-permute-start.11 = (bf16[256,1024]{1,0:T(8,128)(2,1)}, bf16[256,1024]{1,0:T(8,128)(2,1)}, u32[]{:S(2)}, u32[]{:S(2)}) collective-permute-start(bf16[256,1024]{1,0:T(8,128)(2,1)} %get-tuple-element.5), channel_id=1, source_target_pairs={{0,2},{1,3},{2,4},{3,5},{4,6},{5,7},{6,8},{7,9},{8,10},{9,11},{10,... | collective-permute-start | bytes 1572872 | tf_op jit(solution)/shard_map/ppermute | solution.py:15
  74.7 15.9 %collective-permute-start.10 = (bf16[256,1024]{1,0:T(8,128)(2,1)}, bf16[256,1024]{1,0:T(8,128)(2,1)}, u32[]{:S(2)}, u32[]{:S(2)}) collective-permute-start(bf16[256,1024]{1,0:T(8,128)(2,1)} %collective-permute-done.9), channel_id=1, source_target_pairs={{0,1},{1,2},{2,3},{3,4},{4,5},{5,6},{6,7},{7,8},{8,9},{9,10},{10,1... | collective-permute-start | bytes 1572872 | tf_op jit(solution)/shard_map/ppermute | solution.py:15
  76.8 19.0 %collective-permute-start.8 = (bf16[256,1024]{1,0:T(8,128)(2,1)S(1)}, bf16[256,1024]{1,0:T(8,128)(2,1)}, u32[]{:S(2)}, u32[]{:S(2)}) collective-permute-start(bf16[256,1024]{1,0:T(8,128)(2,1)S(1)} %collective-permute-done.7), channel_id=1, source_target_pairs={{0,1},{1,2},{2,3},{3,4},{4,5},{5,6},{6,7},{7,8},{8,9},{9,10},{10,1... | collective-permute-start | bytes 1572872 | tf_op jit(solution)/shard_map/ppermute | solution.py:15
  85.0 15.8 %collective-permute-start.6 = (bf16[256,1024]{1,0:T(8,128)(2,1)S(1)}, bf16[256,1024]{1,0:T(8,128)(2,1)}, u32[]{:S(2)}, u32[]{:S(2)}) collective-permute-start(bf16[256,1024]{1,0:T(8,128)(2,1)S(1)} %collective-permute-done.5), channel_id=1, source_target_pairs={{0,1},{1,2},{2,3},{3,4},{4,5},{5,6},{6,7},{7,8},{8,9},{9,10},{10,1... | collective-permute-start | bytes 1572872 | tf_op jit(solution)/shard_map/ppermute | solution.py:15
  87.1 18.7 %collective-permute-start.12 = (bf16[256,1024]{1,0:T(8,128)(2,1)}, bf16[256,1024]{1,0:T(8,128)(2,1)}, u32[]{:S(2)}, u32[]{:S(2)}) collective-permute-start(bf16[256,1024]{1,0:T(8,128)(2,1)} %collective-permute-done.11), channel_id=1, source_target_pairs={{0,1},{1,2},{2,3},{3,4},{4,5},{5,6},{6,7},{7,8},{8,9},{9,10},{10,1... | collective-permute-start | bytes 1572872 | tf_op jit(solution)/shard_map/ppermute | solution.py:15
  118.5 1.1 collective-permute-start.13
  120.9 3.5 %collective-permute-start.14 = (f32[2]{0:T(128)S(1)}, f32[2]{0:T(128)S(1)}, u32[]{:S(2)}, u32[]{:S(2)}) collective-permute-start(f32[2]{0:T(128)S(1)} %fusion.79), channel_id=1, source_target_pairs={{0,2},{1,3},{2,0},{3,1},{4,6},{5,7},{6,4},{7,5},{8,10},{9,11},{10,... | collective-permute-start | bytes 32 | tf_op jit(solution)/shard_map/ppermute | solution.py:23
  125.8 5.7 %collective-permute-start.15 = (f32[2]{0:T(128)S(1)}, f32[2]{0:T(128)S(1)}, u32[]{:S(2)}, u32[]{:S(2)}) collective-permute-start(f32[2]{0:T(128)S(1)} %fusion.80), channel_id=1, source_target_pairs={{0,4},{1,5},{2,6},{3,7},{4,0},{5,1},{6,2},{7,3},{8,12},{9,13},{10,... | collective-permute-start | bytes 32 | tf_op jit(solution)/shard_map/ppermute | solution.py:23
  131.5 4.6 %collective-permute-start.16 = (f32[2]{0:T(128)S(1)}, f32[2]{0:T(128)S(1)}, u32[]{:S(2)}, u32[]{:S(2)}) collective-permute-start(f32[2]{0:T(128)S(1)} %add.106), channel_id=1, source_target_pairs={{0,8},{1,9},{2,10},{3,11},{4,12},{5,13},{6,14},{7,15},{8,0},{9,1},... | collective-permute-start | bytes 32 | tf_op jit(solution)/shard_map/ppermute | solution.py:23
  136.1 5.4 %collective-permute-start.17 = (f32[2]{0:T(128)S(1)}, f32[2]{0:T(128)S(1)}, u32[]{:S(2)}, u32[]{:S(2)}) collective-permute-start(f32[2]{0:T(128)S(1)} %add.107), channel_id=1, source_target_pairs={{0,16},{1,17},{2,18},{3,19},{4,20},{5,21},{6,22},{7,23},{8,24},{9,... | collective-permute-start | bytes 32 | tf_op jit(solution)/shard_map/ppermute | solution.py:23

commit v3 on v2

--- a/solution.py
+++ b/solution.py
@@ -30,14 +30,11 @@
 
 
 def small_lookup(table, index):
-    places = jnp.arange(table.shape[0], dtype=jnp.int32)
-    return jnp.sum(jnp.where(places == index, table, jnp.zeros_like(table)))
+    return lax.dynamic_index_in_dim(table, index, 0, keepdims=False)
 
 
 def table_entry(table, row, column):
-    rows = jnp.arange(table.shape[0], dtype=jnp.int32)[:, None]
-    columns = jnp.arange(table.shape[1], dtype=jnp.int32)[None, :]
-    return jnp.sum(jnp.where((rows == row) & (columns == column), table, jnp.zeros_like(table)))
+    return small_lookup(small_lookup(table, row), column)
 
 
 def per_device(state, left_env, right_env, site_ops, left_live, right_live):
@@ -79,19 +76,18 @@
     rows = sec_size // CHUNKS
     pieces = [rounded[c * rows:(c + 1) * rows] for c in range(CHUNKS)]
     image_one, pieces[-1] = lax.optimization_barrier((image_one, pieces[-1]))
-    image = image_one
+    parts = []
     for c in range(CHUNKS):
         far_two = shift_up(pieces[c], 2)
         far_three = shift_up(far_two, 1)
         source = (
             weights[0] * far_two.astype(jnp.float32) + weights[1] * far_three.astype(jnp.float32)
         ).astype(jnp.bfloat16)
-        part_zero = jnp.dot(source, right_env[0, 0], preferred_element_type=jnp.float32).astype(
-            jnp.bfloat16
+        parts.append(
+            jnp.dot(source, right_env[0, 0], preferred_element_type=jnp.float32).astype(jnp.bfloat16)
         )
-        image = image + jnp.dot(
-            left_env[0, 0][:, c * rows:(c + 1) * rows], part_zero, preferred_element_type=jnp.float32
-        )
+    part_zero = jnp.concatenate(parts, axis=0)
+    image = jnp.dot(left_env[0, 0], part_zero, preferred_element_type=jnp.float32) + image_one
     image = row_major(image * live)
 
     sums = butterfly_sum(jnp.stack([jnp.sum(vector * image), jnp.sum(image * image)]))

time: 152 us -> 143 us (0.941)
  matrix products: 36 us -> 21.9 us
  waiting for transfers between devices: 24.6 us -> 30.7 us
  other arithmetic: 21.7 us -> 17.7 us
  local copies, waits for them, and re-layouts: 3.7 us -> 6.33 us
    dot_general x4 -> x5, matrix products: 26.7 us -> 12.5 us  [the longest x4 7.16 us: per_device(): jnp.dot(source, right_env[0, 0], preferred_element_type=jnp.float32)]
    ppermute x10, starting transfers between devices: 27.5 us -> 36.3 us  [butterfly_sum(): values = values + lax.ppermute(values, AXES, route)]
    ppermute x8, starting transfers between devices: 27.5 us -> 19.3 us  [shift_up(): return lax.ppermute(block, AXES, route)]
    ppermute x8, waiting for transfers between devices: 15 us -> 21.6 us  [shift_up(): return lax.ppermute(block, AXES, route)]
    reduce_sum x4 -> x0, other arithmetic: 3.95 us -> none  [the longest x3 3.22 us: small_lookup(): return jnp.sum(jnp.where(places == index, table, jnp.zeros_like(table)))]
    dynamic_slice x0 -> x4, local copies, waits for them, and re-layouts: none -> 3.69 us  [small_lookup(): return lax.dynamic_index_in_dim(table, index, 0, keepdims=False)]
    squeeze x1 -> x0, local copies, waits for them, and re-layouts: 1.76 us -> none  [per_device(): left_env[0, 0][:, c * rows:(c + 1) * rows]]
  transfers between devices with their start and end apart: 18 -> 18, of which waited for: 11 -> 13; matrix products, arithmetic and copies ran while one was open for 18% -> 12% of each run, Pallas kernels for 0% -> 0%
where the time goes in v3:
time: 143 us
  starting transfers between devices  55.6 us (39%)
  waiting for transfers between devices  30.7 us (21%)
  matrix products  21.9 us (15%)
  other arithmetic  17.7 us (12%)
  between operations  10.2 us (7%)
  local copies, waits for them, and re-layouts  6.33 us (4%)
    ppermute x10, starting transfers between devices, butterfly_sum(): values = values + lax.ppermute(values, AXES, route)  36.3 us
    ppermute x8, waiting for transfers between devices, shift_up(): return lax.ppermute(block, AXES, route)  21.6 us
    ppermute x8, starting transfers between devices, shift_up(): return lax.ppermute(block, AXES, route)  19.3 us
    dot_general x1, matrix products, per_device(): jnp.dot(left_env[1, 0], part_one, preferred_element_type=jnp.float32)  9.37 us
    ppermute x10, waiting for transfers between devices, butterfly_sum(): values = values + lax.ppermute(values, AXES, route)  9.04 us
    dot_general x4, matrix products, per_device(): jnp.dot(source, right_env[0, 0], preferred_element_type=jnp.float32)  7.16 us
    broadcast_in_dim x1, other arithmetic, per_device(): return (next_vector[None], jnp.stack([alpha_value, beta_value]))  6.42 us
    dot_general x1, matrix products, per_device(): jnp.dot(left_env[0, 0], part_zero, preferred_element_type=jnp.float32)  5.38 us
  transfers between devices with their start and end apart: 18, of which 13 were waited for; matrix products, arithmetic and copies ran while one was open for 12% of the time, Pallas kernels for 0%

profile of v3, /device:TPU:0, one launch (start us, length us, event | category | flops | bytes accessed | tf_op | source)
XLA Modules:
  0.0 142.5 jit_solution(5397568093095613068)
XLA Ops:
  5.7 4.1 %multiply_reduce_fusion.2 = f32[]{:T(128)} fusion(f32[1,1024,1024]{2,1,0:T(8,128)} %param.6, f32[1024]{0:T(1024)S(1)} %get-tuple-element.20, f32[1024]{0:T(1024)S(1)} %get-tuple-element.19), kind=kLoop, calls=%fused_computation.7 | loop fusion | flops 4194303 | bytes 4202500 | tf_op jit(solution)/shard_map/reduce_sum | solution.py:55
  12.6 4.2 %collective-permute-start.1 = (f32[]{:T(128)}, f32[]{:T(128)}, u32[]{:S(2)}, u32[]{:S(2)}) collective-permute-start(f32[]{:T(128)} %add.117), channel_id=1, source_target_pairs={{0,2},{1,3},{2,0},{3,1},{4,6},{5,7},{6,4},{7,5},{8,10},{9,11},{10,... | collective-permute-start | bytes 20 | tf_op jit(solution)/shard_map/ppermute | solution.py:23
  17.8 4.4 %collective-permute-start.2 = (f32[]{:T(128)}, f32[]{:T(128)}, u32[]{:S(2)}, u32[]{:S(2)}) collective-permute-start(f32[]{:T(128)} %add.118), channel_id=1, source_target_pairs={{0,4},{1,5},{2,6},{3,7},{4,0},{5,1},{6,2},{7,3},{8,12},{9,13},{10,... | collective-permute-start | bytes 20 | tf_op jit(solution)/shard_map/ppermute | solution.py:23
  23.0 3.2 %collective-permute-start.3 = (f32[]{:T(128)}, f32[]{:T(128)}, u32[]{:S(2)}, u32[]{:S(2)}) collective-permute-start(f32[]{:T(128)} %add.119), channel_id=1, source_target_pairs={{0,8},{1,9},{2,10},{3,11},{4,12},{5,13},{6,14},{7,15},{8,0},{9,1},... | collective-permute-start | bytes 20 | tf_op jit(solution)/shard_map/ppermute | solution.py:23
  27.3 3.2 %collective-permute-start.4 = (f32[]{:T(128)}, f32[]{:T(128)}, u32[]{:S(2)}, u32[]{:S(2)}) collective-permute-start(f32[]{:T(128)} %add.120), channel_id=1, source_target_pairs={{0,16},{1,17},{2,18},{3,19},{4,20},{5,21},{6,22},{7,23},{8,24},{9,... | collective-permute-start | bytes 20 | tf_op jit(solution)/shard_map/ppermute | solution.py:23
  31.6 2.7 %fusion.55 = bf16[1024,1024]{1,0:T(8,128)(2,1)S(1)} fusion(f32[]{:T(128)S(6)} %sqrt.6, f32[1024]{0:T(1024)S(1)} %get-tuple-element.20, f32[1024]{0:T(1024)S(1)} %get-tuple-element.19, f32[1,1024,1024]{2,1,0:T(8,128)} %param.6), kind=kLoop, calls=%fused_computation.66 | loop fusion | flops 4194304 | bytes 6299652 | tf_op jit(solution)/shard_map/convert_element_type | solution.py:58
  35.5 4.6 %collective-permute-start.5 = (bf16[256,1024]{1,0:T(8,128)(2,1)}, bf16[256,1024]{1,0:T(8,128)(2,1)}, u32[]{:S(2)}, u32[]{:S(2)}) collective-permute-start(bf16[256,1024]{1,0:T(8,128)(2,1)} %get-tuple-element.8), channel_id=1, source_target_pairs={{0,2},{1,3},{2,4},{3,5},{4,6},{5,7},{6,8},{7,9},{8,10},{9,11},{10,... | collective-permute-start | bytes 1572872 | tf_op jit(solution)/shard_map/ppermute | solution.py:15
  40.2 3.5 %collective-permute-start.9 = (bf16[256,1024]{1,0:T(8,128)(2,1)}, bf16[256,1024]{1,0:T(8,128)(2,1)}, u32[]{:S(2)}, u32[]{:S(2)}) collective-permute-start(bf16[256,1024]{1,0:T(8,128)(2,1)} %get-tuple-element.9), channel_id=1, source_target_pairs={{0,2},{1,3},{2,4},{3,5},{4,6},{5,7},{6,8},{7,9},{8,10},{9,11},{10,... | collective-permute-start | bytes 1572872 | tf_op jit(solution)/shard_map/ppermute | solution.py:15
  43.6 3.5 %collective-permute-start.7 = (bf16[256,1024]{1,0:T(8,128)(2,1)S(1)}, bf16[256,1024]{1,0:T(8,128)(2,1)}, u32[]{:S(2)}, u32[]{:S(2)}) collective-permute-start(bf16[256,1024]{1,0:T(8,128)(2,1)S(1)} %get-tuple-element.10), channel_id=1, source_target_pairs={{0,2},{1,3},{2,4},{3,5},{4,6},{5,7},{6,8},{7,9},{8,10},{9,11},{10,... | collective-permute-start | bytes 1572872 | tf_op jit(solution)/shard_map/ppermute | solution.py:15
  47.1 9.4 %multiply_bitcast_fusion = f32[1024,1024]{1,0:T(8,128)} fusion(bf16[2,1,1024,1024]{3,2,1,0:T(8,128)(2,1)} %param.7, f32[]{:T(128)} %bitcast.7, bf16[1024,1024]{1,0:T(8,128)(2,1)S(1)} %fusion.55, bf16[2,1,1024,1024]{3,2,1,0:T(8,128)(2,1)} %param.8), kind=kOutput, calls=%fused_computation.6 | convolution fusion | flops 4297064448 | bytes 10486272 | tf_op jit(solution)/shard_map/dot_general | solution.py:74
  56.5 2.3 %collective-permute-start.11 = (bf16[256,1024]{1,0:T(8,128)(2,1)S(1)}, bf16[256,1024]{1,0:T(8,128)(2,1)S(1)}, u32[]{:S(2)}, u32[]{:S(2)}) collective-permute-start(bf16[256,1024]{1,0:T(8,128)(2,1)S(1)} %get-tuple-element.4), channel_id=1, source_target_pairs={{0,2},{1,3},{2,4},{3,5},{4,6},{5,7},{6,8},{7,9},{8,10},{9,11},{10,... | collective-permute-start | bytes 1572872 | tf_op jit(solution)/shard_map/ppermute | solution.py:15
  60.1 3.1 %collective-permute-done.9 = bf16[256,1024]{1,0:T(8,128)(2,1)} collective-permute-done((bf16[256,1024]{1,0:T(8,128)(2,1)}, bf16[256,1024]{1,0:T(8,128)(2,1)}, u32[]{:S(2)}, u32[]{:S(2)}) %collective-permute-start.9) | collective-permute-done | bytes 524320 | tf_op jit(solution)/shard_map/ppermute | solution.py:15
  65.8 8.6 %collective-permute-done.7 = bf16[256,1024]{1,0:T(8,128)(2,1)} collective-permute-done((bf16[256,1024]{1,0:T(8,128)(2,1)S(1)}, bf16[256,1024]{1,0:T(8,128)(2,1)}, u32[]{:S(2)}, u32[]{:S(2)}) %collective-permute-start.7) | collective-permute-done | bytes 524320 | tf_op jit(solution)/shard_map/ppermute | solution.py:15
  75.7 9.9 %collective-permute-done.11 = bf16[256,1024]{1,0:T(8,128)(2,1)S(1)} collective-permute-done((bf16[256,1024]{1,0:T(8,128)(2,1)S(1)}, bf16[256,1024]{1,0:T(8,128)(2,1)S(1)}, u32[]{:S(2)}, u32[]{:S(2)}) %collective-permute-start.11) | collective-permute-done | bytes 524320 | tf_op jit(solution)/shard_map/ppermute | solution.py:15
  87.1 2.5 %fusion.28 = bf16[256,1024]{1,0:T(8,128)(2,1)S(1)} fusion(bf16[2,1,1024,1024]{3,2,1,0:T(8,128)(2,1)} %param.8, bf16[256,1024]{1,0:T(8,128)(2,1)S(1)} %collective-permute-done.6, bf16[256,1024]{1,0:T(8,128)(2,1)} %collective-permute-done.5, f32[]{:T(128)S(6)} %select_n.75, f32[]{:T(128)S(6)} %select_n.67), kind=kOutput, calls=%fused_computation.36 | convolution fusion | flops 538705920 | bytes 3670024 | tf_op jit(solution)/shard_map/dot_general | solution.py:87
  89.7 2.0 %fusion.34 = bf16[256,1024]{1,0:T(8,128)(2,1)S(1)} fusion(bf16[2,1,1024,1024]{3,2,1,0:T(8,128)(2,1)S(1)} %copy-done.2, bf16[256,1024]{1,0:T(8,128)(2,1)S(1)} %collective-permute-done.10, bf16[256,1024]{1,0:T(8,128)(2,1)} %collective-permute-done.9, f32[]{:T(128)S(6)} %select_n.75, f32[]{:T(128)S(6)} %select_n.67), kind=kOutput, calls=%fused_computation.38 | convolution fusion | flops 538705920 | bytes 3670024 | tf_op jit(solution)/shard_map/dot_general | solution.py:87
  91.7 1.9 %fusion.31 = bf16[256,1024]{1,0:T(8,128)(2,1)S(1)} fusion(bf16[2,1,1024,1024]{3,2,1,0:T(8,128)(2,1)S(1)} %copy-done.2, bf16[256,1024]{1,0:T(8,128)(2,1)S(1)} %collective-permute-done.8, bf16[256,1024]{1,0:T(8,128)(2,1)} %collective-permute-done.7, f32[]{:T(128)S(6)} %select_n.75, f32[]{:T(128)S(6)} %select_n.67), kind=kOutput, calls=%fused_computation.37 | convolution fusion | flops 538705920 | bytes 3670024 | tf_op jit(solution)/shard_map/dot_general | solution.py:87
  95.3 5.4 %multiply_reduce_fusion.1 = (f32[]{:T(128)}, f32[]{:T(128)}, f32[1024,1024]{1,0:T(8,128)}) fusion(f32[]{:T(128)S(6)} %sqrt.6, f32[1024]{0:T(1024)S(1)} %get-tuple-element.20, f32[1024]{0:T(1024)S(1)} %get-tuple-element.19, f32[1,1024,1024]{2,1,0:T(8,128)S(1)} %copy-done, f32[1024,1024]{1,0:T(8,128)S(1)} %copy-done.4, bf16[256,1024]{1,0:T(8,128)(2,1)S(1)} %fusion.37, ...), kind=kOutput, calls=%fused_computation.5 | convolution fusion | flops 2165309440 | bytes 16785420 | tf_op jit(solution)/shard_map/dot_general | solution.py:90
  102.0 7.7 %collective-permute-start.13 = (f32[2]{0:T(128)S(1)}, f32[2]{0:T(128)S(1)}, u32[]{:S(2)}, u32[]{:S(2)}) collective-permute-start(f32[2]{0:T(128)S(1)} %pad_maximum_fusion), channel_id=1, source_target_pairs={{0,1},{1,0},{2,3},{3,2},{4,5},{5,4},{6,7},{7,6},{8,9},{9,8},{10,11... | collective-permute-start | bytes 32 | tf_op jit(solution)/shard_map/ppermute | solution.py:23
  111.7 2.7 %collective-permute-start.14 = (f32[2]{0:T(128)S(1)}, f32[2]{0:T(128)S(1)}, u32[]{:S(2)}, u32[]{:S(2)}) collective-permute-start(f32[2]{0:T(128)S(1)} %fusion.60), channel_id=1, source_target_pairs={{0,2},{1,3},{2,0},{3,1},{4,6},{5,7},{6,4},{7,5},{8,10},{9,11},{10,... | collective-permute-start | bytes 32 | tf_op jit(solution)/shard_map/ppermute | solution.py:23
  117.2 3.0 %collective-permute-start.15 = (f32[2]{0:T(128)S(1)}, f32[2]{0:T(128)S(1)}, u32[]{:S(2)}, u32[]{:S(2)}) collective-permute-start(f32[2]{0:T(128)S(1)} %fusion.61), channel_id=1, source_target_pairs={{0,4},{1,5},{2,6},{3,7},{4,0},{5,1},{6,2},{7,3},{8,12},{9,13},{10,... | collective-permute-start | bytes 32 | tf_op jit(solution)/shard_map/ppermute | solution.py:23
  121.8 4.5 %collective-permute-start.16 = (f32[2]{0:T(128)S(1)}, f32[2]{0:T(128)S(1)}, u32[]{:S(2)}, u32[]{:S(2)}) collective-permute-start(f32[2]{0:T(128)S(1)} %add.132), channel_id=1, source_target_pairs={{0,8},{1,9},{2,10},{3,11},{4,12},{5,13},{6,14},{7,15},{8,0},{9,1},... | collective-permute-start | bytes 32 | tf_op jit(solution)/shard_map/ppermute | solution.py:23
  127.8 3.0 %collective-permute-start.17 = (f32[2]{0:T(128)S(1)}, f32[2]{0:T(128)S(1)}, u32[]{:S(2)}, u32[]{:S(2)}) collective-permute-start(f32[2]{0:T(128)S(1)} %add.133), channel_id=1, source_target_pairs={{0,16},{1,17},{2,18},{3,19},{4,20},{5,21},{6,22},{7,23},{8,24},{9,... | collective-permute-start | bytes 32 | tf_op jit(solution)/shard_map/ppermute | solution.py:23
  136.1 6.4 %divide_bitcast_fusion = f32[1,1024,1024]{2,1,0:T(8,128)} fusion(f32[1024,1024]{1,0:T(8,128)} %get-tuple-element.18, f32[]{:T(128)} %sqrt.7, f32[]{:T(128)} %bitcast.15, f32[]{:T(128)S(6)} %sqrt.6, f32[1024]{0:T(1024)S(1)} %get-tuple-element.20, f32[1024]{0:T(1024)S(1)} %get-tuple-element.19, f32[1,1024,1024]{2,1,0:T(8,128)} %param.6), kind=kLoop, calls=%fused_computation.3 | loop fusion | flops 6291456 | bytes 12591116 | tf_op jit(solution)/shard_map/broadcast_in_dim | solution.py:100
  (47 shorter events, 26.5 us)
Async XLA Ops:
  0.6 9.7 %copy-start.1 = (f32[2,4,4]{2,1,0:T(4,128)S(1)}, f32[2,4,4]{2,1,0:T(4,128)}, u32[]{:S(2)}) copy-start(f32[2,4,4]{2,1,0:T(4,128)} %param.9) | copy-start | bytes 388
  9.9 1.5 %collective-permute-start = (f32[]{:T(128)}, f32[]{:T(128)}, u32[]{:S(2)}, u32[]{:S(2)}) collective-permute-start(f32[]{:T(128)} %multiply_reduce_fusion.2), channel_id=1, source_target_pairs={{0,1},{1,0},{2,3},{3,2},{4,5},{5,4},{6,7},{7,6},{8,9},{9,8},{10,11... | collective-permute-start | bytes 20 | tf_op jit(solution)/shard_map/ppermute | solution.py:23
  12.6 4.6 %collective-permute-start.1 = (f32[]{:T(128)}, f32[]{:T(128)}, u32[]{:S(2)}, u32[]{:S(2)}) collective-permute-start(f32[]{:T(128)} %add.117), channel_id=1, source_target_pairs={{0,2},{1,3},{2,0},{3,1},{4,6},{5,7},{6,4},{7,5},{8,10},{9,11},{10,... | collective-permute-start | bytes 20 | tf_op jit(solution)/shard_map/ppermute | solution.py:23
  17.8 4.7 %collective-permute-start.2 = (f32[]{:T(128)}, f32[]{:T(128)}, u32[]{:S(2)}, u32[]{:S(2)}) collective-permute-start(f32[]{:T(128)} %add.118), channel_id=1, source_target_pairs={{0,4},{1,5},{2,6},{3,7},{4,0},{5,1},{6,2},{7,3},{8,12},{9,13},{10,... | collective-permute-start | bytes 20 | tf_op jit(solution)/shard_map/ppermute | solution.py:23
  23.0 3.7 %collective-permute-start.3 = (f32[]{:T(128)}, f32[]{:T(128)}, u32[]{:S(2)}, u32[]{:S(2)}) collective-permute-start(f32[]{:T(128)} %add.119), channel_id=1, source_target_pairs={{0,8},{1,9},{2,10},{3,11},{4,12},{5,13},{6,14},{7,15},{8,0},{9,1},... | collective-permute-start | bytes 20 | tf_op jit(solution)/shard_map/ppermute | solution.py:23
  27.3 3.7 %collective-permute-start.4 = (f32[]{:T(128)}, f32[]{:T(128)}, u32[]{:S(2)}, u32[]{:S(2)}) collective-permute-start(f32[]{:T(128)} %add.120), channel_id=1, source_target_pairs={{0,16},{1,17},{2,18},{3,19},{4,20},{5,21},{6,22},{7,23},{8,24},{9,... | collective-permute-start | bytes 20 | tf_op jit(solution)/shard_map/ppermute | solution.py:23
  35.5 23.3 %collective-permute-start.5 = (bf16[256,1024]{1,0:T(8,128)(2,1)}, bf16[256,1024]{1,0:T(8,128)(2,1)}, u32[]{:S(2)}, u32[]{:S(2)}) collective-permute-start(bf16[256,1024]{1,0:T(8,128)(2,1)} %get-tuple-element.8), channel_id=1, source_target_pairs={{0,2},{1,3},{2,4},{3,5},{4,6},{5,7},{6,8},{7,9},{8,10},{9,11},{10,... | collective-permute-start | bytes 1572872 | tf_op jit(solution)/shard_map/ppermute | solution.py:15
  40.2 23.1 %collective-permute-start.9 = (bf16[256,1024]{1,0:T(8,128)(2,1)}, bf16[256,1024]{1,0:T(8,128)(2,1)}, u32[]{:S(2)}, u32[]{:S(2)}) collective-permute-start(bf16[256,1024]{1,0:T(8,128)(2,1)} %get-tuple-element.9), channel_id=1, source_target_pairs={{0,2},{1,3},{2,4},{3,5},{4,6},{5,7},{6,8},{7,9},{8,10},{9,11},{10,... | collective-permute-start | bytes 1572872 | tf_op jit(solution)/shard_map/ppermute | solution.py:15
  43.6 30.8 %collective-permute-start.7 = (bf16[256,1024]{1,0:T(8,128)(2,1)S(1)}, bf16[256,1024]{1,0:T(8,128)(2,1)}, u32[]{:S(2)}, u32[]{:S(2)}) collective-permute-start(bf16[256,1024]{1,0:T(8,128)(2,1)S(1)} %get-tuple-element.10), channel_id=1, source_target_pairs={{0,2},{1,3},{2,4},{3,5},{4,6},{5,7},{6,8},{7,9},{8,10},{9,11},{10,... | collective-permute-start | bytes 1572872 | tf_op jit(solution)/shard_map/ppermute | solution.py:15
  56.5 29.1 %collective-permute-start.11 = (bf16[256,1024]{1,0:T(8,128)(2,1)S(1)}, bf16[256,1024]{1,0:T(8,128)(2,1)S(1)}, u32[]{:S(2)}, u32[]{:S(2)}) collective-permute-start(bf16[256,1024]{1,0:T(8,128)(2,1)S(1)} %get-tuple-element.4), channel_id=1, source_target_pairs={{0,2},{1,3},{2,4},{3,5},{4,6},{5,7},{6,8},{7,9},{8,10},{9,11},{10,... | collective-permute-start | bytes 1572872 | tf_op jit(solution)/shard_map/ppermute | solution.py:15
  58.8 28.3 %collective-permute-start.6 = (bf16[256,1024]{1,0:T(8,128)(2,1)}, bf16[256,1024]{1,0:T(8,128)(2,1)S(1)}, u32[]{:S(2)}, u32[]{:S(2)}) collective-permute-start(bf16[256,1024]{1,0:T(8,128)(2,1)} %collective-permute-done.5), channel_id=1, source_target_pairs={{0,1},{1,2},{2,3},{3,4},{4,5},{5,6},{6,7},{7,8},{8,9},{9,10},{10,1... | collective-permute-start | bytes 1572872 | tf_op jit(solution)/shard_map/ppermute | solution.py:15
  63.3 26.4 %collective-permute-start.10 = (bf16[256,1024]{1,0:T(8,128)(2,1)}, bf16[256,1024]{1,0:T(8,128)(2,1)S(1)}, u32[]{:S(2)}, u32[]{:S(2)}) collective-permute-start(bf16[256,1024]{1,0:T(8,128)(2,1)} %collective-permute-done.9), channel_id=1, source_target_pairs={{0,1},{1,2},{2,3},{3,4},{4,5},{5,6},{6,7},{7,8},{8,9},{9,10},{10,1... | collective-permute-start | bytes 1572872 | tf_op jit(solution)/shard_map/ppermute | solution.py:15
  65.8 23.9 %copy-start.2 = (bf16[2,1,1024,1024]{3,2,1,0:T(8,128)(2,1)S(1)}, bf16[2,1,1024,1024]{3,2,1,0:T(8,128)(2,1)}, u32[]{:S(2)}) copy-start(bf16[2,1,1024,1024]{3,2,1,0:T(8,128)(2,1)} %param.8) | copy-start | bytes 12582916
  74.4 17.3 %collective-permute-start.8 = (bf16[256,1024]{1,0:T(8,128)(2,1)}, bf16[256,1024]{1,0:T(8,128)(2,1)S(1)}, u32[]{:S(2)}, u32[]{:S(2)}) collective-permute-start(bf16[256,1024]{1,0:T(8,128)(2,1)} %collective-permute-done.7), channel_id=1, source_target_pairs={{0,1},{1,2},{2,3},{3,4},{4,5},{5,6},{6,7},{7,8},{8,9},{9,10},{10,1... | collective-permute-start | bytes 1572872 | tf_op jit(solution)/shard_map/ppermute | solution.py:15
  85.6 8.0 %collective-permute-start.12 = (bf16[256,1024]{1,0:T(8,128)(2,1)S(1)}, bf16[256,1024]{1,0:T(8,128)(2,1)S(1)}, u32[]{:S(2)}, u32[]{:S(2)}) collective-permute-start(bf16[256,1024]{1,0:T(8,128)(2,1)S(1)} %collective-permute-done.11), channel_id=1, source_target_pairs={{0,1},{1,2},{2,3},{3,4},{4,5},{5,6},{6,7},{7,8},{8,9},{9,10},{10,1... | collective-permute-start | bytes 1572872 | tf_op jit(solution)/shard_map/ppermute | solution.py:15
  89.7 4.7 %copy-start.4 = (f32[1024,1024]{1,0:T(8,128)S(1)}, f32[1024,1024]{1,0:T(8,128)}, u32[]{:S(2)}) copy-start(f32[1024,1024]{1,0:T(8,128)} %multiply_bitcast_fusion) | copy-start | bytes 12582916
  91.7 2.8 %copy-start = (f32[1,1024,1024]{2,1,0:T(8,128)S(1)}, f32[1,1024,1024]{2,1,0:T(8,128)}, u32[]{:S(2)}) copy-start(f32[1,1024,1024]{2,1,0:T(8,128)} %param.6) | copy-start | bytes 12582916
  91.7 3.6 %copy-start.3 = (bf16[2,1,1024,1024]{3,2,1,0:T(8,128)(2,1)S(1)}, bf16[2,1,1024,1024]{3,2,1,0:T(8,128)(2,1)}, u32[]{:S(2)}) copy-start(bf16[2,1,1024,1024]{3,2,1,0:T(8,128)(2,1)} %param.7) | copy-start | bytes 12582916
  102.0 8.5 %collective-permute-start.13 = (f32[2]{0:T(128)S(1)}, f32[2]{0:T(128)S(1)}, u32[]{:S(2)}, u32[]{:S(2)}) collective-permute-start(f32[2]{0:T(128)S(1)} %pad_maximum_fusion), channel_id=1, source_target_pairs={{0,1},{1,0},{2,3},{3,2},{4,5},{5,4},{6,7},{7,6},{8,9},{9,8},{10,11... | collective-permute-start | bytes 32 | tf_op jit(solution)/shard_map/ppermute | solution.py:23
  111.7 4.2 %collective-permute-start.14 = (f32[2]{0:T(128)S(1)}, f32[2]{0:T(128)S(1)}, u32[]{:S(2)}, u32[]{:S(2)}) collective-permute-start(f32[2]{0:T(128)S(1)} %fusion.60), channel_id=1, source_target_pairs={{0,2},{1,3},{2,0},{3,1},{4,6},{5,7},{6,4},{7,5},{8,10},{9,11},{10,... | collective-permute-start | bytes 32 | tf_op jit(solution)/shard_map/ppermute | solution.py:23
  117.2 4.6 %collective-permute-start.15 = (f32[2]{0:T(128)S(1)}, f32[2]{0:T(128)S(1)}, u32[]{:S(2)}, u32[]{:S(2)}) collective-permute-start(f32[2]{0:T(128)S(1)} %fusion.61), channel_id=1, source_target_pairs={{0,4},{1,5},{2,6},{3,7},{4,0},{5,1},{6,2},{7,3},{8,12},{9,13},{10,... | collective-permute-start | bytes 32 | tf_op jit(solution)/shard_map/ppermute | solution.py:23
  121.8 6.0 %collective-permute-start.16 = (f32[2]{0:T(128)S(1)}, f32[2]{0:T(128)S(1)}, u32[]{:S(2)}, u32[]{:S(2)}) collective-permute-start(f32[2]{0:T(128)S(1)} %add.132), channel_id=1, source_target_pairs={{0,8},{1,9},{2,10},{3,11},{4,12},{5,13},{6,14},{7,15},{8,0},{9,1},... | collective-permute-start | bytes 32 | tf_op jit(solution)/shard_map/ppermute | solution.py:23
  127.8 4.5 %collective-permute-start.17 = (f32[2]{0:T(128)S(1)}, f32[2]{0:T(128)S(1)}, u32[]{:S(2)}, u32[]{:S(2)}) collective-permute-start(f32[2]{0:T(128)S(1)} %add.133), channel_id=1, source_target_pairs={{0,16},{1,17},{2,18},{3,19},{4,20},{5,21},{6,22},{7,23},{8,24},{9,... | collective-permute-start | bytes 32 | tf_op jit(solution)/shard_map/ppermute | solution.py:23

commit v4 on v3

--- a/solution.py
+++ b/solution.py
@@ -52,10 +52,17 @@
     entries = float(state.shape[0] * sec_size * sec_size * lax.axis_size(AXES))
 
     masked = state[0] * live
-    start_sum = butterfly_sum(jnp.sum(masked * masked))
+    column_sums = lax.optimization_barrier(jnp.sum(masked * masked, axis=0))
+    start_sum = butterfly_sum(jnp.sum(column_sums))
     start_mean = start_sum / entries
-    vector = masked / jnp.sqrt(start_mean + 1e-06)
-    rounded = row_major(vector.astype(jnp.bfloat16))
+    scale = jnp.sqrt(start_mean + 1e-06)
+    vector = masked / scale
+    rows = sec_size // CHUNKS
+    pieces = [
+        row_major((masked[c * rows:(c + 1) * rows] / scale).astype(jnp.bfloat16))
+        for c in range(CHUNKS)
+    ]
+    rounded = jnp.concatenate(pieces, axis=0)
 
     weights = []
     for offset in (2, 3):
@@ -73,8 +80,6 @@
     diag_weight = table_entry(site_ops[1], own_pair, own_pair)
     image_one = diag_weight * jnp.dot(left_env[1, 0], part_one, preferred_element_type=jnp.float32)
 
-    rows = sec_size // CHUNKS
-    pieces = [rounded[c * rows:(c + 1) * rows] for c in range(CHUNKS)]
     image_one, pieces[-1] = lax.optimization_barrier((image_one, pieces[-1]))
     parts = []
     for c in range(CHUNKS):

time: 143 us -> 145 us (1.014)
  other arithmetic: 17.7 us -> 19.9 us
  starting transfers between devices: 55.6 us -> 57.1 us
    reduce_sum x1 -> x2, other arithmetic: 4.14 us -> 5.48 us  [the longest x1 4.88 us: per_device(): column_sums = lax.optimization_barrier(jnp.sum(masked * masked, axis=0))]
  transfers between devices with their start and end apart: 18 -> 18, of which waited for: 13 -> 13; matrix products, arithmetic and copies ran while one was open for 12% -> 10% of each run, Pallas kernels for 0% -> 0%
where the time goes in v4:
time: 145 us; the launch traced here: 144 us
  starting transfers between devices  57.1 us (39%)
  waiting for transfers between devices  29.7 us (20%)
  matrix products  20.5 us (14%)
  other arithmetic  19.9 us (14%)
  between operations  11 us (8%)
  local copies, waits for them, and re-layouts  6.27 us (4%)
    ppermute x10, starting transfers between devices, butterfly_sum(): values = values + lax.ppermute(values, AXES, route)  37.8 us
    ppermute x8, waiting for transfers between devices, shift_up(): return lax.ppermute(block, AXES, route)  21.4 us
    ppermute x8, starting transfers between devices, shift_up(): return lax.ppermute(block, AXES, route)  19.3 us
    dot_general x1, matrix products, per_device(): jnp.dot(left_env[1, 0], part_one, preferred_element_type=jnp.float32)  9.25 us
    ppermute x10, waiting for transfers between devices, butterfly_sum(): values = values + lax.ppermute(values, AXES, route)  8.25 us
    broadcast_in_dim x1, other arithmetic, per_device(): return (next_vector[None], jnp.stack([alpha_value, beta_value]))  6.96 us
    dot_general x4, matrix products, per_device(): jnp.dot(source, right_env[0, 0], preferred_element_type=jnp.float32)  5.94 us
    dot_general x1, matrix products, per_device(): jnp.dot(left_env[0, 0], part_zero, preferred_element_type=jnp.float32)  5.35 us
  transfers between devices with their start and end apart: 18, of which 13 were waited for; matrix products, arithmetic and copies ran while one was open for 10% of the time, Pallas kernels for 0%

profile of v4, /device:TPU:0, one launch (start us, length us, event | category | flops | bytes accessed | tf_op | source)
XLA Modules:
  0.0 144.4 jit_solution(7136787243897089426)
XLA Ops:
  5.7 4.9 %multiply_reduce_fusion.2 = (f32[1024]{0:T(1024)S(1)}, f32[1024,1024]{1,0:T(8,128)}) fusion(f32[1024]{0:T(1024)S(1)} %get-tuple-element.22, f32[1024]{0:T(1024)S(1)} %get-tuple-element.21, f32[1,1024,1024]{2,1,0:T(8,128)} %param.6), kind=kLoop, calls=%fused_computation.7 | loop fusion | flops 4193280 | bytes 8400896 | tf_op jit(solution)/shard_map/reduce_sum | solution.py:55
  14.0 4.2 %collective-permute-start.1 = (f32[]{:T(128)}, f32[]{:T(128)}, u32[]{:S(2)}, u32[]{:S(2)}) collective-permute-start(f32[]{:T(128)} %add.117), channel_id=1, source_target_pairs={{0,2},{1,3},{2,0},{3,1},{4,6},{5,7},{6,4},{7,5},{8,10},{9,11},{10,... | collective-permute-start | bytes 20 | tf_op jit(solution)/shard_map/ppermute | solution.py:23
  19.0 4.4 %collective-permute-start.2 = (f32[]{:T(128)}, f32[]{:T(128)}, u32[]{:S(2)}, u32[]{:S(2)}) collective-permute-start(f32[]{:T(128)} %add.118), channel_id=1, source_target_pairs={{0,4},{1,5},{2,6},{3,7},{4,0},{5,1},{6,2},{7,3},{8,12},{9,13},{10,... | collective-permute-start | bytes 20 | tf_op jit(solution)/shard_map/ppermute | solution.py:23
  24.3 3.2 %collective-permute-start.3 = (f32[]{:T(128)}, f32[]{:T(128)}, u32[]{:S(2)}, u32[]{:S(2)}) collective-permute-start(f32[]{:T(128)} %add.119), channel_id=1, source_target_pairs={{0,8},{1,9},{2,10},{3,11},{4,12},{5,13},{6,14},{7,15},{8,0},{9,1},... | collective-permute-start | bytes 20 | tf_op jit(solution)/shard_map/ppermute | solution.py:23
  28.6 3.2 %collective-permute-start.4 = (f32[]{:T(128)}, f32[]{:T(128)}, u32[]{:S(2)}, u32[]{:S(2)}) collective-permute-start(f32[]{:T(128)} %add.120), channel_id=1, source_target_pairs={{0,16},{1,17},{2,18},{3,19},{4,20},{5,21},{6,22},{7,23},{8,24},{9,... | collective-permute-start | bytes 20 | tf_op jit(solution)/shard_map/ppermute | solution.py:23
  32.9 2.8 %fusion.49 = (bf16[256,1024]{1,0:T(8,128)(2,1)S(1)}, bf16[256,1024]{1,0:T(8,128)(2,1)S(1)}, bf16[256,1024]{1,0:T(8,128)(2,1)S(1)}, bf16[256,1024]{1,0:T(8,128)(2,1)S(1)}) fusion(f32[1024,1024]{1,0:T(8,128)} %get-tuple-element.9, f32[]{:T(128)S(6)} %sqrt.6), kind=kLoop, calls=%fused_computation.54 | loop fusion | flops 2097152 | bytes 6291460 | tf_op jit(solution)/shard_map/convert_element_type | solution.py:62
  35.6 4.6 %collective-permute-start.5 = (bf16[256,1024]{1,0:T(8,128)(2,1)S(1)}, bf16[256,1024]{1,0:T(8,128)(2,1)}, u32[]{:S(2)}, u32[]{:S(2)}) collective-permute-start(bf16[256,1024]{1,0:T(8,128)(2,1)S(1)} %get-tuple-element.10), channel_id=1, source_target_pairs={{0,2},{1,3},{2,4},{3,5},{4,6},{5,7},{6,8},{7,9},{8,10},{9,11},{10,... | collective-permute-start | bytes 1572872 | tf_op jit(solution)/shard_map/ppermute | solution.py:15
  40.3 3.5 %collective-permute-start.9 = (bf16[256,1024]{1,0:T(8,128)(2,1)S(1)}, bf16[256,1024]{1,0:T(8,128)(2,1)}, u32[]{:S(2)}, u32[]{:S(2)}) collective-permute-start(bf16[256,1024]{1,0:T(8,128)(2,1)S(1)} %get-tuple-element.12), channel_id=1, source_target_pairs={{0,2},{1,3},{2,4},{3,5},{4,6},{5,7},{6,8},{7,9},{8,10},{9,11},{10,... | collective-permute-start | bytes 1572872 | tf_op jit(solution)/shard_map/ppermute | solution.py:15
  43.7 2.7 %collective-permute-start.7 = (bf16[256,1024]{1,0:T(8,128)(2,1)S(1)}, bf16[256,1024]{1,0:T(8,128)(2,1)S(1)}, u32[]{:S(2)}, u32[]{:S(2)}) collective-permute-start(bf16[256,1024]{1,0:T(8,128)(2,1)S(1)} %get-tuple-element.13), channel_id=1, source_target_pairs={{0,2},{1,3},{2,4},{3,5},{4,6},{5,7},{6,8},{7,9},{8,10},{9,11},{10,... | collective-permute-start | bytes 1572872 | tf_op jit(solution)/shard_map/ppermute | solution.py:15
  46.5 9.2 %multiply_bitcast_fusion = f32[1024,1024]{1,0:T(8,128)} fusion(bf16[2,1,1024,1024]{3,2,1,0:T(8,128)(2,1)} %param.7, f32[]{:T(128)} %bitcast.7, bf16[256,1024]{1,0:T(8,128)(2,1)S(1)} %get-tuple-element.4, bf16[256,1024]{1,0:T(8,128)(2,1)S(1)} %get-tuple-element.12, bf16[256,1024]{1,0:T(8,128)(2,1)S(1)} %get-tuple-element.13, ...), kind=kOutput, calls=%fused_computation.6 | convolution fusion | flops 4305453056 | bytes 10486272 | tf_op jit(solution)/shard_map/dot_general | solution.py:81
  55.7 3.0 %collective-permute-start.11 = (bf16[256,1024]{1,0:T(8,128)(2,1)S(1)}, bf16[256,1024]{1,0:T(8,128)(2,1)S(1)}, u32[]{:S(2)}, u32[]{:S(2)}) collective-permute-start(bf16[256,1024]{1,0:T(8,128)(2,1)S(1)} %get-tuple-element.4), channel_id=1, source_target_pairs={{0,2},{1,3},{2,4},{3,5},{4,6},{5,7},{6,8},{7,9},{8,10},{9,11},{10,... | collective-permute-start | bytes 1572872 | tf_op jit(solution)/shard_map/ppermute | solution.py:15
  60.1 2.9 %collective-permute-done.9 = bf16[256,1024]{1,0:T(8,128)(2,1)} collective-permute-done((bf16[256,1024]{1,0:T(8,128)(2,1)S(1)}, bf16[256,1024]{1,0:T(8,128)(2,1)}, u32[]{:S(2)}, u32[]{:S(2)}) %collective-permute-start.9) | collective-permute-done | bytes 524320 | tf_op jit(solution)/shard_map/ppermute | solution.py:15
  65.7 8.5 %collective-permute-done.7 = bf16[256,1024]{1,0:T(8,128)(2,1)S(1)} collective-permute-done((bf16[256,1024]{1,0:T(8,128)(2,1)S(1)}, bf16[256,1024]{1,0:T(8,128)(2,1)S(1)}, u32[]{:S(2)}, u32[]{:S(2)}) %collective-permute-start.7) | collective-permute-done | bytes 524320 | tf_op jit(solution)/shard_map/ppermute | solution.py:15
  75.6 9.9 %collective-permute-done.11 = bf16[256,1024]{1,0:T(8,128)(2,1)S(1)} collective-permute-done((bf16[256,1024]{1,0:T(8,128)(2,1)S(1)}, bf16[256,1024]{1,0:T(8,128)(2,1)S(1)}, u32[]{:S(2)}, u32[]{:S(2)}) %collective-permute-start.11) | collective-permute-done | bytes 524320 | tf_op jit(solution)/shard_map/ppermute | solution.py:15
  87.0 2.5 %fusion.34 = bf16[256,1024]{1,0:T(8,128)(2,1)S(1)} fusion(bf16[2,1,1024,1024]{3,2,1,0:T(8,128)(2,1)} %param.8, bf16[256,1024]{1,0:T(8,128)(2,1)S(1)} %collective-permute-done.6, bf16[256,1024]{1,0:T(8,128)(2,1)} %collective-permute-done.5, f32[]{:T(128)S(6)} %select_n.75, f32[]{:T(128)S(6)} %select_n.67), kind=kOutput, calls=%fused_computation.43 | convolution fusion | flops 538705920 | bytes 3670024 | tf_op jit(solution)/shard_map/dot_general | solution.py:92
  89.5 2.0 %fusion.40 = bf16[256,1024]{1,0:T(8,128)(2,1)S(1)} fusion(bf16[2,1,1024,1024]{3,2,1,0:T(8,128)(2,1)S(1)} %copy-done.2, bf16[256,1024]{1,0:T(8,128)(2,1)S(1)} %collective-permute-done.10, bf16[256,1024]{1,0:T(8,128)(2,1)} %collective-permute-done.9, f32[]{:T(128)S(6)} %select_n.75, f32[]{:T(128)S(6)} %select_n.67), kind=kOutput, calls=%fused_computation.45 | convolution fusion | flops 538705920 | bytes 3670024 | tf_op jit(solution)/shard_map/dot_general | solution.py:92
  95.0 5.4 %multiply_reduce_fusion.1 = (f32[]{:T(128)}, f32[]{:T(128)}, f32[1024,1024]{1,0:T(8,128)}) fusion(f32[1024,1024]{1,0:T(8,128)S(1)} %copy-done, f32[]{:T(128)S(6)} %sqrt.6, f32[1024]{0:T(1024)S(1)} %get-tuple-element.22, f32[1024]{0:T(1024)S(1)} %get-tuple-element.21, f32[1024,1024]{1,0:T(8,128)S(1)} %copy-done.4, bf16[256,1024]{1,0:T(8,128)(2,1)S(1)} %fusion.43, ...), kind=kOutput, calls=%fused_computation.5 | convolution fusion | flops 2164260864 | bytes 16785420 | tf_op jit(solution)/shard_map/dot_general | solution.py:95
  101.7 9.1 %collective-permute-start.13 = (f32[2]{0:T(128)S(1)}, f32[2]{0:T(128)S(1)}, u32[]{:S(2)}, u32[]{:S(2)}) collective-permute-start(f32[2]{0:T(128)S(1)} %pad_maximum_fusion), channel_id=1, source_target_pairs={{0,1},{1,0},{2,3},{3,2},{4,5},{5,4},{6,7},{7,6},{8,9},{9,8},{10,11... | collective-permute-start | bytes 32 | tf_op jit(solution)/shard_map/ppermute | solution.py:23
  113.0 2.7 %collective-permute-start.14 = (f32[2]{0:T(128)S(1)}, f32[2]{0:T(128)S(1)}, u32[]{:S(2)}, u32[]{:S(2)}) collective-permute-start(f32[2]{0:T(128)S(1)} %fusion.72), channel_id=1, source_target_pairs={{0,2},{1,3},{2,0},{3,1},{4,6},{5,7},{6,4},{7,5},{8,10},{9,11},{10,... | collective-permute-start | bytes 32 | tf_op jit(solution)/shard_map/ppermute | solution.py:23
  115.6 1.5 %collective-permute-done.14 = f32[2]{0:T(128)S(1)} collective-permute-done((f32[2]{0:T(128)S(1)}, f32[2]{0:T(128)S(1)}, u32[]{:S(2)}, u32[]{:S(2)}) %collective-permute-start.14) | collective-permute-done | bytes 40 | tf_op jit(solution)/shard_map/ppermute | solution.py:23
  118.5 3.0 %collective-permute-start.15 = (f32[2]{0:T(128)S(1)}, f32[2]{0:T(128)S(1)}, u32[]{:S(2)}, u32[]{:S(2)}) collective-permute-start(f32[2]{0:T(128)S(1)} %fusion.73), channel_id=1, source_target_pairs={{0,4},{1,5},{2,6},{3,7},{4,0},{5,1},{6,2},{7,3},{8,12},{9,13},{10,... | collective-permute-start | bytes 32 | tf_op jit(solution)/shard_map/ppermute | solution.py:23
  123.1 4.5 %collective-permute-start.16 = (f32[2]{0:T(128)S(1)}, f32[2]{0:T(128)S(1)}, u32[]{:S(2)}, u32[]{:S(2)}) collective-permute-start(f32[2]{0:T(128)S(1)} %add.132), channel_id=1, source_target_pairs={{0,8},{1,9},{2,10},{3,11},{4,12},{5,13},{6,14},{7,15},{8,0},{9,1},... | collective-permute-start | bytes 32 | tf_op jit(solution)/shard_map/ppermute | solution.py:23
  129.1 3.0 %collective-permute-start.17 = (f32[2]{0:T(128)S(1)}, f32[2]{0:T(128)S(1)}, u32[]{:S(2)}, u32[]{:S(2)}) collective-permute-start(f32[2]{0:T(128)S(1)} %add.133), channel_id=1, source_target_pairs={{0,16},{1,17},{2,18},{3,19},{4,20},{5,21},{6,22},{7,23},{8,24},{9,... | collective-permute-start | bytes 32 | tf_op jit(solution)/shard_map/ppermute | solution.py:23
  137.4 7.0 %divide_bitcast_fusion = f32[1,1024,1024]{2,1,0:T(8,128)} fusion(f32[1024,1024]{1,0:T(8,128)} %get-tuple-element.20, f32[]{:T(128)} %sqrt.7, f32[]{:T(128)} %bitcast.15, f32[1024,1024]{1,0:T(8,128)} %get-tuple-element.9, f32[]{:T(128)S(6)} %sqrt.6), kind=kLoop, calls=%fused_computation.3 | loop fusion | flops 4194304 | bytes 12582924 | tf_op jit(solution)/shard_map/broadcast_in_dim | solution.py:105
  (47 shorter events, 25.7 us)
Async XLA Ops:
  5.7 5.9 %copy-start.1 = (f32[2,4,4]{2,1,0:T(4,128)S(1)}, f32[2,4,4]{2,1,0:T(4,128)}, u32[]{:S(2)}) copy-start(f32[2,4,4]{2,1,0:T(4,128)} %param.9) | copy-start | bytes 388
  11.2 1.4 collective-permute-start
  14.0 4.4 %collective-permute-start.1 = (f32[]{:T(128)}, f32[]{:T(128)}, u32[]{:S(2)}, u32[]{:S(2)}) collective-permute-start(f32[]{:T(128)} %add.117), channel_id=1, source_target_pairs={{0,2},{1,3},{2,0},{3,1},{4,6},{5,7},{6,4},{7,5},{8,10},{9,11},{10,... | collective-permute-start | bytes 20 | tf_op jit(solution)/shard_map/ppermute | solution.py:23
  19.0 4.6 %collective-permute-start.2 = (f32[]{:T(128)}, f32[]{:T(128)}, u32[]{:S(2)}, u32[]{:S(2)}) collective-permute-start(f32[]{:T(128)} %add.118), channel_id=1, source_target_pairs={{0,4},{1,5},{2,6},{3,7},{4,0},{5,1},{6,2},{7,3},{8,12},{9,13},{10,... | collective-permute-start | bytes 20 | tf_op jit(solution)/shard_map/ppermute | solution.py:23
  24.3 3.6 %collective-permute-start.3 = (f32[]{:T(128)}, f32[]{:T(128)}, u32[]{:S(2)}, u32[]{:S(2)}) collective-permute-start(f32[]{:T(128)} %add.119), channel_id=1, source_target_pairs={{0,8},{1,9},{2,10},{3,11},{4,12},{5,13},{6,14},{7,15},{8,0},{9,1},... | collective-permute-start | bytes 20 | tf_op jit(solution)/shard_map/ppermute | solution.py:23
  28.6 3.6 %collective-permute-start.4 = (f32[]{:T(128)}, f32[]{:T(128)}, u32[]{:S(2)}, u32[]{:S(2)}) collective-permute-start(f32[]{:T(128)} %add.120), channel_id=1, source_target_pairs={{0,16},{1,17},{2,18},{3,19},{4,20},{5,21},{6,22},{7,23},{8,24},{9,... | collective-permute-start | bytes 20 | tf_op jit(solution)/shard_map/ppermute | solution.py:23
  35.6 23.1 %collective-permute-start.5 = (bf16[256,1024]{1,0:T(8,128)(2,1)S(1)}, bf16[256,1024]{1,0:T(8,128)(2,1)}, u32[]{:S(2)}, u32[]{:S(2)}) collective-permute-start(bf16[256,1024]{1,0:T(8,128)(2,1)S(1)} %get-tuple-element.10), channel_id=1, source_target_pairs={{0,2},{1,3},{2,4},{3,5},{4,6},{5,7},{6,8},{7,9},{8,10},{9,11},{10,... | collective-permute-start | bytes 1572872 | tf_op jit(solution)/shard_map/ppermute | solution.py:15
  40.3 22.8 %collective-permute-start.9 = (bf16[256,1024]{1,0:T(8,128)(2,1)S(1)}, bf16[256,1024]{1,0:T(8,128)(2,1)}, u32[]{:S(2)}, u32[]{:S(2)}) collective-permute-start(bf16[256,1024]{1,0:T(8,128)(2,1)S(1)} %get-tuple-element.12), channel_id=1, source_target_pairs={{0,2},{1,3},{2,4},{3,5},{4,6},{5,7},{6,8},{7,9},{8,10},{9,11},{10,... | collective-permute-start | bytes 1572872 | tf_op jit(solution)/shard_map/ppermute | solution.py:15
  43.7 30.5 %collective-permute-start.7 = (bf16[256,1024]{1,0:T(8,128)(2,1)S(1)}, bf16[256,1024]{1,0:T(8,128)(2,1)S(1)}, u32[]{:S(2)}, u32[]{:S(2)}) collective-permute-start(bf16[256,1024]{1,0:T(8,128)(2,1)S(1)} %get-tuple-element.13), channel_id=1, source_target_pairs={{0,2},{1,3},{2,4},{3,5},{4,6},{5,7},{6,8},{7,9},{8,10},{9,11},{10,... | collective-permute-start | bytes 1572872 | tf_op jit(solution)/shard_map/ppermute | solution.py:15
  55.7 29.8 %collective-permute-start.11 = (bf16[256,1024]{1,0:T(8,128)(2,1)S(1)}, bf16[256,1024]{1,0:T(8,128)(2,1)S(1)}, u32[]{:S(2)}, u32[]{:S(2)}) collective-permute-start(bf16[256,1024]{1,0:T(8,128)(2,1)S(1)} %get-tuple-element.4), channel_id=1, source_target_pairs={{0,2},{1,3},{2,4},{3,5},{4,6},{5,7},{6,8},{7,9},{8,10},{9,11},{10,... | collective-permute-start | bytes 1572872 | tf_op jit(solution)/shard_map/ppermute | solution.py:15
  58.8 28.2 %collective-permute-start.6 = (bf16[256,1024]{1,0:T(8,128)(2,1)}, bf16[256,1024]{1,0:T(8,128)(2,1)S(1)}, u32[]{:S(2)}, u32[]{:S(2)}) collective-permute-start(bf16[256,1024]{1,0:T(8,128)(2,1)} %collective-permute-done.5), channel_id=1, source_target_pairs={{0,1},{1,2},{2,3},{3,4},{4,5},{5,6},{6,7},{7,8},{8,9},{9,10},{10,1... | collective-permute-start | bytes 1572872 | tf_op jit(solution)/shard_map/ppermute | solution.py:15
  63.0 26.5 %collective-permute-start.10 = (bf16[256,1024]{1,0:T(8,128)(2,1)}, bf16[256,1024]{1,0:T(8,128)(2,1)S(1)}, u32[]{:S(2)}, u32[]{:S(2)}) collective-permute-start(bf16[256,1024]{1,0:T(8,128)(2,1)} %collective-permute-done.9), channel_id=1, source_target_pairs={{0,1},{1,2},{2,3},{3,4},{4,5},{5,6},{6,7},{7,8},{8,9},{9,10},{10,1... | collective-permute-start | bytes 1572872 | tf_op jit(solution)/shard_map/ppermute | solution.py:15
  65.7 23.8 %copy-start.2 = (bf16[2,1,1024,1024]{3,2,1,0:T(8,128)(2,1)S(1)}, bf16[2,1,1024,1024]{3,2,1,0:T(8,128)(2,1)}, u32[]{:S(2)}) copy-start(bf16[2,1,1024,1024]{3,2,1,0:T(8,128)(2,1)} %param.8) | copy-start | bytes 12582916
  74.3 17.3 %collective-permute-start.8 = (bf16[256,1024]{1,0:T(8,128)(2,1)S(1)}, bf16[256,1024]{1,0:T(8,128)(2,1)S(1)}, u32[]{:S(2)}, u32[]{:S(2)}) collective-permute-start(bf16[256,1024]{1,0:T(8,128)(2,1)S(1)} %collective-permute-done.7), channel_id=1, source_target_pairs={{0,1},{1,2},{2,3},{3,4},{4,5},{5,6},{6,7},{7,8},{8,9},{9,10},{10,1... | collective-permute-start | bytes 1572872 | tf_op jit(solution)/shard_map/ppermute | solution.py:15
  85.5 6.8 %collective-permute-start.12 = (bf16[256,1024]{1,0:T(8,128)(2,1)S(1)}, bf16[256,1024]{1,0:T(8,128)(2,1)S(1)}, u32[]{:S(2)}, u32[]{:S(2)}) collective-permute-start(bf16[256,1024]{1,0:T(8,128)(2,1)S(1)} %collective-permute-done.11), channel_id=1, source_target_pairs={{0,1},{1,2},{2,3},{3,4},{4,5},{5,6},{6,7},{7,8},{8,9},{9,10},{10,1... | collective-permute-start | bytes 1572872 | tf_op jit(solution)/shard_map/ppermute | solution.py:15
  89.5 3.5 %copy-start.4 = (f32[1024,1024]{1,0:T(8,128)S(1)}, f32[1024,1024]{1,0:T(8,128)}, u32[]{:S(2)}) copy-start(f32[1024,1024]{1,0:T(8,128)} %multiply_bitcast_fusion) | copy-start | bytes 12582916
  91.5 2.3 %copy-start = (f32[1024,1024]{1,0:T(8,128)S(1)}, f32[1024,1024]{1,0:T(8,128)}, u32[]{:S(2)}) copy-start(f32[1024,1024]{1,0:T(8,128)} %get-tuple-element.9) | copy-start | bytes 12582916
  91.5 3.5 %copy-start.3 = (bf16[2,1,1024,1024]{3,2,1,0:T(8,128)(2,1)S(1)}, bf16[2,1,1024,1024]{3,2,1,0:T(8,128)(2,1)}, u32[]{:S(2)}) copy-start(bf16[2,1,1024,1024]{3,2,1,0:T(8,128)(2,1)} %param.7) | copy-start | bytes 12582916
  101.7 9.9 %collective-permute-start.13 = (f32[2]{0:T(128)S(1)}, f32[2]{0:T(128)S(1)}, u32[]{:S(2)}, u32[]{:S(2)}) collective-permute-start(f32[2]{0:T(128)S(1)} %pad_maximum_fusion), channel_id=1, source_target_pairs={{0,1},{1,0},{2,3},{3,2},{4,5},{5,4},{6,7},{7,6},{8,9},{9,8},{10,11... | collective-permute-start | bytes 32 | tf_op jit(solution)/shard_map/ppermute | solution.py:23
  113.0 4.2 %collective-permute-start.14 = (f32[2]{0:T(128)S(1)}, f32[2]{0:T(128)S(1)}, u32[]{:S(2)}, u32[]{:S(2)}) collective-permute-start(f32[2]{0:T(128)S(1)} %fusion.72), channel_id=1, source_target_pairs={{0,2},{1,3},{2,0},{3,1},{4,6},{5,7},{6,4},{7,5},{8,10},{9,11},{10,... | collective-permute-start | bytes 32 | tf_op jit(solution)/shard_map/ppermute | solution.py:23
  118.5 4.6 %collective-permute-start.15 = (f32[2]{0:T(128)S(1)}, f32[2]{0:T(128)S(1)}, u32[]{:S(2)}, u32[]{:S(2)}) collective-permute-start(f32[2]{0:T(128)S(1)} %fusion.73), channel_id=1, source_target_pairs={{0,4},{1,5},{2,6},{3,7},{4,0},{5,1},{6,2},{7,3},{8,12},{9,13},{10,... | collective-permute-start | bytes 32 | tf_op jit(solution)/shard_map/ppermute | solution.py:23
  123.1 6.0 %collective-permute-start.16 = (f32[2]{0:T(128)S(1)}, f32[2]{0:T(128)S(1)}, u32[]{:S(2)}, u32[]{:S(2)}) collective-permute-start(f32[2]{0:T(128)S(1)} %add.132), channel_id=1, source_target_pairs={{0,8},{1,9},{2,10},{3,11},{4,12},{5,13},{6,14},{7,15},{8,0},{9,1},... | collective-permute-start | bytes 32 | tf_op jit(solution)/shard_map/ppermute | solution.py:23
  129.1 4.5 %collective-permute-start.17 = (f32[2]{0:T(128)S(1)}, f32[2]{0:T(128)S(1)}, u32[]{:S(2)}, u32[]{:S(2)}) collective-permute-start(f32[2]{0:T(128)S(1)} %add.133), channel_id=1, source_target_pairs={{0,16},{1,17},{2,18},{3,19},{4,20},{5,21},{6,22},{7,23},{8,24},{9,... | collective-permute-start | bytes 32 | tf_op jit(solution)/shard_map/ppermute | solution.py:23

commit v5 on v4

--- a/solution.py
+++ b/solution.py
@@ -15,14 +15,10 @@
     return lax.ppermute(block, AXES, route)
 
 
-def butterfly_sum(values):
+def all_sum(values):
     count = lax.axis_size(AXES)
-    bit = 1
-    while bit < count:
-        route = [(i, i ^ bit) for i in range(count) if (i ^ bit) < count]
-        values = values + lax.ppermute(values, AXES, route)
-        bit *= 2
-    return values
+    spread = jnp.broadcast_to(values[None], (count,) + values.shape)
+    return jnp.sum(lax.all_to_all(spread, AXES, 0, 0, tiled=True), axis=0)
 
 
 def row_major(array):
@@ -53,7 +49,7 @@
 
     masked = state[0] * live
     column_sums = lax.optimization_barrier(jnp.sum(masked * masked, axis=0))
-    start_sum = butterfly_sum(jnp.sum(column_sums))
+    start_sum = all_sum(jnp.sum(column_sums)[None])[0]
     start_mean = start_sum / entries
     scale = jnp.sqrt(start_mean + 1e-06)
     vector = masked / scale
@@ -95,7 +91,7 @@
     image = jnp.dot(left_env[0, 0], part_zero, preferred_element_type=jnp.float32) + image_one
     image = row_major(image * live)
 
-    sums = butterfly_sum(jnp.stack([jnp.sum(vector * image), jnp.sum(image * image)]))
+    sums = all_sum(jnp.stack([jnp.sum(vector * image), jnp.sum(image * image)]))
     alpha_value = sums[0] / entries
     vector_mean = start_mean / (start_mean + 1e-06)
     residual_mean = sums[1] / entries - alpha_value * alpha_value * (2.0 - vector_mean)

time: 145 us -> 134 us (0.924)
  starting transfers between devices: 57.1 us -> 44.5 us
  waiting for transfers between devices: 29.7 us -> 34.7 us
  between operations: 11 us -> 7.53 us
  other arithmetic: 19.9 us -> 17.8 us
  local copies, waits for them, and re-layouts: 6.27 us -> 8.16 us
    ppermute x10 -> x0, starting transfers between devices: 37.8 us -> none  [butterfly_sum(): values = values + lax.ppermute(values, AXES, route)]
    all_to_all x0 -> x2, starting transfers between devices: none -> 26.6 us  [all_sum(): return jnp.sum(lax.all_to_all(spread, AXES, 0, 0, tiled=True), axis=0)]
    all_to_all x0 -> x2, waiting for transfers between devices: none -> 13.5 us  [all_sum(): return jnp.sum(lax.all_to_all(spread, AXES, 0, 0, tiled=True), axis=0)]
    ppermute x10 -> x0, waiting for transfers between devices: 8.25 us -> none  [butterfly_sum(): values = values + lax.ppermute(values, AXES, route)]
    add x5 -> x0, other arithmetic: 2.7 us -> none  [butterfly_sum(): values = values + lax.ppermute(values, AXES, route)]
    broadcast_in_dim x0 -> x2, local copies, waits for them, and re-layouts: none -> 1.86 us  [all_sum(): spread = jnp.broadcast_to(values[None], (count,) + values.shape)]
  transfers between devices with their start and end apart: 18 -> 10, of which waited for: 13 -> 5; matrix products, arithmetic and copies ran while one was open for 10% -> 11% of each run, Pallas kernels for 0% -> 0%
where the time goes in v5:
time: 134 us; the launch traced here: 133 us
  starting transfers between devices  44.5 us (33%)
  waiting for transfers between devices  34.7 us (26%)
  matrix products  20.6 us (15%)
  other arithmetic  17.8 us (13%)
  local copies, waits for them, and re-layouts  8.16 us (6%)
  between operations  7.53 us (6%)
    all_to_all x2, starting transfers between devices, all_sum(): return jnp.sum(lax.all_to_all(spread, AXES, 0, 0, tiled=True), axis=0)  26.6 us
    ppermute x8, waiting for transfers between devices, shift_up(): return lax.ppermute(block, AXES, route)  21.2 us
    ppermute x8, starting transfers between devices, shift_up(): return lax.ppermute(block, AXES, route)  17.9 us
    all_to_all x2, waiting for transfers between devices, all_sum(): return jnp.sum(lax.all_to_all(spread, AXES, 0, 0, tiled=True), axis=0)  13.5 us
    dot_general x1, matrix products, per_device(): jnp.dot(left_env[1, 0], part_one, preferred_element_type=jnp.float32)  9.37 us
    broadcast_in_dim x1, other arithmetic, per_device(): return (next_vector[None], jnp.stack([alpha_value, beta_value]))  6.96 us
    dot_general x4, matrix products, per_device(): jnp.dot(source, right_env[0, 0], preferred_element_type=jnp.float32)  5.95 us
    dot_general x1, matrix products, per_device(): jnp.dot(left_env[0, 0], part_zero, preferred_element_type=jnp.float32)  5.33 us
  transfers between devices with their start and end apart: 10, of which 5 were waited for; matrix products, arithmetic and copies ran while one was open for 11% of the time, Pallas kernels for 0%

profile of v5, /device:TPU:0, one launch (start us, length us, event | category | flops | bytes accessed | tf_op | source)
XLA Modules:
  0.0 133.3 jit_solution(10867885106111591375)
XLA Ops:
  5.7 4.9 %multiply_reduce_fusion.2 = (f32[1024]{0:T(1024)S(1)}, f32[1024,1024]{1,0:T(8,128)}) fusion(f32[1024]{0:T(1024)S(1)} %get-tuple-element.22, f32[1024]{0:T(1024)S(1)} %get-tuple-element.21, f32[1,1024,1024]{2,1,0:T(8,128)} %param.6), kind=kLoop, calls=%fused_computation.7 | loop fusion | flops 4193280 | bytes 8400896 | tf_op jit(solution)/shard_map/reduce_sum | solution.py:51
  11.2 1.3 broadcast_in_dim.6
  12.5 7.3 %all-to-all-start = ((f32[32,1,1]{2,1,0:T(1,128)}), f32[32,1,1]{2,1,0:T(1,128)S(1)}, u32[]{:S(2)}, u32[]{:S(2)}) async-start(f32[32,1,1]{2,1,0:T(1,128)} %broadcast_in_dim.6), calls=%async_computation | async-start | bytes 32768 | tf_op jit(solution)/shard_map/all_to_all | solution.py:21
  20.5 6.4 %all-to-all-done = f32[32,1,1]{2,1,0:T(1,128)S(1)} async-done(((f32[32,1,1]{2,1,0:T(1,128)}), f32[32,1,1]{2,1,0:T(1,128)S(1)}, u32[]{:S(2)}, u32[]{:S(2)}) %all-to-all-start) | async-done | bytes 160 | tf_op jit(solution)/shard_map/all_to_all | solution.py:21
  28.2 2.8 %fusion.49 = (bf16[256,1024]{1,0:T(8,128)(2,1)S(1)}, bf16[256,1024]{1,0:T(8,128)(2,1)S(1)}, bf16[256,1024]{1,0:T(8,128)(2,1)S(1)}, bf16[256,1024]{1,0:T(8,128)(2,1)S(1)}) fusion(f32[1024,1024]{1,0:T(8,128)} %get-tuple-element.9, f32[]{:T(128)S(6)} %sqrt.6), kind=kLoop, calls=%fused_computation.54 | loop fusion | flops 2097152 | bytes 6291460 | tf_op jit(solution)/shard_map/convert_element_type | solution.py:58
  31.0 3.3 %collective-permute-start = (bf16[256,1024]{1,0:T(8,128)(2,1)S(1)}, bf16[256,1024]{1,0:T(8,128)(2,1)}, u32[]{:S(2)}, u32[]{:S(2)}) collective-permute-start(bf16[256,1024]{1,0:T(8,128)(2,1)S(1)} %get-tuple-element.10), channel_id=1, source_target_pairs={{0,2},{1,3},{2,4},{3,5},{4,6},{5,7},{6,8},{7,9},{8,10},{9,11},{10,... | collective-permute-start | bytes 1572872 | tf_op jit(solution)/shard_map/ppermute | solution.py:15
  34.3 2.5 %collective-permute-start.4 = (bf16[256,1024]{1,0:T(8,128)(2,1)S(1)}, bf16[256,1024]{1,0:T(8,128)(2,1)}, u32[]{:S(2)}, u32[]{:S(2)}) collective-permute-start(bf16[256,1024]{1,0:T(8,128)(2,1)S(1)} %get-tuple-element.12), channel_id=1, source_target_pairs={{0,2},{1,3},{2,4},{3,5},{4,6},{5,7},{6,8},{7,9},{8,10},{9,11},{10,... | collective-permute-start | bytes 1572872 | tf_op jit(solution)/shard_map/ppermute | solution.py:15
  36.7 1.7 %collective-permute-start.2 = (bf16[256,1024]{1,0:T(8,128)(2,1)S(1)}, bf16[256,1024]{1,0:T(8,128)(2,1)S(1)}, u32[]{:S(2)}, u32[]{:S(2)}) collective-permute-start(bf16[256,1024]{1,0:T(8,128)(2,1)S(1)} %get-tuple-element.13), channel_id=1, source_target_pairs={{0,2},{1,3},{2,4},{3,5},{4,6},{5,7},{6,8},{7,9},{8,10},{9,11},{10,... | collective-permute-start | bytes 1572872 | tf_op jit(solution)/shard_map/ppermute | solution.py:15
  38.5 9.4 %multiply_bitcast_fusion = f32[1024,1024]{1,0:T(8,128)} fusion(bf16[2,1,1024,1024]{3,2,1,0:T(8,128)(2,1)} %param.7, f32[]{:T(128)} %bitcast.7, bf16[256,1024]{1,0:T(8,128)(2,1)S(1)} %get-tuple-element.4, bf16[256,1024]{1,0:T(8,128)(2,1)S(1)} %get-tuple-element.12, bf16[256,1024]{1,0:T(8,128)(2,1)S(1)} %get-tuple-element.13, ...), kind=kOutput, calls=%fused_computation.6 | convolution fusion | flops 4305453056 | bytes 10486272 | tf_op jit(solution)/shard_map/dot_general | solution.py:77
  47.8 5.2 %collective-permute-start.6 = (bf16[256,1024]{1,0:T(8,128)(2,1)S(1)}, bf16[256,1024]{1,0:T(8,128)(2,1)S(1)}, u32[]{:S(2)}, u32[]{:S(2)}) collective-permute-start(bf16[256,1024]{1,0:T(8,128)(2,1)S(1)} %get-tuple-element.4), channel_id=1, source_target_pairs={{0,2},{1,3},{2,4},{3,5},{4,6},{5,7},{6,8},{7,9},{8,10},{9,11},{10,... | collective-permute-start | bytes 1572872 | tf_op jit(solution)/shard_map/ppermute | solution.py:15
  53.1 1.3 collective-permute-start.1
  54.4 2.6 %collective-permute-done.4 = bf16[256,1024]{1,0:T(8,128)(2,1)} collective-permute-done((bf16[256,1024]{1,0:T(8,128)(2,1)S(1)}, bf16[256,1024]{1,0:T(8,128)(2,1)}, u32[]{:S(2)}, u32[]{:S(2)}) %collective-permute-start.4) | collective-permute-done | bytes 524320 | tf_op jit(solution)/shard_map/ppermute | solution.py:15
  57.0 1.3 collective-permute-start.5
  59.6 8.6 %collective-permute-done.2 = bf16[256,1024]{1,0:T(8,128)(2,1)S(1)} collective-permute-done((bf16[256,1024]{1,0:T(8,128)(2,1)S(1)}, bf16[256,1024]{1,0:T(8,128)(2,1)S(1)}, u32[]{:S(2)}, u32[]{:S(2)}) %collective-permute-start.2) | collective-permute-done | bytes 524320 | tf_op jit(solution)/shard_map/ppermute | solution.py:15
  68.2 1.3 collective-permute-start.3
  69.6 9.9 %collective-permute-done.6 = bf16[256,1024]{1,0:T(8,128)(2,1)S(1)} collective-permute-done((bf16[256,1024]{1,0:T(8,128)(2,1)S(1)}, bf16[256,1024]{1,0:T(8,128)(2,1)S(1)}, u32[]{:S(2)}, u32[]{:S(2)}) %collective-permute-start.6) | collective-permute-done | bytes 524320 | tf_op jit(solution)/shard_map/ppermute | solution.py:15
  79.5 1.3 collective-permute-start.7
  80.8 2.5 %fusion.34 = bf16[256,1024]{1,0:T(8,128)(2,1)S(1)} fusion(bf16[2,1,1024,1024]{3,2,1,0:T(8,128)(2,1)} %param.8, bf16[256,1024]{1,0:T(8,128)(2,1)S(1)} %collective-permute-done.1, bf16[256,1024]{1,0:T(8,128)(2,1)} %collective-permute-done, f32[]{:T(128)S(6)} %select_n.75, f32[]{:T(128)S(6)} %select_n.67), kind=kOutput, calls=%fused_computation.43 | convolution fusion | flops 538705920 | bytes 3670024 | tf_op jit(solution)/shard_map/dot_general | solution.py:88
  83.3 2.0 %fusion.40 = bf16[256,1024]{1,0:T(8,128)(2,1)S(1)} fusion(bf16[2,1,1024,1024]{3,2,1,0:T(8,128)(2,1)S(1)} %copy-done.2, bf16[256,1024]{1,0:T(8,128)(2,1)S(1)} %collective-permute-done.5, bf16[256,1024]{1,0:T(8,128)(2,1)} %collective-permute-done.4, f32[]{:T(128)S(6)} %select_n.75, f32[]{:T(128)S(6)} %select_n.67), kind=kOutput, calls=%fused_computation.45 | convolution fusion | flops 538705920 | bytes 3670024 | tf_op jit(solution)/shard_map/dot_general | solution.py:88
  88.8 5.3 %multiply_reduce_fusion.1 = (f32[]{:T(128)}, f32[]{:T(128)}, f32[1024,1024]{1,0:T(8,128)}) fusion(f32[1024,1024]{1,0:T(8,128)S(1)} %copy-done, f32[]{:T(128)S(6)} %sqrt.6, f32[1024]{0:T(1024)S(1)} %get-tuple-element.22, f32[1024]{0:T(1024)S(1)} %get-tuple-element.21, f32[1024,1024]{1,0:T(8,128)S(1)} %copy-done.4, bf16[256,1024]{1,0:T(8,128)(2,1)S(1)} %fusion.43, ...), kind=kOutput, calls=%fused_computation.5 | convolution fusion | flops 2164260864 | bytes 16785420 | tf_op jit(solution)/shard_map/dot_general | solution.py:91
  94.1 1.3 %pad_maximum_fusion = f32[2]{0:T(128)S(1)} fusion(f32[1]{0:T(128)} %bitcast.14, f32[1]{0:T(128)} %bitcast.13), kind=kLoop, calls=%fused_computation.78 | loop fusion | flops 2 | bytes 16 | tf_op jit(solution)/shard_map/stack | solution.py:94
  96.0 19.3 %all-to-all-start.1 = ((f32[32,1,2]{2,1,0:T(1,128)}), f32[32,1,2]{2,1,0:T(1,128)S(1)}, u32[]{:S(2)}, u32[]{:S(2)}) async-start(f32[32,1,2]{2,1,0:T(1,128)} %broadcast_in_dim.7), calls=%async_computation.1 | async-start | bytes 32768 | tf_op jit(solution)/shard_map/all_to_all | solution.py:21
  115.4 7.1 %all-to-all-done.1 = f32[32,1,2]{2,1,0:T(1,128)S(1)} async-done(((f32[32,1,2]{2,1,0:T(1,128)}), f32[32,1,2]{2,1,0:T(1,128)S(1)}, u32[]{:S(2)}, u32[]{:S(2)}) %all-to-all-start.1) | async-done | bytes 288 | tf_op jit(solution)/shard_map/all_to_all | solution.py:21
  126.4 7.0 %divide_bitcast_fusion = f32[1,1024,1024]{2,1,0:T(8,128)} fusion(f32[1024,1024]{1,0:T(8,128)} %get-tuple-element.20, f32[]{:T(128)} %sqrt.7, f32[]{:T(128)} %bitcast.15, f32[1024,1024]{1,0:T(8,128)} %get-tuple-element.9, f32[]{:T(128)S(6)} %sqrt.6), kind=kLoop, calls=%fused_computation.3 | loop fusion | flops 4194304 | bytes 12582924 | tf_op jit(solution)/shard_map/broadcast_in_dim | solution.py:101
  (30 shorter events, 10.3 us)
Async XLA Ops:
  5.7 14.1 %copy-start.1 = (f32[2,4,4]{2,1,0:T(4,128)S(1)}, f32[2,4,4]{2,1,0:T(4,128)}, u32[]{:S(2)}) copy-start(f32[2,4,4]{2,1,0:T(4,128)} %param.9) | copy-start | bytes 388
  12.5 14.4 %all-to-all-start = ((f32[32,1,1]{2,1,0:T(1,128)}), f32[32,1,1]{2,1,0:T(1,128)S(1)}, u32[]{:S(2)}, u32[]{:S(2)}) async-start(f32[32,1,1]{2,1,0:T(1,128)} %broadcast_in_dim.6), calls=%async_computation | async-start | bytes 32768 | tf_op jit(solution)/shard_map/all_to_all | solution.py:21
  31.0 22.0 %collective-permute-start = (bf16[256,1024]{1,0:T(8,128)(2,1)S(1)}, bf16[256,1024]{1,0:T(8,128)(2,1)}, u32[]{:S(2)}, u32[]{:S(2)}) collective-permute-start(bf16[256,1024]{1,0:T(8,128)(2,1)S(1)} %get-tuple-element.10), channel_id=1, source_target_pairs={{0,2},{1,3},{2,4},{3,5},{4,6},{5,7},{6,8},{7,9},{8,10},{9,11},{10,... | collective-permute-start | bytes 1572872 | tf_op jit(solution)/shard_map/ppermute | solution.py:15
  34.3 22.7 %collective-permute-start.4 = (bf16[256,1024]{1,0:T(8,128)(2,1)S(1)}, bf16[256,1024]{1,0:T(8,128)(2,1)}, u32[]{:S(2)}, u32[]{:S(2)}) collective-permute-start(bf16[256,1024]{1,0:T(8,128)(2,1)S(1)} %get-tuple-element.12), channel_id=1, source_target_pairs={{0,2},{1,3},{2,4},{3,5},{4,6},{5,7},{6,8},{7,9},{8,10},{9,11},{10,... | collective-permute-start | bytes 1572872 | tf_op jit(solution)/shard_map/ppermute | solution.py:15
  36.7 31.5 %collective-permute-start.2 = (bf16[256,1024]{1,0:T(8,128)(2,1)S(1)}, bf16[256,1024]{1,0:T(8,128)(2,1)S(1)}, u32[]{:S(2)}, u32[]{:S(2)}) collective-permute-start(bf16[256,1024]{1,0:T(8,128)(2,1)S(1)} %get-tuple-element.13), channel_id=1, source_target_pairs={{0,2},{1,3},{2,4},{3,5},{4,6},{5,7},{6,8},{7,9},{8,10},{9,11},{10,... | collective-permute-start | bytes 1572872 | tf_op jit(solution)/shard_map/ppermute | solution.py:15
  47.8 31.6 %collective-permute-start.6 = (bf16[256,1024]{1,0:T(8,128)(2,1)S(1)}, bf16[256,1024]{1,0:T(8,128)(2,1)S(1)}, u32[]{:S(2)}, u32[]{:S(2)}) collective-permute-start(bf16[256,1024]{1,0:T(8,128)(2,1)S(1)} %get-tuple-element.4), channel_id=1, source_target_pairs={{0,2},{1,3},{2,4},{3,5},{4,6},{5,7},{6,8},{7,9},{8,10},{9,11},{10,... | collective-permute-start | bytes 1572872 | tf_op jit(solution)/shard_map/ppermute | solution.py:15
  53.1 27.8 %collective-permute-start.1 = (bf16[256,1024]{1,0:T(8,128)(2,1)}, bf16[256,1024]{1,0:T(8,128)(2,1)S(1)}, u32[]{:S(2)}, u32[]{:S(2)}) collective-permute-start(bf16[256,1024]{1,0:T(8,128)(2,1)} %collective-permute-done), channel_id=1, source_target_pairs={{0,1},{1,2},{2,3},{3,4},{4,5},{5,6},{6,7},{7,8},{8,9},{9,10},{10,1... | collective-permute-start | bytes 1572872 | tf_op jit(solution)/shard_map/ppermute | solution.py:15
  57.0 26.3 %collective-permute-start.5 = (bf16[256,1024]{1,0:T(8,128)(2,1)}, bf16[256,1024]{1,0:T(8,128)(2,1)S(1)}, u32[]{:S(2)}, u32[]{:S(2)}) collective-permute-start(bf16[256,1024]{1,0:T(8,128)(2,1)} %collective-permute-done.4), channel_id=1, source_target_pairs={{0,1},{1,2},{2,3},{3,4},{4,5},{5,6},{6,7},{7,8},{8,9},{9,10},{10,1... | collective-permute-start | bytes 1572872 | tf_op jit(solution)/shard_map/ppermute | solution.py:15
  59.6 23.7 %copy-start.2 = (bf16[2,1,1024,1024]{3,2,1,0:T(8,128)(2,1)S(1)}, bf16[2,1,1024,1024]{3,2,1,0:T(8,128)(2,1)}, u32[]{:S(2)}) copy-start(bf16[2,1,1024,1024]{3,2,1,0:T(8,128)(2,1)} %param.8) | copy-start | bytes 12582916
  68.2 17.1 %collective-permute-start.3 = (bf16[256,1024]{1,0:T(8,128)(2,1)S(1)}, bf16[256,1024]{1,0:T(8,128)(2,1)S(1)}, u32[]{:S(2)}, u32[]{:S(2)}) collective-permute-start(bf16[256,1024]{1,0:T(8,128)(2,1)S(1)} %collective-permute-done.2), channel_id=1, source_target_pairs={{0,1},{1,2},{2,3},{3,4},{4,5},{5,6},{6,7},{7,8},{8,9},{9,10},{10,1... | collective-permute-start | bytes 1572872 | tf_op jit(solution)/shard_map/ppermute | solution.py:15
  79.5 6.6 %collective-permute-start.7 = (bf16[256,1024]{1,0:T(8,128)(2,1)S(1)}, bf16[256,1024]{1,0:T(8,128)(2,1)S(1)}, u32[]{:S(2)}, u32[]{:S(2)}) collective-permute-start(bf16[256,1024]{1,0:T(8,128)(2,1)S(1)} %collective-permute-done.6), channel_id=1, source_target_pairs={{0,1},{1,2},{2,3},{3,4},{4,5},{5,6},{6,7},{7,8},{8,9},{9,10},{10,1... | collective-permute-start | bytes 1572872 | tf_op jit(solution)/shard_map/ppermute | solution.py:15
  83.3 3.5 %copy-start.4 = (f32[1024,1024]{1,0:T(8,128)S(1)}, f32[1024,1024]{1,0:T(8,128)}, u32[]{:S(2)}) copy-start(f32[1024,1024]{1,0:T(8,128)} %multiply_bitcast_fusion) | copy-start | bytes 12582916
  85.3 2.3 %copy-start = (f32[1024,1024]{1,0:T(8,128)S(1)}, f32[1024,1024]{1,0:T(8,128)}, u32[]{:S(2)}) copy-start(f32[1024,1024]{1,0:T(8,128)} %get-tuple-element.9) | copy-start | bytes 12582916
  85.3 3.5 %copy-start.3 = (bf16[2,1,1024,1024]{3,2,1,0:T(8,128)(2,1)S(1)}, bf16[2,1,1024,1024]{3,2,1,0:T(8,128)(2,1)}, u32[]{:S(2)}) copy-start(bf16[2,1,1024,1024]{3,2,1,0:T(8,128)(2,1)} %param.7) | copy-start | bytes 12582916
  96.0 26.5 %all-to-all-start.1 = ((f32[32,1,2]{2,1,0:T(1,128)}), f32[32,1,2]{2,1,0:T(1,128)S(1)}, u32[]{:S(2)}, u32[]{:S(2)}) async-start(f32[32,1,2]{2,1,0:T(1,128)} %broadcast_in_dim.7), calls=%async_computation.1 | async-start | bytes 32768 | tf_op jit(solution)/shard_map/all_to_all | solution.py:21

commit v6 on v5

--- a/solution.py
+++ b/solution.py
@@ -87,8 +87,14 @@
         parts.append(
             jnp.dot(source, right_env[0, 0], preferred_element_type=jnp.float32).astype(jnp.bfloat16)
         )
-    part_zero = jnp.concatenate(parts, axis=0)
-    image = jnp.dot(left_env[0, 0], part_zero, preferred_element_type=jnp.float32) + image_one
+    early = (CHUNKS - 1) * rows
+    image = image_one + jnp.dot(
+        left_env[0, 0][:, :early], jnp.concatenate(parts[:-1], axis=0),
+        preferred_element_type=jnp.float32,
+    )
+    image = image + jnp.dot(
+        left_env[0, 0][:, early:], parts[-1], preferred_element_type=jnp.float32
+    )
     image = row_major(image * live)
 
     sums = all_sum(jnp.stack([jnp.sum(vector * image), jnp.sum(image * image)]))

time: 134 us -> 142 us (1.060)
  matrix products: 20.6 us -> 30.5 us
  waiting for transfers between devices: 34.7 us -> 31.6 us
    dot_general x1 -> x2, matrix products: 5.33 us -> 13.2 us  [the longest x1 8.36 us: per_device(): jnp.dot(left_env[0, 0][:, :early], jnp.concatenate(parts[:-1], axis=0), p...]
    ppermute x8, waiting for transfers between devices: 21.2 us -> 18 us  [shift_up(): return lax.ppermute(block, AXES, route)]
    dot_general x4 -> x3, matrix products: 5.95 us -> 7.94 us  [per_device(): jnp.dot(source, right_env[0, 0], preferred_element_type=jnp.float32)]
    unnamed x10 -> x4, local copies, waits for them, and re-layouts: 1.92 us -> 0.01 us
    squeeze x0 -> x1, local copies, waits for them, and re-layouts: none -> 1.76 us  [per_device(): left_env[0, 0][:, :early]]
    ppermute x8, starting transfers between devices: 17.9 us -> 19.4 us  [shift_up(): return lax.ppermute(block, AXES, route)]
  transfers between devices with their start and end apart: 10 -> 10, of which waited for: 5 -> 5; matrix products, arithmetic and copies ran while one was open for 11% -> 14% of each run, Pallas kernels for 0% -> 0%
where the time goes in v6:
time: 142 us; the launch traced here: 141 us
  starting transfers between devices  45.2 us (32%)
  waiting for transfers between devices  31.6 us (22%)
  matrix products  30.5 us (21%)
  other arithmetic  18.7 us (13%)
  local copies, waits for them, and re-layouts  7.91 us (6%)
  between operations  7.35 us (5%)
    all_to_all x2, starting transfers between devices, all_sum(): return jnp.sum(lax.all_to_all(spread, AXES, 0, 0, tiled=True), axis=0)  25.8 us
    ppermute x8, starting transfers between devices, shift_up(): return lax.ppermute(block, AXES, route)  19.4 us
    ppermute x8, waiting for transfers between devices, shift_up(): return lax.ppermute(block, AXES, route)  18 us
    all_to_all x2, waiting for transfers between devices, all_sum(): return jnp.sum(lax.all_to_all(spread, AXES, 0, 0, tiled=True), axis=0)  13.5 us
    dot_general x1, matrix products, per_device(): jnp.dot(left_env[1, 0], part_one, preferred_element_type=jnp.float32)  9.39 us
    dot_general x1, matrix products, per_device(): jnp.dot(left_env[0, 0][:, :early], jnp.concatenate(parts[:-1], axis=0), p...  8.36 us
    dot_general x3, matrix products, per_device(): jnp.dot(source, right_env[0, 0], preferred_element_type=jnp.float32)  7.94 us
    broadcast_in_dim x1, other arithmetic, per_device(): return (next_vector[None], jnp.stack([alpha_value, beta_value]))  6.96 us
  transfers between devices with their start and end apart: 10, of which 5 were waited for; matrix products, arithmetic and copies ran while one was open for 14% of the time, Pallas kernels for 0%

profile of v6, /device:TPU:0, one launch (start us, length us, event | category | flops | bytes accessed | tf_op | source)
XLA Modules:
  0.0 141.2 jit_solution(3242478847881420482)
XLA Ops:
  5.7 4.9 %multiply_reduce_fusion.2 = (f32[1024]{0:T(1024)S(1)}, f32[1024,1024]{1,0:T(8,128)}) fusion(f32[1024]{0:T(1024)S(1)} %get-tuple-element.22, f32[1024]{0:T(1024)S(1)} %get-tuple-element.21, f32[1,1024,1024]{2,1,0:T(8,128)} %param.6), kind=kLoop, calls=%fused_computation.8 | loop fusion | flops 4193280 | bytes 8400896 | tf_op jit(solution)/shard_map/reduce_sum | solution.py:51
  12.5 7.3 %all-to-all-start = ((f32[32,1,1]{2,1,0:T(1,128)}), f32[32,1,1]{2,1,0:T(1,128)S(1)}, u32[]{:S(2)}, u32[]{:S(2)}) async-start(f32[32,1,1]{2,1,0:T(1,128)} %broadcast_in_dim.6), calls=%async_computation | async-start | bytes 32768 | tf_op jit(solution)/shard_map/all_to_all | solution.py:21
  20.5 6.5 %all-to-all-done = f32[32,1,1]{2,1,0:T(1,128)S(1)} async-done(((f32[32,1,1]{2,1,0:T(1,128)}), f32[32,1,1]{2,1,0:T(1,128)S(1)}, u32[]{:S(2)}, u32[]{:S(2)}) %all-to-all-start) | async-done | bytes 160 | tf_op jit(solution)/shard_map/all_to_all | solution.py:21
  28.2 3.5 %fusion.49 = (bf16[256,1024]{1,0:T(8,128)(2,1)S(1)}, bf16[256,1024]{1,0:T(8,128)(2,1)S(1)}, bf16[256,1024]{1,0:T(8,128)(2,1)S(1)}, bf16[256,1024]{1,0:T(8,128)(2,1)}) fusion(f32[1024,1024]{1,0:T(8,128)} %get-tuple-element.9, f32[]{:T(128)S(6)} %sqrt.6), kind=kLoop, calls=%fused_computation.54 | loop fusion | flops 2097152 | bytes 6291460 | tf_op jit(solution)/shard_map/convert_element_type | solution.py:58
  31.8 3.3 %collective-permute-start = (bf16[256,1024]{1,0:T(8,128)(2,1)S(1)}, bf16[256,1024]{1,0:T(8,128)(2,1)}, u32[]{:S(2)}, u32[]{:S(2)}) collective-permute-start(bf16[256,1024]{1,0:T(8,128)(2,1)S(1)} %get-tuple-element.10), channel_id=1, source_target_pairs={{0,2},{1,3},{2,4},{3,5},{4,6},{5,7},{6,8},{7,9},{8,10},{9,11},{10,... | collective-permute-start | bytes 1572872 | tf_op jit(solution)/shard_map/ppermute | solution.py:15
  35.0 2.5 %collective-permute-start.4 = (bf16[256,1024]{1,0:T(8,128)(2,1)S(1)}, bf16[256,1024]{1,0:T(8,128)(2,1)}, u32[]{:S(2)}, u32[]{:S(2)}) collective-permute-start(bf16[256,1024]{1,0:T(8,128)(2,1)S(1)} %get-tuple-element.12), channel_id=1, source_target_pairs={{0,2},{1,3},{2,4},{3,5},{4,6},{5,7},{6,8},{7,9},{8,10},{9,11},{10,... | collective-permute-start | bytes 1572872 | tf_op jit(solution)/shard_map/ppermute | solution.py:15
  37.5 2.5 %collective-permute-start.2 = (bf16[256,1024]{1,0:T(8,128)(2,1)}, bf16[256,1024]{1,0:T(8,128)(2,1)}, u32[]{:S(2)}, u32[]{:S(2)}) collective-permute-start(bf16[256,1024]{1,0:T(8,128)(2,1)} %get-tuple-element.13), channel_id=1, source_target_pairs={{0,2},{1,3},{2,4},{3,5},{4,6},{5,7},{6,8},{7,9},{8,10},{9,11},{10,... | collective-permute-start | bytes 1572872 | tf_op jit(solution)/shard_map/ppermute | solution.py:15
  40.0 9.4 %multiply_bitcast_fusion = f32[1024,1024]{1,0:T(8,128)} fusion(bf16[2,1,1024,1024]{3,2,1,0:T(8,128)(2,1)} %param.7, f32[]{:T(128)} %bitcast, bf16[256,1024]{1,0:T(8,128)(2,1)S(1)} %get-tuple-element.5, bf16[256,1024]{1,0:T(8,128)(2,1)S(1)} %get-tuple-element.12, bf16[256,1024]{1,0:T(8,128)(2,1)} %get-tuple-element.13, ...), kind=kOutput, calls=%fused_computation.7 | convolution fusion | flops 4305453056 | bytes 10486272 | tf_op jit(solution)/shard_map/dot_general | solution.py:77
  49.4 4.4 %collective-permute-start.6 = (bf16[256,1024]{1,0:T(8,128)(2,1)S(1)}, bf16[256,1024]{1,0:T(8,128)(2,1)S(1)}, u32[]{:S(2)}, u32[]{:S(2)}) collective-permute-start(bf16[256,1024]{1,0:T(8,128)(2,1)S(1)} %get-tuple-element.5), channel_id=1, source_target_pairs={{0,2},{1,3},{2,4},{3,5},{4,6},{5,7},{6,8},{7,9},{8,10},{9,11},{10,... | collective-permute-start | bytes 1572872 | tf_op jit(solution)/shard_map/ppermute | solution.py:15
  53.8 2.1 %collective-permute-start.1 = (bf16[256,1024]{1,0:T(8,128)(2,1)}, bf16[256,1024]{1,0:T(8,128)(2,1)}, u32[]{:S(2)}, u32[]{:S(2)}) collective-permute-start(bf16[256,1024]{1,0:T(8,128)(2,1)} %collective-permute-done), channel_id=1, source_target_pairs={{0,1},{1,2},{2,3},{3,4},{4,5},{5,6},{6,7},{7,8},{8,9},{9,10},{10,1... | collective-permute-start | bytes 1572872 | tf_op jit(solution)/shard_map/ppermute | solution.py:15
  57.8 2.0 %collective-permute-start.5 = (bf16[256,1024]{1,0:T(8,128)(2,1)}, bf16[256,1024]{1,0:T(8,128)(2,1)S(1)}, u32[]{:S(2)}, u32[]{:S(2)}) collective-permute-start(bf16[256,1024]{1,0:T(8,128)(2,1)} %collective-permute-done.4), channel_id=1, source_target_pairs={{0,1},{1,2},{2,3},{3,4},{4,5},{5,6},{6,7},{7,8},{8,9},{9,10},{10,1... | collective-permute-start | bytes 1572872 | tf_op jit(solution)/shard_map/ppermute | solution.py:15
  59.8 1.8 %slice_bitcast_fusion = bf16[1024,1024]{1,0:T(8,128)(2,1)S(1)} fusion(bf16[2,1,1024,1024]{3,2,1,0:T(8,128)(2,1)} %param.7), kind=kLoop, calls=%fused_computation.28 | loop fusion | bytes 4194304 | tf_op jit(solution)/shard_map/squeeze | solution.py:92
  61.5 7.6 %collective-permute-done.2 = bf16[256,1024]{1,0:T(8,128)(2,1)} collective-permute-done((bf16[256,1024]{1,0:T(8,128)(2,1)}, bf16[256,1024]{1,0:T(8,128)(2,1)}, u32[]{:S(2)}, u32[]{:S(2)}) %collective-permute-start.2) | collective-permute-done | bytes 524320 | tf_op jit(solution)/shard_map/ppermute | solution.py:15
  70.4 9.8 %collective-permute-done.6 = bf16[256,1024]{1,0:T(8,128)(2,1)S(1)} collective-permute-done((bf16[256,1024]{1,0:T(8,128)(2,1)S(1)}, bf16[256,1024]{1,0:T(8,128)(2,1)S(1)}, u32[]{:S(2)}, u32[]{:S(2)}) %collective-permute-start.6) | collective-permute-done | bytes 524320 | tf_op jit(solution)/shard_map/ppermute | solution.py:15
  80.2 1.3 collective-permute-start.7
  81.6 2.8 %fusion.31 = bf16[256,1024]{1,0:T(8,128)(2,1)} fusion(bf16[2,1,1024,1024]{3,2,1,0:T(8,128)(2,1)S(1)} %copy-done, bf16[256,1024]{1,0:T(8,128)(2,1)} %collective-permute-done.1, bf16[256,1024]{1,0:T(8,128)(2,1)} %collective-permute-done, f32[]{:T(128)S(6)} %select_n.75, f32[]{:T(128)S(6)} %select_n.71), kind=kOutput, calls=%fused_computation.42 | convolution fusion | flops 538705920 | bytes 3670024 | tf_op jit(solution)/shard_map/dot_general | solution.py:88
  84.4 2.6 %fusion.37 = bf16[256,1024]{1,0:T(8,128)(2,1)} fusion(bf16[2,1,1024,1024]{3,2,1,0:T(8,128)(2,1)S(1)} %copy-done, bf16[256,1024]{1,0:T(8,128)(2,1)S(1)} %collective-permute-done.5, bf16[256,1024]{1,0:T(8,128)(2,1)} %collective-permute-done.4, f32[]{:T(128)S(6)} %select_n.75, f32[]{:T(128)S(6)} %select_n.71), kind=kOutput, calls=%fused_computation.44 | convolution fusion | flops 538705920 | bytes 3670024 | tf_op jit(solution)/shard_map/dot_general | solution.py:88
  87.0 2.6 %fusion.34 = bf16[256,1024]{1,0:T(8,128)(2,1)} fusion(bf16[2,1,1024,1024]{3,2,1,0:T(8,128)(2,1)S(1)} %copy-done, bf16[256,1024]{1,0:T(8,128)(2,1)S(1)} %collective-permute-done.3, bf16[256,1024]{1,0:T(8,128)(2,1)} %collective-permute-done.2, f32[]{:T(128)S(6)} %select_n.75, f32[]{:T(128)S(6)} %select_n.71), kind=kOutput, calls=%fused_computation.43 | convolution fusion | flops 538705920 | bytes 3670024 | tf_op jit(solution)/shard_map/dot_general | solution.py:88
  89.5 4.8 %fusion.44 = f32[1024,1024]{0,1:T(8,128)} fusion(bf16[2,1,1024,1024]{3,2,1,0:T(8,128)(2,1)} %param.8, bf16[256,1024]{1,0:T(8,128)(2,1)S(1)} %collective-permute-done.7, bf16[256,1024]{1,0:T(8,128)(2,1)S(1)} %collective-permute-done.6, bf16[1024,1024]{1,0:T(8,128)(2,1)S(1)} %slice_bitcast_fusion, f32[]{:T(128)S(6)} %select_n.75, f32[]{:T(128)S(6)} %select_n.71), kind=kOutput, calls=%fused_computation.46 | convolution fusion | flops 1075576832 | bytes 7864328 | tf_op jit(solution)/shard_map/dot_general | solution.py:95
  94.4 8.4 %multiply_reduce_fusion.1 = (f32[]{:T(128)}, f32[]{:T(128)}, f32[1024,1024]{1,0:T(8,128)}) fusion(f32[1024,1024]{1,0:T(8,128)} %get-tuple-element.9, f32[]{:T(128)S(6)} %sqrt.6, f32[1024]{0:T(1024)S(1)} %get-tuple-element.22, f32[1024]{0:T(1024)S(1)} %get-tuple-element.21, f32[1024,1024]{0,1:T(8,128)} %fusion.44, f32[1024,1024]{1,0:T(8,128)} %multiply_bitcast_fusion, ...), kind=kOutput, calls=%fused_computation.6 | convolution fusion | flops 1624768512 | bytes 19931148 | tf_op jit(solution)/shard_map/dot_general | solution.py:91
  102.7 1.4 pad_maximum_fusion
  104.7 18.5 %all-to-all-start.1 = ((f32[32,1,2]{2,1,0:T(1,128)}), f32[32,1,2]{2,1,0:T(1,128)S(1)}, u32[]{:S(2)}, u32[]{:S(2)}) async-start(f32[32,1,2]{2,1,0:T(1,128)} %broadcast_in_dim.7), calls=%async_computation.1 | async-start | bytes 32768 | tf_op jit(solution)/shard_map/all_to_all | solution.py:21
  123.3 7.1 %all-to-all-done.1 = f32[32,1,2]{2,1,0:T(1,128)S(1)} async-done(((f32[32,1,2]{2,1,0:T(1,128)}), f32[32,1,2]{2,1,0:T(1,128)S(1)}, u32[]{:S(2)}, u32[]{:S(2)}) %all-to-all-start.1) | async-done | bytes 288 | tf_op jit(solution)/shard_map/all_to_all | solution.py:21
  134.2 7.0 %divide_bitcast_fusion = f32[1,1024,1024]{2,1,0:T(8,128)} fusion(f32[1024,1024]{1,0:T(8,128)} %get-tuple-element.20, f32[]{:T(128)} %sqrt.7, f32[]{:T(128)} %bitcast.16, f32[1024,1024]{1,0:T(8,128)} %get-tuple-element.9, f32[]{:T(128)S(6)} %sqrt.6), kind=kLoop, calls=%fused_computation.4 | loop fusion | flops 4194304 | bytes 12582924 | tf_op jit(solution)/shard_map/broadcast_in_dim | solution.py:107
  (25 shorter events, 10.0 us)
Async XLA Ops:
  5.7 14.1 %copy-start.1 = (f32[2,4,4]{2,1,0:T(4,128)S(1)}, f32[2,4,4]{2,1,0:T(4,128)}, u32[]{:S(2)}) copy-start(f32[2,4,4]{2,1,0:T(4,128)} %param.9) | copy-start | bytes 388
  12.5 14.4 %all-to-all-start = ((f32[32,1,1]{2,1,0:T(1,128)}), f32[32,1,1]{2,1,0:T(1,128)S(1)}, u32[]{:S(2)}, u32[]{:S(2)}) async-start(f32[32,1,1]{2,1,0:T(1,128)} %broadcast_in_dim.6), calls=%async_computation | async-start | bytes 32768 | tf_op jit(solution)/shard_map/all_to_all | solution.py:21
  31.8 22.0 %collective-permute-start = (bf16[256,1024]{1,0:T(8,128)(2,1)S(1)}, bf16[256,1024]{1,0:T(8,128)(2,1)}, u32[]{:S(2)}, u32[]{:S(2)}) collective-permute-start(bf16[256,1024]{1,0:T(8,128)(2,1)S(1)} %get-tuple-element.10), channel_id=1, source_target_pairs={{0,2},{1,3},{2,4},{3,5},{4,6},{5,7},{6,8},{7,9},{8,10},{9,11},{10,... | collective-permute-start | bytes 1572872 | tf_op jit(solution)/shard_map/ppermute | solution.py:15
  35.0 22.7 %collective-permute-start.4 = (bf16[256,1024]{1,0:T(8,128)(2,1)S(1)}, bf16[256,1024]{1,0:T(8,128)(2,1)}, u32[]{:S(2)}, u32[]{:S(2)}) collective-permute-start(bf16[256,1024]{1,0:T(8,128)(2,1)S(1)} %get-tuple-element.12), channel_id=1, source_target_pairs={{0,2},{1,3},{2,4},{3,5},{4,6},{5,7},{6,8},{7,9},{8,10},{9,11},{10,... | collective-permute-start | bytes 1572872 | tf_op jit(solution)/shard_map/ppermute | solution.py:15
  37.5 31.6 %collective-permute-start.2 = (bf16[256,1024]{1,0:T(8,128)(2,1)}, bf16[256,1024]{1,0:T(8,128)(2,1)}, u32[]{:S(2)}, u32[]{:S(2)}) collective-permute-start(bf16[256,1024]{1,0:T(8,128)(2,1)} %get-tuple-element.13), channel_id=1, source_target_pairs={{0,2},{1,3},{2,4},{3,5},{4,6},{5,7},{6,8},{7,9},{8,10},{9,11},{10,... | collective-permute-start | bytes 1572872 | tf_op jit(solution)/shard_map/ppermute | solution.py:15
  49.4 30.9 %collective-permute-start.6 = (bf16[256,1024]{1,0:T(8,128)(2,1)S(1)}, bf16[256,1024]{1,0:T(8,128)(2,1)S(1)}, u32[]{:S(2)}, u32[]{:S(2)}) collective-permute-start(bf16[256,1024]{1,0:T(8,128)(2,1)S(1)} %get-tuple-element.5), channel_id=1, source_target_pairs={{0,2},{1,3},{2,4},{3,5},{4,6},{5,7},{6,8},{7,9},{8,10},{9,11},{10,... | collective-permute-start | bytes 1572872 | tf_op jit(solution)/shard_map/ppermute | solution.py:15
  53.8 27.7 %collective-permute-start.1 = (bf16[256,1024]{1,0:T(8,128)(2,1)}, bf16[256,1024]{1,0:T(8,128)(2,1)}, u32[]{:S(2)}, u32[]{:S(2)}) collective-permute-start(bf16[256,1024]{1,0:T(8,128)(2,1)} %collective-permute-done), channel_id=1, source_target_pairs={{0,1},{1,2},{2,3},{3,4},{4,5},{5,6},{6,7},{7,8},{8,9},{9,10},{10,1... | collective-permute-start | bytes 1572872 | tf_op jit(solution)/shard_map/ppermute | solution.py:15
  57.1 24.5 %copy-start = (bf16[2,1,1024,1024]{3,2,1,0:T(8,128)(2,1)S(1)}, bf16[2,1,1024,1024]{3,2,1,0:T(8,128)(2,1)}, u32[]{:S(2)}) copy-start(bf16[2,1,1024,1024]{3,2,1,0:T(8,128)(2,1)} %param.8) | copy-start | bytes 12582916
  57.8 26.6 %collective-permute-start.5 = (bf16[256,1024]{1,0:T(8,128)(2,1)}, bf16[256,1024]{1,0:T(8,128)(2,1)S(1)}, u32[]{:S(2)}, u32[]{:S(2)}) collective-permute-start(bf16[256,1024]{1,0:T(8,128)(2,1)} %collective-permute-done.4), channel_id=1, source_target_pairs={{0,1},{1,2},{2,3},{3,4},{4,5},{5,6},{6,7},{7,8},{8,9},{9,10},{10,1... | collective-permute-start | bytes 1572872 | tf_op jit(solution)/shard_map/ppermute | solution.py:15
  69.1 17.9 %collective-permute-start.3 = (bf16[256,1024]{1,0:T(8,128)(2,1)}, bf16[256,1024]{1,0:T(8,128)(2,1)S(1)}, u32[]{:S(2)}, u32[]{:S(2)}) collective-permute-start(bf16[256,1024]{1,0:T(8,128)(2,1)} %collective-permute-done.2), channel_id=1, source_target_pairs={{0,1},{1,2},{2,3},{3,4},{4,5},{5,6},{6,7},{7,8},{8,9},{9,10},{10,1... | collective-permute-start | bytes 1572872 | tf_op jit(solution)/shard_map/ppermute | solution.py:15
  80.2 9.3 %collective-permute-start.7 = (bf16[256,1024]{1,0:T(8,128)(2,1)S(1)}, bf16[256,1024]{1,0:T(8,128)(2,1)S(1)}, u32[]{:S(2)}, u32[]{:S(2)}) collective-permute-start(bf16[256,1024]{1,0:T(8,128)(2,1)S(1)} %collective-permute-done.6), channel_id=1, source_target_pairs={{0,1},{1,2},{2,3},{3,4},{4,5},{5,6},{6,7},{7,8},{8,9},{9,10},{10,1... | collective-permute-start | bytes 1572872 | tf_op jit(solution)/shard_map/ppermute | solution.py:15
  104.7 25.7 %all-to-all-start.1 = ((f32[32,1,2]{2,1,0:T(1,128)}), f32[32,1,2]{2,1,0:T(1,128)S(1)}, u32[]{:S(2)}, u32[]{:S(2)}) async-start(f32[32,1,2]{2,1,0:T(1,128)} %broadcast_in_dim.7), calls=%async_computation.1 | async-start | bytes 32768 | tf_op jit(solution)/shard_map/all_to_all | solution.py:21

commit v7 on v5

--- a/solution.py
+++ b/solution.py
@@ -1,8 +1,12 @@
+import functools
+
 import jax
 import jax.numpy as jnp
 from jax import lax
 from jax.sharding import PartitionSpec as P
 from jax.experimental.layout import Layout, with_layout_constraint
+from jax.experimental import pallas as pl
+from jax.experimental.pallas import tpu as pltpu
 
 BLOCK = 256
 AXES = ("left", "right")
@@ -19,6 +23,45 @@
     count = lax.axis_size(AXES)
     spread = jnp.broadcast_to(values[None], (count,) + values.shape)
     return jnp.sum(lax.all_to_all(spread, AXES, 0, 0, tiled=True), axis=0)
+
+
+def square_sum_kernel(pairs, index_ref, left_ref, right_ref, state_ref, out_ref, acc_ref):
+    step = pl.program_id(0)
+    rows, cols = state_ref.shape[1], state_ref.shape[2]
+    sector = index_ref[0] // pairs
+    pair = index_ref[0] % pairs
+    row_limit = left_ref[sector] * BLOCK
+    col_limit = right_ref[sector + (pair + 1) // 2] * BLOCK
+
+    @pl.when(step == 0)
+    def _():
+        acc_ref[...] = jnp.zeros_like(acc_ref)
+
+    x = state_ref[0]
+    row_ids = step * rows + lax.broadcasted_iota(jnp.int32, (rows, cols), 0)
+    col_ids = lax.broadcasted_iota(jnp.int32, (rows, cols), 1)
+    x = jnp.where((row_ids < row_limit) & (col_ids < col_limit), x, 0.0)
+    acc_ref[...] += jnp.sum((x * x).reshape(rows // 8, 8, cols), axis=0)
+
+    @pl.when(step == pl.num_programs(0) - 1)
+    def _():
+        out_ref[0, 0] = jnp.sum(acc_ref[...])
+
+
+def masked_square_sum(pairs, block_index, left_live, right_live, state):
+    sec_size = state.shape[1]
+    rows = 256
+    return pl.pallas_call(
+        functools.partial(square_sum_kernel, pairs),
+        grid_spec=pltpu.PrefetchScalarGridSpec(
+            num_scalar_prefetch=3,
+            grid=(sec_size // rows,),
+            in_specs=[pl.BlockSpec((1, rows, sec_size), lambda i, *_: (0, i, 0))],
+            out_specs=pl.BlockSpec(memory_space=pltpu.SMEM),
+            scratch_shapes=[pltpu.VMEM((8, sec_size), jnp.float32)],
+        ),
+        out_shape=jax.ShapeDtypeStruct((1, 1), jnp.float32),
+    )(block_index.reshape(1), left_live, right_live, state)
 
 
 def row_major(array):
@@ -48,8 +91,9 @@
     entries = float(state.shape[0] * sec_size * sec_size * lax.axis_size(AXES))
 
     masked = state[0] * live
-    column_sums = lax.optimization_barrier(jnp.sum(masked * masked, axis=0))
-    start_sum = all_sum(jnp.sum(column_sums)[None])[0]
+    start_sum = all_sum(
+        masked_square_sum(pairs, block_index.astype(jnp.int32), left_live, right_live, state)[0]
+    )[0]
     start_mean = start_sum / entries
     scale = jnp.sqrt(start_mean + 1e-06)
     vector = masked / scale

time: 134 us -> 131 us (0.978)
  waiting for transfers between devices: 34.7 us -> 28.2 us
  Pallas kernels: 0 us -> 4.71 us
  starting transfers between devices: 44.5 us -> 46.2 us
  other arithmetic: 17.8 us -> 16.4 us
    all_to_all x2, waiting for transfers between devices: 13.5 us -> 7.1 us  [all_sum(): return jnp.sum(lax.all_to_all(spread, AXES, 0, 0, tiled=True), axis=0)]
    reduce_sum x2 -> x0, other arithmetic: 5.48 us -> none  [the longest x1 4.88 us: per_device(): column_sums = lax.optimization_barrier(jnp.sum(masked * masked, axis=0))]
    pallas_call x0 -> x1, Pallas kernels: none -> 4.71 us  [masked_square_sum(): pl.pallas_call(functools.partial(square_sum_kernel, pairs), grid_spec=plt...]
    mul x0 -> x1, other arithmetic: none -> 4.61 us  [per_device(): masked = state[0] * live]
  transfers between devices with their start and end apart: 10 -> 10, of which waited for: 5 -> 4; matrix products, arithmetic and copies ran while one was open for 11% -> 17% of each run, Pallas kernels for 0% -> 0%
where the time goes in v7:
time: 131 us
  starting transfers between devices  46.2 us (35%)
  waiting for transfers between devices  28.2 us (22%)
  matrix products  20.9 us (16%)
  other arithmetic  16.4 us (13%)
  between operations  7.47 us (6%)
  local copies, waits for them, and re-layouts  6.92 us (5%)
  Pallas kernels  4.71 us (4%)
    all_to_all x2, starting transfers between devices, all_sum(): return jnp.sum(lax.all_to_all(spread, AXES, 0, 0, tiled=True), axis=0)  27 us
    ppermute x8, waiting for transfers between devices, shift_up(): return lax.ppermute(block, AXES, route)  21.1 us
    ppermute x8, starting transfers between devices, shift_up(): return lax.ppermute(block, AXES, route)  19.2 us
    dot_general x1, matrix products, per_device(): jnp.dot(left_env[1, 0], part_one, preferred_element_type=jnp.float32)  9.37 us
    all_to_all x2, waiting for transfers between devices, all_sum(): return jnp.sum(lax.all_to_all(spread, AXES, 0, 0, tiled=True), axis=0)  7.1 us
    broadcast_in_dim x1, other arithmetic, per_device(): return (next_vector[None], jnp.stack([alpha_value, beta_value]))  6.43 us
    dot_general x4, matrix products, per_device(): jnp.dot(source, right_env[0, 0], preferred_element_type=jnp.float32)  5.94 us
    dot_general x1, matrix products, per_device(): jnp.dot(left_env[0, 0], part_zero, preferred_element_type=jnp.float32)  5.56 us
  transfers between devices with their start and end apart: 10, of which 4 were waited for; matrix products, arithmetic and copies ran while one was open for 17% of the time, Pallas kernels for 0%

profile of v7, /device:TPU:0, one launch (start us, length us, event | category | flops | bytes accessed | tf_op | source)
XLA Modules:
  0.0 130.8 jit_solution(15747179832368452361)
XLA Ops:
  0.7 4.7 %shard_map.77 = f32[1,1]{1,0:T(1,128)} custom-call(s32[1]{0:T(128)} %bitcast.5.index_ref, s32[8]{0:T(128)} %left_ref.1, s32[10]{0:T(128)} %right_ref.1, f32[1,1024,1024]{2,1,0:T(8,128)} %state_ref.1), custom_call_target="tpu_custom_call" | custom-call | tf_op jit(solution)/shard_map/pallas_call | solution.py:54
  5.4 1.3 broadcast_in_dim.9
  6.6 7.3 %all-to-all-start = ((f32[32,1,1]{2,1,0:T(1,128)}), f32[32,1,1]{2,1,0:T(1,128)S(1)}, u32[]{:S(2)}, u32[]{:S(2)}) async-start(f32[32,1,1]{2,1,0:T(1,128)} %broadcast_in_dim.9), calls=%async_computation | async-start | bytes 32768 | tf_op jit(solution)/shard_map/all_to_all | solution.py:25
  17.9 4.6 %multiply_multiply_fusion.1 = f32[1024,1024]{1,0:T(8,128)} fusion(f32[1,1024,1024]{2,1,0:T(8,128)} %state_ref.1, f32[1024]{0:T(1024)S(1)} %get-tuple-element.20, f32[1024]{0:T(1024)S(1)} %get-tuple-element.19), kind=kLoop, calls=%fused_computation.1 | loop fusion | flops 2097152 | bytes 8396800 | tf_op jit(solution)/shard_map/mul | solution.py:93
  24.4 2.8 %fusion.49 = (bf16[256,1024]{1,0:T(8,128)(2,1)S(1)}, bf16[256,1024]{1,0:T(8,128)(2,1)S(1)}, bf16[256,1024]{1,0:T(8,128)(2,1)S(1)}, bf16[256,1024]{1,0:T(8,128)(2,1)S(1)}) fusion(f32[1024,1024]{1,0:T(8,128)} %multiply_multiply_fusion.1, f32[]{:T(128)S(6)} %sqrt.6), kind=kLoop, calls=%fused_computation.53 | loop fusion | flops 2097152 | bytes 6291460 | tf_op jit(solution)/shard_map/convert_element_type | solution.py:102
  27.2 4.5 %collective-permute-start = (bf16[256,1024]{1,0:T(8,128)(2,1)S(1)}, bf16[256,1024]{1,0:T(8,128)(2,1)}, u32[]{:S(2)}, u32[]{:S(2)}) collective-permute-start(bf16[256,1024]{1,0:T(8,128)(2,1)S(1)} %get-tuple-element.8), channel_id=1, source_target_pairs={{0,2},{1,3},{2,4},{3,5},{4,6},{5,7},{6,8},{7,9},{8,10},{9,11},{10,... | collective-permute-start | bytes 1572872 | tf_op jit(solution)/shard_map/ppermute | solution.py:19
  31.6 3.4 %collective-permute-start.4 = (bf16[256,1024]{1,0:T(8,128)(2,1)S(1)}, bf16[256,1024]{1,0:T(8,128)(2,1)}, u32[]{:S(2)}, u32[]{:S(2)}) collective-permute-start(bf16[256,1024]{1,0:T(8,128)(2,1)S(1)} %get-tuple-element.10), channel_id=1, source_target_pairs={{0,2},{1,3},{2,4},{3,5},{4,6},{5,7},{6,8},{7,9},{8,10},{9,11},{10,... | collective-permute-start | bytes 1572872 | tf_op jit(solution)/shard_map/ppermute | solution.py:19
  35.0 2.7 %collective-permute-start.2 = (bf16[256,1024]{1,0:T(8,128)(2,1)S(1)}, bf16[256,1024]{1,0:T(8,128)(2,1)S(1)}, u32[]{:S(2)}, u32[]{:S(2)}) collective-permute-start(bf16[256,1024]{1,0:T(8,128)(2,1)S(1)} %get-tuple-element.11), channel_id=1, source_target_pairs={{0,2},{1,3},{2,4},{3,5},{4,6},{5,7},{6,8},{7,9},{8,10},{9,11},{10,... | collective-permute-start | bytes 1572872 | tf_op jit(solution)/shard_map/ppermute | solution.py:19
  37.7 9.4 %multiply_bitcast_fusion = f32[1024,1024]{1,0:T(8,128)} fusion(bf16[2,1,1024,1024]{3,2,1,0:T(8,128)(2,1)} %param.7, f32[]{:T(128)} %bitcast.9, bf16[256,1024]{1,0:T(8,128)(2,1)S(1)} %get-tuple-element.4, bf16[256,1024]{1,0:T(8,128)(2,1)S(1)} %get-tuple-element.10, bf16[256,1024]{1,0:T(8,128)(2,1)S(1)} %get-tuple-element.11, ...), kind=kOutput, calls=%fused_computation.6 | convolution fusion | flops 4305453056 | bytes 10486272 | tf_op jit(solution)/shard_map/dot_general | solution.py:121
  47.1 3.3 %collective-permute-start.6 = (bf16[256,1024]{1,0:T(8,128)(2,1)S(1)}, bf16[256,1024]{1,0:T(8,128)(2,1)S(1)}, u32[]{:S(2)}, u32[]{:S(2)}) collective-permute-start(bf16[256,1024]{1,0:T(8,128)(2,1)S(1)} %get-tuple-element.4), channel_id=1, source_target_pairs={{0,2},{1,3},{2,4},{3,5},{4,6},{5,7},{6,8},{7,9},{8,10},{9,11},{10,... | collective-permute-start | bytes 1572872 | tf_op jit(solution)/shard_map/ppermute | solution.py:19
  50.4 1.3 %collective-permute-start.1 = (bf16[256,1024]{1,0:T(8,128)(2,1)}, bf16[256,1024]{1,0:T(8,128)(2,1)S(1)}, u32[]{:S(2)}, u32[]{:S(2)}) collective-permute-start(bf16[256,1024]{1,0:T(8,128)(2,1)} %collective-permute-done), channel_id=1, source_target_pairs={{0,1},{1,2},{2,3},{3,4},{4,5},{5,6},{6,7},{7,8},{8,9},{9,10},{10,1... | collective-permute-start | bytes 1572872 | tf_op jit(solution)/shard_map/ppermute | solution.py:19
  51.7 2.6 %collective-permute-done.4 = bf16[256,1024]{1,0:T(8,128)(2,1)} collective-permute-done((bf16[256,1024]{1,0:T(8,128)(2,1)S(1)}, bf16[256,1024]{1,0:T(8,128)(2,1)}, u32[]{:S(2)}, u32[]{:S(2)}) %collective-permute-start.4) | collective-permute-done | bytes 524320 | tf_op jit(solution)/shard_map/ppermute | solution.py:19
  54.3 1.4 %collective-permute-start.5 = (bf16[256,1024]{1,0:T(8,128)(2,1)}, bf16[256,1024]{1,0:T(8,128)(2,1)S(1)}, u32[]{:S(2)}, u32[]{:S(2)}) collective-permute-start(bf16[256,1024]{1,0:T(8,128)(2,1)} %collective-permute-done.4), channel_id=1, source_target_pairs={{0,1},{1,2},{2,3},{3,4},{4,5},{5,6},{6,7},{7,8},{8,9},{9,10},{10,1... | collective-permute-start | bytes 1572872 | tf_op jit(solution)/shard_map/ppermute | solution.py:19
  57.1 8.5 %collective-permute-done.2 = bf16[256,1024]{1,0:T(8,128)(2,1)S(1)} collective-permute-done((bf16[256,1024]{1,0:T(8,128)(2,1)S(1)}, bf16[256,1024]{1,0:T(8,128)(2,1)S(1)}, u32[]{:S(2)}, u32[]{:S(2)}) %collective-permute-start.2) | collective-permute-done | bytes 524320 | tf_op jit(solution)/shard_map/ppermute | solution.py:19
  65.6 1.3 %collective-permute-start.3 = (bf16[256,1024]{1,0:T(8,128)(2,1)S(1)}, bf16[256,1024]{1,0:T(8,128)(2,1)S(1)}, u32[]{:S(2)}, u32[]{:S(2)}) collective-permute-start(bf16[256,1024]{1,0:T(8,128)(2,1)S(1)} %collective-permute-done.2), channel_id=1, source_target_pairs={{0,1},{1,2},{2,3},{3,4},{4,5},{5,6},{6,7},{7,8},{8,9},{9,10},{10,1... | collective-permute-start | bytes 1572872 | tf_op jit(solution)/shard_map/ppermute | solution.py:19
  66.9 9.9 %collective-permute-done.6 = bf16[256,1024]{1,0:T(8,128)(2,1)S(1)} collective-permute-done((bf16[256,1024]{1,0:T(8,128)(2,1)S(1)}, bf16[256,1024]{1,0:T(8,128)(2,1)S(1)}, u32[]{:S(2)}, u32[]{:S(2)}) %collective-permute-start.6) | collective-permute-done | bytes 524320 | tf_op jit(solution)/shard_map/ppermute | solution.py:19
  76.8 1.3 %collective-permute-start.7 = (bf16[256,1024]{1,0:T(8,128)(2,1)S(1)}, bf16[256,1024]{1,0:T(8,128)(2,1)S(1)}, u32[]{:S(2)}, u32[]{:S(2)}) collective-permute-start(bf16[256,1024]{1,0:T(8,128)(2,1)S(1)} %collective-permute-done.6), channel_id=1, source_target_pairs={{0,1},{1,2},{2,3},{3,4},{4,5},{5,6},{6,7},{7,8},{8,9},{9,10},{10,1... | collective-permute-start | bytes 1572872 | tf_op jit(solution)/shard_map/ppermute | solution.py:19
  78.1 2.5 %fusion.34 = bf16[256,1024]{1,0:T(8,128)(2,1)S(1)} fusion(bf16[2,1,1024,1024]{3,2,1,0:T(8,128)(2,1)} %param.8, bf16[256,1024]{1,0:T(8,128)(2,1)S(1)} %collective-permute-done.1, bf16[256,1024]{1,0:T(8,128)(2,1)} %collective-permute-done, f32[]{:T(128)S(6)} %select_n.75, f32[]{:T(128)S(6)} %select_n.67), kind=kOutput, calls=%fused_computation.42 | convolution fusion | flops 538705920 | bytes 3670024 | tf_op jit(solution)/shard_map/dot_general | solution.py:132
  80.7 2.0 %fusion.40 = bf16[256,1024]{1,0:T(8,128)(2,1)S(1)} fusion(bf16[2,1,1024,1024]{3,2,1,0:T(8,128)(2,1)S(1)} %copy-done.4, bf16[256,1024]{1,0:T(8,128)(2,1)S(1)} %collective-permute-done.5, bf16[256,1024]{1,0:T(8,128)(2,1)} %collective-permute-done.4, f32[]{:T(128)S(6)} %select_n.75, f32[]{:T(128)S(6)} %select_n.67), kind=kOutput, calls=%fused_computation.44 | convolution fusion | flops 538705920 | bytes 3670024 | tf_op jit(solution)/shard_map/dot_general | solution.py:132
  86.1 5.6 %multiply_reduce_fusion.1 = (f32[]{:T(128)}, f32[]{:T(128)}, f32[1024,1024]{1,0:T(8,128)}) fusion(f32[]{:T(128)S(6)} %sqrt.6, f32[1024]{0:T(1024)S(1)} %get-tuple-element.20, f32[1024]{0:T(1024)S(1)} %get-tuple-element.19, f32[1024,1024]{1,0:T(8,128)S(1)} %copy-done.6, bf16[256,1024]{1,0:T(8,128)(2,1)S(1)} %fusion.43, bf16[256,1024]{1,0:T(8,128)(2,1)S(1)} %fusion.40, ...), kind=kOutput, calls=%fused_computation.5 | convolution fusion | flops 2166358016 | bytes 16793612 | tf_op jit(solution)/shard_map/dot_general | solution.py:135
  91.7 1.3 pad_maximum_fusion
  93.6 19.7 %all-to-all-start.1 = ((f32[32,1,2]{2,1,0:T(1,128)}), f32[32,1,2]{2,1,0:T(1,128)S(1)}, u32[]{:S(2)}, u32[]{:S(2)}) async-start(f32[32,1,2]{2,1,0:T(1,128)} %broadcast_in_dim.20), calls=%async_computation.1 | async-start | bytes 32768 | tf_op jit(solution)/shard_map/all_to_all | solution.py:25
  113.3 7.1 %all-to-all-done.1 = f32[32,1,2]{2,1,0:T(1,128)S(1)} async-done(((f32[32,1,2]{2,1,0:T(1,128)}), f32[32,1,2]{2,1,0:T(1,128)S(1)}, u32[]{:S(2)}, u32[]{:S(2)}) %all-to-all-start.1) | async-done | bytes 288 | tf_op jit(solution)/shard_map/all_to_all | solution.py:25
  124.3 6.4 %divide_bitcast_fusion = f32[1,1024,1024]{2,1,0:T(8,128)} fusion(f32[1024,1024]{1,0:T(8,128)} %get-tuple-element.18, f32[]{:T(128)} %sqrt.7, f32[]{:T(128)} %bitcast.17, f32[]{:T(128)S(6)} %sqrt.6, f32[1024]{0:T(1024)S(1)} %get-tuple-element.20, f32[1024]{0:T(1024)S(1)} %get-tuple-element.19, f32[1,1024,1024]{2,1,0:T(8,128)} %state_ref.1), kind=kLoop, calls=%fused_computation.3 | loop fusion | flops 6291456 | bytes 12591116 | tf_op jit(solution)/shard_map/broadcast_in_dim | solution.py:145
  (34 shorter events, 8.5 us)
Async XLA Ops:
  0.6 15.3 %copy-start.3 = (s32[10]{0:T(128)S(1)}, s32[10]{0:T(128)}, u32[]{:S(2)}) copy-start(s32[10]{0:T(128)} %right_ref.1) | copy-start | bytes 124
  0.6 13.4 %copy-start.2 = (s32[8]{0:T(128)S(1)}, s32[8]{0:T(128)}, u32[]{:S(2)}) copy-start(s32[8]{0:T(128)} %left_ref.1) | copy-start | bytes 100
  0.7 17.2 %copy-start.1 = (f32[2,4,4]{2,1,0:T(4,128)S(1)}, f32[2,4,4]{2,1,0:T(4,128)}, u32[]{:S(2)}) copy-start(f32[2,4,4]{2,1,0:T(4,128)} %param.9) | copy-start | bytes 388
  6.6 16.5 %all-to-all-start = ((f32[32,1,1]{2,1,0:T(1,128)}), f32[32,1,1]{2,1,0:T(1,128)S(1)}, u32[]{:S(2)}, u32[]{:S(2)}) async-start(f32[32,1,1]{2,1,0:T(1,128)} %broadcast_in_dim.9), calls=%async_computation | async-start | bytes 32768 | tf_op jit(solution)/shard_map/all_to_all | solution.py:25
  27.2 23.2 %collective-permute-start = (bf16[256,1024]{1,0:T(8,128)(2,1)S(1)}, bf16[256,1024]{1,0:T(8,128)(2,1)}, u32[]{:S(2)}, u32[]{:S(2)}) collective-permute-start(bf16[256,1024]{1,0:T(8,128)(2,1)S(1)} %get-tuple-element.8), channel_id=1, source_target_pairs={{0,2},{1,3},{2,4},{3,5},{4,6},{5,7},{6,8},{7,9},{8,10},{9,11},{10,... | collective-permute-start | bytes 1572872 | tf_op jit(solution)/shard_map/ppermute | solution.py:19
  31.6 22.7 %collective-permute-start.4 = (bf16[256,1024]{1,0:T(8,128)(2,1)S(1)}, bf16[256,1024]{1,0:T(8,128)(2,1)}, u32[]{:S(2)}, u32[]{:S(2)}) collective-permute-start(bf16[256,1024]{1,0:T(8,128)(2,1)S(1)} %get-tuple-element.10), channel_id=1, source_target_pairs={{0,2},{1,3},{2,4},{3,5},{4,6},{5,7},{6,8},{7,9},{8,10},{9,11},{10,... | collective-permute-start | bytes 1572872 | tf_op jit(solution)/shard_map/ppermute | solution.py:19
  35.0 30.6 %collective-permute-start.2 = (bf16[256,1024]{1,0:T(8,128)(2,1)S(1)}, bf16[256,1024]{1,0:T(8,128)(2,1)S(1)}, u32[]{:S(2)}, u32[]{:S(2)}) collective-permute-start(bf16[256,1024]{1,0:T(8,128)(2,1)S(1)} %get-tuple-element.11), channel_id=1, source_target_pairs={{0,2},{1,3},{2,4},{3,5},{4,6},{5,7},{6,8},{7,9},{8,10},{9,11},{10,... | collective-permute-start | bytes 1572872 | tf_op jit(solution)/shard_map/ppermute | solution.py:19
  47.1 29.8 %collective-permute-start.6 = (bf16[256,1024]{1,0:T(8,128)(2,1)S(1)}, bf16[256,1024]{1,0:T(8,128)(2,1)S(1)}, u32[]{:S(2)}, u32[]{:S(2)}) collective-permute-start(bf16[256,1024]{1,0:T(8,128)(2,1)S(1)} %get-tuple-element.4), channel_id=1, source_target_pairs={{0,2},{1,3},{2,4},{3,5},{4,6},{5,7},{6,8},{7,9},{8,10},{9,11},{10,... | collective-permute-start | bytes 1572872 | tf_op jit(solution)/shard_map/ppermute | solution.py:19
  50.4 27.8 %collective-permute-start.1 = (bf16[256,1024]{1,0:T(8,128)(2,1)}, bf16[256,1024]{1,0:T(8,128)(2,1)S(1)}, u32[]{:S(2)}, u32[]{:S(2)}) collective-permute-start(bf16[256,1024]{1,0:T(8,128)(2,1)} %collective-permute-done), channel_id=1, source_target_pairs={{0,1},{1,2},{2,3},{3,4},{4,5},{5,6},{6,7},{7,8},{8,9},{9,10},{10,1... | collective-permute-start | bytes 1572872 | tf_op jit(solution)/shard_map/ppermute | solution.py:19
  54.3 26.3 %collective-permute-start.5 = (bf16[256,1024]{1,0:T(8,128)(2,1)}, bf16[256,1024]{1,0:T(8,128)(2,1)S(1)}, u32[]{:S(2)}, u32[]{:S(2)}) collective-permute-start(bf16[256,1024]{1,0:T(8,128)(2,1)} %collective-permute-done.4), channel_id=1, source_target_pairs={{0,1},{1,2},{2,3},{3,4},{4,5},{5,6},{6,7},{7,8},{8,9},{9,10},{10,1... | collective-permute-start | bytes 1572872 | tf_op jit(solution)/shard_map/ppermute | solution.py:19
  57.1 23.6 %copy-start.4 = (bf16[2,1,1024,1024]{3,2,1,0:T(8,128)(2,1)S(1)}, bf16[2,1,1024,1024]{3,2,1,0:T(8,128)(2,1)}, u32[]{:S(2)}) copy-start(bf16[2,1,1024,1024]{3,2,1,0:T(8,128)(2,1)} %param.8) | copy-start | bytes 12582916
  65.6 17.1 %collective-permute-start.3 = (bf16[256,1024]{1,0:T(8,128)(2,1)S(1)}, bf16[256,1024]{1,0:T(8,128)(2,1)S(1)}, u32[]{:S(2)}, u32[]{:S(2)}) collective-permute-start(bf16[256,1024]{1,0:T(8,128)(2,1)S(1)} %collective-permute-done.2), channel_id=1, source_target_pairs={{0,1},{1,2},{2,3},{3,4},{4,5},{5,6},{6,7},{7,8},{8,9},{9,10},{10,1... | collective-permute-start | bytes 1572872 | tf_op jit(solution)/shard_map/ppermute | solution.py:19
  76.8 6.6 %collective-permute-start.7 = (bf16[256,1024]{1,0:T(8,128)(2,1)S(1)}, bf16[256,1024]{1,0:T(8,128)(2,1)S(1)}, u32[]{:S(2)}, u32[]{:S(2)}) collective-permute-start(bf16[256,1024]{1,0:T(8,128)(2,1)S(1)} %collective-permute-done.6), channel_id=1, source_target_pairs={{0,1},{1,2},{2,3},{3,4},{4,5},{5,6},{6,7},{7,8},{8,9},{9,10},{10,1... | collective-permute-start | bytes 1572872 | tf_op jit(solution)/shard_map/ppermute | solution.py:19
  80.7 3.5 %copy-start.6 = (f32[1024,1024]{1,0:T(8,128)S(1)}, f32[1024,1024]{1,0:T(8,128)}, u32[]{:S(2)}) copy-start(f32[1024,1024]{1,0:T(8,128)} %multiply_bitcast_fusion) | copy-start | bytes 12582916
  82.6 2.3 %copy-start = (f32[1,1024,1024]{2,1,0:T(8,128)S(1)}, f32[1,1024,1024]{2,1,0:T(8,128)}, u32[]{:S(2)}) copy-start(f32[1,1024,1024]{2,1,0:T(8,128)} %state_ref.1) | copy-start | bytes 12582916
  82.6 3.5 %copy-start.5 = (bf16[2,1,1024,1024]{3,2,1,0:T(8,128)(2,1)S(1)}, bf16[2,1,1024,1024]{3,2,1,0:T(8,128)(2,1)}, u32[]{:S(2)}) copy-start(bf16[2,1,1024,1024]{3,2,1,0:T(8,128)(2,1)} %param.7) | copy-start | bytes 12582916
  93.6 26.9 %all-to-all-start.1 = ((f32[32,1,2]{2,1,0:T(1,128)}), f32[32,1,2]{2,1,0:T(1,128)S(1)}, u32[]{:S(2)}, u32[]{:S(2)}) async-start(f32[32,1,2]{2,1,0:T(1,128)} %broadcast_in_dim.20), calls=%async_computation.1 | async-start | bytes 32768 | tf_op jit(solution)/shard_map/all_to_all | solution.py:25

commit v8 on v7

--- a/solution.py
+++ b/solution.py
@@ -21,7 +21,10 @@
 
 def all_sum(values):
     count = lax.axis_size(AXES)
-    spread = jnp.broadcast_to(values[None], (count,) + values.shape)
+    return exchange_sum(jnp.broadcast_to(values[None], (count,) + values.shape))
+
+
+def exchange_sum(spread):
     return jnp.sum(lax.all_to_all(spread, AXES, 0, 0, tiled=True), axis=0)
 
 
@@ -45,10 +48,11 @@
 
     @pl.when(step == pl.num_programs(0) - 1)
     def _():
-        out_ref[0, 0] = jnp.sum(acc_ref[...])
+        out_ref[...] = jnp.full(out_ref.shape, jnp.sum(acc_ref[...]), jnp.float32)
 
 
 def masked_square_sum(pairs, block_index, left_live, right_live, state):
+    count = lax.axis_size(AXES)
     sec_size = state.shape[1]
     rows = 256
     return pl.pallas_call(
@@ -57,10 +61,10 @@
             num_scalar_prefetch=3,
             grid=(sec_size // rows,),
             in_specs=[pl.BlockSpec((1, rows, sec_size), lambda i, *_: (0, i, 0))],
-            out_specs=pl.BlockSpec(memory_space=pltpu.SMEM),
+            out_specs=pl.BlockSpec((count, 1, 1), lambda i, *_: (0, 0, 0)),
             scratch_shapes=[pltpu.VMEM((8, sec_size), jnp.float32)],
         ),
-        out_shape=jax.ShapeDtypeStruct((1, 1), jnp.float32),
+        out_shape=jax.ShapeDtypeStruct((count, 1, 1), jnp.float32),
     )(block_index.reshape(1), left_live, right_live, state)
 
 
@@ -91,9 +95,9 @@
     entries = float(state.shape[0] * sec_size * sec_size * lax.axis_size(AXES))
 
     masked = state[0] * live
-    start_sum = all_sum(
-        masked_square_sum(pairs, block_index.astype(jnp.int32), left_live, right_live, state)[0]
-    )[0]
+    start_sum = exchange_sum(
+        masked_square_sum(pairs, block_index.astype(jnp.int32), left_live, right_live, state)
+    )[0, 0]
     start_mean = start_sum / entries
     scale = jnp.sqrt(start_mean + 1e-06)
     vector = masked / scale

time: 131 us -> 130 us (level)
  no operation moved by 1% of the time
where the time goes in v8:
time: 130 us
  starting transfers between devices  46.2 us (36%)
  waiting for transfers between devices  28.2 us (22%)
  matrix products  20.8 us (16%)
  other arithmetic  16.4 us (13%)
  between operations  7.46 us (6%)
  local copies, waits for them, and re-layouts  5.7 us (4%)
  Pallas kernels  4.77 us (4%)
    all_to_all x2, starting transfers between devices, exchange_sum(): return jnp.sum(lax.all_to_all(spread, AXES, 0, 0, tiled=True), axis=0)  27 us
    ppermute x8, waiting for transfers between devices, shift_up(): return lax.ppermute(block, AXES, route)  21.1 us
    ppermute x8, starting transfers between devices, shift_up(): return lax.ppermute(block, AXES, route)  19.2 us
    dot_general x1, matrix products, per_device(): jnp.dot(left_env[1, 0], part_one, preferred_element_type=jnp.float32)  9.36 us
    all_to_all x2, waiting for transfers between devices, exchange_sum(): return jnp.sum(lax.all_to_all(spread, AXES, 0, 0, tiled=True), axis=0)  7.1 us
    broadcast_in_dim x1, other arithmetic, per_device(): return (next_vector[None], jnp.stack([alpha_value, beta_value]))  6.43 us
    dot_general x4, matrix products, per_device(): jnp.dot(source, right_env[0, 0], preferred_element_type=jnp.float32)  5.89 us
    dot_general x1, matrix products, per_device(): jnp.dot(left_env[0, 0], part_zero, preferred_element_type=jnp.float32)  5.54 us
  transfers between devices with their start and end apart: 10, of which 4 were waited for; matrix products, arithmetic and copies ran while one was open for 17% of the time, Pallas kernels for 0%

profile of v8, /device:TPU:0, one launch (start us, length us, event | category | flops | bytes accessed | tf_op | source)
XLA Modules:
  0.0 129.5 jit_solution(15972128748956435150)
XLA Ops:
  0.7 4.8 %shard_map.77 = f32[32,1,1]{2,1,0:T(1,128)} custom-call(s32[1]{0:T(128)} %bitcast.5.index_ref, s32[8]{0:T(128)} %left_ref.1, s32[10]{0:T(128)} %right_ref.1, f32[1,1024,1024]{2,1,0:T(8,128)} %state_ref.1), custom_call_target="tpu_custom_call" | custom-call | tf_op jit(solution)/shard_map/pallas_call | solution.py:58
  5.4 7.3 %all-to-all-start = ((f32[32,1,1]{2,1,0:T(1,128)}), f32[32,1,1]{2,1,0:T(1,128)S(1)}, u32[]{:S(2)}, u32[]{:S(2)}) async-start(f32[32,1,1]{2,1,0:T(1,128)} %shard_map.77), calls=%async_computation | async-start | bytes 32768 | tf_op jit(solution)/shard_map/all_to_all | solution.py:28
  16.7 4.6 %multiply_multiply_fusion.1 = f32[1024,1024]{1,0:T(8,128)} fusion(f32[1,1024,1024]{2,1,0:T(8,128)} %state_ref.1, f32[1024]{0:T(1024)S(1)} %get-tuple-element.20, f32[1024]{0:T(1024)S(1)} %get-tuple-element.19), kind=kLoop, calls=%fused_computation.1 | loop fusion | flops 2097152 | bytes 8396800 | tf_op jit(solution)/shard_map/mul | solution.py:97
  23.2 2.8 %fusion.49 = (bf16[256,1024]{1,0:T(8,128)(2,1)S(1)}, bf16[256,1024]{1,0:T(8,128)(2,1)S(1)}, bf16[256,1024]{1,0:T(8,128)(2,1)S(1)}, bf16[256,1024]{1,0:T(8,128)(2,1)S(1)}) fusion(f32[1024,1024]{1,0:T(8,128)} %multiply_multiply_fusion.1, f32[]{:T(128)S(6)} %sqrt.6), kind=kLoop, calls=%fused_computation.53 | loop fusion | flops 2097152 | bytes 6291460 | tf_op jit(solution)/shard_map/convert_element_type | solution.py:106
  25.9 4.5 %collective-permute-start = (bf16[256,1024]{1,0:T(8,128)(2,1)S(1)}, bf16[256,1024]{1,0:T(8,128)(2,1)}, u32[]{:S(2)}, u32[]{:S(2)}) collective-permute-start(bf16[256,1024]{1,0:T(8,128)(2,1)S(1)} %get-tuple-element.8), channel_id=1, source_target_pairs={{0,2},{1,3},{2,4},{3,5},{4,6},{5,7},{6,8},{7,9},{8,10},{9,11},{10,... | collective-permute-start | bytes 1572872 | tf_op jit(solution)/shard_map/ppermute | solution.py:19
  30.4 3.4 %collective-permute-start.4 = (bf16[256,1024]{1,0:T(8,128)(2,1)S(1)}, bf16[256,1024]{1,0:T(8,128)(2,1)}, u32[]{:S(2)}, u32[]{:S(2)}) collective-permute-start(bf16[256,1024]{1,0:T(8,128)(2,1)S(1)} %get-tuple-element.10), channel_id=1, source_target_pairs={{0,2},{1,3},{2,4},{3,5},{4,6},{5,7},{6,8},{7,9},{8,10},{9,11},{10,... | collective-permute-start | bytes 1572872 | tf_op jit(solution)/shard_map/ppermute | solution.py:19
  33.8 2.7 %collective-permute-start.2 = (bf16[256,1024]{1,0:T(8,128)(2,1)S(1)}, bf16[256,1024]{1,0:T(8,128)(2,1)S(1)}, u32[]{:S(2)}, u32[]{:S(2)}) collective-permute-start(bf16[256,1024]{1,0:T(8,128)(2,1)S(1)} %get-tuple-element.11), channel_id=1, source_target_pairs={{0,2},{1,3},{2,4},{3,5},{4,6},{5,7},{6,8},{7,9},{8,10},{9,11},{10,... | collective-permute-start | bytes 1572872 | tf_op jit(solution)/shard_map/ppermute | solution.py:19
  36.5 9.4 %multiply_bitcast_fusion = f32[1024,1024]{1,0:T(8,128)} fusion(bf16[2,1,1024,1024]{3,2,1,0:T(8,128)(2,1)} %param.7, f32[]{:T(128)} %bitcast.8, bf16[256,1024]{1,0:T(8,128)(2,1)S(1)} %get-tuple-element.4, bf16[256,1024]{1,0:T(8,128)(2,1)S(1)} %get-tuple-element.10, bf16[256,1024]{1,0:T(8,128)(2,1)S(1)} %get-tuple-element.11, ...), kind=kOutput, calls=%fused_computation.6 | convolution fusion | flops 4305453056 | bytes 10486272 | tf_op jit(solution)/shard_map/dot_general | solution.py:125
  45.8 3.3 %collective-permute-start.6 = (bf16[256,1024]{1,0:T(8,128)(2,1)S(1)}, bf16[256,1024]{1,0:T(8,128)(2,1)S(1)}, u32[]{:S(2)}, u32[]{:S(2)}) collective-permute-start(bf16[256,1024]{1,0:T(8,128)(2,1)S(1)} %get-tuple-element.4), channel_id=1, source_target_pairs={{0,2},{1,3},{2,4},{3,5},{4,6},{5,7},{6,8},{7,9},{8,10},{9,11},{10,... | collective-permute-start | bytes 1572872 | tf_op jit(solution)/shard_map/ppermute | solution.py:19
  49.2 1.3 %collective-permute-start.1 = (bf16[256,1024]{1,0:T(8,128)(2,1)}, bf16[256,1024]{1,0:T(8,128)(2,1)S(1)}, u32[]{:S(2)}, u32[]{:S(2)}) collective-permute-start(bf16[256,1024]{1,0:T(8,128)(2,1)} %collective-permute-done), channel_id=1, source_target_pairs={{0,1},{1,2},{2,3},{3,4},{4,5},{5,6},{6,7},{7,8},{8,9},{9,10},{10,1... | collective-permute-start | bytes 1572872 | tf_op jit(solution)/shard_map/ppermute | solution.py:19
  50.5 2.6 %collective-permute-done.4 = bf16[256,1024]{1,0:T(8,128)(2,1)} collective-permute-done((bf16[256,1024]{1,0:T(8,128)(2,1)S(1)}, bf16[256,1024]{1,0:T(8,128)(2,1)}, u32[]{:S(2)}, u32[]{:S(2)}) %collective-permute-start.4) | collective-permute-done | bytes 524320 | tf_op jit(solution)/shard_map/ppermute | solution.py:19
  53.1 1.4 %collective-permute-start.5 = (bf16[256,1024]{1,0:T(8,128)(2,1)}, bf16[256,1024]{1,0:T(8,128)(2,1)S(1)}, u32[]{:S(2)}, u32[]{:S(2)}) collective-permute-start(bf16[256,1024]{1,0:T(8,128)(2,1)} %collective-permute-done.4), channel_id=1, source_target_pairs={{0,1},{1,2},{2,3},{3,4},{4,5},{5,6},{6,7},{7,8},{8,9},{9,10},{10,1... | collective-permute-start | bytes 1572872 | tf_op jit(solution)/shard_map/ppermute | solution.py:19
  55.9 8.5 %collective-permute-done.2 = bf16[256,1024]{1,0:T(8,128)(2,1)S(1)} collective-permute-done((bf16[256,1024]{1,0:T(8,128)(2,1)S(1)}, bf16[256,1024]{1,0:T(8,128)(2,1)S(1)}, u32[]{:S(2)}, u32[]{:S(2)}) %collective-permute-start.2) | collective-permute-done | bytes 524320 | tf_op jit(solution)/shard_map/ppermute | solution.py:19
  64.4 1.3 %collective-permute-start.3 = (bf16[256,1024]{1,0:T(8,128)(2,1)S(1)}, bf16[256,1024]{1,0:T(8,128)(2,1)S(1)}, u32[]{:S(2)}, u32[]{:S(2)}) collective-permute-start(bf16[256,1024]{1,0:T(8,128)(2,1)S(1)} %collective-permute-done.2), channel_id=1, source_target_pairs={{0,1},{1,2},{2,3},{3,4},{4,5},{5,6},{6,7},{7,8},{8,9},{9,10},{10,1... | collective-permute-start | bytes 1572872 | tf_op jit(solution)/shard_map/ppermute | solution.py:19
  65.7 9.9 %collective-permute-done.6 = bf16[256,1024]{1,0:T(8,128)(2,1)S(1)} collective-permute-done((bf16[256,1024]{1,0:T(8,128)(2,1)S(1)}, bf16[256,1024]{1,0:T(8,128)(2,1)S(1)}, u32[]{:S(2)}, u32[]{:S(2)}) %collective-permute-start.6) | collective-permute-done | bytes 524320 | tf_op jit(solution)/shard_map/ppermute | solution.py:19
  75.6 1.3 %collective-permute-start.7 = (bf16[256,1024]{1,0:T(8,128)(2,1)S(1)}, bf16[256,1024]{1,0:T(8,128)(2,1)S(1)}, u32[]{:S(2)}, u32[]{:S(2)}) collective-permute-start(bf16[256,1024]{1,0:T(8,128)(2,1)S(1)} %collective-permute-done.6), channel_id=1, source_target_pairs={{0,1},{1,2},{2,3},{3,4},{4,5},{5,6},{6,7},{7,8},{8,9},{9,10},{10,1... | collective-permute-start | bytes 1572872 | tf_op jit(solution)/shard_map/ppermute | solution.py:19
  76.9 2.5 %fusion.34 = bf16[256,1024]{1,0:T(8,128)(2,1)S(1)} fusion(bf16[2,1,1024,1024]{3,2,1,0:T(8,128)(2,1)} %param.8, bf16[256,1024]{1,0:T(8,128)(2,1)S(1)} %collective-permute-done.1, bf16[256,1024]{1,0:T(8,128)(2,1)} %collective-permute-done, f32[]{:T(128)S(6)} %select_n.75, f32[]{:T(128)S(6)} %select_n.67), kind=kOutput, calls=%fused_computation.42 | convolution fusion | flops 538705920 | bytes 3670024 | tf_op jit(solution)/shard_map/dot_general | solution.py:136
  79.5 1.9 %fusion.40 = bf16[256,1024]{1,0:T(8,128)(2,1)S(1)} fusion(bf16[2,1,1024,1024]{3,2,1,0:T(8,128)(2,1)S(1)} %copy-done.4, bf16[256,1024]{1,0:T(8,128)(2,1)S(1)} %collective-permute-done.5, bf16[256,1024]{1,0:T(8,128)(2,1)} %collective-permute-done.4, f32[]{:T(128)S(6)} %select_n.75, f32[]{:T(128)S(6)} %select_n.67), kind=kOutput, calls=%fused_computation.44 | convolution fusion | flops 538705920 | bytes 3670024 | tf_op jit(solution)/shard_map/dot_general | solution.py:136
  83.7 1.2 copy-done.5
  84.9 5.5 %multiply_reduce_fusion.1 = (f32[]{:T(128)}, f32[]{:T(128)}, f32[1024,1024]{1,0:T(8,128)}) fusion(f32[]{:T(128)S(6)} %sqrt.6, f32[1024]{0:T(1024)S(1)} %get-tuple-element.20, f32[1024]{0:T(1024)S(1)} %get-tuple-element.19, f32[1024,1024]{1,0:T(8,128)S(1)} %copy-done.6, bf16[256,1024]{1,0:T(8,128)(2,1)S(1)} %fusion.43, bf16[256,1024]{1,0:T(8,128)(2,1)S(1)} %fusion.40, ...), kind=kOutput, calls=%fused_computation.5 | convolution fusion | flops 2166358016 | bytes 16793612 | tf_op jit(solution)/shard_map/dot_general | solution.py:139
  90.4 1.3 pad_maximum_fusion
  92.3 19.7 %all-to-all-start.1 = ((f32[32,1,2]{2,1,0:T(1,128)}), f32[32,1,2]{2,1,0:T(1,128)S(1)}, u32[]{:S(2)}, u32[]{:S(2)}) async-start(f32[32,1,2]{2,1,0:T(1,128)} %broadcast_in_dim.4), calls=%async_computation.1 | async-start | bytes 32768 | tf_op jit(solution)/shard_map/all_to_all | solution.py:28
  112.1 7.1 %all-to-all-done.1 = f32[32,1,2]{2,1,0:T(1,128)S(1)} async-done(((f32[32,1,2]{2,1,0:T(1,128)}), f32[32,1,2]{2,1,0:T(1,128)S(1)}, u32[]{:S(2)}, u32[]{:S(2)}) %all-to-all-start.1) | async-done | bytes 288 | tf_op jit(solution)/shard_map/all_to_all | solution.py:28
  123.1 6.4 %divide_bitcast_fusion = f32[1,1024,1024]{2,1,0:T(8,128)} fusion(f32[1024,1024]{1,0:T(8,128)} %get-tuple-element.18, f32[]{:T(128)} %sqrt.7, f32[]{:T(128)} %bitcast.16, f32[]{:T(128)S(6)} %sqrt.6, f32[1024]{0:T(1024)S(1)} %get-tuple-element.20, f32[1024]{0:T(1024)S(1)} %get-tuple-element.19, f32[1,1024,1024]{2,1,0:T(8,128)} %state_ref.1), kind=kLoop, calls=%fused_computation.3 | loop fusion | flops 6291456 | bytes 12591116 | tf_op jit(solution)/shard_map/broadcast_in_dim | solution.py:149
  (33 shorter events, 7.3 us)
Async XLA Ops:
  0.6 14.1 %copy-start.3 = (s32[10]{0:T(128)S(1)}, s32[10]{0:T(128)}, u32[]{:S(2)}) copy-start(s32[10]{0:T(128)} %right_ref.1) | copy-start | bytes 124
  0.6 12.2 %copy-start.2 = (s32[8]{0:T(128)S(1)}, s32[8]{0:T(128)}, u32[]{:S(2)}) copy-start(s32[8]{0:T(128)} %left_ref.1) | copy-start | bytes 100
  0.7 16.0 %copy-start.1 = (f32[2,4,4]{2,1,0:T(4,128)S(1)}, f32[2,4,4]{2,1,0:T(4,128)}, u32[]{:S(2)}) copy-start(f32[2,4,4]{2,1,0:T(4,128)} %param.9) | copy-start | bytes 388
  5.4 16.5 %all-to-all-start = ((f32[32,1,1]{2,1,0:T(1,128)}), f32[32,1,1]{2,1,0:T(1,128)S(1)}, u32[]{:S(2)}, u32[]{:S(2)}) async-start(f32[32,1,1]{2,1,0:T(1,128)} %shard_map.77), calls=%async_computation | async-start | bytes 32768 | tf_op jit(solution)/shard_map/all_to_all | solution.py:28
  25.9 23.2 %collective-permute-start = (bf16[256,1024]{1,0:T(8,128)(2,1)S(1)}, bf16[256,1024]{1,0:T(8,128)(2,1)}, u32[]{:S(2)}, u32[]{:S(2)}) collective-permute-start(bf16[256,1024]{1,0:T(8,128)(2,1)S(1)} %get-tuple-element.8), channel_id=1, source_target_pairs={{0,2},{1,3},{2,4},{3,5},{4,6},{5,7},{6,8},{7,9},{8,10},{9,11},{10,... | collective-permute-start | bytes 1572872 | tf_op jit(solution)/shard_map/ppermute | solution.py:19
  30.4 22.7 %collective-permute-start.4 = (bf16[256,1024]{1,0:T(8,128)(2,1)S(1)}, bf16[256,1024]{1,0:T(8,128)(2,1)}, u32[]{:S(2)}, u32[]{:S(2)}) collective-permute-start(bf16[256,1024]{1,0:T(8,128)(2,1)S(1)} %get-tuple-element.10), channel_id=1, source_target_pairs={{0,2},{1,3},{2,4},{3,5},{4,6},{5,7},{6,8},{7,9},{8,10},{9,11},{10,... | collective-permute-start | bytes 1572872 | tf_op jit(solution)/shard_map/ppermute | solution.py:19
  33.8 30.6 %collective-permute-start.2 = (bf16[256,1024]{1,0:T(8,128)(2,1)S(1)}, bf16[256,1024]{1,0:T(8,128)(2,1)S(1)}, u32[]{:S(2)}, u32[]{:S(2)}) collective-permute-start(bf16[256,1024]{1,0:T(8,128)(2,1)S(1)} %get-tuple-element.11), channel_id=1, source_target_pairs={{0,2},{1,3},{2,4},{3,5},{4,6},{5,7},{6,8},{7,9},{8,10},{9,11},{10,... | collective-permute-start | bytes 1572872 | tf_op jit(solution)/shard_map/ppermute | solution.py:19
  45.8 29.8 %collective-permute-start.6 = (bf16[256,1024]{1,0:T(8,128)(2,1)S(1)}, bf16[256,1024]{1,0:T(8,128)(2,1)S(1)}, u32[]{:S(2)}, u32[]{:S(2)}) collective-permute-start(bf16[256,1024]{1,0:T(8,128)(2,1)S(1)} %get-tuple-element.4), channel_id=1, source_target_pairs={{0,2},{1,3},{2,4},{3,5},{4,6},{5,7},{6,8},{7,9},{8,10},{9,11},{10,... | collective-permute-start | bytes 1572872 | tf_op jit(solution)/shard_map/ppermute | solution.py:19
  49.2 27.8 %collective-permute-start.1 = (bf16[256,1024]{1,0:T(8,128)(2,1)}, bf16[256,1024]{1,0:T(8,128)(2,1)S(1)}, u32[]{:S(2)}, u32[]{:S(2)}) collective-permute-start(bf16[256,1024]{1,0:T(8,128)(2,1)} %collective-permute-done), channel_id=1, source_target_pairs={{0,1},{1,2},{2,3},{3,4},{4,5},{5,6},{6,7},{7,8},{8,9},{9,10},{10,1... | collective-permute-start | bytes 1572872 | tf_op jit(solution)/shard_map/ppermute | solution.py:19
  53.1 26.3 %collective-permute-start.5 = (bf16[256,1024]{1,0:T(8,128)(2,1)}, bf16[256,1024]{1,0:T(8,128)(2,1)S(1)}, u32[]{:S(2)}, u32[]{:S(2)}) collective-permute-start(bf16[256,1024]{1,0:T(8,128)(2,1)} %collective-permute-done.4), channel_id=1, source_target_pairs={{0,1},{1,2},{2,3},{3,4},{4,5},{5,6},{6,7},{7,8},{8,9},{9,10},{10,1... | collective-permute-start | bytes 1572872 | tf_op jit(solution)/shard_map/ppermute | solution.py:19
  55.8 23.6 %copy-start.4 = (bf16[2,1,1024,1024]{3,2,1,0:T(8,128)(2,1)S(1)}, bf16[2,1,1024,1024]{3,2,1,0:T(8,128)(2,1)}, u32[]{:S(2)}) copy-start(bf16[2,1,1024,1024]{3,2,1,0:T(8,128)(2,1)} %param.8) | copy-start | bytes 12582916
  64.4 17.1 %collective-permute-start.3 = (bf16[256,1024]{1,0:T(8,128)(2,1)S(1)}, bf16[256,1024]{1,0:T(8,128)(2,1)S(1)}, u32[]{:S(2)}, u32[]{:S(2)}) collective-permute-start(bf16[256,1024]{1,0:T(8,128)(2,1)S(1)} %collective-permute-done.2), channel_id=1, source_target_pairs={{0,1},{1,2},{2,3},{3,4},{4,5},{5,6},{6,7},{7,8},{8,9},{9,10},{10,1... | collective-permute-start | bytes 1572872 | tf_op jit(solution)/shard_map/ppermute | solution.py:19
  75.6 6.6 %collective-permute-start.7 = (bf16[256,1024]{1,0:T(8,128)(2,1)S(1)}, bf16[256,1024]{1,0:T(8,128)(2,1)S(1)}, u32[]{:S(2)}, u32[]{:S(2)}) collective-permute-start(bf16[256,1024]{1,0:T(8,128)(2,1)S(1)} %collective-permute-done.6), channel_id=1, source_target_pairs={{0,1},{1,2},{2,3},{3,4},{4,5},{5,6},{6,7},{7,8},{8,9},{9,10},{10,1... | collective-permute-start | bytes 1572872 | tf_op jit(solution)/shard_map/ppermute | solution.py:19
  79.4 3.5 %copy-start.6 = (f32[1024,1024]{1,0:T(8,128)S(1)}, f32[1024,1024]{1,0:T(8,128)}, u32[]{:S(2)}) copy-start(f32[1024,1024]{1,0:T(8,128)} %multiply_bitcast_fusion) | copy-start | bytes 12582916
  81.4 2.3 %copy-start = (f32[1,1024,1024]{2,1,0:T(8,128)S(1)}, f32[1,1024,1024]{2,1,0:T(8,128)}, u32[]{:S(2)}) copy-start(f32[1,1024,1024]{2,1,0:T(8,128)} %state_ref.1) | copy-start | bytes 12582916
  81.4 3.5 %copy-start.5 = (bf16[2,1,1024,1024]{3,2,1,0:T(8,128)(2,1)S(1)}, bf16[2,1,1024,1024]{3,2,1,0:T(8,128)(2,1)}, u32[]{:S(2)}) copy-start(bf16[2,1,1024,1024]{3,2,1,0:T(8,128)(2,1)} %param.7) | copy-start | bytes 12582916
  92.3 26.9 %all-to-all-start.1 = ((f32[32,1,2]{2,1,0:T(1,128)}), f32[32,1,2]{2,1,0:T(1,128)S(1)}, u32[]{:S(2)}, u32[]{:S(2)}) async-start(f32[32,1,2]{2,1,0:T(1,128)} %broadcast_in_dim.4), calls=%async_computation.1 | async-start | bytes 32768 | tf_op jit(solution)/shard_map/all_to_all | solution.py:28

commit v9 on v8

--- a/solution.py
+++ b/solution.py
@@ -68,6 +68,69 @@
     )(block_index.reshape(1), left_live, right_live, state)
 
 
+def live_limits(pairs, index_ref, left_ref, right_ref):
+    sector = index_ref[0] // pairs
+    pair = index_ref[0] % pairs
+    return left_ref[sector] * BLOCK, right_ref[sector + (pair + 1) // 2] * BLOCK
+
+
+def image_kernel(pairs, index_ref, left_ref, right_ref, scale_ref, env_ref, part_ref, one_ref,
+                 state_ref, image_ref, sums_ref, acc_ref):
+    step = pl.program_id(0)
+    rows, cols = one_ref.shape
+    row_limit, col_limit = live_limits(pairs, index_ref, left_ref, right_ref)
+
+    @pl.when(step == 0)
+    def _():
+        acc_ref[...] = jnp.zeros_like(acc_ref)
+
+    row_ids = step * rows + lax.broadcasted_iota(jnp.int32, (rows, cols), 0)
+    col_ids = lax.broadcasted_iota(jnp.int32, (rows, cols), 1)
+    live = ((row_ids < row_limit) & (col_ids < col_limit)).astype(jnp.float32)
+    image = jnp.dot(env_ref[...], part_ref[...], preferred_element_type=jnp.float32) + one_ref[...]
+    image = image * live
+    image_ref[...] = image
+    vector = state_ref[0] * live / scale_ref[0]
+    acc_ref[0] += jnp.sum((vector * image).reshape(rows // 8, 8, cols), axis=0)
+    acc_ref[1] += jnp.sum((image * image).reshape(rows // 8, 8, cols), axis=0)
+
+    @pl.when(step == pl.num_programs(0) - 1)
+    def _():
+        which = lax.broadcasted_iota(jnp.int32, sums_ref.shape, 2)
+        sums_ref[...] = jnp.where(which == 0, jnp.sum(acc_ref[0]), jnp.sum(acc_ref[1]))
+
+
+def masked_image(pairs, block_index, left_live, right_live, scale, left_zero, part_zero,
+                 image_one, state):
+    count = lax.axis_size(AXES)
+    sec_size = state.shape[1]
+    rows = 256
+    return pl.pallas_call(
+        functools.partial(image_kernel, pairs),
+        grid_spec=pltpu.PrefetchScalarGridSpec(
+            num_scalar_prefetch=3,
+            grid=(sec_size // rows,),
+            in_specs=[
+                pl.BlockSpec(memory_space=pltpu.SMEM),
+                pl.BlockSpec((rows, sec_size), lambda i, *_: (i, 0)),
+                pl.BlockSpec((sec_size, sec_size), lambda i, *_: (0, 0)),
+                pl.BlockSpec((rows, sec_size), lambda i, *_: (i, 0)),
+                pl.BlockSpec((1, rows, sec_size), lambda i, *_: (0, i, 0)),
+            ],
+            out_specs=[
+                pl.BlockSpec((rows, sec_size), lambda i, *_: (i, 0)),
+                pl.BlockSpec((count, 1, 2), lambda i, *_: (0, 0, 0)),
+            ],
+            scratch_shapes=[pltpu.VMEM((2, 8, sec_size), jnp.float32)],
+        ),
+        out_shape=[
+            jax.ShapeDtypeStruct((sec_size, sec_size), jnp.float32),
+            jax.ShapeDtypeStruct((count, 1, 2), jnp.float32),
+        ],
+    )(block_index.reshape(1), left_live, right_live, scale.reshape(1), left_zero, part_zero,
+      image_one, state)
+
+
 def row_major(array):
     return with_layout_constraint(array, Layout(major_to_minor=tuple(range(array.ndim))))
 
@@ -136,10 +199,11 @@
             jnp.dot(source, right_env[0, 0], preferred_element_type=jnp.float32).astype(jnp.bfloat16)
         )
     part_zero = jnp.concatenate(parts, axis=0)
-    image = jnp.dot(left_env[0, 0], part_zero, preferred_element_type=jnp.float32) + image_one
-    image = row_major(image * live)
-
-    sums = all_sum(jnp.stack([jnp.sum(vector * image), jnp.sum(image * image)]))
+    image, spread = masked_image(
+        pairs, block_index.astype(jnp.int32), left_live, right_live, scale, left_env[0, 0],
+        part_zero, image_one, state,
+    )
+    sums = exchange_sum(spread)[0]
     alpha_value = sums[0] / entries
     vector_mean = start_mean / (start_mean + 1e-06)
     residual_mean = sums[1] / entries - alpha_value * alpha_value * (2.0 - vector_mean)

time: 130 us -> 134 us (1.031)
  Pallas kernels: 4.77 us -> 14.4 us
  matrix products: 20.8 us -> 15 us
  waiting for transfers between devices: 28.2 us -> 23.5 us
  starting transfers between devices: 46.2 us -> 49.9 us
    pallas_call x0 -> x1, Pallas kernels: none -> 9.66 us  [masked_image(): pl.pallas_call(functools.partial(image_kernel, pairs), grid_spec=pltpu.Pr...]
    dot_general x1 -> x0, matrix products: 5.54 us -> none  [per_device(): jnp.dot(left_env[0, 0], part_zero, preferred_element_type=jnp.float32)]
    ppermute x8, waiting for transfers between devices: 21.1 us -> 16.4 us  [shift_up(): return lax.ppermute(block, AXES, route)]
    squeeze x0 -> x1, local copies, waits for them, and re-layouts: none -> 3.12 us  [per_device(): left_env[0, 0]]
    all_to_all x2, starting transfers between devices: 27 us -> 29.1 us  [exchange_sum(): return jnp.sum(lax.all_to_all(spread, AXES, 0, 0, tiled=True), axis=0)]
    unnamed x14 -> x8, local copies, waits for them, and re-layouts: 1.97 us -> 0.02 us
    ppermute x8, starting transfers between devices: 19.2 us -> 20.7 us  [shift_up(): return lax.ppermute(block, AXES, route)]
    concatenate x0 -> x1, other arithmetic: none -> 1.53 us  [per_device(): part_zero = jnp.concatenate(parts, axis=0)]
  transfers between devices with their start and end apart: 10 -> 10, of which waited for: 4 -> 4; matrix products, arithmetic and copies ran while one was open for 17% -> 18% of each run, Pallas kernels for 0% -> 0%
where the time goes in v9:
time: 134 us; the launch traced here: 133 us
  starting transfers between devices  49.9 us (37%)
  waiting for transfers between devices  23.5 us (18%)
  other arithmetic  16.6 us (12%)
  matrix products  15 us (11%)
  Pallas kernels  14.4 us (11%)
  between operations  7.4 us (6%)
  local copies, waits for them, and re-layouts  6.07 us (5%)
    all_to_all x2, starting transfers between devices, exchange_sum(): return jnp.sum(lax.all_to_all(spread, AXES, 0, 0, tiled=True), axis=0)  29.1 us
    ppermute x8, starting transfers between devices, shift_up(): return lax.ppermute(block, AXES, route)  20.7 us
    ppermute x8, waiting for transfers between devices, shift_up(): return lax.ppermute(block, AXES, route)  16.4 us
    pallas_call x1, Pallas kernels, masked_image(): pl.pallas_call(functools.partial(image_kernel, pairs), grid_spec=pltpu.Pr...  9.66 us
    dot_general x1, matrix products, per_device(): jnp.dot(left_env[1, 0], part_one, preferred_element_type=jnp.float32)  9.31 us
    all_to_all x2, waiting for transfers between devices, exchange_sum(): return jnp.sum(lax.all_to_all(spread, AXES, 0, 0, tiled=True), axis=0)  7.09 us
    broadcast_in_dim x1, other arithmetic, per_device(): return (next_vector[None], jnp.stack([alpha_value, beta_value]))  6.44 us
    dot_general x4, matrix products, per_device(): jnp.dot(source, right_env[0, 0], preferred_element_type=jnp.float32)  5.7 us
  transfers between devices with their start and end apart: 10, of which 4 were waited for; matrix products, arithmetic and copies ran while one was open for 18% of the time, Pallas kernels for 0%

profile of v9, /device:TPU:0, one launch (start us, length us, event | category | flops | bytes accessed | tf_op | source)
XLA Modules:
  0.0 133.0 jit_solution(2984132630867290840)
XLA Ops:
  0.7 4.8 %shard_map.77 = f32[32,1,1]{2,1,0:T(1,128)} custom-call(s32[1]{0:T(128)} %bitcast.index_ref, s32[8]{0:T(128)} %left_ref.3, s32[10]{0:T(128)} %right_ref.3, f32[1,1024,1024]{2,1,0:T(8,128)} %state_ref.3), custom_call_target="tpu_custom_call" | custom-call | tf_op jit(solution)/shard_map/pallas_call | solution.py:58
  5.4 7.3 %all-to-all-start = ((f32[32,1,1]{2,1,0:T(1,128)}), f32[32,1,1]{2,1,0:T(1,128)S(1)}, u32[]{:S(2)}, u32[]{:S(2)}) async-start(f32[32,1,1]{2,1,0:T(1,128)} %shard_map.77), calls=%async_computation | async-start | bytes 32768 | tf_op jit(solution)/shard_map/all_to_all | solution.py:28
  16.4 4.6 %bitcast_multiply_fusion = f32[1024,1024]{1,0:T(8,128)} fusion(f32[1,1024,1024]{2,1,0:T(8,128)} %state_ref.3, f32[1024]{0:T(1024)S(1)} %get-tuple-element.22, f32[1024]{0:T(1024)S(1)} %get-tuple-element.21), kind=kLoop, calls=%fused_computation | loop fusion | flops 2097152 | bytes 8396800 | tf_op jit(solution)/shard_map/mul | solution.py:160
  23.0 2.8 %fusion.40 = (bf16[256,1024]{1,0:T(8,128)(2,1)S(1)}, bf16[256,1024]{1,0:T(8,128)(2,1)S(1)}, bf16[256,1024]{1,0:T(8,128)(2,1)S(1)}, bf16[256,1024]{1,0:T(8,128)(2,1)S(1)}) fusion(f32[1024,1024]{1,0:T(8,128)} %bitcast_multiply_fusion, f32[]{:T(128)} %sqrt.6), kind=kLoop, calls=%fused_computation.41 | loop fusion | flops 2097152 | bytes 6291460 | tf_op jit(solution)/shard_map/convert_element_type | solution.py:169
  25.7 4.5 %collective-permute-start = (bf16[256,1024]{1,0:T(8,128)(2,1)S(1)}, bf16[256,1024]{1,0:T(8,128)(2,1)}, u32[]{:S(2)}, u32[]{:S(2)}) collective-permute-start(bf16[256,1024]{1,0:T(8,128)(2,1)S(1)} %get-tuple-element.10), channel_id=1, source_target_pairs={{0,2},{1,3},{2,4},{3,5},{4,6},{5,7},{6,8},{7,9},{8,10},{9,11},{10,... | collective-permute-start | bytes 1572872 | tf_op jit(solution)/shard_map/ppermute | solution.py:19
  30.2 3.4 %collective-permute-start.4 = (bf16[256,1024]{1,0:T(8,128)(2,1)S(1)}, bf16[256,1024]{1,0:T(8,128)(2,1)}, u32[]{:S(2)}, u32[]{:S(2)}) collective-permute-start(bf16[256,1024]{1,0:T(8,128)(2,1)S(1)} %get-tuple-element.12), channel_id=1, source_target_pairs={{0,2},{1,3},{2,4},{3,5},{4,6},{5,7},{6,8},{7,9},{8,10},{9,11},{10,... | collective-permute-start | bytes 1572872 | tf_op jit(solution)/shard_map/ppermute | solution.py:19
  33.6 2.7 %collective-permute-start.2 = (bf16[256,1024]{1,0:T(8,128)(2,1)S(1)}, bf16[256,1024]{1,0:T(8,128)(2,1)S(1)}, u32[]{:S(2)}, u32[]{:S(2)}) collective-permute-start(bf16[256,1024]{1,0:T(8,128)(2,1)S(1)} %get-tuple-element.13), channel_id=1, source_target_pairs={{0,2},{1,3},{2,4},{3,5},{4,6},{5,7},{6,8},{7,9},{8,10},{9,11},{10,... | collective-permute-start | bytes 1572872 | tf_op jit(solution)/shard_map/ppermute | solution.py:19
  36.2 9.3 %multiply_bitcast_fusion.one_ref = f32[1024,1024]{1,0:T(8,128)} fusion(bf16[2,1,1024,1024]{3,2,1,0:T(8,128)(2,1)} %param.7, f32[]{:T(128)} %bitcast.10, bf16[256,1024]{1,0:T(8,128)(2,1)S(1)} %get-tuple-element.6, bf16[256,1024]{1,0:T(8,128)(2,1)S(1)} %get-tuple-element.12, bf16[256,1024]{1,0:T(8,128)(2,1)S(1)} %get-tuple-element.13, ...), kind=kOutput, calls=%fused_computation.2 | convolution fusion | flops 4305453056 | bytes 10486272 | tf_op jit(solution)/shard_map/dot_general | solution.py:188
  45.6 3.3 %collective-permute-start.6 = (bf16[256,1024]{1,0:T(8,128)(2,1)S(1)}, bf16[256,1024]{1,0:T(8,128)(2,1)S(1)}, u32[]{:S(2)}, u32[]{:S(2)}) collective-permute-start(bf16[256,1024]{1,0:T(8,128)(2,1)S(1)} %get-tuple-element.6), channel_id=1, source_target_pairs={{0,2},{1,3},{2,4},{3,5},{4,6},{5,7},{6,8},{7,9},{8,10},{9,11},{10,... | collective-permute-start | bytes 1572872 | tf_op jit(solution)/shard_map/ppermute | solution.py:19
  48.9 1.3 collective-permute-start.1
  51.5 1.4 %collective-permute-done.4 = bf16[256,1024]{1,0:T(8,128)(2,1)} collective-permute-done((bf16[256,1024]{1,0:T(8,128)(2,1)S(1)}, bf16[256,1024]{1,0:T(8,128)(2,1)}, u32[]{:S(2)}, u32[]{:S(2)}) %collective-permute-start.4) | collective-permute-done | bytes 524320 | tf_op jit(solution)/shard_map/ppermute | solution.py:19
  52.9 3.0 %collective-permute-start.5 = (bf16[256,1024]{1,0:T(8,128)(2,1)}, bf16[256,1024]{1,0:T(8,128)(2,1)S(1)}, u32[]{:S(2)}, u32[]{:S(2)}) collective-permute-start(bf16[256,1024]{1,0:T(8,128)(2,1)} %collective-permute-done.4), channel_id=1, source_target_pairs={{0,1},{1,2},{2,3},{3,4},{4,5},{5,6},{6,7},{7,8},{8,9},{9,10},{10,1... | collective-permute-start | bytes 1572872 | tf_op jit(solution)/shard_map/ppermute | solution.py:19
  55.9 3.1 %slice_bitcast_fusion.env_ref = bf16[1024,1024]{1,0:T(8,128)(2,1)} fusion(bf16[2,1,1024,1024]{3,2,1,0:T(8,128)(2,1)} %param.7), kind=kLoop, calls=%fused_computation.25 | loop fusion | bytes 4194304 | tf_op jit(solution)/shard_map/squeeze | solution.py:203
  59.0 5.1 %collective-permute-done.2 = bf16[256,1024]{1,0:T(8,128)(2,1)S(1)} collective-permute-done((bf16[256,1024]{1,0:T(8,128)(2,1)S(1)}, bf16[256,1024]{1,0:T(8,128)(2,1)S(1)}, u32[]{:S(2)}, u32[]{:S(2)}) %collective-permute-start.2) | collective-permute-done | bytes 524320 | tf_op jit(solution)/shard_map/ppermute | solution.py:19
  64.1 1.3 collective-permute-start.3
  65.5 9.9 %collective-permute-done.6 = bf16[256,1024]{1,0:T(8,128)(2,1)S(1)} collective-permute-done((bf16[256,1024]{1,0:T(8,128)(2,1)S(1)}, bf16[256,1024]{1,0:T(8,128)(2,1)S(1)}, u32[]{:S(2)}, u32[]{:S(2)}) %collective-permute-start.6) | collective-permute-done | bytes 524320 | tf_op jit(solution)/shard_map/ppermute | solution.py:19
  75.4 1.3 collective-permute-start.7
  76.7 2.5 %fusion.25 = bf16[256,1024]{1,0:T(8,128)(2,1)S(1)} fusion(bf16[2,1,1024,1024]{3,2,1,0:T(8,128)(2,1)} %param.8, bf16[256,1024]{1,0:T(8,128)(2,1)S(1)} %collective-permute-done.1, bf16[256,1024]{1,0:T(8,128)(2,1)} %collective-permute-done, f32[]{:T(128)S(6)} %select_n.75, f32[]{:T(128)S(6)} %select_n.67), kind=kOutput, calls=%fused_computation.30 | convolution fusion | flops 538705920 | bytes 3670024 | tf_op jit(solution)/shard_map/dot_general | solution.py:199
  79.2 1.8 %fusion.31 = bf16[256,1024]{1,0:T(8,128)(2,1)S(1)} fusion(bf16[2,1,1024,1024]{3,2,1,0:T(8,128)(2,1)S(1)} %copy-done.3, bf16[256,1024]{1,0:T(8,128)(2,1)S(1)} %collective-permute-done.5, bf16[256,1024]{1,0:T(8,128)(2,1)} %collective-permute-done.4, f32[]{:T(128)S(6)} %select_n.75, f32[]{:T(128)S(6)} %select_n.67), kind=kOutput, calls=%fused_computation.32 | convolution fusion | flops 538705920 | bytes 3670024 | tf_op jit(solution)/shard_map/dot_general | solution.py:199
  82.5 1.5 %pad_maximum_fusion.part_ref = bf16[1024,1024]{1,0:T(8,128)(2,1)} fusion(bf16[256,1024]{1,0:T(8,128)(2,1)S(1)} %fusion.34, bf16[256,1024]{1,0:T(8,128)(2,1)S(1)} %fusion.31, bf16[256,1024]{1,0:T(8,128)(2,1)S(1)} %fusion.28, bf16[256,1024]{1,0:T(8,128)(2,1)S(1)} %fusion.25), kind=kLoop, calls=%fused_computation.11 | loop fusion | flops 8388608 | bytes 4194304 | tf_op jit(solution)/shard_map/concatenate | solution.py:201
  84.0 9.7 %shard_map.78 = (f32[1024,1024]{1,0:T(8,128)}, f32[32,1,2]{2,1,0:T(1,128)}) custom-call(s32[1]{0:T(128)} %bitcast.index_ref, s32[8]{0:T(128)} %left_ref.3, s32[10]{0:T(128)} %right_ref.3, f32[1]{0:T(128)} %bitcast.1.scale_ref, bf16[1024,1024]{1,0:T(8,128)(2,1)} %slice_bitcast_fusion.env_ref, bf16[1024,1024]{1,0:T(8,128)(2,1)} %pad_maximum_fusion.part_ref, ...), custom_call_target="tpu_custom_call" | custom-call | tf_op jit(solution)/shard_map/pallas_call | solution.py:108
  93.7 21.9 %all-to-all-start.1 = ((f32[32,1,2]{2,1,0:T(1,128)}), f32[32,1,2]{2,1,0:T(1,128)S(1)}, u32[]{:S(2)}, u32[]{:S(2)}) async-start(f32[32,1,2]{2,1,0:T(1,128)} %get-tuple-element.9), calls=%async_computation.1 | async-start | bytes 32768 | tf_op jit(solution)/shard_map/all_to_all | solution.py:28
  115.6 7.1 %all-to-all-done.1 = f32[32,1,2]{2,1,0:T(1,128)S(1)} async-done(((f32[32,1,2]{2,1,0:T(1,128)}), f32[32,1,2]{2,1,0:T(1,128)S(1)}, u32[]{:S(2)}, u32[]{:S(2)}) %all-to-all-start.1) | async-done | bytes 288 | tf_op jit(solution)/shard_map/all_to_all | solution.py:28
  125.9 6.4 %divide_bitcast_fusion = f32[1,1024,1024]{2,1,0:T(8,128)} fusion(f32[1024,1024]{1,0:T(8,128)} %get-tuple-element.8, f32[]{:T(128)} %sqrt.7, f32[]{:T(128)} %sqrt.6, f32[]{:T(128)} %bitcast.15, f32[1024]{0:T(1024)S(1)} %get-tuple-element.22, f32[1024]{0:T(1024)S(1)} %get-tuple-element.21, f32[1,1024,1024]{2,1,0:T(8,128)} %state_ref.3), kind=kLoop, calls=%fused_computation.1 | loop fusion | flops 6291456 | bytes 12591116 | tf_op jit(solution)/shard_map/broadcast_in_dim | solution.py:213
  (27 shorter events, 5.7 us)
Async XLA Ops:
  0.6 13.9 %copy-start.2 = (s32[10]{0:T(128)S(1)}, s32[10]{0:T(128)}, u32[]{:S(2)}) copy-start(s32[10]{0:T(128)} %right_ref.3) | copy-start | bytes 124
  0.6 12.2 %copy-start.1 = (s32[8]{0:T(128)S(1)}, s32[8]{0:T(128)}, u32[]{:S(2)}) copy-start(s32[8]{0:T(128)} %left_ref.3) | copy-start | bytes 100
  0.7 15.7 %copy-start = (f32[2,4,4]{2,1,0:T(4,128)S(1)}, f32[2,4,4]{2,1,0:T(4,128)}, u32[]{:S(2)}) copy-start(f32[2,4,4]{2,1,0:T(4,128)} %param.9) | copy-start | bytes 388
  5.4 16.2 %all-to-all-start = ((f32[32,1,1]{2,1,0:T(1,128)}), f32[32,1,1]{2,1,0:T(1,128)S(1)}, u32[]{:S(2)}, u32[]{:S(2)}) async-start(f32[32,1,1]{2,1,0:T(1,128)} %shard_map.77), calls=%async_computation | async-start | bytes 32768 | tf_op jit(solution)/shard_map/all_to_all | solution.py:28
  25.7 23.1 %collective-permute-start = (bf16[256,1024]{1,0:T(8,128)(2,1)S(1)}, bf16[256,1024]{1,0:T(8,128)(2,1)}, u32[]{:S(2)}, u32[]{:S(2)}) collective-permute-start(bf16[256,1024]{1,0:T(8,128)(2,1)S(1)} %get-tuple-element.10), channel_id=1, source_target_pairs={{0,2},{1,3},{2,4},{3,5},{4,6},{5,7},{6,8},{7,9},{8,10},{9,11},{10,... | collective-permute-start | bytes 1572872 | tf_op jit(solution)/shard_map/ppermute | solution.py:19
  30.2 22.7 %collective-permute-start.4 = (bf16[256,1024]{1,0:T(8,128)(2,1)S(1)}, bf16[256,1024]{1,0:T(8,128)(2,1)}, u32[]{:S(2)}, u32[]{:S(2)}) collective-permute-start(bf16[256,1024]{1,0:T(8,128)(2,1)S(1)} %get-tuple-element.12), channel_id=1, source_target_pairs={{0,2},{1,3},{2,4},{3,5},{4,6},{5,7},{6,8},{7,9},{8,10},{9,11},{10,... | collective-permute-start | bytes 1572872 | tf_op jit(solution)/shard_map/ppermute | solution.py:19
  33.6 30.6 %collective-permute-start.2 = (bf16[256,1024]{1,0:T(8,128)(2,1)S(1)}, bf16[256,1024]{1,0:T(8,128)(2,1)S(1)}, u32[]{:S(2)}, u32[]{:S(2)}) collective-permute-start(bf16[256,1024]{1,0:T(8,128)(2,1)S(1)} %get-tuple-element.13), channel_id=1, source_target_pairs={{0,2},{1,3},{2,4},{3,5},{4,6},{5,7},{6,8},{7,9},{8,10},{9,11},{10,... | collective-permute-start | bytes 1572872 | tf_op jit(solution)/shard_map/ppermute | solution.py:19
  45.6 29.8 %collective-permute-start.6 = (bf16[256,1024]{1,0:T(8,128)(2,1)S(1)}, bf16[256,1024]{1,0:T(8,128)(2,1)S(1)}, u32[]{:S(2)}, u32[]{:S(2)}) collective-permute-start(bf16[256,1024]{1,0:T(8,128)(2,1)S(1)} %get-tuple-element.6), channel_id=1, source_target_pairs={{0,2},{1,3},{2,4},{3,5},{4,6},{5,7},{6,8},{7,9},{8,10},{9,11},{10,... | collective-permute-start | bytes 1572872 | tf_op jit(solution)/shard_map/ppermute | solution.py:19
  48.9 27.8 %collective-permute-start.1 = (bf16[256,1024]{1,0:T(8,128)(2,1)}, bf16[256,1024]{1,0:T(8,128)(2,1)S(1)}, u32[]{:S(2)}, u32[]{:S(2)}) collective-permute-start(bf16[256,1024]{1,0:T(8,128)(2,1)} %collective-permute-done), channel_id=1, source_target_pairs={{0,1},{1,2},{2,3},{3,4},{4,5},{5,6},{6,7},{7,8},{8,9},{9,10},{10,1... | collective-permute-start | bytes 1572872 | tf_op jit(solution)/shard_map/ppermute | solution.py:19
  51.5 27.7 %copy-start.3 = (bf16[2,1,1024,1024]{3,2,1,0:T(8,128)(2,1)S(1)}, bf16[2,1,1024,1024]{3,2,1,0:T(8,128)(2,1)}, u32[]{:S(2)}) copy-start(bf16[2,1,1024,1024]{3,2,1,0:T(8,128)(2,1)} %param.8) | copy-start | bytes 12582916
  52.9 26.3 %collective-permute-start.5 = (bf16[256,1024]{1,0:T(8,128)(2,1)}, bf16[256,1024]{1,0:T(8,128)(2,1)S(1)}, u32[]{:S(2)}, u32[]{:S(2)}) collective-permute-start(bf16[256,1024]{1,0:T(8,128)(2,1)} %collective-permute-done.4), channel_id=1, source_target_pairs={{0,1},{1,2},{2,3},{3,4},{4,5},{5,6},{6,7},{7,8},{8,9},{9,10},{10,1... | collective-permute-start | bytes 1572872 | tf_op jit(solution)/shard_map/ppermute | solution.py:19
  64.1 16.9 %collective-permute-start.3 = (bf16[256,1024]{1,0:T(8,128)(2,1)S(1)}, bf16[256,1024]{1,0:T(8,128)(2,1)S(1)}, u32[]{:S(2)}, u32[]{:S(2)}) collective-permute-start(bf16[256,1024]{1,0:T(8,128)(2,1)S(1)} %collective-permute-done.2), channel_id=1, source_target_pairs={{0,1},{1,2},{2,3},{3,4},{4,5},{5,6},{6,7},{7,8},{8,9},{9,10},{10,1... | collective-permute-start | bytes 1572872 | tf_op jit(solution)/shard_map/ppermute | solution.py:19
  75.4 6.4 %collective-permute-start.7 = (bf16[256,1024]{1,0:T(8,128)(2,1)S(1)}, bf16[256,1024]{1,0:T(8,128)(2,1)S(1)}, u32[]{:S(2)}, u32[]{:S(2)}) collective-permute-start(bf16[256,1024]{1,0:T(8,128)(2,1)S(1)} %collective-permute-done.6), channel_id=1, source_target_pairs={{0,1},{1,2},{2,3},{3,4},{4,5},{5,6},{6,7},{7,8},{8,9},{9,10},{10,1... | collective-permute-start | bytes 1572872 | tf_op jit(solution)/shard_map/ppermute | solution.py:19
  93.7 29.0 %all-to-all-start.1 = ((f32[32,1,2]{2,1,0:T(1,128)}), f32[32,1,2]{2,1,0:T(1,128)S(1)}, u32[]{:S(2)}, u32[]{:S(2)}) async-start(f32[32,1,2]{2,1,0:T(1,128)} %get-tuple-element.9), calls=%async_computation.1 | async-start | bytes 32768 | tf_op jit(solution)/shard_map/all_to_all | solution.py:28

commit v10 on v8

--- a/solution.py
+++ b/solution.py
@@ -139,14 +139,14 @@
     image = jnp.dot(left_env[0, 0], part_zero, preferred_element_type=jnp.float32) + image_one
     image = row_major(image * live)
 
-    sums = all_sum(jnp.stack([jnp.sum(vector * image), jnp.sum(image * image)]))
-    alpha_value = sums[0] / entries
+    sums = all_sum(jnp.sum(jnp.stack([vector * image, image * image]), axis=(1, 2)))
+    alpha_value = sums[0:1] / entries
     vector_mean = start_mean / (start_mean + 1e-06)
-    residual_mean = sums[1] / entries - alpha_value * alpha_value * (2.0 - vector_mean)
-    residual = image - alpha_value * vector
+    residual_mean = sums[1:2] / entries - alpha_value * alpha_value * (2.0 - vector_mean)
     beta_value = jnp.sqrt(residual_mean + 1e-06)
-    next_vector = residual / beta_value
-    return (next_vector[None], jnp.stack([alpha_value, beta_value]))
+    residual = image - alpha_value[:, None] * vector
+    next_vector = residual / beta_value[:, None]
+    return (next_vector[None], jnp.concatenate([alpha_value, beta_value]))
 
 
 def solution(mesh):

time: 130 us -> 129 us (level)
  matrix products: 20.8 us -> 17.6 us
    dot_general x1, matrix products: 5.54 us -> 2.43 us  [per_device(): jnp.dot(left_env[0, 0], part_zero, preferred_element_type=jnp.float32)]
    unnamed x14 -> x16, local copies, waits for them, and re-layouts: 1.97 us -> 3.11 us
where the time goes in v10:
time: 129 us
  starting transfers between devices  46.4 us (36%)
  waiting for transfers between devices  28.2 us (22%)
  matrix products  17.6 us (14%)
  other arithmetic  17.1 us (13%)
  between operations  7.63 us (6%)
  local copies, waits for them, and re-layouts  6.95 us (5%)
  Pallas kernels  4.77 us (4%)
    all_to_all x2, starting transfers between devices, exchange_sum(): return jnp.sum(lax.all_to_all(spread, AXES, 0, 0, tiled=True), axis=0)  27.2 us
    ppermute x8, waiting for transfers between devices, shift_up(): return lax.ppermute(block, AXES, route)  21.1 us
    ppermute x8, starting transfers between devices, shift_up(): return lax.ppermute(block, AXES, route)  19.2 us
    dot_general x1, matrix products, per_device(): jnp.dot(left_env[1, 0], part_one, preferred_element_type=jnp.float32)  9.37 us
    all_to_all x2, waiting for transfers between devices, exchange_sum(): return jnp.sum(lax.all_to_all(spread, AXES, 0, 0, tiled=True), axis=0)  7.1 us
    broadcast_in_dim x1, other arithmetic, per_device(): return (next_vector[None], jnp.concatenate([alpha_value, beta_value]))  6.43 us
    dot_general x4, matrix products, per_device(): jnp.dot(source, right_env[0, 0], preferred_element_type=jnp.float32)  5.77 us
    pallas_call x1, Pallas kernels, masked_square_sum(): pl.pallas_call(functools.partial(square_sum_kernel, pairs), grid_spec=plt...  4.77 us
  transfers between devices with their start and end apart: 10, of which 4 were waited for; matrix products, arithmetic and copies ran while one was open for 17% of the time, Pallas kernels for 0%

profile of v10, /device:TPU:0, one launch (start us, length us, event | category | flops | bytes accessed | tf_op | source)
XLA Modules:
  0.0 128.6 jit_solution(13987992390552326657)
XLA Ops:
  0.7 4.8 %shard_map.77 = f32[32,1,1]{2,1,0:T(1,128)} custom-call(s32[1]{0:T(128)} %bitcast.5.index_ref, s32[8]{0:T(128)} %left_ref.1, s32[10]{0:T(128)} %right_ref.1, f32[1,1024,1024]{2,1,0:T(8,128)} %state_ref.1), custom_call_target="tpu_custom_call" | custom-call | tf_op jit(solution)/shard_map/pallas_call | solution.py:58
  5.4 7.3 %all-to-all-start = ((f32[32,1,1]{2,1,0:T(1,128)}), f32[32,1,1]{2,1,0:T(1,128)S(1)}, u32[]{:S(2)}, u32[]{:S(2)}) async-start(f32[32,1,1]{2,1,0:T(1,128)} %shard_map.77), calls=%async_computation | async-start | bytes 32768 | tf_op jit(solution)/shard_map/all_to_all | solution.py:28
  16.9 4.6 %multiply_multiply_fusion.1 = f32[1024,1024]{1,0:T(8,128)} fusion(f32[1,1024,1024]{2,1,0:T(8,128)} %state_ref.1, f32[1024]{0:T(1024)S(1)} %get-tuple-element.20, f32[1024]{0:T(1024)S(1)} %get-tuple-element.19), kind=kLoop, calls=%fused_computation.2 | loop fusion | flops 2097152 | bytes 8396800 | tf_op jit(solution)/shard_map/mul | solution.py:97
  23.3 2.8 %fusion.49 = (bf16[256,1024]{1,0:T(8,128)(2,1)S(1)}, bf16[256,1024]{1,0:T(8,128)(2,1)S(1)}, bf16[256,1024]{1,0:T(8,128)(2,1)S(1)}, bf16[256,1024]{1,0:T(8,128)(2,1)S(1)}) fusion(f32[1024,1024]{1,0:T(8,128)} %multiply_multiply_fusion.1, f32[]{:T(128)S(6)} %sqrt.6), kind=kLoop, calls=%fused_computation.54 | loop fusion | flops 2097152 | bytes 6291460 | tf_op jit(solution)/shard_map/convert_element_type | solution.py:106
  26.1 4.5 %collective-permute-start = (bf16[256,1024]{1,0:T(8,128)(2,1)S(1)}, bf16[256,1024]{1,0:T(8,128)(2,1)}, u32[]{:S(2)}, u32[]{:S(2)}) collective-permute-start(bf16[256,1024]{1,0:T(8,128)(2,1)S(1)} %get-tuple-element.8), channel_id=1, source_target_pairs={{0,2},{1,3},{2,4},{3,5},{4,6},{5,7},{6,8},{7,9},{8,10},{9,11},{10,... | collective-permute-start | bytes 1572872 | tf_op jit(solution)/shard_map/ppermute | solution.py:19
  30.6 3.4 %collective-permute-start.4 = (bf16[256,1024]{1,0:T(8,128)(2,1)S(1)}, bf16[256,1024]{1,0:T(8,128)(2,1)}, u32[]{:S(2)}, u32[]{:S(2)}) collective-permute-start(bf16[256,1024]{1,0:T(8,128)(2,1)S(1)} %get-tuple-element.10), channel_id=1, source_target_pairs={{0,2},{1,3},{2,4},{3,5},{4,6},{5,7},{6,8},{7,9},{8,10},{9,11},{10,... | collective-permute-start | bytes 1572872 | tf_op jit(solution)/shard_map/ppermute | solution.py:19
  34.0 2.7 %collective-permute-start.2 = (bf16[256,1024]{1,0:T(8,128)(2,1)S(1)}, bf16[256,1024]{1,0:T(8,128)(2,1)S(1)}, u32[]{:S(2)}, u32[]{:S(2)}) collective-permute-start(bf16[256,1024]{1,0:T(8,128)(2,1)S(1)} %get-tuple-element.11), channel_id=1, source_target_pairs={{0,2},{1,3},{2,4},{3,5},{4,6},{5,7},{6,8},{7,9},{8,10},{9,11},{10,... | collective-permute-start | bytes 1572872 | tf_op jit(solution)/shard_map/ppermute | solution.py:19
  36.6 9.4 %multiply_bitcast_fusion.2 = f32[1024,1024]{1,0:T(8,128)} fusion(bf16[2,1,1024,1024]{3,2,1,0:T(8,128)(2,1)} %param.7, f32[]{:T(128)} %bitcast.8, bf16[256,1024]{1,0:T(8,128)(2,1)S(1)} %get-tuple-element.4, bf16[256,1024]{1,0:T(8,128)(2,1)S(1)} %get-tuple-element.10, bf16[256,1024]{1,0:T(8,128)(2,1)S(1)} %get-tuple-element.11, ...), kind=kOutput, calls=%fused_computation.7 | convolution fusion | flops 4305453056 | bytes 10486272 | tf_op jit(solution)/shard_map/dot_general | solution.py:125
  46.0 3.3 %collective-permute-start.6 = (bf16[256,1024]{1,0:T(8,128)(2,1)S(1)}, bf16[256,1024]{1,0:T(8,128)(2,1)S(1)}, u32[]{:S(2)}, u32[]{:S(2)}) collective-permute-start(bf16[256,1024]{1,0:T(8,128)(2,1)S(1)} %get-tuple-element.4), channel_id=1, source_target_pairs={{0,2},{1,3},{2,4},{3,5},{4,6},{5,7},{6,8},{7,9},{8,10},{9,11},{10,... | collective-permute-start | bytes 1572872 | tf_op jit(solution)/shard_map/ppermute | solution.py:19
  49.3 1.3 %collective-permute-start.1 = (bf16[256,1024]{1,0:T(8,128)(2,1)}, bf16[256,1024]{1,0:T(8,128)(2,1)S(1)}, u32[]{:S(2)}, u32[]{:S(2)}) collective-permute-start(bf16[256,1024]{1,0:T(8,128)(2,1)} %collective-permute-done), channel_id=1, source_target_pairs={{0,1},{1,2},{2,3},{3,4},{4,5},{5,6},{6,7},{7,8},{8,9},{9,10},{10,1... | collective-permute-start | bytes 1572872 | tf_op jit(solution)/shard_map/ppermute | solution.py:19
  50.6 2.6 %collective-permute-done.4 = bf16[256,1024]{1,0:T(8,128)(2,1)} collective-permute-done((bf16[256,1024]{1,0:T(8,128)(2,1)S(1)}, bf16[256,1024]{1,0:T(8,128)(2,1)}, u32[]{:S(2)}, u32[]{:S(2)}) %collective-permute-start.4) | collective-permute-done | bytes 524320 | tf_op jit(solution)/shard_map/ppermute | solution.py:19
  53.3 1.5 %collective-permute-start.5 = (bf16[256,1024]{1,0:T(8,128)(2,1)}, bf16[256,1024]{1,0:T(8,128)(2,1)S(1)}, u32[]{:S(2)}, u32[]{:S(2)}) collective-permute-start(bf16[256,1024]{1,0:T(8,128)(2,1)} %collective-permute-done.4), channel_id=1, source_target_pairs={{0,1},{1,2},{2,3},{3,4},{4,5},{5,6},{6,7},{7,8},{8,9},{9,10},{10,1... | collective-permute-start | bytes 1572872 | tf_op jit(solution)/shard_map/ppermute | solution.py:19
  56.0 8.5 %collective-permute-done.2 = bf16[256,1024]{1,0:T(8,128)(2,1)S(1)} collective-permute-done((bf16[256,1024]{1,0:T(8,128)(2,1)S(1)}, bf16[256,1024]{1,0:T(8,128)(2,1)S(1)}, u32[]{:S(2)}, u32[]{:S(2)}) %collective-permute-start.2) | collective-permute-done | bytes 524320 | tf_op jit(solution)/shard_map/ppermute | solution.py:19
  64.5 1.3 %collective-permute-start.3 = (bf16[256,1024]{1,0:T(8,128)(2,1)S(1)}, bf16[256,1024]{1,0:T(8,128)(2,1)S(1)}, u32[]{:S(2)}, u32[]{:S(2)}) collective-permute-start(bf16[256,1024]{1,0:T(8,128)(2,1)S(1)} %collective-permute-done.2), channel_id=1, source_target_pairs={{0,1},{1,2},{2,3},{3,4},{4,5},{5,6},{6,7},{7,8},{8,9},{9,10},{10,1... | collective-permute-start | bytes 1572872 | tf_op jit(solution)/shard_map/ppermute | solution.py:19
  65.8 9.9 %collective-permute-done.6 = bf16[256,1024]{1,0:T(8,128)(2,1)S(1)} collective-permute-done((bf16[256,1024]{1,0:T(8,128)(2,1)S(1)}, bf16[256,1024]{1,0:T(8,128)(2,1)S(1)}, u32[]{:S(2)}, u32[]{:S(2)}) %collective-permute-start.6) | collective-permute-done | bytes 524320 | tf_op jit(solution)/shard_map/ppermute | solution.py:19
  75.8 1.3 %collective-permute-start.7 = (bf16[256,1024]{1,0:T(8,128)(2,1)S(1)}, bf16[256,1024]{1,0:T(8,128)(2,1)S(1)}, u32[]{:S(2)}, u32[]{:S(2)}) collective-permute-start(bf16[256,1024]{1,0:T(8,128)(2,1)S(1)} %collective-permute-done.6), channel_id=1, source_target_pairs={{0,1},{1,2},{2,3},{3,4},{4,5},{5,6},{6,7},{7,8},{8,9},{9,10},{10,1... | collective-permute-start | bytes 1572872 | tf_op jit(solution)/shard_map/ppermute | solution.py:19
  77.1 2.5 %fusion.34 = bf16[256,1024]{1,0:T(8,128)(2,1)S(1)} fusion(bf16[2,1,1024,1024]{3,2,1,0:T(8,128)(2,1)} %param.8, bf16[256,1024]{1,0:T(8,128)(2,1)S(1)} %collective-permute-done.1, bf16[256,1024]{1,0:T(8,128)(2,1)} %collective-permute-done, f32[]{:T(128)S(6)} %select_n.75, f32[]{:T(128)S(6)} %select_n.67), kind=kOutput, calls=%fused_computation.43 | convolution fusion | flops 538705920 | bytes 3670024 | tf_op jit(solution)/shard_map/dot_general | solution.py:136
  79.6 1.8 %fusion.40 = bf16[256,1024]{1,0:T(8,128)(2,1)S(1)} fusion(bf16[2,1,1024,1024]{3,2,1,0:T(8,128)(2,1)S(1)} %copy-done.5, bf16[256,1024]{1,0:T(8,128)(2,1)S(1)} %collective-permute-done.5, bf16[256,1024]{1,0:T(8,128)(2,1)} %collective-permute-done.4, f32[]{:T(128)S(6)} %select_n.75, f32[]{:T(128)S(6)} %select_n.67), kind=kOutput, calls=%fused_computation.45 | convolution fusion | flops 538705920 | bytes 3670024 | tf_op jit(solution)/shard_map/dot_general | solution.py:136
  83.6 1.3 copy-done.7
  84.9 2.4 %multiply_multiply_fusion = f32[1024,1024]{1,0:T(8,128)S(1)} fusion(f32[1024,1024]{1,0:T(8,128)S(1)} %copy-done.7, bf16[256,1024]{1,0:T(8,128)(2,1)S(1)} %fusion.43, bf16[256,1024]{1,0:T(8,128)(2,1)S(1)} %fusion.40, bf16[256,1024]{1,0:T(8,128)(2,1)S(1)} %fusion.37, bf16[256,1024]{1,0:T(8,128)(2,1)S(1)} %fusion.34, ...), kind=kOutput, calls=%fused_computation.1 | convolution fusion | flops 2159017984 | bytes 12591104 | tf_op jit(solution)/shard_map/dot_general | solution.py:139
  89.3 1.2 maximum_reduce_fusion
  91.1 19.9 %all-to-all-start.1 = ((f32[32,1,2]{2,1,0:T(1,128)}), f32[32,1,2]{2,1,0:T(1,128)S(1)}, u32[]{:S(2)}, u32[]{:S(2)}) async-start(f32[32,1,2]{2,1,0:T(1,128)} %broadcast_in_dim.4), calls=%async_computation.1 | async-start | bytes 32768 | tf_op jit(solution)/shard_map/all_to_all | solution.py:28
  111.1 7.1 %all-to-all-done.1 = f32[32,1,2]{2,1,0:T(1,128)S(1)} async-done(((f32[32,1,2]{2,1,0:T(1,128)}), f32[32,1,2]{2,1,0:T(1,128)S(1)}, u32[]{:S(2)}, u32[]{:S(2)}) %all-to-all-start.1) | async-done | bytes 288 | tf_op jit(solution)/shard_map/all_to_all | solution.py:28
  122.2 6.4 %divide_bitcast_fusion = f32[1,1024,1024]{2,1,0:T(8,128)} fusion(f32[1024,1024]{1,0:T(8,128)} %copy-done.1, f32[]{:T(128)} %bitcast.18, f32[]{:T(128)} %bitcast.16, f32[]{:T(128)S(6)} %sqrt.6, f32[1024]{0:T(1024)S(1)} %get-tuple-element.20, f32[1024]{0:T(1024)S(1)} %get-tuple-element.19, f32[1,1024,1024]{2,1,0:T(8,128)} %state_ref.1), kind=kLoop, calls=%fused_computation.4 | loop fusion | flops 6291456 | bytes 12591116 | tf_op jit(solution)/shard_map/broadcast_in_dim | solution.py:149
  (36 shorter events, 9.3 us)
Async XLA Ops:
  0.6 14.2 %copy-start.4 = (s32[10]{0:T(128)S(1)}, s32[10]{0:T(128)}, u32[]{:S(2)}) copy-start(s32[10]{0:T(128)} %right_ref.1) | copy-start | bytes 124
  0.6 12.2 %copy-start.3 = (s32[8]{0:T(128)S(1)}, s32[8]{0:T(128)}, u32[]{:S(2)}) copy-start(s32[8]{0:T(128)} %left_ref.1) | copy-start | bytes 100
  0.7 16.2 %copy-start.2 = (f32[2,4,4]{2,1,0:T(4,128)S(1)}, f32[2,4,4]{2,1,0:T(4,128)}, u32[]{:S(2)}) copy-start(f32[2,4,4]{2,1,0:T(4,128)} %param.9) | copy-start | bytes 388
  5.4 16.7 %all-to-all-start = ((f32[32,1,1]{2,1,0:T(1,128)}), f32[32,1,1]{2,1,0:T(1,128)S(1)}, u32[]{:S(2)}, u32[]{:S(2)}) async-start(f32[32,1,1]{2,1,0:T(1,128)} %shard_map.77), calls=%async_computation | async-start | bytes 32768 | tf_op jit(solution)/shard_map/all_to_all | solution.py:28
  26.1 23.2 %collective-permute-start = (bf16[256,1024]{1,0:T(8,128)(2,1)S(1)}, bf16[256,1024]{1,0:T(8,128)(2,1)}, u32[]{:S(2)}, u32[]{:S(2)}) collective-permute-start(bf16[256,1024]{1,0:T(8,128)(2,1)S(1)} %get-tuple-element.8), channel_id=1, source_target_pairs={{0,2},{1,3},{2,4},{3,5},{4,6},{5,7},{6,8},{7,9},{8,10},{9,11},{10,... | collective-permute-start | bytes 1572872 | tf_op jit(solution)/shard_map/ppermute | solution.py:19
  30.6 22.7 %collective-permute-start.4 = (bf16[256,1024]{1,0:T(8,128)(2,1)S(1)}, bf16[256,1024]{1,0:T(8,128)(2,1)}, u32[]{:S(2)}, u32[]{:S(2)}) collective-permute-start(bf16[256,1024]{1,0:T(8,128)(2,1)S(1)} %get-tuple-element.10), channel_id=1, source_target_pairs={{0,2},{1,3},{2,4},{3,5},{4,6},{5,7},{6,8},{7,9},{8,10},{9,11},{10,... | collective-permute-start | bytes 1572872 | tf_op jit(solution)/shard_map/ppermute | solution.py:19
  34.0 30.6 %collective-permute-start.2 = (bf16[256,1024]{1,0:T(8,128)(2,1)S(1)}, bf16[256,1024]{1,0:T(8,128)(2,1)S(1)}, u32[]{:S(2)}, u32[]{:S(2)}) collective-permute-start(bf16[256,1024]{1,0:T(8,128)(2,1)S(1)} %get-tuple-element.11), channel_id=1, source_target_pairs={{0,2},{1,3},{2,4},{3,5},{4,6},{5,7},{6,8},{7,9},{8,10},{9,11},{10,... | collective-permute-start | bytes 1572872 | tf_op jit(solution)/shard_map/ppermute | solution.py:19
  46.0 29.8 %collective-permute-start.6 = (bf16[256,1024]{1,0:T(8,128)(2,1)S(1)}, bf16[256,1024]{1,0:T(8,128)(2,1)S(1)}, u32[]{:S(2)}, u32[]{:S(2)}) collective-permute-start(bf16[256,1024]{1,0:T(8,128)(2,1)S(1)} %get-tuple-element.4), channel_id=1, source_target_pairs={{0,2},{1,3},{2,4},{3,5},{4,6},{5,7},{6,8},{7,9},{8,10},{9,11},{10,... | collective-permute-start | bytes 1572872 | tf_op jit(solution)/shard_map/ppermute | solution.py:19
  49.3 27.8 %collective-permute-start.1 = (bf16[256,1024]{1,0:T(8,128)(2,1)}, bf16[256,1024]{1,0:T(8,128)(2,1)S(1)}, u32[]{:S(2)}, u32[]{:S(2)}) collective-permute-start(bf16[256,1024]{1,0:T(8,128)(2,1)} %collective-permute-done), channel_id=1, source_target_pairs={{0,1},{1,2},{2,3},{3,4},{4,5},{5,6},{6,7},{7,8},{8,9},{9,10},{10,1... | collective-permute-start | bytes 1572872 | tf_op jit(solution)/shard_map/ppermute | solution.py:19
  53.3 26.3 %collective-permute-start.5 = (bf16[256,1024]{1,0:T(8,128)(2,1)}, bf16[256,1024]{1,0:T(8,128)(2,1)S(1)}, u32[]{:S(2)}, u32[]{:S(2)}) collective-permute-start(bf16[256,1024]{1,0:T(8,128)(2,1)} %collective-permute-done.4), channel_id=1, source_target_pairs={{0,1},{1,2},{2,3},{3,4},{4,5},{5,6},{6,7},{7,8},{8,9},{9,10},{10,1... | collective-permute-start | bytes 1572872 | tf_op jit(solution)/shard_map/ppermute | solution.py:19
  56.0 23.6 %copy-start.5 = (bf16[2,1,1024,1024]{3,2,1,0:T(8,128)(2,1)S(1)}, bf16[2,1,1024,1024]{3,2,1,0:T(8,128)(2,1)}, u32[]{:S(2)}) copy-start(bf16[2,1,1024,1024]{3,2,1,0:T(8,128)(2,1)} %param.8) | copy-start | bytes 12582916
  64.5 16.9 %collective-permute-start.3 = (bf16[256,1024]{1,0:T(8,128)(2,1)S(1)}, bf16[256,1024]{1,0:T(8,128)(2,1)S(1)}, u32[]{:S(2)}, u32[]{:S(2)}) collective-permute-start(bf16[256,1024]{1,0:T(8,128)(2,1)S(1)} %collective-permute-done.2), channel_id=1, source_target_pairs={{0,1},{1,2},{2,3},{3,4},{4,5},{5,6},{6,7},{7,8},{8,9},{9,10},{10,1... | collective-permute-start | bytes 1572872 | tf_op jit(solution)/shard_map/ppermute | solution.py:19
  75.8 6.4 %collective-permute-start.7 = (bf16[256,1024]{1,0:T(8,128)(2,1)S(1)}, bf16[256,1024]{1,0:T(8,128)(2,1)S(1)}, u32[]{:S(2)}, u32[]{:S(2)}) collective-permute-start(bf16[256,1024]{1,0:T(8,128)(2,1)S(1)} %collective-permute-done.6), channel_id=1, source_target_pairs={{0,1},{1,2},{2,3},{3,4},{4,5},{5,6},{6,7},{7,8},{8,9},{9,10},{10,1... | collective-permute-start | bytes 1572872 | tf_op jit(solution)/shard_map/ppermute | solution.py:19
  81.4 2.2 %copy-start.6 = (bf16[2,1,1024,1024]{3,2,1,0:T(8,128)(2,1)S(1)}, bf16[2,1,1024,1024]{3,2,1,0:T(8,128)(2,1)}, u32[]{:S(2)}) copy-start(bf16[2,1,1024,1024]{3,2,1,0:T(8,128)(2,1)} %param.7) | copy-start | bytes 12582916
  81.4 3.5 %copy-start.7 = (f32[1024,1024]{1,0:T(8,128)S(1)}, f32[1024,1024]{1,0:T(8,128)}, u32[]{:S(2)}) copy-start(f32[1024,1024]{1,0:T(8,128)} %multiply_bitcast_fusion.2) | copy-start | bytes 12582916
  84.9 2.4 %copy-start = (f32[1,1024,1024]{2,1,0:T(8,128)S(1)}, f32[1,1024,1024]{2,1,0:T(8,128)}, u32[]{:S(2)}) copy-start(f32[1,1024,1024]{2,1,0:T(8,128)} %state_ref.1) | copy-start | bytes 12582916
  87.3 2.0 %copy-start.1 = (f32[1024,1024]{1,0:T(8,128)}, f32[1024,1024]{1,0:T(8,128)S(1)}, u32[]{:S(2)}) copy-start(f32[1024,1024]{1,0:T(8,128)S(1)} %multiply_multiply_fusion) | copy-start | bytes 12582916
  91.1 27.1 %all-to-all-start.1 = ((f32[32,1,2]{2,1,0:T(1,128)}), f32[32,1,2]{2,1,0:T(1,128)S(1)}, u32[]{:S(2)}, u32[]{:S(2)}) async-start(f32[32,1,2]{2,1,0:T(1,128)} %broadcast_in_dim.4), calls=%async_computation.1 | async-start | bytes 32768 | tf_op jit(solution)/shard_map/all_to_all | solution.py:28

commit v11 on v10

--- a/solution.py
+++ b/solution.py
@@ -95,17 +95,19 @@
     entries = float(state.shape[0] * sec_size * sec_size * lax.axis_size(AXES))
 
     masked = state[0] * live
-    start_sum = exchange_sum(
-        masked_square_sum(pairs, block_index.astype(jnp.int32), left_live, right_live, state)
-    )[0, 0]
+    rows = sec_size // CHUNKS
+    spread = masked_square_sum(pairs, block_index.astype(jnp.int32), left_live, right_live, state)
+    spread, head = lax.optimization_barrier((spread, masked[:rows]))
+    head_far = shift_up(head, 2)
+    start_sum = exchange_sum(spread)[0, 0]
     start_mean = start_sum / entries
     scale = jnp.sqrt(start_mean + 1e-06)
     vector = masked / scale
-    rows = sec_size // CHUNKS
     pieces = [
         row_major((masked[c * rows:(c + 1) * rows] / scale).astype(jnp.bfloat16))
         for c in range(CHUNKS)
     ]
+    head_two = row_major((head_far / scale).astype(jnp.bfloat16))
     rounded = jnp.concatenate(pieces, axis=0)
 
     weights = []
@@ -127,7 +129,7 @@
     image_one, pieces[-1] = lax.optimization_barrier((image_one, pieces[-1]))
     parts = []
     for c in range(CHUNKS):
-        far_two = shift_up(pieces[c], 2)
+        far_two = head_two if c == 0 else shift_up(pieces[c], 2)
         far_three = shift_up(far_two, 1)
         source = (
             weights[0] * far_two.astype(jnp.float32) + weights[1] * far_three.astype(jnp.float32)

time: 129 us -> 137 us (1.062)
  waiting for transfers between devices: 28.2 us -> 35.8 us
  starting transfers between devices: 46.4 us -> 43.5 us
  local copies, waits for them, and re-layouts: 6.95 us -> 9.23 us
  matrix products: 17.6 us -> 19.1 us
    all_to_all x2, starting transfers between devices: 27.2 us -> 21.3 us  [exchange_sum(): return jnp.sum(lax.all_to_all(spread, AXES, 0, 0, tiled=True), axis=0)]
    ppermute x8, waiting for transfers between devices: 21.1 us -> 26 us  [shift_up(): return lax.ppermute(block, AXES, route)]
    ppermute x8, starting transfers between devices: 19.2 us -> 22.1 us  [shift_up(): return lax.ppermute(block, AXES, route)]
    all_to_all x2, waiting for transfers between devices: 7.1 us -> 9.75 us  [exchange_sum(): return jnp.sum(lax.all_to_all(spread, AXES, 0, 0, tiled=True), axis=0)]
    mul x1, other arithmetic: 4.61 us -> 2.6 us  [per_device(): masked = state[0] * live]
    unnamed x16 -> x14, local copies, waits for them, and re-layouts: 3.11 us -> 4.1 us
  transfers between devices with their start and end apart: 10 -> 10, of which waited for: 4 -> 5; matrix products, arithmetic and copies ran while one was open for 17% -> 16% of each run, Pallas kernels for 0% -> 0%
where the time goes in v11:
time: 137 us; the launch traced here: 136 us
  starting transfers between devices  43.5 us (32%)
  waiting for transfers between devices  35.8 us (26%)
  matrix products  19.1 us (14%)
  other arithmetic  16.2 us (12%)
  local copies, waits for them, and re-layouts  9.23 us (7%)
  between operations  7.66 us (6%)
  Pallas kernels  4.64 us (3%)
    ppermute x8, waiting for transfers between devices, shift_up(): return lax.ppermute(block, AXES, route)  26 us
    ppermute x8, starting transfers between devices, shift_up(): return lax.ppermute(block, AXES, route)  22.1 us
    all_to_all x2, starting transfers between devices, exchange_sum(): return jnp.sum(lax.all_to_all(spread, AXES, 0, 0, tiled=True), axis=0)  21.3 us
    all_to_all x2, waiting for transfers between devices, exchange_sum(): return jnp.sum(lax.all_to_all(spread, AXES, 0, 0, tiled=True), axis=0)  9.75 us
    dot_general x1, matrix products, per_device(): jnp.dot(left_env[1, 0], part_one, preferred_element_type=jnp.float32)  9.61 us
    dot_general x4, matrix products, per_device(): jnp.dot(source, right_env[0, 0], preferred_element_type=jnp.float32)  7.09 us
    broadcast_in_dim x1, other arithmetic, per_device(): return (next_vector[None], jnp.concatenate([alpha_value, beta_value]))  6.43 us
    pallas_call x1, Pallas kernels, masked_square_sum(): pl.pallas_call(functools.partial(square_sum_kernel, pairs), grid_spec=plt...  4.64 us
  transfers between devices with their start and end apart: 10, of which 5 were waited for; matrix products, arithmetic and copies ran while one was open for 16% of the time, Pallas kernels for 0%

profile of v11, /device:TPU:0, one launch (start us, length us, event | category | flops | bytes accessed | tf_op | source)
XLA Modules:
  0.0 136.1 jit_solution(1855878339481444919)
XLA Ops:
  5.7 4.6 %shard_map.77 = f32[32,1,1]{2,1,0:T(1,128)} custom-call(s32[1]{0:T(128)} %bitcast.1.index_ref, s32[8]{0:T(128)} %left_ref.1, s32[10]{0:T(128)} %right_ref.1, f32[1,1024,1024]{2,1,0:T(8,128)} %state_ref.1), custom_call_target="tpu_custom_call" | custom-call | tf_op jit(solution)/shard_map/pallas_call | solution.py:58
  10.4 2.6 %multiply_multiply_fusion.1 = f32[1024,1024]{1,0:T(8,128)S(1)} fusion(f32[1,1024,1024]{2,1,0:T(8,128)} %state_ref.1, f32[1024]{0:T(1024)S(1)} %get-tuple-element.24, f32[1024]{0:T(1024)S(1)} %get-tuple-element.23), kind=kLoop, calls=%fused_computation.2 | loop fusion | flops 2097152 | bytes 8396800 | tf_op jit(solution)/shard_map/mul | solution.py:97
  13.0 2.0 %copy-done.1 = f32[1024,1024]{1,0:T(8,128)} copy-done((f32[1024,1024]{1,0:T(8,128)}, f32[1024,1024]{1,0:T(8,128)S(1)}, u32[]{:S(2)}) %copy-start.1) | copy-done | bytes 4194328
  15.1 7.3 %all-to-all-start = ((f32[32,1,1]{2,1,0:T(1,128)}), f32[32,1,1]{2,1,0:T(1,128)S(1)}, u32[]{:S(2)}, u32[]{:S(2)}) async-start(f32[32,1,1]{2,1,0:T(1,128)} %shard_map.77), calls=%async_computation | async-start | bytes 32768 | tf_op jit(solution)/shard_map/all_to_all | solution.py:28
  22.4 3.7 %collective-permute-start = (f32[256,1024]{1,0:T(8,128)S(1)}, f32[256,1024]{1,0:T(8,128)S(1)}, u32[]{:S(2)}, u32[]{:S(2)}) collective-permute-start(f32[256,1024]{1,0:T(8,128)S(1)} %slice.53), channel_id=1, source_target_pairs={{0,2},{1,3},{2,4},{3,5},{4,6},{5,7},{6,8},{7,9},{8,10},{9,11},{10,... | collective-permute-start | bytes 3145736 | tf_op jit(solution)/shard_map/ppermute | solution.py:19
  26.9 2.6 %all-to-all-done = f32[32,1,1]{2,1,0:T(1,128)S(1)} async-done(((f32[32,1,1]{2,1,0:T(1,128)}), f32[32,1,1]{2,1,0:T(1,128)S(1)}, u32[]{:S(2)}, u32[]{:S(2)}) %all-to-all-start) | async-done | bytes 160 | tf_op jit(solution)/shard_map/all_to_all | solution.py:28
  30.9 3.8 %divide_convert_fusion = (bf16[256,1024]{1,0:T(8,128)(2,1)}, bf16[256,1024]{1,0:T(8,128)(2,1)}, bf16[256,1024]{1,0:T(8,128)(2,1)S(1)}, bf16[256,1024]{1,0:T(8,128)(2,1)S(1)}) fusion(f32[]{:T(128)S(6)} %sqrt.6, f32[1024,1024]{1,0:T(8,128)} %copy-done.1), kind=kLoop, calls=%fused_computation.54 | loop fusion | flops 2097152 | bytes 6291460 | tf_op jit(solution)/shard_map/convert_element_type | solution.py:107
  34.7 3.2 %collective-permute-start.2 = (bf16[256,1024]{1,0:T(8,128)(2,1)}, bf16[256,1024]{1,0:T(8,128)(2,1)}, u32[]{:S(2)}, u32[]{:S(2)}) collective-permute-start(bf16[256,1024]{1,0:T(8,128)(2,1)} %get-tuple-element.13), channel_id=1, source_target_pairs={{0,2},{1,3},{2,4},{3,5},{4,6},{5,7},{6,8},{7,9},{8,10},{9,11},{10,... | collective-permute-start | bytes 1572872 | tf_op jit(solution)/shard_map/ppermute | solution.py:19
  37.9 2.4 %collective-permute-start.4 = (bf16[256,1024]{1,0:T(8,128)(2,1)S(1)}, bf16[256,1024]{1,0:T(8,128)(2,1)}, u32[]{:S(2)}, u32[]{:S(2)}) collective-permute-start(bf16[256,1024]{1,0:T(8,128)(2,1)S(1)} %get-tuple-element.14), channel_id=1, source_target_pairs={{0,2},{1,3},{2,4},{3,5},{4,6},{5,7},{6,8},{7,9},{8,10},{9,11},{10,... | collective-permute-start | bytes 1572872 | tf_op jit(solution)/shard_map/ppermute | solution.py:19
  40.4 9.6 %multiply_bitcast_fusion.2 = f32[1024,1024]{1,0:T(8,128)} fusion(bf16[2,1,1024,1024]{3,2,1,0:T(8,128)(2,1)} %param.7, f32[]{:T(128)} %bitcast.8, bf16[256,1024]{1,0:T(8,128)(2,1)S(1)} %get-tuple-element.8, bf16[256,1024]{1,0:T(8,128)(2,1)S(1)} %get-tuple-element.14, bf16[256,1024]{1,0:T(8,128)(2,1)} %get-tuple-element.13, ...), kind=kOutput, calls=%fused_computation.7 | convolution fusion | flops 4305453056 | bytes 10486272 | tf_op jit(solution)/shard_map/dot_general | solution.py:127
  50.0 2.6 %collective-permute-start.6 = (bf16[256,1024]{1,0:T(8,128)(2,1)S(1)}, bf16[256,1024]{1,0:T(8,128)(2,1)}, u32[]{:S(2)}, u32[]{:S(2)}) collective-permute-start(bf16[256,1024]{1,0:T(8,128)(2,1)S(1)} %get-tuple-element.8), channel_id=1, source_target_pairs={{0,2},{1,3},{2,4},{3,5},{4,6},{5,7},{6,8},{7,9},{8,10},{9,11},{10,... | collective-permute-start | bytes 1572872 | tf_op jit(solution)/shard_map/ppermute | solution.py:19
  52.5 8.4 %collective-permute-done.2 = bf16[256,1024]{1,0:T(8,128)(2,1)} collective-permute-done((bf16[256,1024]{1,0:T(8,128)(2,1)}, bf16[256,1024]{1,0:T(8,128)(2,1)}, u32[]{:S(2)}, u32[]{:S(2)}) %collective-permute-start.2) | collective-permute-done | bytes 524320 | tf_op jit(solution)/shard_map/ppermute | solution.py:19
  61.0 2.1 %collective-permute-start.3 = (bf16[256,1024]{1,0:T(8,128)(2,1)}, bf16[256,1024]{1,0:T(8,128)(2,1)}, u32[]{:S(2)}, u32[]{:S(2)}) collective-permute-start(bf16[256,1024]{1,0:T(8,128)(2,1)} %collective-permute-done.2), channel_id=1, source_target_pairs={{0,1},{1,2},{2,3},{3,4},{4,5},{5,6},{6,7},{7,8},{8,9},{9,10},{10,1... | collective-permute-start | bytes 1572872 | tf_op jit(solution)/shard_map/ppermute | solution.py:19
  64.4 7.7 %collective-permute-done.4 = bf16[256,1024]{1,0:T(8,128)(2,1)} collective-permute-done((bf16[256,1024]{1,0:T(8,128)(2,1)S(1)}, bf16[256,1024]{1,0:T(8,128)(2,1)}, u32[]{:S(2)}, u32[]{:S(2)}) %collective-permute-start.4) | collective-permute-done | bytes 524320 | tf_op jit(solution)/shard_map/ppermute | solution.py:19
  72.1 1.3 collective-permute-start.5
  73.4 9.9 %collective-permute-done.6 = bf16[256,1024]{1,0:T(8,128)(2,1)} collective-permute-done((bf16[256,1024]{1,0:T(8,128)(2,1)S(1)}, bf16[256,1024]{1,0:T(8,128)(2,1)}, u32[]{:S(2)}, u32[]{:S(2)}) %collective-permute-start.6) | collective-permute-done | bytes 524320 | tf_op jit(solution)/shard_map/ppermute | solution.py:19
  84.7 5.4 %collective-permute-start.1 = (bf16[256,1024]{1,0:T(8,128)(2,1)S(1)}, bf16[256,1024]{1,0:T(8,128)(2,1)S(1)}, u32[]{:S(2)}, u32[]{:S(2)}) collective-permute-start(bf16[256,1024]{1,0:T(8,128)(2,1)S(1)} %divide_convert_fusion.1), channel_id=1, source_target_pairs={{0,1},{1,2},{2,3},{3,4},{4,5},{5,6},{6,7},{7,8},{8,9},{9,10},{10,1... | collective-permute-start | bytes 1572872 | tf_op jit(solution)/shard_map/ppermute | solution.py:19
  90.2 2.6 %fusion.37 = bf16[256,1024]{1,0:T(8,128)(2,1)S(1)} fusion(bf16[2,1,1024,1024]{3,2,1,0:T(8,128)(2,1)} %param.8, bf16[256,1024]{1,0:T(8,128)(2,1)} %collective-permute-done.3, bf16[256,1024]{1,0:T(8,128)(2,1)} %collective-permute-done.2, f32[]{:T(128)S(6)} %select_n.75, f32[]{:T(128)S(6)} %select_n.67), kind=kOutput, calls=%fused_computation.44 | convolution fusion | flops 538705920 | bytes 3670024 | tf_op jit(solution)/shard_map/dot_general | solution.py:138
  92.8 1.8 %fusion.40 = bf16[256,1024]{1,0:T(8,128)(2,1)S(1)} fusion(bf16[2,1,1024,1024]{3,2,1,0:T(8,128)(2,1)S(1)} %copy-done.4, bf16[256,1024]{1,0:T(8,128)(2,1)S(1)} %collective-permute-done.5, bf16[256,1024]{1,0:T(8,128)(2,1)} %collective-permute-done.4, f32[]{:T(128)S(6)} %select_n.75, f32[]{:T(128)S(6)} %select_n.67), kind=kOutput, calls=%fused_computation.45 | convolution fusion | flops 538705920 | bytes 3670024 | tf_op jit(solution)/shard_map/dot_general | solution.py:138
  94.7 1.9 %fusion.43 = bf16[256,1024]{1,0:T(8,128)(2,1)S(1)} fusion(bf16[2,1,1024,1024]{3,2,1,0:T(8,128)(2,1)S(1)} %copy-done.4, bf16[256,1024]{1,0:T(8,128)(2,1)S(1)} %collective-permute-done.7, bf16[256,1024]{1,0:T(8,128)(2,1)} %collective-permute-done.6, f32[]{:T(128)S(6)} %select_n.75, f32[]{:T(128)S(6)} %select_n.67), kind=kOutput, calls=%fused_computation.46 | convolution fusion | flops 538705920 | bytes 3670024 | tf_op jit(solution)/shard_map/dot_general | solution.py:138
  98.3 2.4 %multiply_multiply_fusion = f32[1024,1024]{1,0:T(8,128)S(1)} fusion(f32[1024,1024]{1,0:T(8,128)S(1)} %copy-done.6, bf16[256,1024]{1,0:T(8,128)(2,1)S(1)} %fusion.43, bf16[256,1024]{1,0:T(8,128)(2,1)S(1)} %fusion.40, bf16[256,1024]{1,0:T(8,128)(2,1)S(1)} %fusion.37, bf16[256,1024]{1,0:T(8,128)(2,1)S(1)} %fusion.34, ...), kind=kOutput, calls=%fused_computation.1 | convolution fusion | flops 2159017984 | bytes 12591104 | tf_op jit(solution)/shard_map/dot_general | solution.py:141
  104.5 14.0 %all-to-all-start.1 = ((f32[32,1,2]{2,1,0:T(1,128)}), f32[32,1,2]{2,1,0:T(1,128)S(1)}, u32[]{:S(2)}, u32[]{:S(2)}) async-start(f32[32,1,2]{2,1,0:T(1,128)} %broadcast_in_dim.4), calls=%async_computation.1 | async-start | bytes 32768 | tf_op jit(solution)/shard_map/all_to_all | solution.py:28
  118.6 7.1 %all-to-all-done.1 = f32[32,1,2]{2,1,0:T(1,128)S(1)} async-done(((f32[32,1,2]{2,1,0:T(1,128)}), f32[32,1,2]{2,1,0:T(1,128)S(1)}, u32[]{:S(2)}, u32[]{:S(2)}) %all-to-all-start.1) | async-done | bytes 288 | tf_op jit(solution)/shard_map/all_to_all | solution.py:28
  129.7 6.4 %divide_bitcast_fusion = f32[1,1024,1024]{2,1,0:T(8,128)} fusion(f32[1024,1024]{1,0:T(8,128)} %copy-done.2, f32[]{:T(128)} %bitcast.18, f32[]{:T(128)} %bitcast.16, f32[]{:T(128)S(6)} %sqrt.6, f32[1024]{0:T(1024)S(1)} %get-tuple-element.24, f32[1024]{0:T(1024)S(1)} %get-tuple-element.23, f32[1,1024,1024]{2,1,0:T(8,128)} %state_ref.1), kind=kLoop, calls=%fused_computation.4 | loop fusion | flops 6291456 | bytes 12591116 | tf_op jit(solution)/shard_map/broadcast_in_dim | solution.py:151
  (36 shorter events, 12.7 us)
Async XLA Ops:
  10.4 15.9 %copy-start.3 = (f32[2,4,4]{2,1,0:T(4,128)S(1)}, f32[2,4,4]{2,1,0:T(4,128)}, u32[]{:S(2)}) copy-start(f32[2,4,4]{2,1,0:T(4,128)} %param.9) | copy-start | bytes 388
  13.0 2.0 %copy-start.1 = (f32[1024,1024]{1,0:T(8,128)}, f32[1024,1024]{1,0:T(8,128)S(1)}, u32[]{:S(2)}) copy-start(f32[1024,1024]{1,0:T(8,128)S(1)} %multiply_multiply_fusion.1) | copy-start | bytes 12582916
  15.1 14.5 %all-to-all-start = ((f32[32,1,1]{2,1,0:T(1,128)}), f32[32,1,1]{2,1,0:T(1,128)S(1)}, u32[]{:S(2)}, u32[]{:S(2)}) async-start(f32[32,1,1]{2,1,0:T(1,128)} %shard_map.77), calls=%async_computation | async-start | bytes 32768 | tf_op jit(solution)/shard_map/all_to_all | solution.py:28
  22.4 62.2 %collective-permute-start = (f32[256,1024]{1,0:T(8,128)S(1)}, f32[256,1024]{1,0:T(8,128)S(1)}, u32[]{:S(2)}, u32[]{:S(2)}) collective-permute-start(f32[256,1024]{1,0:T(8,128)S(1)} %slice.53), channel_id=1, source_target_pairs={{0,2},{1,3},{2,4},{3,5},{4,6},{5,7},{6,8},{7,9},{8,10},{9,11},{10,... | collective-permute-start | bytes 3145736 | tf_op jit(solution)/shard_map/ppermute | solution.py:19
  34.7 26.3 %collective-permute-start.2 = (bf16[256,1024]{1,0:T(8,128)(2,1)}, bf16[256,1024]{1,0:T(8,128)(2,1)}, u32[]{:S(2)}, u32[]{:S(2)}) collective-permute-start(bf16[256,1024]{1,0:T(8,128)(2,1)} %get-tuple-element.13), channel_id=1, source_target_pairs={{0,2},{1,3},{2,4},{3,5},{4,6},{5,7},{6,8},{7,9},{8,10},{9,11},{10,... | collective-permute-start | bytes 1572872 | tf_op jit(solution)/shard_map/ppermute | solution.py:19
  37.9 34.2 %collective-permute-start.4 = (bf16[256,1024]{1,0:T(8,128)(2,1)S(1)}, bf16[256,1024]{1,0:T(8,128)(2,1)}, u32[]{:S(2)}, u32[]{:S(2)}) collective-permute-start(bf16[256,1024]{1,0:T(8,128)(2,1)S(1)} %get-tuple-element.14), channel_id=1, source_target_pairs={{0,2},{1,3},{2,4},{3,5},{4,6},{5,7},{6,8},{7,9},{8,10},{9,11},{10,... | collective-permute-start | bytes 1572872 | tf_op jit(solution)/shard_map/ppermute | solution.py:19
  50.0 33.4 %collective-permute-start.6 = (bf16[256,1024]{1,0:T(8,128)(2,1)S(1)}, bf16[256,1024]{1,0:T(8,128)(2,1)}, u32[]{:S(2)}, u32[]{:S(2)}) collective-permute-start(bf16[256,1024]{1,0:T(8,128)(2,1)S(1)} %get-tuple-element.8), channel_id=1, source_target_pairs={{0,2},{1,3},{2,4},{3,5},{4,6},{5,7},{6,8},{7,9},{8,10},{9,11},{10,... | collective-permute-start | bytes 1572872 | tf_op jit(solution)/shard_map/ppermute | solution.py:19
  61.0 29.2 %collective-permute-start.3 = (bf16[256,1024]{1,0:T(8,128)(2,1)}, bf16[256,1024]{1,0:T(8,128)(2,1)}, u32[]{:S(2)}, u32[]{:S(2)}) collective-permute-start(bf16[256,1024]{1,0:T(8,128)(2,1)} %collective-permute-done.2), channel_id=1, source_target_pairs={{0,1},{1,2},{2,3},{3,4},{4,5},{5,6},{6,7},{7,8},{8,9},{9,10},{10,1... | collective-permute-start | bytes 1572872 | tf_op jit(solution)/shard_map/ppermute | solution.py:19
  64.4 28.4 %copy-start.4 = (bf16[2,1,1024,1024]{3,2,1,0:T(8,128)(2,1)S(1)}, bf16[2,1,1024,1024]{3,2,1,0:T(8,128)(2,1)}, u32[]{:S(2)}) copy-start(bf16[2,1,1024,1024]{3,2,1,0:T(8,128)(2,1)} %param.8) | copy-start | bytes 12582916
  72.1 20.7 %collective-permute-start.5 = (bf16[256,1024]{1,0:T(8,128)(2,1)}, bf16[256,1024]{1,0:T(8,128)(2,1)S(1)}, u32[]{:S(2)}, u32[]{:S(2)}) collective-permute-start(bf16[256,1024]{1,0:T(8,128)(2,1)} %collective-permute-done.4), channel_id=1, source_target_pairs={{0,1},{1,2},{2,3},{3,4},{4,5},{5,6},{6,7},{7,8},{8,9},{9,10},{10,1... | collective-permute-start | bytes 1572872 | tf_op jit(solution)/shard_map/ppermute | solution.py:19
  83.3 11.3 %collective-permute-start.7 = (bf16[256,1024]{1,0:T(8,128)(2,1)}, bf16[256,1024]{1,0:T(8,128)(2,1)S(1)}, u32[]{:S(2)}, u32[]{:S(2)}) collective-permute-start(bf16[256,1024]{1,0:T(8,128)(2,1)} %collective-permute-done.6), channel_id=1, source_target_pairs={{0,1},{1,2},{2,3},{3,4},{4,5},{5,6},{6,7},{7,8},{8,9},{9,10},{10,1... | collective-permute-start | bytes 1572872 | tf_op jit(solution)/shard_map/ppermute | solution.py:19
  84.7 11.9 %collective-permute-start.1 = (bf16[256,1024]{1,0:T(8,128)(2,1)S(1)}, bf16[256,1024]{1,0:T(8,128)(2,1)S(1)}, u32[]{:S(2)}, u32[]{:S(2)}) collective-permute-start(bf16[256,1024]{1,0:T(8,128)(2,1)S(1)} %divide_convert_fusion.1), channel_id=1, source_target_pairs={{0,1},{1,2},{2,3},{3,4},{4,5},{5,6},{6,7},{7,8},{8,9},{9,10},{10,1... | collective-permute-start | bytes 1572872 | tf_op jit(solution)/shard_map/ppermute | solution.py:19
  94.6 2.7 %copy-start.5 = (bf16[2,1,1024,1024]{3,2,1,0:T(8,128)(2,1)S(1)}, bf16[2,1,1024,1024]{3,2,1,0:T(8,128)(2,1)}, u32[]{:S(2)}) copy-start(bf16[2,1,1024,1024]{3,2,1,0:T(8,128)(2,1)} %param.7) | copy-start | bytes 12582916
  94.6 3.6 %copy-start.6 = (f32[1024,1024]{1,0:T(8,128)S(1)}, f32[1024,1024]{1,0:T(8,128)}, u32[]{:S(2)}) copy-start(f32[1024,1024]{1,0:T(8,128)} %multiply_bitcast_fusion.2) | copy-start | bytes 12582916
  98.3 2.4 %copy-start = (f32[1,1024,1024]{2,1,0:T(8,128)S(1)}, f32[1,1024,1024]{2,1,0:T(8,128)}, u32[]{:S(2)}) copy-start(f32[1,1024,1024]{2,1,0:T(8,128)} %state_ref.1) | copy-start | bytes 12582916
  100.7 2.0 %copy-start.2 = (f32[1024,1024]{1,0:T(8,128)}, f32[1024,1024]{1,0:T(8,128)S(1)}, u32[]{:S(2)}) copy-start(f32[1024,1024]{1,0:T(8,128)S(1)} %multiply_multiply_fusion) | copy-start | bytes 12582916
  104.5 21.2 %all-to-all-start.1 = ((f32[32,1,2]{2,1,0:T(1,128)}), f32[32,1,2]{2,1,0:T(1,128)S(1)}, u32[]{:S(2)}, u32[]{:S(2)}) async-start(f32[32,1,2]{2,1,0:T(1,128)} %broadcast_in_dim.4), calls=%async_computation.1 | async-start | bytes 32768 | tf_op jit(solution)/shard_map/all_to_all | solution.py:28

commit v12 on v11

--- a/solution.py
+++ b/solution.py
@@ -108,6 +108,7 @@
         for c in range(CHUNKS)
     ]
     head_two = row_major((head_far / scale).astype(jnp.bfloat16))
+    head_two, pieces[1] = lax.optimization_barrier((head_two, pieces[1]))
     rounded = jnp.concatenate(pieces, axis=0)
 
     weights = []

time: 137 us -> 145 us (1.058)
  starting transfers between devices: 43.5 us -> 53.5 us
    all_to_all x2, starting transfers between devices: 21.3 us -> 27.4 us  [exchange_sum(): return jnp.sum(lax.all_to_all(spread, AXES, 0, 0, tiled=True), axis=0)]
    ppermute x8, starting transfers between devices: 22.1 us -> 26 us  [shift_up(): return lax.ppermute(block, AXES, route)]
    ppermute x8, waiting for transfers between devices: 26 us -> 24.2 us  [shift_up(): return lax.ppermute(block, AXES, route)]
  transfers between devices with their start and end apart: 10 -> 10, of which waited for: 5 -> 4; matrix products, arithmetic and copies ran while one was open for 16% -> 14% of each run, Pallas kernels for 0% -> 0%
where the time goes in v12:
time: 145 us
  starting transfers between devices  53.5 us (37%)
  waiting for transfers between devices  34.7 us (24%)
  matrix products  17.9 us (12%)
  other arithmetic  16.2 us (11%)
  local copies, waits for them, and re-layouts  10.3 us (7%)
  between operations  7.6 us (5%)
  Pallas kernels  4.64 us (3%)
    all_to_all x2, starting transfers between devices, exchange_sum(): return jnp.sum(lax.all_to_all(spread, AXES, 0, 0, tiled=True), axis=0)  27.4 us
    ppermute x8, starting transfers between devices, shift_up(): return lax.ppermute(block, AXES, route)  26 us
    ppermute x8, waiting for transfers between devices, shift_up(): return lax.ppermute(block, AXES, route)  24.2 us
    all_to_all x2, waiting for transfers between devices, exchange_sum(): return jnp.sum(lax.all_to_all(spread, AXES, 0, 0, tiled=True), axis=0)  10.5 us
    dot_general x1, matrix products, per_device(): jnp.dot(left_env[1, 0], part_one, preferred_element_type=jnp.float32)  9.61 us
    broadcast_in_dim x1, other arithmetic, per_device(): return (next_vector[None], jnp.concatenate([alpha_value, beta_value]))  6.43 us
    dot_general x4, matrix products, per_device(): jnp.dot(source, right_env[0, 0], preferred_element_type=jnp.float32)  5.86 us
    unnamed x14, local copies, waits for them, and re-layouts  5.18 us
  transfers between devices with their start and end apart: 10, of which 4 were waited for; matrix products, arithmetic and copies ran while one was open for 14% of the time, Pallas kernels for 0%

profile of v12, /device:TPU:0, one launch (start us, length us, event | category | flops | bytes accessed | tf_op | source)
XLA Modules:
  0.0 144.8 jit_solution(14282016013149102184)
XLA Ops:
  5.7 4.6 %shard_map.77 = f32[32,1,1]{2,1,0:T(1,128)} custom-call(s32[1]{0:T(128)} %bitcast.1.index_ref, s32[8]{0:T(128)} %left_ref.1, s32[10]{0:T(128)} %right_ref.1, f32[1,1024,1024]{2,1,0:T(8,128)} %state_ref.1), custom_call_target="tpu_custom_call" | custom-call | tf_op jit(solution)/shard_map/pallas_call | solution.py:58
  10.4 2.6 %multiply_multiply_fusion.1 = f32[1024,1024]{1,0:T(8,128)S(1)} fusion(f32[1,1024,1024]{2,1,0:T(8,128)} %state_ref.1, f32[1024]{0:T(1024)S(1)} %get-tuple-element.28, f32[1024]{0:T(1024)S(1)} %get-tuple-element.27), kind=kLoop, calls=%fused_computation.2 | loop fusion | flops 2097152 | bytes 8396800 | tf_op jit(solution)/shard_map/mul | solution.py:97
  13.0 2.0 %copy-done.1 = f32[1024,1024]{1,0:T(8,128)} copy-done((f32[1024,1024]{1,0:T(8,128)}, f32[1024,1024]{1,0:T(8,128)S(1)}, u32[]{:S(2)}) %copy-start.1) | copy-done | bytes 4194328
  15.1 7.3 %all-to-all-start = ((f32[32,1,1]{2,1,0:T(1,128)}), f32[32,1,1]{2,1,0:T(1,128)S(1)}, u32[]{:S(2)}, u32[]{:S(2)}) async-start(f32[32,1,1]{2,1,0:T(1,128)} %shard_map.77), calls=%async_computation | async-start | bytes 32768 | tf_op jit(solution)/shard_map/all_to_all | solution.py:28
  22.4 3.7 %collective-permute-start = (f32[256,1024]{1,0:T(8,128)S(1)}, f32[256,1024]{1,0:T(8,128)S(1)}, u32[]{:S(2)}, u32[]{:S(2)}) collective-permute-start(f32[256,1024]{1,0:T(8,128)S(1)} %slice.53), channel_id=1, source_target_pairs={{0,2},{1,3},{2,4},{3,5},{4,6},{5,7},{6,8},{7,9},{8,10},{9,11},{10,... | collective-permute-start | bytes 3145736 | tf_op jit(solution)/shard_map/ppermute | solution.py:19
  26.2 3.4 %all-to-all-done = f32[32,1,1]{2,1,0:T(1,128)S(1)} async-done(((f32[32,1,1]{2,1,0:T(1,128)}), f32[32,1,1]{2,1,0:T(1,128)S(1)}, u32[]{:S(2)}, u32[]{:S(2)}) %all-to-all-start) | async-done | bytes 160 | tf_op jit(solution)/shard_map/all_to_all | solution.py:28
  30.9 3.8 %divide_convert_fusion = (bf16[256,1024]{1,0:T(8,128)(2,1)}, bf16[256,1024]{1,0:T(8,128)(2,1)S(1)}, bf16[256,1024]{1,0:T(8,128)(2,1)}, bf16[256,1024]{1,0:T(8,128)(2,1)S(1)}) fusion(f32[]{:T(128)S(6)} %sqrt.6, f32[1024,1024]{1,0:T(8,128)} %copy-done.1), kind=kLoop, calls=%fused_computation.54 | loop fusion | flops 2097152 | bytes 6291460 | tf_op jit(solution)/shard_map/convert_element_type | solution.py:107
  34.7 3.2 %collective-permute-start.4 = (bf16[256,1024]{1,0:T(8,128)(2,1)}, bf16[256,1024]{1,0:T(8,128)(2,1)}, u32[]{:S(2)}, u32[]{:S(2)}) collective-permute-start(bf16[256,1024]{1,0:T(8,128)(2,1)} %get-tuple-element.18), channel_id=1, source_target_pairs={{0,2},{1,3},{2,4},{3,5},{4,6},{5,7},{6,8},{7,9},{8,10},{9,11},{10,... | collective-permute-start | bytes 1572872 | tf_op jit(solution)/shard_map/ppermute | solution.py:19
  38.6 21.6 %collective-permute-done.4 = bf16[256,1024]{1,0:T(8,128)(2,1)} collective-permute-done((bf16[256,1024]{1,0:T(8,128)(2,1)}, bf16[256,1024]{1,0:T(8,128)(2,1)}, u32[]{:S(2)}, u32[]{:S(2)}) %collective-permute-start.4) | collective-permute-done | bytes 524320 | tf_op jit(solution)/shard_map/ppermute | solution.py:19
  60.1 2.1 %collective-permute-start.5 = (bf16[256,1024]{1,0:T(8,128)(2,1)}, bf16[256,1024]{1,0:T(8,128)(2,1)}, u32[]{:S(2)}, u32[]{:S(2)}) collective-permute-start(bf16[256,1024]{1,0:T(8,128)(2,1)} %collective-permute-done.4), channel_id=1, source_target_pairs={{0,1},{1,2},{2,3},{3,4},{4,5},{5,6},{6,7},{7,8},{8,9},{9,10},{10,1... | collective-permute-start | bytes 1572872 | tf_op jit(solution)/shard_map/ppermute | solution.py:19
  62.3 4.3 %collective-permute-start.2 = (bf16[256,1024]{1,0:T(8,128)(2,1)S(1)}, bf16[256,1024]{1,0:T(8,128)(2,1)S(1)}, u32[]{:S(2)}, u32[]{:S(2)}) collective-permute-start(bf16[256,1024]{1,0:T(8,128)(2,1)S(1)} %get-tuple-element.11), channel_id=1, source_target_pairs={{0,2},{1,3},{2,4},{3,5},{4,6},{5,7},{6,8},{7,9},{8,10},{9,11},{10,... | collective-permute-start | bytes 1572872 | tf_op jit(solution)/shard_map/ppermute | solution.py:19
  66.6 9.6 %multiply_bitcast_fusion.2 = f32[1024,1024]{1,0:T(8,128)} fusion(bf16[2,1,1024,1024]{3,2,1,0:T(8,128)(2,1)} %param.7, f32[]{:T(128)} %bitcast.8, bf16[256,1024]{1,0:T(8,128)(2,1)S(1)} %get-tuple-element.12, bf16[256,1024]{1,0:T(8,128)(2,1)} %get-tuple-element.18, bf16[256,1024]{1,0:T(8,128)(2,1)S(1)} %get-tuple-element.11, ...), kind=kOutput, calls=%fused_computation.7 | convolution fusion | flops 4305453056 | bytes 10486272 | tf_op jit(solution)/shard_map/dot_general | solution.py:128
  76.2 3.4 %collective-permute-start.6 = (bf16[256,1024]{1,0:T(8,128)(2,1)S(1)}, bf16[256,1024]{1,0:T(8,128)(2,1)S(1)}, u32[]{:S(2)}, u32[]{:S(2)}) collective-permute-start(bf16[256,1024]{1,0:T(8,128)(2,1)S(1)} %get-tuple-element.12), channel_id=1, source_target_pairs={{0,2},{1,3},{2,4},{3,5},{4,6},{5,7},{6,8},{7,9},{8,10},{9,11},{10,... | collective-permute-start | bytes 1572872 | tf_op jit(solution)/shard_map/ppermute | solution.py:19
  79.6 3.8 %collective-permute-start.1 = (bf16[256,1024]{1,0:T(8,128)(2,1)S(1)}, bf16[256,1024]{1,0:T(8,128)(2,1)}, u32[]{:S(2)}, u32[]{:S(2)}) collective-permute-start(bf16[256,1024]{1,0:T(8,128)(2,1)S(1)} %divide_convert_fusion.1), channel_id=1, source_target_pairs={{0,1},{1,2},{2,3},{3,4},{4,5},{5,6},{6,7},{7,8},{8,9},{9,10},{10,1... | collective-permute-start | bytes 1572872 | tf_op jit(solution)/shard_map/ppermute | solution.py:19
  84.7 1.9 %collective-permute-start.3 = (bf16[256,1024]{1,0:T(8,128)(2,1)S(1)}, bf16[256,1024]{1,0:T(8,128)(2,1)S(1)}, u32[]{:S(2)}, u32[]{:S(2)}) collective-permute-start(bf16[256,1024]{1,0:T(8,128)(2,1)S(1)} %collective-permute-done.2), channel_id=1, source_target_pairs={{0,1},{1,2},{2,3},{3,4},{4,5},{5,6},{6,7},{7,8},{8,9},{9,10},{10,1... | collective-permute-start | bytes 1572872 | tf_op jit(solution)/shard_map/ppermute | solution.py:19
  86.7 2.6 %fusion.40 = bf16[256,1024]{1,0:T(8,128)(2,1)S(1)} fusion(bf16[2,1,1024,1024]{3,2,1,0:T(8,128)(2,1)} %param.8, bf16[256,1024]{1,0:T(8,128)(2,1)} %collective-permute-done.5, bf16[256,1024]{1,0:T(8,128)(2,1)} %collective-permute-done.4, f32[]{:T(128)S(6)} %select_n.75, f32[]{:T(128)S(6)} %select_n.67), kind=kOutput, calls=%fused_computation.45 | convolution fusion | flops 538705920 | bytes 3670024 | tf_op jit(solution)/shard_map/dot_general | solution.py:139
  89.3 2.6 %collective-permute-done.6 = bf16[256,1024]{1,0:T(8,128)(2,1)S(1)} collective-permute-done((bf16[256,1024]{1,0:T(8,128)(2,1)S(1)}, bf16[256,1024]{1,0:T(8,128)(2,1)S(1)}, u32[]{:S(2)}, u32[]{:S(2)}) %collective-permute-start.6) | collective-permute-done | bytes 524320 | tf_op jit(solution)/shard_map/ppermute | solution.py:19
  91.9 3.6 %collective-permute-start.7 = (bf16[256,1024]{1,0:T(8,128)(2,1)S(1)}, bf16[256,1024]{1,0:T(8,128)(2,1)S(1)}, u32[]{:S(2)}, u32[]{:S(2)}) collective-permute-start(bf16[256,1024]{1,0:T(8,128)(2,1)S(1)} %collective-permute-done.6), channel_id=1, source_target_pairs={{0,1},{1,2},{2,3},{3,4},{4,5},{5,6},{6,7},{7,8},{8,9},{9,10},{10,1... | collective-permute-start | bytes 1572872 | tf_op jit(solution)/shard_map/ppermute | solution.py:19
  95.6 1.8 %fusion.34 = bf16[256,1024]{1,0:T(8,128)(2,1)S(1)} fusion(bf16[2,1,1024,1024]{3,2,1,0:T(8,128)(2,1)S(1)} %copy-done.4, bf16[256,1024]{1,0:T(8,128)(2,1)} %collective-permute-done.1, bf16[256,1024]{1,0:T(8,128)(2,1)S(1)} %divide_convert_fusion.1, f32[]{:T(128)S(6)} %select_n.75, f32[]{:T(128)S(6)} %select_n.67), kind=kOutput, calls=%fused_computation.43 | convolution fusion | flops 538705920 | bytes 3670024 | tf_op jit(solution)/shard_map/dot_general | solution.py:139
  99.6 1.3 copy-done.6
  100.8 2.4 %multiply_multiply_fusion = f32[1024,1024]{1,0:T(8,128)S(1)} fusion(f32[1024,1024]{1,0:T(8,128)S(1)} %copy-done.6, bf16[256,1024]{1,0:T(8,128)(2,1)S(1)} %fusion.43, bf16[256,1024]{1,0:T(8,128)(2,1)S(1)} %fusion.40, bf16[256,1024]{1,0:T(8,128)(2,1)S(1)} %fusion.37, bf16[256,1024]{1,0:T(8,128)(2,1)S(1)} %fusion.34, ...), kind=kOutput, calls=%fused_computation.1 | convolution fusion | flops 2159017984 | bytes 12591104 | tf_op jit(solution)/shard_map/dot_general | solution.py:142
  107.1 20.1 %all-to-all-start.1 = ((f32[32,1,2]{2,1,0:T(1,128)}), f32[32,1,2]{2,1,0:T(1,128)S(1)}, u32[]{:S(2)}, u32[]{:S(2)}) async-start(f32[32,1,2]{2,1,0:T(1,128)} %broadcast_in_dim.4), calls=%async_computation.1 | async-start | bytes 32768 | tf_op jit(solution)/shard_map/all_to_all | solution.py:28
  127.2 7.1 %all-to-all-done.1 = f32[32,1,2]{2,1,0:T(1,128)S(1)} async-done(((f32[32,1,2]{2,1,0:T(1,128)}), f32[32,1,2]{2,1,0:T(1,128)S(1)}, u32[]{:S(2)}, u32[]{:S(2)}) %all-to-all-start.1) | async-done | bytes 288 | tf_op jit(solution)/shard_map/all_to_all | solution.py:28
  138.3 6.4 %divide_bitcast_fusion = f32[1,1024,1024]{2,1,0:T(8,128)} fusion(f32[1024,1024]{1,0:T(8,128)} %copy-done.2, f32[]{:T(128)} %bitcast.18, f32[]{:T(128)} %bitcast.16, f32[]{:T(128)S(6)} %sqrt.6, f32[1024]{0:T(1024)S(1)} %get-tuple-element.28, f32[1024]{0:T(1024)S(1)} %get-tuple-element.27, f32[1,1024,1024]{2,1,0:T(8,128)} %state_ref.1), kind=kLoop, calls=%fused_computation.4 | loop fusion | flops 6291456 | bytes 12591116 | tf_op jit(solution)/shard_map/broadcast_in_dim | solution.py:152
  (36 shorter events, 11.9 us)
Async XLA Ops:
  13.0 2.0 %copy-start.1 = (f32[1024,1024]{1,0:T(8,128)}, f32[1024,1024]{1,0:T(8,128)S(1)}, u32[]{:S(2)}) copy-start(f32[1024,1024]{1,0:T(8,128)S(1)} %multiply_multiply_fusion.1) | copy-start | bytes 12582916
  15.0 22.9 %copy-start.3 = (f32[2,4,4]{2,1,0:T(4,128)S(1)}, f32[2,4,4]{2,1,0:T(4,128)}, u32[]{:S(2)}) copy-start(f32[2,4,4]{2,1,0:T(4,128)} %param.9) | copy-start | bytes 388
  15.1 14.5 %all-to-all-start = ((f32[32,1,1]{2,1,0:T(1,128)}), f32[32,1,1]{2,1,0:T(1,128)S(1)}, u32[]{:S(2)}, u32[]{:S(2)}) async-start(f32[32,1,1]{2,1,0:T(1,128)} %shard_map.77), calls=%async_computation | async-start | bytes 32768 | tf_op jit(solution)/shard_map/all_to_all | solution.py:28
  22.4 39.8 %collective-permute-start = (f32[256,1024]{1,0:T(8,128)S(1)}, f32[256,1024]{1,0:T(8,128)S(1)}, u32[]{:S(2)}, u32[]{:S(2)}) collective-permute-start(f32[256,1024]{1,0:T(8,128)S(1)} %slice.53), channel_id=1, source_target_pairs={{0,2},{1,3},{2,4},{3,5},{4,6},{5,7},{6,8},{7,9},{8,10},{9,11},{10,... | collective-permute-start | bytes 3145736 | tf_op jit(solution)/shard_map/ppermute | solution.py:19
  34.7 25.5 %collective-permute-start.4 = (bf16[256,1024]{1,0:T(8,128)(2,1)}, bf16[256,1024]{1,0:T(8,128)(2,1)}, u32[]{:S(2)}, u32[]{:S(2)}) collective-permute-start(bf16[256,1024]{1,0:T(8,128)(2,1)} %get-tuple-element.18), channel_id=1, source_target_pairs={{0,2},{1,3},{2,4},{3,5},{4,6},{5,7},{6,8},{7,9},{8,10},{9,11},{10,... | collective-permute-start | bytes 1572872 | tf_op jit(solution)/shard_map/ppermute | solution.py:19
  60.1 26.5 %collective-permute-start.5 = (bf16[256,1024]{1,0:T(8,128)(2,1)}, bf16[256,1024]{1,0:T(8,128)(2,1)}, u32[]{:S(2)}, u32[]{:S(2)}) collective-permute-start(bf16[256,1024]{1,0:T(8,128)(2,1)} %collective-permute-done.4), channel_id=1, source_target_pairs={{0,1},{1,2},{2,3},{3,4},{4,5},{5,6},{6,7},{7,8},{8,9},{9,10},{10,1... | collective-permute-start | bytes 1572872 | tf_op jit(solution)/shard_map/ppermute | solution.py:19
  62.3 22.4 %collective-permute-start.2 = (bf16[256,1024]{1,0:T(8,128)(2,1)S(1)}, bf16[256,1024]{1,0:T(8,128)(2,1)S(1)}, u32[]{:S(2)}, u32[]{:S(2)}) collective-permute-start(bf16[256,1024]{1,0:T(8,128)(2,1)S(1)} %get-tuple-element.11), channel_id=1, source_target_pairs={{0,2},{1,3},{2,4},{3,5},{4,6},{5,7},{6,8},{7,9},{8,10},{9,11},{10,... | collective-permute-start | bytes 1572872 | tf_op jit(solution)/shard_map/ppermute | solution.py:19
  76.2 15.7 %collective-permute-start.6 = (bf16[256,1024]{1,0:T(8,128)(2,1)S(1)}, bf16[256,1024]{1,0:T(8,128)(2,1)S(1)}, u32[]{:S(2)}, u32[]{:S(2)}) collective-permute-start(bf16[256,1024]{1,0:T(8,128)(2,1)S(1)} %get-tuple-element.12), channel_id=1, source_target_pairs={{0,2},{1,3},{2,4},{3,5},{4,6},{5,7},{6,8},{7,9},{8,10},{9,11},{10,... | collective-permute-start | bytes 1572872 | tf_op jit(solution)/shard_map/ppermute | solution.py:19
  79.6 16.0 %collective-permute-start.1 = (bf16[256,1024]{1,0:T(8,128)(2,1)S(1)}, bf16[256,1024]{1,0:T(8,128)(2,1)}, u32[]{:S(2)}, u32[]{:S(2)}) collective-permute-start(bf16[256,1024]{1,0:T(8,128)(2,1)S(1)} %divide_convert_fusion.1), channel_id=1, source_target_pairs={{0,1},{1,2},{2,3},{3,4},{4,5},{5,6},{6,7},{7,8},{8,9},{9,10},{10,1... | collective-permute-start | bytes 1572872 | tf_op jit(solution)/shard_map/ppermute | solution.py:19
  84.7 10.9 %copy-start.4 = (bf16[2,1,1024,1024]{3,2,1,0:T(8,128)(2,1)S(1)}, bf16[2,1,1024,1024]{3,2,1,0:T(8,128)(2,1)}, u32[]{:S(2)}) copy-start(bf16[2,1,1024,1024]{3,2,1,0:T(8,128)(2,1)} %param.8) | copy-start | bytes 12582916
  84.7 12.7 %collective-permute-start.3 = (bf16[256,1024]{1,0:T(8,128)(2,1)S(1)}, bf16[256,1024]{1,0:T(8,128)(2,1)S(1)}, u32[]{:S(2)}, u32[]{:S(2)}) collective-permute-start(bf16[256,1024]{1,0:T(8,128)(2,1)S(1)} %collective-permute-done.2), channel_id=1, source_target_pairs={{0,1},{1,2},{2,3},{3,4},{4,5},{5,6},{6,7},{7,8},{8,9},{9,10},{10,1... | collective-permute-start | bytes 1572872 | tf_op jit(solution)/shard_map/ppermute | solution.py:19
  91.9 6.2 %collective-permute-start.7 = (bf16[256,1024]{1,0:T(8,128)(2,1)S(1)}, bf16[256,1024]{1,0:T(8,128)(2,1)S(1)}, u32[]{:S(2)}, u32[]{:S(2)}) collective-permute-start(bf16[256,1024]{1,0:T(8,128)(2,1)S(1)} %collective-permute-done.6), channel_id=1, source_target_pairs={{0,1},{1,2},{2,3},{3,4},{4,5},{5,6},{6,7},{7,8},{8,9},{9,10},{10,1... | collective-permute-start | bytes 1572872 | tf_op jit(solution)/shard_map/ppermute | solution.py:19
  97.4 2.2 %copy-start.5 = (bf16[2,1,1024,1024]{3,2,1,0:T(8,128)(2,1)S(1)}, bf16[2,1,1024,1024]{3,2,1,0:T(8,128)(2,1)}, u32[]{:S(2)}) copy-start(bf16[2,1,1024,1024]{3,2,1,0:T(8,128)(2,1)} %param.7) | copy-start | bytes 12582916
  97.4 3.5 %copy-start.6 = (f32[1024,1024]{1,0:T(8,128)S(1)}, f32[1024,1024]{1,0:T(8,128)}, u32[]{:S(2)}) copy-start(f32[1024,1024]{1,0:T(8,128)} %multiply_bitcast_fusion.2) | copy-start | bytes 12582916
  100.8 2.4 %copy-start = (f32[1,1024,1024]{2,1,0:T(8,128)S(1)}, f32[1,1024,1024]{2,1,0:T(8,128)}, u32[]{:S(2)}) copy-start(f32[1,1024,1024]{2,1,0:T(8,128)} %state_ref.1) | copy-start | bytes 12582916
  103.3 2.0 %copy-start.2 = (f32[1024,1024]{1,0:T(8,128)}, f32[1024,1024]{1,0:T(8,128)S(1)}, u32[]{:S(2)}) copy-start(f32[1024,1024]{1,0:T(8,128)S(1)} %multiply_multiply_fusion) | copy-start | bytes 12582916
  107.1 27.3 %all-to-all-start.1 = ((f32[32,1,2]{2,1,0:T(1,128)}), f32[32,1,2]{2,1,0:T(1,128)S(1)}, u32[]{:S(2)}, u32[]{:S(2)}) async-start(f32[32,1,2]{2,1,0:T(1,128)} %broadcast_in_dim.4), calls=%async_computation.1 | async-start | bytes 32768 | tf_op jit(solution)/shard_map/all_to_all | solution.py:28

commit v13 on v10

--- a/solution.py
+++ b/solution.py
@@ -10,7 +10,7 @@
 
 BLOCK = 256
 AXES = ("left", "right")
-CHUNKS = 4
+CHUNKS = 8
 
 
 def shift_up(block, distance):

time: 129 us -> 138 us (1.070)
  starting transfers between devices: 46.4 us -> 67.7 us
  waiting for transfers between devices: 28.2 us -> 9.91 us
  other arithmetic: 17.1 us -> 19.2 us
  matrix products: 17.6 us -> 19.3 us
  local copies, waits for them, and re-layouts: 6.95 us -> 8.34 us
    ppermute x8 -> x16, starting transfers between devices: 19.2 us -> 52.8 us  [shift_up(): return lax.ppermute(block, AXES, route)]
    ppermute x8 -> x16, waiting for transfers between devices: 21.1 us -> 2.82 us  [shift_up(): return lax.ppermute(block, AXES, route)]
    all_to_all x2, starting transfers between devices: 27.2 us -> 15 us  [exchange_sum(): return jnp.sum(lax.all_to_all(spread, AXES, 0, 0, tiled=True), axis=0)]
    unnamed x0 -> x7, other arithmetic: none -> 4.82 us
    convert_element_type x1 -> x0, other arithmetic: 2.76 us -> none  [per_device(): (masked[c * rows:(c + 1) * rows] / scale).astype(jnp.bfloat16)]
    unnamed x16 -> x20, local copies, waits for them, and re-layouts: 3.11 us -> 4.67 us
    dot_general x4 -> x8, matrix products: 5.77 us -> 6.85 us  [per_device(): jnp.dot(source, right_env[0, 0], preferred_element_type=jnp.float32)]
  transfers between devices with their start and end apart: 10 -> 18, of which waited for: 4 -> 2; matrix products, arithmetic and copies ran while one was open for 17% -> 17% of each run, Pallas kernels for 0% -> 0%
where the time goes in v13:
time: 138 us; the launch traced here: 137 us
  starting transfers between devices  67.7 us (49%)
  matrix products  19.3 us (14%)
  other arithmetic  19.2 us (14%)
  waiting for transfers between devices  9.91 us (7%)
  local copies, waits for them, and re-layouts  8.34 us (6%)
  between operations  7.86 us (6%)
  Pallas kernels  4.77 us (3%)
    ppermute x16, starting transfers between devices, shift_up(): return lax.ppermute(block, AXES, route)  52.8 us
    all_to_all x2, starting transfers between devices, exchange_sum(): return jnp.sum(lax.all_to_all(spread, AXES, 0, 0, tiled=True), axis=0)  15 us
    dot_general x1, matrix products, per_device(): jnp.dot(left_env[1, 0], part_one, preferred_element_type=jnp.float32)  10 us
    all_to_all x2, waiting for transfers between devices, exchange_sum(): return jnp.sum(lax.all_to_all(spread, AXES, 0, 0, tiled=True), axis=0)  7.09 us
    dot_general x8, matrix products, per_device(): jnp.dot(source, right_env[0, 0], preferred_element_type=jnp.float32)  6.85 us
    broadcast_in_dim x1, other arithmetic, per_device(): return (next_vector[None], jnp.concatenate([alpha_value, beta_value]))  6.43 us
    unnamed x7, other arithmetic  4.82 us
    pallas_call x1, Pallas kernels, masked_square_sum(): pl.pallas_call(functools.partial(square_sum_kernel, pairs), grid_spec=plt...  4.77 us
  transfers between devices with their start and end apart: 18, of which 2 were waited for; matrix products, arithmetic and copies ran while one was open for 17% of the time, Pallas kernels for 0%

profile of v13, /device:TPU:0, one launch (start us, length us, event | category | flops | bytes accessed | tf_op | source)
XLA Modules:
  0.0 137.1 jit_solution(14541138393746371265)
XLA Ops:
  0.7 4.8 %shard_map.77 = f32[32,1,1]{2,1,0:T(1,128)} custom-call(s32[1]{0:T(128)} %bitcast.5.index_ref, s32[8]{0:T(128)} %left_ref.1, s32[10]{0:T(128)} %right_ref.1, f32[1,1024,1024]{2,1,0:T(8,128)} %state_ref.1), custom_call_target="tpu_custom_call" | custom-call | tf_op jit(solution)/shard_map/pallas_call | solution.py:58
  5.4 7.3 %all-to-all-start = ((f32[32,1,1]{2,1,0:T(1,128)}), f32[32,1,1]{2,1,0:T(1,128)S(1)}, u32[]{:S(2)}, u32[]{:S(2)}) async-start(f32[32,1,1]{2,1,0:T(1,128)} %shard_map.77), calls=%async_computation | async-start | bytes 32768 | tf_op jit(solution)/shard_map/all_to_all | solution.py:28
  16.6 4.6 %multiply_multiply_fusion.1 = f32[1024,1024]{1,0:T(8,128)} fusion(f32[1,1024,1024]{2,1,0:T(8,128)} %state_ref.1, f32[1024]{0:T(1024)S(1)} %get-tuple-element.32, f32[1024]{0:T(1024)S(1)} %get-tuple-element.31), kind=kLoop, calls=%fused_computation.2 | loop fusion | flops 2097152 | bytes 8396800 | tf_op jit(solution)/shard_map/mul | solution.py:97
  29.3 3.7 %collective-permute-start = (bf16[128,1024]{1,0:T(8,128)(2,1)S(1)}, bf16[128,1024]{1,0:T(8,128)(2,1)S(1)}, u32[]{:S(2)}, u32[]{:S(2)}) collective-permute-start(bf16[128,1024]{1,0:T(8,128)(2,1)S(1)} %get-tuple-element.21), channel_id=1, source_target_pairs={{0,2},{1,3},{2,4},{3,5},{4,6},{5,7},{6,8},{7,9},{8,10},{9,11},{10,... | collective-permute-start | bytes 786440 | tf_op jit(solution)/shard_map/ppermute | solution.py:19
  33.0 3.4 %collective-permute-start.12 = (bf16[128,1024]{1,0:T(8,128)(2,1)S(1)}, bf16[128,1024]{1,0:T(8,128)(2,1)S(1)}, u32[]{:S(2)}, u32[]{:S(2)}) collective-permute-start(bf16[128,1024]{1,0:T(8,128)(2,1)S(1)} %get-tuple-element.9), channel_id=1, source_target_pairs={{0,2},{1,3},{2,4},{3,5},{4,6},{5,7},{6,8},{7,9},{8,10},{9,11},{10,... | collective-permute-start | bytes 786440 | tf_op jit(solution)/shard_map/ppermute | solution.py:19
  36.4 3.4 %collective-permute-start.10 = (bf16[128,1024]{1,0:T(8,128)(2,1)S(1)}, bf16[128,1024]{1,0:T(8,128)(2,1)S(1)}, u32[]{:S(2)}, u32[]{:S(2)}) collective-permute-start(bf16[128,1024]{1,0:T(8,128)(2,1)S(1)} %get-tuple-element.11), channel_id=1, source_target_pairs={{0,2},{1,3},{2,4},{3,5},{4,6},{5,7},{6,8},{7,9},{8,10},{9,11},{10,... | collective-permute-start | bytes 786440 | tf_op jit(solution)/shard_map/ppermute | solution.py:19
  39.8 3.3 %collective-permute-start.8 = (bf16[128,1024]{1,0:T(8,128)(2,1)S(1)}, bf16[128,1024]{1,0:T(8,128)(2,1)S(1)}, u32[]{:S(2)}, u32[]{:S(2)}) collective-permute-start(bf16[128,1024]{1,0:T(8,128)(2,1)S(1)} %get-tuple-element.13), channel_id=1, source_target_pairs={{0,2},{1,3},{2,4},{3,5},{4,6},{5,7},{6,8},{7,9},{8,10},{9,11},{10,... | collective-permute-start | bytes 786440 | tf_op jit(solution)/shard_map/ppermute | solution.py:19
  43.2 3.4 %collective-permute-start.2 = (bf16[128,1024]{1,0:T(8,128)(2,1)S(1)}, bf16[128,1024]{1,0:T(8,128)(2,1)S(1)}, u32[]{:S(2)}, u32[]{:S(2)}) collective-permute-start(bf16[128,1024]{1,0:T(8,128)(2,1)S(1)} %get-tuple-element.19), channel_id=1, source_target_pairs={{0,2},{1,3},{2,4},{3,5},{4,6},{5,7},{6,8},{7,9},{8,10},{9,11},{10,... | collective-permute-start | bytes 786440 | tf_op jit(solution)/shard_map/ppermute | solution.py:19
  49.3 10.0 %multiply_bitcast_fusion.2 = f32[1024,1024]{1,0:T(8,128)} fusion(bf16[2,1,1024,1024]{3,2,1,0:T(8,128)(2,1)} %param.7, f32[]{:T(128)} %bitcast.8, bf16[1024,1024]{1,0:T(8,128)(2,1)} %copy-done.3, bf16[2,1,1024,1024]{3,2,1,0:T(8,128)(2,1)} %param.8), kind=kOutput, calls=%fused_computation.7 | convolution fusion | flops 4297064448 | bytes 10486272 | tf_op jit(solution)/shard_map/dot_general | solution.py:125
  59.3 2.8 %collective-permute-done.2 = bf16[128,1024]{1,0:T(8,128)(2,1)S(1)} collective-permute-done((bf16[128,1024]{1,0:T(8,128)(2,1)S(1)}, bf16[128,1024]{1,0:T(8,128)(2,1)S(1)}, u32[]{:S(2)}, u32[]{:S(2)}) %collective-permute-start.2) | collective-permute-done | bytes 262176 | tf_op jit(solution)/shard_map/ppermute | solution.py:19
  62.1 4.4 %collective-permute-start.4 = (bf16[128,1024]{1,0:T(8,128)(2,1)S(1)}, bf16[128,1024]{1,0:T(8,128)(2,1)S(1)}, u32[]{:S(2)}, u32[]{:S(2)}) collective-permute-start(bf16[128,1024]{1,0:T(8,128)(2,1)S(1)} %get-tuple-element.17), channel_id=1, source_target_pairs={{0,2},{1,3},{2,4},{3,5},{4,6},{5,7},{6,8},{7,9},{8,10},{9,11},{10,... | collective-permute-start | bytes 786440 | tf_op jit(solution)/shard_map/ppermute | solution.py:19
  67.8 2.1 %fusion.27 = bf16[1024,1024]{1,0:T(8,128)(2,1)S(1)} fusion(bf16[2,1,1024,1024]{3,2,1,0:T(8,128)(2,1)} %param.8, bf16[128,1024]{1,0:T(8,128)(2,1)S(1)} %collective-permute-done.1, bf16[128,1024]{1,0:T(8,128)(2,1)S(1)} %collective-permute-done, f32[]{:T(128)S(6)} %select_n.75, f32[]{:T(128)S(6)} %select_n.67), kind=kOutput, calls=%fused_computation.34 | convolution fusion | flops 269352960 | bytes 2883592 | tf_op jit(solution)/shard_map/dot_general | solution.py:136
  69.9 4.0 %collective-permute-start.6 = (bf16[128,1024]{1,0:T(8,128)(2,1)S(1)}, bf16[128,1024]{1,0:T(8,128)(2,1)S(1)}, u32[]{:S(2)}, u32[]{:S(2)}) collective-permute-start(bf16[128,1024]{1,0:T(8,128)(2,1)S(1)} %get-tuple-element.15), channel_id=1, source_target_pairs={{0,2},{1,3},{2,4},{3,5},{4,6},{5,7},{6,8},{7,9},{8,10},{9,11},{10,... | collective-permute-start | bytes 786440 | tf_op jit(solution)/shard_map/ppermute | solution.py:19
  73.9 3.4 %collective-permute-start.14 = (bf16[128,1024]{1,0:T(8,128)(2,1)S(1)}, bf16[128,1024]{1,0:T(8,128)(2,1)S(1)}, u32[]{:S(2)}, u32[]{:S(2)}) collective-permute-start(bf16[128,1024]{1,0:T(8,128)(2,1)S(1)} %get-tuple-element.4), channel_id=1, source_target_pairs={{0,2},{1,3},{2,4},{3,5},{4,6},{5,7},{6,8},{7,9},{8,10},{9,11},{10,... | collective-permute-start | bytes 786440 | tf_op jit(solution)/shard_map/ppermute | solution.py:19
  77.3 5.6 %collective-permute-start.5 = (bf16[128,1024]{1,0:T(8,128)(2,1)S(1)}, bf16[128,1024]{1,0:T(8,128)(2,1)S(1)}, u32[]{:S(2)}, u32[]{:S(2)}) collective-permute-start(bf16[128,1024]{1,0:T(8,128)(2,1)S(1)} %collective-permute-done.4), channel_id=1, source_target_pairs={{0,1},{1,2},{2,3},{3,4},{4,5},{5,6},{6,7},{7,8},{8,9},{9,10},{10,1... | collective-permute-start | bytes 786440 | tf_op jit(solution)/shard_map/ppermute | solution.py:19
  82.9 2.0 %fusion.33 = bf16[1024,1024]{1,0:T(8,128)(2,1)S(1)} fusion(bf16[1024,1024]{1,0:T(8,128)(2,1)S(1)} %fusion.27, bf16[2,1,1024,1024]{3,2,1,0:T(8,128)(2,1)} %param.8, bf16[128,1024]{1,0:T(8,128)(2,1)S(1)} %collective-permute-done.3, bf16[128,1024]{1,0:T(8,128)(2,1)S(1)} %collective-permute-done.2, f32[]{:T(128)S(6)} %select_n.75, f32[]{:T(128)S(6)} %select_n.67), kind=kOutput, calls=%fused_computation.36 | convolution fusion | flops 269352960 | bytes 2883592 | tf_op jit(solution)/shard_map/dot_general | solution.py:136
  85.0 2.5 %collective-permute-start.13 = (bf16[128,1024]{1,0:T(8,128)(2,1)S(1)}, bf16[128,1024]{1,0:T(8,128)(2,1)S(1)}, u32[]{:S(2)}, u32[]{:S(2)}) collective-permute-start(bf16[128,1024]{1,0:T(8,128)(2,1)S(1)} %collective-permute-done.12), channel_id=1, source_target_pairs={{0,1},{1,2},{2,3},{3,4},{4,5},{5,6},{6,7},{7,8},{8,9},{9,10},{10,1... | collective-permute-start | bytes 786440 | tf_op jit(solution)/shard_map/ppermute | solution.py:19
  89.4 2.1 %collective-permute-start.9 = (bf16[128,1024]{1,0:T(8,128)(2,1)S(1)}, bf16[128,1024]{1,0:T(8,128)(2,1)S(1)}, u32[]{:S(2)}, u32[]{:S(2)}) collective-permute-start(bf16[128,1024]{1,0:T(8,128)(2,1)S(1)} %collective-permute-done.8), channel_id=1, source_target_pairs={{0,1},{1,2},{2,3},{3,4},{4,5},{5,6},{6,7},{7,8},{8,9},{9,10},{10,1... | collective-permute-start | bytes 786440 | tf_op jit(solution)/shard_map/ppermute | solution.py:19
  91.5 1.9 %collective-permute-start.7 = (bf16[128,1024]{1,0:T(8,128)(2,1)S(1)}, bf16[128,1024]{1,0:T(8,128)(2,1)S(1)}, u32[]{:S(2)}, u32[]{:S(2)}) collective-permute-start(bf16[128,1024]{1,0:T(8,128)(2,1)S(1)} %collective-permute-done.6), channel_id=1, source_target_pairs={{0,1},{1,2},{2,3},{3,4},{4,5},{5,6},{6,7},{7,8},{8,9},{9,10},{10,1... | collective-permute-start | bytes 786440 | tf_op jit(solution)/shard_map/ppermute | solution.py:19
  93.5 7.2 %collective-permute-start.15 = (bf16[128,1024]{1,0:T(8,128)(2,1)S(1)}, bf16[128,1024]{1,0:T(8,128)(2,1)S(1)}, u32[]{:S(2)}, u32[]{:S(2)}) collective-permute-start(bf16[128,1024]{1,0:T(8,128)(2,1)S(1)} %collective-permute-done.14), channel_id=1, source_target_pairs={{0,1},{1,2},{2,3},{3,4},{4,5},{5,6},{6,7},{7,8},{8,9},{9,10},{10,1... | collective-permute-start | bytes 786440 | tf_op jit(solution)/shard_map/ppermute | solution.py:19
  105.7 2.4 %multiply_multiply_fusion = f32[1024,1024]{1,0:T(8,128)S(1)} fusion(f32[1024,1024]{1,0:T(8,128)S(1)} %copy-done.9, bf16[1024,1024]{1,0:T(8,128)(2,1)S(1)} %fusion.69, bf16[2,1,1024,1024]{3,2,1,0:T(8,128)(2,1)S(1)} %copy-done.8, f32[1024]{0:T(1024)S(1)} %get-tuple-element.32, f32[1024]{0:T(1024)S(1)} %get-tuple-element.31), kind=kOutput, calls=%fused_computation.1 | convolution fusion | flops 2150629376 | bytes 12591104 | tf_op jit(solution)/shard_map/dot_general | solution.py:139
  112.0 7.7 %all-to-all-start.1 = ((f32[32,1,2]{2,1,0:T(1,128)}), f32[32,1,2]{2,1,0:T(1,128)S(1)}, u32[]{:S(2)}, u32[]{:S(2)}) async-start(f32[32,1,2]{2,1,0:T(1,128)} %broadcast_in_dim.4), calls=%async_computation.1 | async-start | bytes 32768 | tf_op jit(solution)/shard_map/all_to_all | solution.py:28
  119.7 7.1 %all-to-all-done.1 = f32[32,1,2]{2,1,0:T(1,128)S(1)} async-done(((f32[32,1,2]{2,1,0:T(1,128)}), f32[32,1,2]{2,1,0:T(1,128)S(1)}, u32[]{:S(2)}, u32[]{:S(2)}) %all-to-all-start.1) | async-done | bytes 288 | tf_op jit(solution)/shard_map/all_to_all | solution.py:28
  130.7 6.4 %divide_bitcast_fusion = f32[1,1024,1024]{2,1,0:T(8,128)} fusion(f32[1024,1024]{1,0:T(8,128)} %copy-done.2, f32[]{:T(128)} %bitcast.18, f32[]{:T(128)} %bitcast.16, f32[]{:T(128)S(6)} %sqrt.6, f32[1024]{0:T(1024)S(1)} %get-tuple-element.32, f32[1024]{0:T(1024)S(1)} %get-tuple-element.31, f32[1,1024,1024]{2,1,0:T(8,128)} %state_ref.1), kind=kLoop, calls=%fused_computation.4 | loop fusion | flops 6291456 | bytes 12591116 | tf_op jit(solution)/shard_map/broadcast_in_dim | solution.py:149
  (67 shorter events, 23.8 us)
Async XLA Ops:
  0.6 14.1 %copy-start.6 = (s32[10]{0:T(128)S(1)}, s32[10]{0:T(128)}, u32[]{:S(2)}) copy-start(s32[10]{0:T(128)} %right_ref.1) | copy-start | bytes 124
  0.6 12.2 %copy-start.5 = (s32[8]{0:T(128)S(1)}, s32[8]{0:T(128)}, u32[]{:S(2)}) copy-start(s32[8]{0:T(128)} %left_ref.1) | copy-start | bytes 100
  0.7 15.9 %copy-start.4 = (f32[2,4,4]{2,1,0:T(4,128)S(1)}, f32[2,4,4]{2,1,0:T(4,128)}, u32[]{:S(2)}) copy-start(f32[2,4,4]{2,1,0:T(4,128)} %param.9) | copy-start | bytes 388
  5.4 17.7 %all-to-all-start = ((f32[32,1,1]{2,1,0:T(1,128)}), f32[32,1,1]{2,1,0:T(1,128)S(1)}, u32[]{:S(2)}, u32[]{:S(2)}) async-start(f32[32,1,1]{2,1,0:T(1,128)} %shard_map.77), calls=%async_computation | async-start | bytes 32768 | tf_op jit(solution)/shard_map/all_to_all | solution.py:28
  24.4 4.7 %copy-start.1 = (f32[1024,1024]{1,0:T(8,128)S(1)}, f32[1024,1024]{1,0:T(8,128)}, u32[]{:S(2)}) copy-start(f32[1024,1024]{1,0:T(8,128)} %multiply_multiply_fusion.1) | copy-start | bytes 12582916
  29.3 17.3 %collective-permute-start = (bf16[128,1024]{1,0:T(8,128)(2,1)S(1)}, bf16[128,1024]{1,0:T(8,128)(2,1)S(1)}, u32[]{:S(2)}, u32[]{:S(2)}) collective-permute-start(bf16[128,1024]{1,0:T(8,128)(2,1)S(1)} %get-tuple-element.21), channel_id=1, source_target_pairs={{0,2},{1,3},{2,4},{3,5},{4,6},{5,7},{6,8},{7,9},{8,10},{9,11},{10,... | collective-permute-start | bytes 786440 | tf_op jit(solution)/shard_map/ppermute | solution.py:19
  33.0 36.8 %collective-permute-start.12 = (bf16[128,1024]{1,0:T(8,128)(2,1)S(1)}, bf16[128,1024]{1,0:T(8,128)(2,1)S(1)}, u32[]{:S(2)}, u32[]{:S(2)}) collective-permute-start(bf16[128,1024]{1,0:T(8,128)(2,1)S(1)} %get-tuple-element.9), channel_id=1, source_target_pairs={{0,2},{1,3},{2,4},{3,5},{4,6},{5,7},{6,8},{7,9},{8,10},{9,11},{10,... | collective-permute-start | bytes 786440 | tf_op jit(solution)/shard_map/ppermute | solution.py:19
  36.4 48.5 %collective-permute-start.10 = (bf16[128,1024]{1,0:T(8,128)(2,1)S(1)}, bf16[128,1024]{1,0:T(8,128)(2,1)S(1)}, u32[]{:S(2)}, u32[]{:S(2)}) collective-permute-start(bf16[128,1024]{1,0:T(8,128)(2,1)S(1)} %get-tuple-element.11), channel_id=1, source_target_pairs={{0,2},{1,3},{2,4},{3,5},{4,6},{5,7},{6,8},{7,9},{8,10},{9,11},{10,... | collective-permute-start | bytes 786440 | tf_op jit(solution)/shard_map/ppermute | solution.py:19
  39.8 47.6 %collective-permute-start.8 = (bf16[128,1024]{1,0:T(8,128)(2,1)S(1)}, bf16[128,1024]{1,0:T(8,128)(2,1)S(1)}, u32[]{:S(2)}, u32[]{:S(2)}) collective-permute-start(bf16[128,1024]{1,0:T(8,128)(2,1)S(1)} %get-tuple-element.13), channel_id=1, source_target_pairs={{0,2},{1,3},{2,4},{3,5},{4,6},{5,7},{6,8},{7,9},{8,10},{9,11},{10,... | collective-permute-start | bytes 786440 | tf_op jit(solution)/shard_map/ppermute | solution.py:19
  43.2 18.9 %collective-permute-start.2 = (bf16[128,1024]{1,0:T(8,128)(2,1)S(1)}, bf16[128,1024]{1,0:T(8,128)(2,1)S(1)}, u32[]{:S(2)}, u32[]{:S(2)}) collective-permute-start(bf16[128,1024]{1,0:T(8,128)(2,1)S(1)} %get-tuple-element.19), channel_id=1, source_target_pairs={{0,2},{1,3},{2,4},{3,5},{4,6},{5,7},{6,8},{7,9},{8,10},{9,11},{10,... | collective-permute-start | bytes 786440 | tf_op jit(solution)/shard_map/ppermute | solution.py:19
  48.0 18.5 %collective-permute-start.1 = (bf16[128,1024]{1,0:T(8,128)(2,1)S(1)}, bf16[128,1024]{1,0:T(8,128)(2,1)S(1)}, u32[]{:S(2)}, u32[]{:S(2)}) collective-permute-start(bf16[128,1024]{1,0:T(8,128)(2,1)S(1)} %collective-permute-done), channel_id=1, source_target_pairs={{0,1},{1,2},{2,3},{3,4},{4,5},{5,6},{6,7},{7,8},{8,9},{9,10},{10,1... | collective-permute-start | bytes 786440 | tf_op jit(solution)/shard_map/ppermute | solution.py:19
  59.3 41.4 %copy-start.7 = (bf16[2,1,1024,1024]{3,2,1,0:T(8,128)(2,1)S(1)}, bf16[2,1,1024,1024]{3,2,1,0:T(8,128)(2,1)}, u32[]{:S(2)}) copy-start(bf16[2,1,1024,1024]{3,2,1,0:T(8,128)(2,1)} %param.8) | copy-start | bytes 12582916
  62.1 11.8 %collective-permute-start.4 = (bf16[128,1024]{1,0:T(8,128)(2,1)S(1)}, bf16[128,1024]{1,0:T(8,128)(2,1)S(1)}, u32[]{:S(2)}, u32[]{:S(2)}) collective-permute-start(bf16[128,1024]{1,0:T(8,128)(2,1)S(1)} %get-tuple-element.17), channel_id=1, source_target_pairs={{0,2},{1,3},{2,4},{3,5},{4,6},{5,7},{6,8},{7,9},{8,10},{9,11},{10,... | collective-permute-start | bytes 786440 | tf_op jit(solution)/shard_map/ppermute | solution.py:19
  66.5 10.8 %collective-permute-start.3 = (bf16[128,1024]{1,0:T(8,128)(2,1)S(1)}, bf16[128,1024]{1,0:T(8,128)(2,1)S(1)}, u32[]{:S(2)}, u32[]{:S(2)}) collective-permute-start(bf16[128,1024]{1,0:T(8,128)(2,1)S(1)} %collective-permute-done.2), channel_id=1, source_target_pairs={{0,1},{1,2},{2,3},{3,4},{4,5},{5,6},{6,7},{7,8},{8,9},{9,10},{10,1... | collective-permute-start | bytes 786440 | tf_op jit(solution)/shard_map/ppermute | solution.py:19
  69.9 19.5 %collective-permute-start.6 = (bf16[128,1024]{1,0:T(8,128)(2,1)S(1)}, bf16[128,1024]{1,0:T(8,128)(2,1)S(1)}, u32[]{:S(2)}, u32[]{:S(2)}) collective-permute-start(bf16[128,1024]{1,0:T(8,128)(2,1)S(1)} %get-tuple-element.15), channel_id=1, source_target_pairs={{0,2},{1,3},{2,4},{3,5},{4,6},{5,7},{6,8},{7,9},{8,10},{9,11},{10,... | collective-permute-start | bytes 786440 | tf_op jit(solution)/shard_map/ppermute | solution.py:19
  73.9 17.6 %collective-permute-start.14 = (bf16[128,1024]{1,0:T(8,128)(2,1)S(1)}, bf16[128,1024]{1,0:T(8,128)(2,1)S(1)}, u32[]{:S(2)}, u32[]{:S(2)}) collective-permute-start(bf16[128,1024]{1,0:T(8,128)(2,1)S(1)} %get-tuple-element.4), channel_id=1, source_target_pairs={{0,2},{1,3},{2,4},{3,5},{4,6},{5,7},{6,8},{7,9},{8,10},{9,11},{10,... | collective-permute-start | bytes 786440 | tf_op jit(solution)/shard_map/ppermute | solution.py:19
  77.3 16.1 %collective-permute-start.5 = (bf16[128,1024]{1,0:T(8,128)(2,1)S(1)}, bf16[128,1024]{1,0:T(8,128)(2,1)S(1)}, u32[]{:S(2)}, u32[]{:S(2)}) collective-permute-start(bf16[128,1024]{1,0:T(8,128)(2,1)S(1)} %collective-permute-done.4), channel_id=1, source_target_pairs={{0,1},{1,2},{2,3},{3,4},{4,5},{5,6},{6,7},{7,8},{8,9},{9,10},{10,1... | collective-permute-start | bytes 786440 | tf_op jit(solution)/shard_map/ppermute | solution.py:19
  85.0 17.7 %collective-permute-start.13 = (bf16[128,1024]{1,0:T(8,128)(2,1)S(1)}, bf16[128,1024]{1,0:T(8,128)(2,1)S(1)}, u32[]{:S(2)}, u32[]{:S(2)}) collective-permute-start(bf16[128,1024]{1,0:T(8,128)(2,1)S(1)} %collective-permute-done.12), channel_id=1, source_target_pairs={{0,1},{1,2},{2,3},{3,4},{4,5},{5,6},{6,7},{7,8},{8,9},{9,10},{10,1... | collective-permute-start | bytes 786440 | tf_op jit(solution)/shard_map/ppermute | solution.py:19
  87.4 14.7 %collective-permute-start.11 = (bf16[128,1024]{1,0:T(8,128)(2,1)S(1)}, bf16[128,1024]{1,0:T(8,128)(2,1)S(1)}, u32[]{:S(2)}, u32[]{:S(2)}) collective-permute-start(bf16[128,1024]{1,0:T(8,128)(2,1)S(1)} %collective-permute-done.10), channel_id=1, source_target_pairs={{0,1},{1,2},{2,3},{3,4},{4,5},{5,6},{6,7},{7,8},{8,9},{9,10},{10,1... | collective-permute-start | bytes 786440 | tf_op jit(solution)/shard_map/ppermute | solution.py:19
  89.4 12.3 %collective-permute-start.9 = (bf16[128,1024]{1,0:T(8,128)(2,1)S(1)}, bf16[128,1024]{1,0:T(8,128)(2,1)S(1)}, u32[]{:S(2)}, u32[]{:S(2)}) collective-permute-start(bf16[128,1024]{1,0:T(8,128)(2,1)S(1)} %collective-permute-done.8), channel_id=1, source_target_pairs={{0,1},{1,2},{2,3},{3,4},{4,5},{5,6},{6,7},{7,8},{8,9},{9,10},{10,1... | collective-permute-start | bytes 786440 | tf_op jit(solution)/shard_map/ppermute | solution.py:19
  91.5 9.7 %collective-permute-start.7 = (bf16[128,1024]{1,0:T(8,128)(2,1)S(1)}, bf16[128,1024]{1,0:T(8,128)(2,1)S(1)}, u32[]{:S(2)}, u32[]{:S(2)}) collective-permute-start(bf16[128,1024]{1,0:T(8,128)(2,1)S(1)} %collective-permute-done.6), channel_id=1, source_target_pairs={{0,1},{1,2},{2,3},{3,4},{4,5},{5,6},{6,7},{7,8},{8,9},{9,10},{10,1... | collective-permute-start | bytes 786440 | tf_op jit(solution)/shard_map/ppermute | solution.py:19
  93.5 9.6 %collective-permute-start.15 = (bf16[128,1024]{1,0:T(8,128)(2,1)S(1)}, bf16[128,1024]{1,0:T(8,128)(2,1)S(1)}, u32[]{:S(2)}, u32[]{:S(2)}) collective-permute-start(bf16[128,1024]{1,0:T(8,128)(2,1)S(1)} %collective-permute-done.14), channel_id=1, source_target_pairs={{0,1},{1,2},{2,3},{3,4},{4,5},{5,6},{6,7},{7,8},{8,9},{9,10},{10,1... | collective-permute-start | bytes 786440 | tf_op jit(solution)/shard_map/ppermute | solution.py:19
  102.6 3.1 %copy-start.8 = (bf16[2,1,1024,1024]{3,2,1,0:T(8,128)(2,1)S(1)}, bf16[2,1,1024,1024]{3,2,1,0:T(8,128)(2,1)}, u32[]{:S(2)}) copy-start(bf16[2,1,1024,1024]{3,2,1,0:T(8,128)(2,1)} %param.7) | copy-start | bytes 12582916
  112.0 14.8 %all-to-all-start.1 = ((f32[32,1,2]{2,1,0:T(1,128)}), f32[32,1,2]{2,1,0:T(1,128)S(1)}, u32[]{:S(2)}, u32[]{:S(2)}) async-start(f32[32,1,2]{2,1,0:T(1,128)} %broadcast_in_dim.4), calls=%async_computation.1 | async-start | bytes 32768 | tf_op jit(solution)/shard_map/all_to_all | solution.py:28
  (4 other events, 8.0 us)

commit v14 on v13

--- a/solution.py
+++ b/solution.py
@@ -10,7 +10,7 @@
 
 BLOCK = 256
 AXES = ("left", "right")
-CHUNKS = 8
+CHUNKS = 2
 
 
 def shift_up(block, distance):

time: 138 us -> 131 us (0.949)
  starting transfers between devices: 67.7 us -> 39.3 us
  waiting for transfers between devices: 9.91 us -> 38 us
  local copies, waits for them, and re-layouts: 8.34 us -> 6.03 us
  other arithmetic: 19.2 us -> 17.2 us
  matrix products: 19.3 us -> 17.4 us
    ppermute x16 -> x4, starting transfers between devices: 52.8 us -> 10.7 us  [shift_up(): return lax.ppermute(block, AXES, route)]
    ppermute x16 -> x4, waiting for transfers between devices: 2.82 us -> 30.9 us  [shift_up(): return lax.ppermute(block, AXES, route)]
    all_to_all x2, starting transfers between devices: 15 us -> 28.6 us  [exchange_sum(): return jnp.sum(lax.all_to_all(spread, AXES, 0, 0, tiled=True), axis=0)]
    unnamed x7 -> x0, other arithmetic: 4.82 us -> none
    convert_element_type x0 -> x1, other arithmetic: none -> 2.81 us  [per_device(): (masked[c * rows:(c + 1) * rows] / scale).astype(jnp.bfloat16)]
    unnamed x20 -> x16, local copies, waits for them, and re-layouts: 4.67 us -> 2.27 us
    dot_general x8 -> x2, matrix products: 6.85 us -> 5.66 us  [per_device(): jnp.dot(source, right_env[0, 0], preferred_element_type=jnp.float32)]
  transfers between devices with their start and end apart: 18 -> 6, of which waited for: 2 -> 3; matrix products, arithmetic and copies ran while one was open for 17% -> 15% of each run, Pallas kernels for 0% -> 0%
where the time goes in v14:
time: 131 us; the launch traced here: 130 us
  starting transfers between devices  39.3 us (30%)
  waiting for transfers between devices  38 us (29%)
  matrix products  17.4 us (13%)
  other arithmetic  17.2 us (13%)
  between operations  7.41 us (6%)
  local copies, waits for them, and re-layouts  6.03 us (5%)
  Pallas kernels  4.77 us (4%)
    ppermute x4, waiting for transfers between devices, shift_up(): return lax.ppermute(block, AXES, route)  30.9 us
    all_to_all x2, starting transfers between devices, exchange_sum(): return jnp.sum(lax.all_to_all(spread, AXES, 0, 0, tiled=True), axis=0)  28.6 us
    ppermute x4, starting transfers between devices, shift_up(): return lax.ppermute(block, AXES, route)  10.7 us
    dot_general x1, matrix products, per_device(): jnp.dot(left_env[1, 0], part_one, preferred_element_type=jnp.float32)  9.37 us
    all_to_all x2, waiting for transfers between devices, exchange_sum(): return jnp.sum(lax.all_to_all(spread, AXES, 0, 0, tiled=True), axis=0)  7.1 us
    broadcast_in_dim x1, other arithmetic, per_device(): return (next_vector[None], jnp.concatenate([alpha_value, beta_value]))  6.43 us
    dot_general x2, matrix products, per_device(): jnp.dot(source, right_env[0, 0], preferred_element_type=jnp.float32)  5.66 us
    pallas_call x1, Pallas kernels, masked_square_sum(): pl.pallas_call(functools.partial(square_sum_kernel, pairs), grid_spec=plt...  4.77 us
  transfers between devices with their start and end apart: 6, of which 3 were waited for; matrix products, arithmetic and copies ran while one was open for 15% of the time, Pallas kernels for 0%

profile of v14, /device:TPU:0, one launch (start us, length us, event | category | flops | bytes accessed | tf_op | source)
XLA Modules:
  0.0 130.1 jit_solution(12711508786774146975)
XLA Ops:
  0.7 4.8 %shard_map.77 = f32[32,1,1]{2,1,0:T(1,128)} custom-call(s32[1]{0:T(128)} %bitcast.5.index_ref, s32[8]{0:T(128)} %left_ref.1, s32[10]{0:T(128)} %right_ref.1, f32[1,1024,1024]{2,1,0:T(8,128)} %state_ref.1), custom_call_target="tpu_custom_call" | custom-call | tf_op jit(solution)/shard_map/pallas_call | solution.py:58
  5.4 7.3 %all-to-all-start = ((f32[32,1,1]{2,1,0:T(1,128)}), f32[32,1,1]{2,1,0:T(1,128)S(1)}, u32[]{:S(2)}, u32[]{:S(2)}) async-start(f32[32,1,1]{2,1,0:T(1,128)} %shard_map.77), calls=%async_computation | async-start | bytes 32768 | tf_op jit(solution)/shard_map/all_to_all | solution.py:28
  16.7 4.6 %multiply_multiply_fusion.1 = f32[1024,1024]{1,0:T(8,128)} fusion(f32[1,1024,1024]{2,1,0:T(8,128)} %state_ref.1, f32[1024]{0:T(1024)S(1)} %get-tuple-element.18, f32[1024]{0:T(1024)S(1)} %get-tuple-element.17), kind=kLoop, calls=%fused_computation.2 | loop fusion | flops 2097152 | bytes 8396800 | tf_op jit(solution)/shard_map/mul | solution.py:97
  21.3 0.7 constant_dynamic-slice_fusion.2
  21.9 0.6 reduce_sum.27
  23.2 2.8 %fusion.1 = (bf16[512,1024]{1,0:T(8,128)(2,1)S(1)}, bf16[512,1024]{1,0:T(8,128)(2,1)S(1)}) fusion(f32[1024,1024]{1,0:T(8,128)} %multiply_multiply_fusion.1, f32[]{:T(128)S(6)} %sqrt.6), kind=kLoop, calls=%fused_computation.11 | loop fusion | flops 2097152 | bytes 6291460 | tf_op jit(solution)/shard_map/convert_element_type | solution.py:106
  26.0 3.7 %collective-permute-start = (bf16[512,1024]{1,0:T(8,128)(2,1)S(1)}, bf16[512,1024]{1,0:T(8,128)(2,1)S(1)}, u32[]{:S(2)}, u32[]{:S(2)}) collective-permute-start(bf16[512,1024]{1,0:T(8,128)(2,1)S(1)} %get-tuple-element.8), channel_id=1, source_target_pairs={{0,2},{1,3},{2,4},{3,5},{4,6},{5,7},{6,8},{7,9},{8,10},{9,11},{10,... | collective-permute-start | bytes 3145736 | tf_op jit(solution)/shard_map/ppermute | solution.py:19
  29.7 9.4 %multiply_bitcast_fusion.2 = f32[1024,1024]{1,0:T(8,128)} fusion(bf16[2,1,1024,1024]{3,2,1,0:T(8,128)(2,1)} %param.7, f32[]{:T(128)} %bitcast.8, bf16[512,1024]{1,0:T(8,128)(2,1)S(1)} %get-tuple-element.4, bf16[512,1024]{1,0:T(8,128)(2,1)S(1)} %get-tuple-element.8, bf16[2,1,1024,1024]{3,2,1,0:T(8,128)(2,1)} %param.8), kind=kOutput, calls=%fused_computation.7 | convolution fusion | flops 4301258752 | bytes 10486272 | tf_op jit(solution)/shard_map/dot_general | solution.py:125
  39.1 4.3 %collective-permute-start.2 = (bf16[512,1024]{1,0:T(8,128)(2,1)S(1)}, bf16[512,1024]{1,0:T(8,128)(2,1)}, u32[]{:S(2)}, u32[]{:S(2)}) collective-permute-start(bf16[512,1024]{1,0:T(8,128)(2,1)S(1)} %get-tuple-element.4), channel_id=1, source_target_pairs={{0,2},{1,3},{2,4},{3,5},{4,6},{5,7},{6,8},{7,9},{8,10},{9,11},{10,... | collective-permute-start | bytes 3145736 | tf_op jit(solution)/shard_map/ppermute | solution.py:19
  43.4 9.8 %collective-permute-done = bf16[512,1024]{1,0:T(8,128)(2,1)S(1)} collective-permute-done((bf16[512,1024]{1,0:T(8,128)(2,1)S(1)}, bf16[512,1024]{1,0:T(8,128)(2,1)S(1)}, u32[]{:S(2)}, u32[]{:S(2)}) %collective-permute-start) | collective-permute-done | bytes 1048608 | tf_op jit(solution)/shard_map/ppermute | solution.py:19
  53.2 1.3 %collective-permute-start.1 = (bf16[512,1024]{1,0:T(8,128)(2,1)S(1)}, bf16[512,1024]{1,0:T(8,128)(2,1)S(1)}, u32[]{:S(2)}, u32[]{:S(2)}) collective-permute-start(bf16[512,1024]{1,0:T(8,128)(2,1)S(1)} %collective-permute-done), channel_id=1, source_target_pairs={{0,1},{1,2},{2,3},{3,4},{4,5},{5,6},{6,7},{7,8},{8,9},{9,10},{10,1... | collective-permute-start | bytes 3145736 | tf_op jit(solution)/shard_map/ppermute | solution.py:19
  54.5 21.1 %collective-permute-done.2 = bf16[512,1024]{1,0:T(8,128)(2,1)} collective-permute-done((bf16[512,1024]{1,0:T(8,128)(2,1)S(1)}, bf16[512,1024]{1,0:T(8,128)(2,1)}, u32[]{:S(2)}, u32[]{:S(2)}) %collective-permute-start.2) | collective-permute-done | bytes 1048608 | tf_op jit(solution)/shard_map/ppermute | solution.py:19
  75.7 1.3 %collective-permute-start.3 = (bf16[512,1024]{1,0:T(8,128)(2,1)}, bf16[512,1024]{1,0:T(8,128)(2,1)S(1)}, u32[]{:S(2)}, u32[]{:S(2)}) collective-permute-start(bf16[512,1024]{1,0:T(8,128)(2,1)} %collective-permute-done.2), channel_id=1, source_target_pairs={{0,1},{1,2},{2,3},{3,4},{4,5},{5,6},{6,7},{7,8},{8,9},{9,10},{10,1... | collective-permute-start | bytes 3145736 | tf_op jit(solution)/shard_map/ppermute | solution.py:19
  78.3 3.0 %fusion.22 = bf16[512,1024]{1,0:T(8,128)(2,1)S(1)} fusion(bf16[2,1,1024,1024]{3,2,1,0:T(8,128)(2,1)} %param.8, bf16[512,1024]{1,0:T(8,128)(2,1)S(1)} %collective-permute-done.1, bf16[512,1024]{1,0:T(8,128)(2,1)S(1)} %collective-permute-done, f32[]{:T(128)S(6)} %select_n.75, f32[]{:T(128)S(6)} %select_n.67), kind=kOutput, calls=%fused_computation.35 | convolution fusion | flops 1077411840 | bytes 5242888 | tf_op jit(solution)/shard_map/dot_general | solution.py:136
  81.4 2.7 %fusion.25 = bf16[512,1024]{1,0:T(8,128)(2,1)S(1)} fusion(bf16[2,1,1024,1024]{3,2,1,0:T(8,128)(2,1)S(1)} %copy-done.5, bf16[512,1024]{1,0:T(8,128)(2,1)S(1)} %collective-permute-done.3, bf16[512,1024]{1,0:T(8,128)(2,1)} %collective-permute-done.2, f32[]{:T(128)S(6)} %select_n.75, f32[]{:T(128)S(6)} %select_n.67), kind=kOutput, calls=%fused_computation.36 | convolution fusion | flops 1077411840 | bytes 5242888 | tf_op jit(solution)/shard_map/dot_general | solution.py:136
  84.0 1.1 copy-done.7
  85.1 2.4 %multiply_multiply_fusion = f32[1024,1024]{1,0:T(8,128)S(1)} fusion(f32[1024,1024]{1,0:T(8,128)S(1)} %copy-done.7, bf16[512,1024]{1,0:T(8,128)(2,1)S(1)} %fusion.25, bf16[512,1024]{1,0:T(8,128)(2,1)S(1)} %fusion.22, bf16[2,1,1024,1024]{3,2,1,0:T(8,128)(2,1)S(1)} %copy-done.6, f32[1024]{0:T(1024)S(1)} %get-tuple-element.18, f32[1024]{0:T(1024)S(1)} %get-tuple-element.17), kind=kOutput, calls=%fused_computation.1 | convolution fusion | flops 2154823680 | bytes 12591104 | tf_op jit(solution)/shard_map/dot_general | solution.py:139
  87.5 0.8 multiply_bitcast_fusion.1
  88.3 1.2 copy-done.1
  89.5 1.2 maximum_reduce_fusion
  91.3 21.3 %all-to-all-start.1 = ((f32[32,1,2]{2,1,0:T(1,128)}), f32[32,1,2]{2,1,0:T(1,128)S(1)}, u32[]{:S(2)}, u32[]{:S(2)}) async-start(f32[32,1,2]{2,1,0:T(1,128)} %broadcast_in_dim.4), calls=%async_computation.1 | async-start | bytes 32768 | tf_op jit(solution)/shard_map/all_to_all | solution.py:28
  112.7 7.1 %all-to-all-done.1 = f32[32,1,2]{2,1,0:T(1,128)S(1)} async-done(((f32[32,1,2]{2,1,0:T(1,128)}), f32[32,1,2]{2,1,0:T(1,128)S(1)}, u32[]{:S(2)}, u32[]{:S(2)}) %all-to-all-start.1) | async-done | bytes 288 | tf_op jit(solution)/shard_map/all_to_all | solution.py:28
  119.8 0.6 fusion.46
  123.7 6.4 %divide_bitcast_fusion = f32[1,1024,1024]{2,1,0:T(8,128)} fusion(f32[1024,1024]{1,0:T(8,128)} %copy-done.1, f32[]{:T(128)} %bitcast.18, f32[]{:T(128)} %bitcast.16, f32[]{:T(128)S(6)} %sqrt.6, f32[1024]{0:T(1024)S(1)} %get-tuple-element.18, f32[1024]{0:T(1024)S(1)} %get-tuple-element.17, f32[1,1024,1024]{2,1,0:T(8,128)} %state_ref.1), kind=kLoop, calls=%fused_computation.4 | loop fusion | flops 6291456 | bytes 12591116 | tf_op jit(solution)/shard_map/broadcast_in_dim | solution.py:149
  (26 shorter events, 3.1 us)
Async XLA Ops:
  0.6 14.1 %copy-start.4 = (s32[10]{0:T(128)S(1)}, s32[10]{0:T(128)}, u32[]{:S(2)}) copy-start(s32[10]{0:T(128)} %right_ref.1) | copy-start | bytes 124
  0.6 12.2 %copy-start.3 = (s32[8]{0:T(128)S(1)}, s32[8]{0:T(128)}, u32[]{:S(2)}) copy-start(s32[8]{0:T(128)} %left_ref.1) | copy-start | bytes 100
  0.7 16.0 %copy-start.2 = (f32[2,4,4]{2,1,0:T(4,128)S(1)}, f32[2,4,4]{2,1,0:T(4,128)}, u32[]{:S(2)}) copy-start(f32[2,4,4]{2,1,0:T(4,128)} %param.9) | copy-start | bytes 388
  5.4 16.5 %all-to-all-start = ((f32[32,1,1]{2,1,0:T(1,128)}), f32[32,1,1]{2,1,0:T(1,128)S(1)}, u32[]{:S(2)}, u32[]{:S(2)}) async-start(f32[32,1,1]{2,1,0:T(1,128)} %shard_map.77), calls=%async_computation | async-start | bytes 32768 | tf_op jit(solution)/shard_map/all_to_all | solution.py:28
  26.0 27.2 %collective-permute-start = (bf16[512,1024]{1,0:T(8,128)(2,1)S(1)}, bf16[512,1024]{1,0:T(8,128)(2,1)S(1)}, u32[]{:S(2)}, u32[]{:S(2)}) collective-permute-start(bf16[512,1024]{1,0:T(8,128)(2,1)S(1)} %get-tuple-element.8), channel_id=1, source_target_pairs={{0,2},{1,3},{2,4},{3,5},{4,6},{5,7},{6,8},{7,9},{8,10},{9,11},{10,... | collective-permute-start | bytes 3145736 | tf_op jit(solution)/shard_map/ppermute | solution.py:19
  39.1 36.5 %collective-permute-start.2 = (bf16[512,1024]{1,0:T(8,128)(2,1)S(1)}, bf16[512,1024]{1,0:T(8,128)(2,1)}, u32[]{:S(2)}, u32[]{:S(2)}) collective-permute-start(bf16[512,1024]{1,0:T(8,128)(2,1)S(1)} %get-tuple-element.4), channel_id=1, source_target_pairs={{0,2},{1,3},{2,4},{3,5},{4,6},{5,7},{6,8},{7,9},{8,10},{9,11},{10,... | collective-permute-start | bytes 3145736 | tf_op jit(solution)/shard_map/ppermute | solution.py:19
  53.2 25.1 %collective-permute-start.1 = (bf16[512,1024]{1,0:T(8,128)(2,1)S(1)}, bf16[512,1024]{1,0:T(8,128)(2,1)S(1)}, u32[]{:S(2)}, u32[]{:S(2)}) collective-permute-start(bf16[512,1024]{1,0:T(8,128)(2,1)S(1)} %collective-permute-done), channel_id=1, source_target_pairs={{0,1},{1,2},{2,3},{3,4},{4,5},{5,6},{6,7},{7,8},{8,9},{9,10},{10,1... | collective-permute-start | bytes 3145736 | tf_op jit(solution)/shard_map/ppermute | solution.py:19
  75.7 5.7 %collective-permute-start.3 = (bf16[512,1024]{1,0:T(8,128)(2,1)}, bf16[512,1024]{1,0:T(8,128)(2,1)S(1)}, u32[]{:S(2)}, u32[]{:S(2)}) collective-permute-start(bf16[512,1024]{1,0:T(8,128)(2,1)} %collective-permute-done.2), channel_id=1, source_target_pairs={{0,1},{1,2},{2,3},{3,4},{4,5},{5,6},{6,7},{7,8},{8,9},{9,10},{10,1... | collective-permute-start | bytes 3145736 | tf_op jit(solution)/shard_map/ppermute | solution.py:19
  78.3 3.1 %copy-start.5 = (bf16[2,1,1024,1024]{3,2,1,0:T(8,128)(2,1)S(1)}, bf16[2,1,1024,1024]{3,2,1,0:T(8,128)(2,1)}, u32[]{:S(2)}) copy-start(bf16[2,1,1024,1024]{3,2,1,0:T(8,128)(2,1)} %param.8) | copy-start | bytes 12582916
  81.3 2.7 %copy-start.6 = (bf16[2,1,1024,1024]{3,2,1,0:T(8,128)(2,1)S(1)}, bf16[2,1,1024,1024]{3,2,1,0:T(8,128)(2,1)}, u32[]{:S(2)}) copy-start(bf16[2,1,1024,1024]{3,2,1,0:T(8,128)(2,1)} %param.7) | copy-start | bytes 12582916
  81.3 3.8 %copy-start.7 = (f32[1024,1024]{1,0:T(8,128)S(1)}, f32[1024,1024]{1,0:T(8,128)}, u32[]{:S(2)}) copy-start(f32[1024,1024]{1,0:T(8,128)} %multiply_bitcast_fusion.2) | copy-start | bytes 12582916
  85.1 2.4 %copy-start = (f32[1,1024,1024]{2,1,0:T(8,128)S(1)}, f32[1,1024,1024]{2,1,0:T(8,128)}, u32[]{:S(2)}) copy-start(f32[1,1024,1024]{2,1,0:T(8,128)} %state_ref.1) | copy-start | bytes 12582916
  87.5 2.0 %copy-start.1 = (f32[1024,1024]{1,0:T(8,128)}, f32[1024,1024]{1,0:T(8,128)S(1)}, u32[]{:S(2)}) copy-start(f32[1024,1024]{1,0:T(8,128)S(1)} %multiply_multiply_fusion) | copy-start | bytes 12582916
  91.3 28.5 %all-to-all-start.1 = ((f32[32,1,2]{2,1,0:T(1,128)}), f32[32,1,2]{2,1,0:T(1,128)S(1)}, u32[]{:S(2)}, u32[]{:S(2)}) async-start(f32[32,1,2]{2,1,0:T(1,128)} %broadcast_in_dim.4), calls=%async_computation.1 | async-start | bytes 32768 | tf_op jit(solution)/shard_map/all_to_all | solution.py:28

commit v15 on v10

--- a/solution.py
+++ b/solution.py
@@ -124,10 +124,11 @@
     diag_weight = table_entry(site_ops[1], own_pair, own_pair)
     image_one = diag_weight * jnp.dot(left_env[1, 0], part_one, preferred_element_type=jnp.float32)
 
-    image_one, pieces[-1] = lax.optimization_barrier((image_one, pieces[-1]))
     parts = []
     for c in range(CHUNKS):
         far_two = shift_up(pieces[c], 2)
+        if c == 0:
+            image_one, far_two = lax.optimization_barrier((image_one, far_two))
         far_three = shift_up(far_two, 1)
         source = (
             weights[0] * far_two.astype(jnp.float32) + weights[1] * far_three.astype(jnp.float32)

time: 129 us -> 137 us (1.062)
  starting transfers between devices: 46.4 us -> 54.4 us
  waiting for transfers between devices: 28.2 us -> 22 us
  matrix products: 17.6 us -> 21.7 us
  other arithmetic: 17.1 us -> 21.2 us
  local copies, waits for them, and re-layouts: 6.95 us -> 5.17 us
    ppermute x8, waiting for transfers between devices: 21.1 us -> 14.9 us  [shift_up(): return lax.ppermute(block, AXES, route)]
    ppermute x8, starting transfers between devices: 19.2 us -> 24.9 us  [shift_up(): return lax.ppermute(block, AXES, route)]
    another operation x1 -> x2, other arithmetic: 0.83 us -> 4.89 us  [per_device(): jnp.stack([vector * image, image * image])]
    all_to_all x2, starting transfers between devices: 27.2 us -> 29.5 us  [exchange_sum(): return jnp.sum(lax.all_to_all(spread, AXES, 0, 0, tiled=True), axis=0)]
    dot_general x4, matrix products: 5.77 us -> 7.99 us  [per_device(): jnp.dot(source, right_env[0, 0], preferred_element_type=jnp.float32)]
    dot_general x1, matrix products: 2.43 us -> 4.31 us  [per_device(): jnp.dot(left_env[0, 0], part_zero, preferred_element_type=jnp.float32)]
    unnamed x16 -> x14, local copies, waits for them, and re-layouts: 3.11 us -> 1.59 us
  transfers between devices with their start and end apart: 10 -> 10, of which waited for: 4 -> 3; matrix products, arithmetic and copies ran while one was open for 17% -> 16% of each run, Pallas kernels for 0% -> 0%
where the time goes in v15:
time: 137 us
  starting transfers between devices  54.4 us (40%)
  waiting for transfers between devices  22 us (16%)
  matrix products  21.7 us (16%)
  other arithmetic  21.2 us (15%)
  between operations  7.44 us (5%)
  local copies, waits for them, and re-layouts  5.17 us (4%)
  Pallas kernels  4.76 us (3%)
    all_to_all x2, starting transfers between devices, exchange_sum(): return jnp.sum(lax.all_to_all(spread, AXES, 0, 0, tiled=True), axis=0)  29.5 us
    ppermute x8, starting transfers between devices, shift_up(): return lax.ppermute(block, AXES, route)  24.9 us
    ppermute x8, waiting for transfers between devices, shift_up(): return lax.ppermute(block, AXES, route)  14.9 us
    dot_general x1, matrix products, per_device(): jnp.dot(left_env[1, 0], part_one, preferred_element_type=jnp.float32)  9.36 us
    dot_general x4, matrix products, per_device(): jnp.dot(source, right_env[0, 0], preferred_element_type=jnp.float32)  7.99 us
    all_to_all x2, waiting for transfers between devices, exchange_sum(): return jnp.sum(lax.all_to_all(spread, AXES, 0, 0, tiled=True), axis=0)  7.1 us
    broadcast_in_dim x1, other arithmetic, per_device(): return (next_vector[None], jnp.concatenate([alpha_value, beta_value]))  6.43 us
    another operation x2, other arithmetic, per_device(): jnp.stack([vector * image, image * image])  4.89 us
  transfers between devices with their start and end apart: 10, of which 3 were waited for; matrix products, arithmetic and copies ran while one was open for 16% of the time, Pallas kernels for 0%

profile of v15, /device:TPU:0, one launch (start us, length us, event | category | flops | bytes accessed | tf_op | source)
XLA Modules:
  0.0 136.6 jit_solution(6437633977942331309)
XLA Ops:
  0.7 4.8 %shard_map.77 = f32[32,1,1]{2,1,0:T(1,128)} custom-call(s32[1]{0:T(128)} %bitcast.6.index_ref, s32[8]{0:T(128)} %left_ref.1, s32[10]{0:T(128)} %right_ref.1, f32[1,1024,1024]{2,1,0:T(8,128)} %state_ref.1), custom_call_target="tpu_custom_call" | custom-call | tf_op jit(solution)/shard_map/pallas_call | solution.py:58
  5.4 7.3 %all-to-all-start = ((f32[32,1,1]{2,1,0:T(1,128)}), f32[32,1,1]{2,1,0:T(1,128)S(1)}, u32[]{:S(2)}, u32[]{:S(2)}) async-start(f32[32,1,1]{2,1,0:T(1,128)} %shard_map.77), calls=%async_computation | async-start | bytes 32768 | tf_op jit(solution)/shard_map/all_to_all | solution.py:28
  16.2 4.6 %multiply_multiply_fusion.1 = f32[1024,1024]{1,0:T(8,128)} fusion(f32[1,1024,1024]{2,1,0:T(8,128)} %state_ref.1, f32[1024]{0:T(1024)S(1)} %get-tuple-element.19, f32[1024]{0:T(1024)S(1)} %get-tuple-element.18), kind=kLoop, calls=%fused_computation.2 | loop fusion | flops 2097152 | bytes 8396800 | tf_op jit(solution)/shard_map/mul | solution.py:97
  22.2 2.8 %fusion.50 = (bf16[256,1024]{1,0:T(8,128)(2,1)S(1)}, bf16[256,1024]{1,0:T(8,128)(2,1)S(1)}, bf16[256,1024]{1,0:T(8,128)(2,1)S(1)}, bf16[256,1024]{1,0:T(8,128)(2,1)S(1)}) fusion(f32[1024,1024]{1,0:T(8,128)} %multiply_multiply_fusion.1, f32[]{:T(128)S(6)} %sqrt.6), kind=kLoop, calls=%fused_computation.55 | loop fusion | flops 2097152 | bytes 6291460 | tf_op jit(solution)/shard_map/convert_element_type | solution.py:106
  25.0 3.7 %collective-permute-start.6 = (bf16[256,1024]{1,0:T(8,128)(2,1)S(1)}, bf16[256,1024]{1,0:T(8,128)(2,1)S(1)}, u32[]{:S(2)}, u32[]{:S(2)}) collective-permute-start(bf16[256,1024]{1,0:T(8,128)(2,1)S(1)} %get-tuple-element.9), channel_id=1, source_target_pairs={{0,2},{1,3},{2,4},{3,5},{4,6},{5,7},{6,8},{7,9},{8,10},{9,11},{10,... | collective-permute-start | bytes 1572872 | tf_op jit(solution)/shard_map/ppermute | solution.py:19
  28.7 3.4 %collective-permute-start.4 = (bf16[256,1024]{1,0:T(8,128)(2,1)S(1)}, bf16[256,1024]{1,0:T(8,128)(2,1)S(1)}, u32[]{:S(2)}, u32[]{:S(2)}) collective-permute-start(bf16[256,1024]{1,0:T(8,128)(2,1)S(1)} %get-tuple-element.10), channel_id=1, source_target_pairs={{0,2},{1,3},{2,4},{3,5},{4,6},{5,7},{6,8},{7,9},{8,10},{9,11},{10,... | collective-permute-start | bytes 1572872 | tf_op jit(solution)/shard_map/ppermute | solution.py:19
  34.1 4.2 %collective-permute-start = (bf16[256,1024]{1,0:T(8,128)(2,1)S(1)}, bf16[256,1024]{1,0:T(8,128)(2,1)}, u32[]{:S(2)}, u32[]{:S(2)}) collective-permute-start(bf16[256,1024]{1,0:T(8,128)(2,1)S(1)} %get-tuple-element.8), channel_id=1, source_target_pairs={{0,2},{1,3},{2,4},{3,5},{4,6},{5,7},{6,8},{7,9},{8,10},{9,11},{10,... | collective-permute-start | bytes 1572872 | tf_op jit(solution)/shard_map/ppermute | solution.py:19
  38.2 3.3 %collective-permute-start.2 = (bf16[256,1024]{1,0:T(8,128)(2,1)S(1)}, bf16[256,1024]{1,0:T(8,128)(2,1)}, u32[]{:S(2)}, u32[]{:S(2)}) collective-permute-start(bf16[256,1024]{1,0:T(8,128)(2,1)S(1)} %get-tuple-element.11), channel_id=1, source_target_pairs={{0,2},{1,3},{2,4},{3,5},{4,6},{5,7},{6,8},{7,9},{8,10},{9,11},{10,... | collective-permute-start | bytes 1572872 | tf_op jit(solution)/shard_map/ppermute | solution.py:19
  41.6 2.1 %collective-permute-start.7 = (bf16[256,1024]{1,0:T(8,128)(2,1)S(1)}, bf16[256,1024]{1,0:T(8,128)(2,1)}, u32[]{:S(2)}, u32[]{:S(2)}) collective-permute-start(bf16[256,1024]{1,0:T(8,128)(2,1)S(1)} %collective-permute-done.6), channel_id=1, source_target_pairs={{0,1},{1,2},{2,3},{3,4},{4,5},{5,6},{6,7},{7,8},{8,9},{9,10},{10,1... | collective-permute-start | bytes 1572872 | tf_op jit(solution)/shard_map/ppermute | solution.py:19
  43.7 8.5 %collective-permute-done.4 = bf16[256,1024]{1,0:T(8,128)(2,1)S(1)} collective-permute-done((bf16[256,1024]{1,0:T(8,128)(2,1)S(1)}, bf16[256,1024]{1,0:T(8,128)(2,1)S(1)}, u32[]{:S(2)}, u32[]{:S(2)}) %collective-permute-start.4) | collective-permute-done | bytes 524320 | tf_op jit(solution)/shard_map/ppermute | solution.py:19
  52.2 2.1 %collective-permute-start.5 = (bf16[256,1024]{1,0:T(8,128)(2,1)S(1)}, bf16[256,1024]{1,0:T(8,128)(2,1)}, u32[]{:S(2)}, u32[]{:S(2)}) collective-permute-start(bf16[256,1024]{1,0:T(8,128)(2,1)S(1)} %collective-permute-done.4), channel_id=1, source_target_pairs={{0,1},{1,2},{2,3},{3,4},{4,5},{5,6},{6,7},{7,8},{8,9},{9,10},{10,1... | collective-permute-start | bytes 1572872 | tf_op jit(solution)/shard_map/ppermute | solution.py:19
  54.3 9.4 %multiply_bitcast_fusion.2 = f32[1024,1024]{1,0:T(8,128)} fusion(bf16[2,1,1024,1024]{3,2,1,0:T(8,128)(2,1)} %param.7, f32[]{:T(128)} %bitcast.1, bf16[256,1024]{1,0:T(8,128)(2,1)S(1)} %get-tuple-element.9, bf16[256,1024]{1,0:T(8,128)(2,1)S(1)} %get-tuple-element.10, bf16[256,1024]{1,0:T(8,128)(2,1)S(1)} %get-tuple-element.11, ...), kind=kOutput, calls=%fused_computation.7 | convolution fusion | flops 4305453056 | bytes 10486272 | tf_op jit(solution)/shard_map/dot_general | solution.py:125
  63.6 4.6 %collective-permute-start.1 = (bf16[256,1024]{1,0:T(8,128)(2,1)}, bf16[256,1024]{1,0:T(8,128)(2,1)S(1)}, u32[]{:S(2)}, u32[]{:S(2)}) collective-permute-start(bf16[256,1024]{1,0:T(8,128)(2,1)} %collective-permute-done), channel_id=1, source_target_pairs={{0,1},{1,2},{2,3},{3,4},{4,5},{5,6},{6,7},{7,8},{8,9},{9,10},{10,1... | collective-permute-start | bytes 1572872 | tf_op jit(solution)/shard_map/ppermute | solution.py:19
  68.2 6.4 %collective-permute-done.2 = bf16[256,1024]{1,0:T(8,128)(2,1)} collective-permute-done((bf16[256,1024]{1,0:T(8,128)(2,1)S(1)}, bf16[256,1024]{1,0:T(8,128)(2,1)}, u32[]{:S(2)}, u32[]{:S(2)}) %collective-permute-start.2) | collective-permute-done | bytes 524320 | tf_op jit(solution)/shard_map/ppermute | solution.py:19
  76.1 2.5 %fusion.44 = bf16[256,1024]{1,0:T(8,128)(2,1)S(1)} fusion(bf16[2,1,1024,1024]{3,2,1,0:T(8,128)(2,1)} %param.8, bf16[256,1024]{1,0:T(8,128)(2,1)} %collective-permute-done.7, bf16[256,1024]{1,0:T(8,128)(2,1)S(1)} %collective-permute-done.6, f32[]{:T(128)S(6)} %select_n.75, f32[]{:T(128)S(6)} %select_n.67), kind=kOutput, calls=%fused_computation.47 | convolution fusion | flops 538705920 | bytes 3670024 | tf_op jit(solution)/shard_map/dot_general | solution.py:137
  78.7 1.8 %fusion.41 = bf16[256,1024]{1,0:T(8,128)(2,1)S(1)} fusion(bf16[2,1,1024,1024]{3,2,1,0:T(8,128)(2,1)S(1)} %copy-done.5, bf16[256,1024]{1,0:T(8,128)(2,1)} %collective-permute-done.5, bf16[256,1024]{1,0:T(8,128)(2,1)S(1)} %collective-permute-done.4, f32[]{:T(128)S(6)} %select_n.75, f32[]{:T(128)S(6)} %select_n.67), kind=kOutput, calls=%fused_computation.46 | convolution fusion | flops 538705920 | bytes 3670024 | tf_op jit(solution)/shard_map/dot_general | solution.py:137
  80.5 1.9 %fusion.38 = bf16[256,1024]{1,0:T(8,128)(2,1)S(1)} fusion(bf16[2,1,1024,1024]{3,2,1,0:T(8,128)(2,1)S(1)} %copy-done.5, bf16[256,1024]{1,0:T(8,128)(2,1)S(1)} %collective-permute-done.3, bf16[256,1024]{1,0:T(8,128)(2,1)} %collective-permute-done.2, f32[]{:T(128)S(6)} %select_n.75, f32[]{:T(128)S(6)} %select_n.67), kind=kOutput, calls=%fused_computation.45 | convolution fusion | flops 538705920 | bytes 3670024 | tf_op jit(solution)/shard_map/dot_general | solution.py:137
  82.4 1.8 %fusion.35 = bf16[256,1024]{1,0:T(8,128)(2,1)S(1)} fusion(bf16[2,1,1024,1024]{3,2,1,0:T(8,128)(2,1)S(1)} %copy-done.5, bf16[256,1024]{1,0:T(8,128)(2,1)S(1)} %collective-permute-done.1, bf16[256,1024]{1,0:T(8,128)(2,1)} %collective-permute-done, f32[]{:T(128)S(6)} %select_n.75, f32[]{:T(128)S(6)} %select_n.67), kind=kOutput, calls=%fused_computation.44 | convolution fusion | flops 538705920 | bytes 3670024 | tf_op jit(solution)/shard_map/dot_general | solution.py:137
  84.2 4.3 %fusion.8 = f32[1024,1024]{0,1:T(8,128)} fusion(bf16[256,1024]{1,0:T(8,128)(2,1)S(1)} %fusion.44, bf16[256,1024]{1,0:T(8,128)(2,1)S(1)} %fusion.41, bf16[256,1024]{1,0:T(8,128)(2,1)S(1)} %fusion.38, bf16[256,1024]{1,0:T(8,128)(2,1)S(1)} %fusion.35, bf16[2,1,1024,1024]{3,2,1,0:T(8,128)(2,1)S(1)} %copy-done.6), kind=kOutput, calls=%fused_computation.16 | convolution fusion | flops 2155872256 | bytes 8388608 | tf_op jit(solution)/shard_map/dot_general | solution.py:140
  88.5 4.5 %multiply_bitcast_fusion.1 = (f32[1,1024,1024]{2,1,0:T(8,128)S(1)}, f32[1024,1024]{1,0:T(8,128)S(1)}) fusion(f32[]{:T(128)S(6)} %sqrt.6, f32[1024]{0:T(1024)S(1)} %get-tuple-element.19, f32[1024]{0:T(1024)S(1)} %get-tuple-element.18, f32[1024,1024]{1,0:T(8,128)} %multiply_bitcast_fusion.2, f32[1024,1024]{0,1:T(8,128)} %fusion.8, f32[1,1024,1024]{2,1,0:T(8,128)S(1)} %copy-done), kind=kLoop, calls=%fused_computation.6 | loop fusion | flops 6291456 | bytes 20979716 | tf_op jit(solution)/shard_map/stack | solution.py:143
  93.5 1.6 %copy-done.1 = f32[1024,1024]{1,0:T(8,128)} copy-done((f32[1024,1024]{1,0:T(8,128)}, f32[1024,1024]{1,0:T(8,128)S(1)}, u32[]{:S(2)}) %copy-start.1) | copy-done | bytes 4194328
  96.8 22.2 %all-to-all-start.1 = ((f32[32,1,2]{2,1,0:T(1,128)}), f32[32,1,2]{2,1,0:T(1,128)S(1)}, u32[]{:S(2)}, u32[]{:S(2)}) async-start(f32[32,1,2]{2,1,0:T(1,128)} %broadcast_in_dim.4), calls=%async_computation.1 | async-start | bytes 32768 | tf_op jit(solution)/shard_map/all_to_all | solution.py:28
  119.1 7.1 %all-to-all-done.1 = f32[32,1,2]{2,1,0:T(1,128)S(1)} async-done(((f32[32,1,2]{2,1,0:T(1,128)}), f32[32,1,2]{2,1,0:T(1,128)S(1)}, u32[]{:S(2)}, u32[]{:S(2)}) %all-to-all-start.1) | async-done | bytes 288 | tf_op jit(solution)/shard_map/all_to_all | solution.py:28
  130.2 6.4 %divide_bitcast_fusion = f32[1,1024,1024]{2,1,0:T(8,128)} fusion(f32[1024,1024]{1,0:T(8,128)} %copy-done.1, f32[]{:T(128)} %bitcast.18, f32[]{:T(128)} %bitcast.16, f32[]{:T(128)S(6)} %sqrt.6, f32[1024]{0:T(1024)S(1)} %get-tuple-element.19, f32[1024]{0:T(1024)S(1)} %get-tuple-element.18, f32[1,1024,1024]{2,1,0:T(8,128)} %state_ref.1), kind=kLoop, calls=%fused_computation.4 | loop fusion | flops 6291456 | bytes 12591116 | tf_op jit(solution)/shard_map/broadcast_in_dim | solution.py:150
  (35 shorter events, 8.0 us)
Async XLA Ops:
  0.6 13.8 %copy-start.4 = (s32[10]{0:T(128)S(1)}, s32[10]{0:T(128)}, u32[]{:S(2)}) copy-start(s32[10]{0:T(128)} %right_ref.1) | copy-start | bytes 124
  0.6 12.1 %copy-start.3 = (s32[8]{0:T(128)S(1)}, s32[8]{0:T(128)}, u32[]{:S(2)}) copy-start(s32[8]{0:T(128)} %left_ref.1) | copy-start | bytes 100
  5.4 15.4 %all-to-all-start = ((f32[32,1,1]{2,1,0:T(1,128)}), f32[32,1,1]{2,1,0:T(1,128)S(1)}, u32[]{:S(2)}, u32[]{:S(2)}) async-start(f32[32,1,1]{2,1,0:T(1,128)} %shard_map.77), calls=%async_computation | async-start | bytes 32768 | tf_op jit(solution)/shard_map/all_to_all | solution.py:28
  20.9 11.3 %copy-start.2 = (f32[2,4,4]{2,1,0:T(4,128)S(1)}, f32[2,4,4]{2,1,0:T(4,128)}, u32[]{:S(2)}) copy-start(f32[2,4,4]{2,1,0:T(4,128)} %param.9) | copy-start | bytes 388
  25.0 16.6 %collective-permute-start.6 = (bf16[256,1024]{1,0:T(8,128)(2,1)S(1)}, bf16[256,1024]{1,0:T(8,128)(2,1)S(1)}, u32[]{:S(2)}, u32[]{:S(2)}) collective-permute-start(bf16[256,1024]{1,0:T(8,128)(2,1)S(1)} %get-tuple-element.9), channel_id=1, source_target_pairs={{0,2},{1,3},{2,4},{3,5},{4,6},{5,7},{6,8},{7,9},{8,10},{9,11},{10,... | collective-permute-start | bytes 1572872 | tf_op jit(solution)/shard_map/ppermute | solution.py:19
  28.7 23.5 %collective-permute-start.4 = (bf16[256,1024]{1,0:T(8,128)(2,1)S(1)}, bf16[256,1024]{1,0:T(8,128)(2,1)S(1)}, u32[]{:S(2)}, u32[]{:S(2)}) collective-permute-start(bf16[256,1024]{1,0:T(8,128)(2,1)S(1)} %get-tuple-element.10), channel_id=1, source_target_pairs={{0,2},{1,3},{2,4},{3,5},{4,6},{5,7},{6,8},{7,9},{8,10},{9,11},{10,... | collective-permute-start | bytes 1572872 | tf_op jit(solution)/shard_map/ppermute | solution.py:19
  34.1 29.6 %collective-permute-start = (bf16[256,1024]{1,0:T(8,128)(2,1)S(1)}, bf16[256,1024]{1,0:T(8,128)(2,1)}, u32[]{:S(2)}, u32[]{:S(2)}) collective-permute-start(bf16[256,1024]{1,0:T(8,128)(2,1)S(1)} %get-tuple-element.8), channel_id=1, source_target_pairs={{0,2},{1,3},{2,4},{3,5},{4,6},{5,7},{6,8},{7,9},{8,10},{9,11},{10,... | collective-permute-start | bytes 1572872 | tf_op jit(solution)/shard_map/ppermute | solution.py:19
  38.2 36.4 %collective-permute-start.2 = (bf16[256,1024]{1,0:T(8,128)(2,1)S(1)}, bf16[256,1024]{1,0:T(8,128)(2,1)}, u32[]{:S(2)}, u32[]{:S(2)}) collective-permute-start(bf16[256,1024]{1,0:T(8,128)(2,1)S(1)} %get-tuple-element.11), channel_id=1, source_target_pairs={{0,2},{1,3},{2,4},{3,5},{4,6},{5,7},{6,8},{7,9},{8,10},{9,11},{10,... | collective-permute-start | bytes 1572872 | tf_op jit(solution)/shard_map/ppermute | solution.py:19
  41.6 34.5 %collective-permute-start.7 = (bf16[256,1024]{1,0:T(8,128)(2,1)S(1)}, bf16[256,1024]{1,0:T(8,128)(2,1)}, u32[]{:S(2)}, u32[]{:S(2)}) collective-permute-start(bf16[256,1024]{1,0:T(8,128)(2,1)S(1)} %collective-permute-done.6), channel_id=1, source_target_pairs={{0,1},{1,2},{2,3},{3,4},{4,5},{5,6},{6,7},{7,8},{8,9},{9,10},{10,1... | collective-permute-start | bytes 1572872 | tf_op jit(solution)/shard_map/ppermute | solution.py:19
  52.2 26.5 %collective-permute-start.5 = (bf16[256,1024]{1,0:T(8,128)(2,1)S(1)}, bf16[256,1024]{1,0:T(8,128)(2,1)}, u32[]{:S(2)}, u32[]{:S(2)}) collective-permute-start(bf16[256,1024]{1,0:T(8,128)(2,1)S(1)} %collective-permute-done.4), channel_id=1, source_target_pairs={{0,1},{1,2},{2,3},{3,4},{4,5},{5,6},{6,7},{7,8},{8,9},{9,10},{10,1... | collective-permute-start | bytes 1572872 | tf_op jit(solution)/shard_map/ppermute | solution.py:19
  63.6 15.0 %copy-start.5 = (bf16[2,1,1024,1024]{3,2,1,0:T(8,128)(2,1)S(1)}, bf16[2,1,1024,1024]{3,2,1,0:T(8,128)(2,1)}, u32[]{:S(2)}) copy-start(bf16[2,1,1024,1024]{3,2,1,0:T(8,128)(2,1)} %param.8) | copy-start | bytes 12582916
  63.6 18.8 %collective-permute-start.1 = (bf16[256,1024]{1,0:T(8,128)(2,1)}, bf16[256,1024]{1,0:T(8,128)(2,1)S(1)}, u32[]{:S(2)}, u32[]{:S(2)}) collective-permute-start(bf16[256,1024]{1,0:T(8,128)(2,1)} %collective-permute-done), channel_id=1, source_target_pairs={{0,1},{1,2},{2,3},{3,4},{4,5},{5,6},{6,7},{7,8},{8,9},{9,10},{10,1... | collective-permute-start | bytes 1572872 | tf_op jit(solution)/shard_map/ppermute | solution.py:19
  74.6 5.8 %collective-permute-start.3 = (bf16[256,1024]{1,0:T(8,128)(2,1)}, bf16[256,1024]{1,0:T(8,128)(2,1)S(1)}, u32[]{:S(2)}, u32[]{:S(2)}) collective-permute-start(bf16[256,1024]{1,0:T(8,128)(2,1)} %collective-permute-done.2), channel_id=1, source_target_pairs={{0,1},{1,2},{2,3},{3,4},{4,5},{5,6},{6,7},{7,8},{8,9},{9,10},{10,1... | collective-permute-start | bytes 1572872 | tf_op jit(solution)/shard_map/ppermute | solution.py:19
  80.4 3.8 %copy-start.6 = (bf16[2,1,1024,1024]{3,2,1,0:T(8,128)(2,1)S(1)}, bf16[2,1,1024,1024]{3,2,1,0:T(8,128)(2,1)}, u32[]{:S(2)}) copy-start(bf16[2,1,1024,1024]{3,2,1,0:T(8,128)(2,1)} %param.7) | copy-start | bytes 12582916
  84.2 4.3 %copy-start = (f32[1,1024,1024]{2,1,0:T(8,128)S(1)}, f32[1,1024,1024]{2,1,0:T(8,128)}, u32[]{:S(2)}) copy-start(f32[1,1024,1024]{2,1,0:T(8,128)} %state_ref.1) | copy-start | bytes 12582916
  93.0 2.0 %copy-start.1 = (f32[1024,1024]{1,0:T(8,128)}, f32[1024,1024]{1,0:T(8,128)S(1)}, u32[]{:S(2)}) copy-start(f32[1024,1024]{1,0:T(8,128)S(1)} %get-tuple-element.7) | copy-start | bytes 12582916
  96.8 29.4 %all-to-all-start.1 = ((f32[32,1,2]{2,1,0:T(1,128)}), f32[32,1,2]{2,1,0:T(1,128)S(1)}, u32[]{:S(2)}, u32[]{:S(2)}) async-start(f32[32,1,2]{2,1,0:T(1,128)} %broadcast_in_dim.4), calls=%async_computation.1 | async-start | bytes 32768 | tf_op jit(solution)/shard_map/all_to_all | solution.py:28

commit v16 on v10

--- a/solution.py
+++ b/solution.py
@@ -140,13 +140,16 @@
     image = row_major(image * live)
 
     sums = all_sum(jnp.sum(jnp.stack([vector * image, image * image]), axis=(1, 2)))
-    alpha_value = sums[0:1] / entries
     vector_mean = start_mean / (start_mean + 1e-06)
-    residual_mean = sums[1:2] / entries - alpha_value * alpha_value * (2.0 - vector_mean)
-    beta_value = jnp.sqrt(residual_mean + 1e-06)
-    residual = image - alpha_value[:, None] * vector
-    next_vector = residual / beta_value[:, None]
-    return (next_vector[None], jnp.concatenate([alpha_value, beta_value]))
+    means = sums / entries
+    swapped = means[::-1]
+    lane = lax.broadcasted_iota(jnp.int32, means.shape, 0)
+    coefficients = jnp.where(
+        lane == 0, means, jnp.sqrt(means - swapped * swapped * (2.0 - vector_mean) + 1e-06)
+    )
+    residual = image - coefficients[0] * vector
+    next_vector = residual / coefficients[1]
+    return (next_vector[None], coefficients)
 
 
 def solution(mesh):

time: 129 us -> 128 us (level)
  between operations: 7.63 us -> 5.07 us
    broadcast_in_dim x1, other arithmetic: 6.43 us -> 7.81 us  [per_device(): return (next_vector[None], coefficients)]
    unnamed x16 -> x18, local copies, waits for them, and re-layouts: 3.11 us -> 3.11 us
where the time goes in v16:
time: 128 us; the launch traced here: 127 us
  starting transfers between devices  46.4 us (36%)
  waiting for transfers between devices  28.2 us (22%)
  other arithmetic  18 us (14%)
  matrix products  17.6 us (14%)
  local copies, waits for them, and re-layouts  7.05 us (6%)
  between operations  5.07 us (4%)
  Pallas kernels  4.77 us (4%)
    all_to_all x2, starting transfers between devices, exchange_sum(): return jnp.sum(lax.all_to_all(spread, AXES, 0, 0, tiled=True), axis=0)  27.2 us
    ppermute x8, waiting for transfers between devices, shift_up(): return lax.ppermute(block, AXES, route)  21.1 us
    ppermute x8, starting transfers between devices, shift_up(): return lax.ppermute(block, AXES, route)  19.2 us
    dot_general x1, matrix products, per_device(): jnp.dot(left_env[1, 0], part_one, preferred_element_type=jnp.float32)  9.38 us
    broadcast_in_dim x1, other arithmetic, per_device(): return (next_vector[None], coefficients)  7.81 us
    all_to_all x2, waiting for transfers between devices, exchange_sum(): return jnp.sum(lax.all_to_all(spread, AXES, 0, 0, tiled=True), axis=0)  7.09 us
    dot_general x4, matrix products, per_device(): jnp.dot(source, right_env[0, 0], preferred_element_type=jnp.float32)  5.79 us
    pallas_call x1, Pallas kernels, masked_square_sum(): pl.pallas_call(functools.partial(square_sum_kernel, pairs), grid_spec=plt...  4.77 us
  transfers between devices with their start and end apart: 10, of which 4 were waited for; matrix products, arithmetic and copies ran while one was open for 17% of the time, Pallas kernels for 0%

profile of v16, /device:TPU:0, one launch (start us, length us, event | category | flops | bytes accessed | tf_op | source)
XLA Modules:
  0.0 127.1 jit_solution(12969752924874697369)
XLA Ops:
  0.7 4.8 %shard_map.77 = f32[32,1,1]{2,1,0:T(1,128)} custom-call(s32[1]{0:T(128)} %bitcast.5.index_ref, s32[8]{0:T(128)} %left_ref.1, s32[10]{0:T(128)} %right_ref.1, f32[1,1024,1024]{2,1,0:T(8,128)} %state_ref.1), custom_call_target="tpu_custom_call" | custom-call | tf_op jit(solution)/shard_map/pallas_call | solution.py:58
  5.4 7.3 %all-to-all-start = ((f32[32,1,1]{2,1,0:T(1,128)}), f32[32,1,1]{2,1,0:T(1,128)S(1)}, u32[]{:S(2)}, u32[]{:S(2)}) async-start(f32[32,1,1]{2,1,0:T(1,128)} %shard_map.77), calls=%async_computation | async-start | bytes 32768 | tf_op jit(solution)/shard_map/all_to_all | solution.py:28
  16.9 4.6 %multiply_multiply_fusion.1 = f32[1024,1024]{1,0:T(8,128)} fusion(f32[1,1024,1024]{2,1,0:T(8,128)} %state_ref.1, f32[1024]{0:T(1024)S(1)} %get-tuple-element.20, f32[1024]{0:T(1024)S(1)} %get-tuple-element.19), kind=kLoop, calls=%fused_computation.2 | loop fusion | flops 2097152 | bytes 8396800 | tf_op jit(solution)/shard_map/mul | solution.py:97
  23.6 2.8 %fusion.49 = (bf16[256,1024]{1,0:T(8,128)(2,1)S(1)}, bf16[256,1024]{1,0:T(8,128)(2,1)S(1)}, bf16[256,1024]{1,0:T(8,128)(2,1)S(1)}, bf16[256,1024]{1,0:T(8,128)(2,1)S(1)}) fusion(f32[1024,1024]{1,0:T(8,128)} %multiply_multiply_fusion.1, f32[]{:T(128)S(6)} %sqrt.6), kind=kLoop, calls=%fused_computation.54 | loop fusion | flops 2097152 | bytes 6291460 | tf_op jit(solution)/shard_map/convert_element_type | solution.py:106
  26.3 4.5 %collective-permute-start = (bf16[256,1024]{1,0:T(8,128)(2,1)S(1)}, bf16[256,1024]{1,0:T(8,128)(2,1)}, u32[]{:S(2)}, u32[]{:S(2)}) collective-permute-start(bf16[256,1024]{1,0:T(8,128)(2,1)S(1)} %get-tuple-element.8), channel_id=1, source_target_pairs={{0,2},{1,3},{2,4},{3,5},{4,6},{5,7},{6,8},{7,9},{8,10},{9,11},{10,... | collective-permute-start | bytes 1572872 | tf_op jit(solution)/shard_map/ppermute | solution.py:19
  30.8 3.4 %collective-permute-start.4 = (bf16[256,1024]{1,0:T(8,128)(2,1)S(1)}, bf16[256,1024]{1,0:T(8,128)(2,1)}, u32[]{:S(2)}, u32[]{:S(2)}) collective-permute-start(bf16[256,1024]{1,0:T(8,128)(2,1)S(1)} %get-tuple-element.10), channel_id=1, source_target_pairs={{0,2},{1,3},{2,4},{3,5},{4,6},{5,7},{6,8},{7,9},{8,10},{9,11},{10,... | collective-permute-start | bytes 1572872 | tf_op jit(solution)/shard_map/ppermute | solution.py:19
  34.2 2.6 %collective-permute-start.2 = (bf16[256,1024]{1,0:T(8,128)(2,1)S(1)}, bf16[256,1024]{1,0:T(8,128)(2,1)S(1)}, u32[]{:S(2)}, u32[]{:S(2)}) collective-permute-start(bf16[256,1024]{1,0:T(8,128)(2,1)S(1)} %get-tuple-element.11), channel_id=1, source_target_pairs={{0,2},{1,3},{2,4},{3,5},{4,6},{5,7},{6,8},{7,9},{8,10},{9,11},{10,... | collective-permute-start | bytes 1572872 | tf_op jit(solution)/shard_map/ppermute | solution.py:19
  36.9 9.4 %multiply_bitcast_fusion.2 = f32[1024,1024]{1,0:T(8,128)} fusion(bf16[2,1,1024,1024]{3,2,1,0:T(8,128)(2,1)} %param.7, f32[]{:T(128)} %bitcast.8, bf16[256,1024]{1,0:T(8,128)(2,1)S(1)} %get-tuple-element.4, bf16[256,1024]{1,0:T(8,128)(2,1)S(1)} %get-tuple-element.10, bf16[256,1024]{1,0:T(8,128)(2,1)S(1)} %get-tuple-element.11, ...), kind=kOutput, calls=%fused_computation.7 | convolution fusion | flops 4305453056 | bytes 10486272 | tf_op jit(solution)/shard_map/dot_general | solution.py:125
  46.2 3.3 %collective-permute-start.6 = (bf16[256,1024]{1,0:T(8,128)(2,1)S(1)}, bf16[256,1024]{1,0:T(8,128)(2,1)S(1)}, u32[]{:S(2)}, u32[]{:S(2)}) collective-permute-start(bf16[256,1024]{1,0:T(8,128)(2,1)S(1)} %get-tuple-element.4), channel_id=1, source_target_pairs={{0,2},{1,3},{2,4},{3,5},{4,6},{5,7},{6,8},{7,9},{8,10},{9,11},{10,... | collective-permute-start | bytes 1572872 | tf_op jit(solution)/shard_map/ppermute | solution.py:19
  49.6 1.3 %collective-permute-start.1 = (bf16[256,1024]{1,0:T(8,128)(2,1)}, bf16[256,1024]{1,0:T(8,128)(2,1)S(1)}, u32[]{:S(2)}, u32[]{:S(2)}) collective-permute-start(bf16[256,1024]{1,0:T(8,128)(2,1)} %collective-permute-done), channel_id=1, source_target_pairs={{0,1},{1,2},{2,3},{3,4},{4,5},{5,6},{6,7},{7,8},{8,9},{9,10},{10,1... | collective-permute-start | bytes 1572872 | tf_op jit(solution)/shard_map/ppermute | solution.py:19
  50.9 2.6 %collective-permute-done.4 = bf16[256,1024]{1,0:T(8,128)(2,1)} collective-permute-done((bf16[256,1024]{1,0:T(8,128)(2,1)S(1)}, bf16[256,1024]{1,0:T(8,128)(2,1)}, u32[]{:S(2)}, u32[]{:S(2)}) %collective-permute-start.4) | collective-permute-done | bytes 524320 | tf_op jit(solution)/shard_map/ppermute | solution.py:19
  53.5 1.5 %collective-permute-start.5 = (bf16[256,1024]{1,0:T(8,128)(2,1)}, bf16[256,1024]{1,0:T(8,128)(2,1)S(1)}, u32[]{:S(2)}, u32[]{:S(2)}) collective-permute-start(bf16[256,1024]{1,0:T(8,128)(2,1)} %collective-permute-done.4), channel_id=1, source_target_pairs={{0,1},{1,2},{2,3},{3,4},{4,5},{5,6},{6,7},{7,8},{8,9},{9,10},{10,1... | collective-permute-start | bytes 1572872 | tf_op jit(solution)/shard_map/ppermute | solution.py:19
  56.2 8.5 %collective-permute-done.2 = bf16[256,1024]{1,0:T(8,128)(2,1)S(1)} collective-permute-done((bf16[256,1024]{1,0:T(8,128)(2,1)S(1)}, bf16[256,1024]{1,0:T(8,128)(2,1)S(1)}, u32[]{:S(2)}, u32[]{:S(2)}) %collective-permute-start.2) | collective-permute-done | bytes 524320 | tf_op jit(solution)/shard_map/ppermute | solution.py:19
  64.8 1.3 %collective-permute-start.3 = (bf16[256,1024]{1,0:T(8,128)(2,1)S(1)}, bf16[256,1024]{1,0:T(8,128)(2,1)S(1)}, u32[]{:S(2)}, u32[]{:S(2)}) collective-permute-start(bf16[256,1024]{1,0:T(8,128)(2,1)S(1)} %collective-permute-done.2), channel_id=1, source_target_pairs={{0,1},{1,2},{2,3},{3,4},{4,5},{5,6},{6,7},{7,8},{8,9},{9,10},{10,1... | collective-permute-start | bytes 1572872 | tf_op jit(solution)/shard_map/ppermute | solution.py:19
  66.1 9.9 %collective-permute-done.6 = bf16[256,1024]{1,0:T(8,128)(2,1)S(1)} collective-permute-done((bf16[256,1024]{1,0:T(8,128)(2,1)S(1)}, bf16[256,1024]{1,0:T(8,128)(2,1)S(1)}, u32[]{:S(2)}, u32[]{:S(2)}) %collective-permute-start.6) | collective-permute-done | bytes 524320 | tf_op jit(solution)/shard_map/ppermute | solution.py:19
  76.0 1.3 %collective-permute-start.7 = (bf16[256,1024]{1,0:T(8,128)(2,1)S(1)}, bf16[256,1024]{1,0:T(8,128)(2,1)S(1)}, u32[]{:S(2)}, u32[]{:S(2)}) collective-permute-start(bf16[256,1024]{1,0:T(8,128)(2,1)S(1)} %collective-permute-done.6), channel_id=1, source_target_pairs={{0,1},{1,2},{2,3},{3,4},{4,5},{5,6},{6,7},{7,8},{8,9},{9,10},{10,1... | collective-permute-start | bytes 1572872 | tf_op jit(solution)/shard_map/ppermute | solution.py:19
  77.3 2.5 %fusion.34 = bf16[256,1024]{1,0:T(8,128)(2,1)S(1)} fusion(bf16[2,1,1024,1024]{3,2,1,0:T(8,128)(2,1)} %param.8, bf16[256,1024]{1,0:T(8,128)(2,1)S(1)} %collective-permute-done.1, bf16[256,1024]{1,0:T(8,128)(2,1)} %collective-permute-done, f32[]{:T(128)S(6)} %select_n.79, f32[]{:T(128)S(6)} %select_n.71), kind=kOutput, calls=%fused_computation.43 | convolution fusion | flops 538705920 | bytes 3670024 | tf_op jit(solution)/shard_map/dot_general | solution.py:136
  79.8 1.8 %fusion.40 = bf16[256,1024]{1,0:T(8,128)(2,1)S(1)} fusion(bf16[2,1,1024,1024]{3,2,1,0:T(8,128)(2,1)S(1)} %copy-done.6, bf16[256,1024]{1,0:T(8,128)(2,1)S(1)} %collective-permute-done.5, bf16[256,1024]{1,0:T(8,128)(2,1)} %collective-permute-done.4, f32[]{:T(128)S(6)} %select_n.79, f32[]{:T(128)S(6)} %select_n.71), kind=kOutput, calls=%fused_computation.45 | convolution fusion | flops 538705920 | bytes 3670024 | tf_op jit(solution)/shard_map/dot_general | solution.py:136
  83.9 1.3 %copy-done.8 = f32[1024,1024]{1,0:T(8,128)S(1)} copy-done((f32[1024,1024]{1,0:T(8,128)S(1)}, f32[1024,1024]{1,0:T(8,128)}, u32[]{:S(2)}) %copy-start.8) | copy-done | bytes 4194328
  85.1 2.4 %multiply_multiply_fusion = f32[1024,1024]{1,0:T(8,128)S(1)} fusion(f32[1024,1024]{1,0:T(8,128)S(1)} %copy-done.8, bf16[256,1024]{1,0:T(8,128)(2,1)S(1)} %fusion.43, bf16[256,1024]{1,0:T(8,128)(2,1)S(1)} %fusion.40, bf16[256,1024]{1,0:T(8,128)(2,1)S(1)} %fusion.37, bf16[256,1024]{1,0:T(8,128)(2,1)S(1)} %fusion.34, ...), kind=kOutput, calls=%fused_computation.1 | convolution fusion | flops 2159017984 | bytes 12591104 | tf_op jit(solution)/shard_map/dot_general | solution.py:139
  89.6 1.2 maximum_reduce_fusion
  91.4 19.9 %all-to-all-start.1 = ((f32[32,1,2]{2,1,0:T(1,128)}), f32[32,1,2]{2,1,0:T(1,128)S(1)}, u32[]{:S(2)}, u32[]{:S(2)}) async-start(f32[32,1,2]{2,1,0:T(1,128)} %broadcast_in_dim.4), calls=%async_computation.1 | async-start | bytes 32768 | tf_op jit(solution)/shard_map/all_to_all | solution.py:28
  111.3 7.1 %all-to-all-done.1 = f32[32,1,2]{2,1,0:T(1,128)S(1)} async-done(((f32[32,1,2]{2,1,0:T(1,128)}), f32[32,1,2]{2,1,0:T(1,128)S(1)}, u32[]{:S(2)}, u32[]{:S(2)}) %all-to-all-start.1) | async-done | bytes 288 | tf_op jit(solution)/shard_map/all_to_all | solution.py:28
  119.3 7.8 %divide_bitcast_fusion = f32[1,1024,1024]{2,1,0:T(8,128)} fusion(f32[1024,1024]{1,0:T(8,128)} %copy-done.1, f32[]{:T(128)} %bitcast.17, f32[]{:T(128)} %bitcast.16, f32[]{:T(128)S(6)} %sqrt.6, f32[1024]{0:T(1024)S(1)} %get-tuple-element.20, f32[1024]{0:T(1024)S(1)} %get-tuple-element.19, f32[1,1024,1024]{2,1,0:T(8,128)} %state_ref.1), kind=kLoop, calls=%fused_computation.4 | loop fusion | flops 6291456 | bytes 12591116 | tf_op jit(solution)/shard_map/broadcast_in_dim | solution.py:152
  (39 shorter events, 8.9 us)
Async XLA Ops:
  0.6 14.2 %copy-start.5 = (s32[10]{0:T(128)S(1)}, s32[10]{0:T(128)}, u32[]{:S(2)}) copy-start(s32[10]{0:T(128)} %right_ref.1) | copy-start | bytes 124
  0.6 12.2 %copy-start.4 = (s32[8]{0:T(128)S(1)}, s32[8]{0:T(128)}, u32[]{:S(2)}) copy-start(s32[8]{0:T(128)} %left_ref.1) | copy-start | bytes 100
  0.7 16.2 %copy-start.3 = (f32[2,4,4]{2,1,0:T(4,128)S(1)}, f32[2,4,4]{2,1,0:T(4,128)}, u32[]{:S(2)}) copy-start(f32[2,4,4]{2,1,0:T(4,128)} %param.9) | copy-start | bytes 388
  5.4 16.7 %all-to-all-start = ((f32[32,1,1]{2,1,0:T(1,128)}), f32[32,1,1]{2,1,0:T(1,128)S(1)}, u32[]{:S(2)}, u32[]{:S(2)}) async-start(f32[32,1,1]{2,1,0:T(1,128)} %shard_map.77), calls=%async_computation | async-start | bytes 32768 | tf_op jit(solution)/shard_map/all_to_all | solution.py:28
  26.3 23.2 %collective-permute-start = (bf16[256,1024]{1,0:T(8,128)(2,1)S(1)}, bf16[256,1024]{1,0:T(8,128)(2,1)}, u32[]{:S(2)}, u32[]{:S(2)}) collective-permute-start(bf16[256,1024]{1,0:T(8,128)(2,1)S(1)} %get-tuple-element.8), channel_id=1, source_target_pairs={{0,2},{1,3},{2,4},{3,5},{4,6},{5,7},{6,8},{7,9},{8,10},{9,11},{10,... | collective-permute-start | bytes 1572872 | tf_op jit(solution)/shard_map/ppermute | solution.py:19
  30.8 22.7 %collective-permute-start.4 = (bf16[256,1024]{1,0:T(8,128)(2,1)S(1)}, bf16[256,1024]{1,0:T(8,128)(2,1)}, u32[]{:S(2)}, u32[]{:S(2)}) collective-permute-start(bf16[256,1024]{1,0:T(8,128)(2,1)S(1)} %get-tuple-element.10), channel_id=1, source_target_pairs={{0,2},{1,3},{2,4},{3,5},{4,6},{5,7},{6,8},{7,9},{8,10},{9,11},{10,... | collective-permute-start | bytes 1572872 | tf_op jit(solution)/shard_map/ppermute | solution.py:19
  34.2 30.5 %collective-permute-start.2 = (bf16[256,1024]{1,0:T(8,128)(2,1)S(1)}, bf16[256,1024]{1,0:T(8,128)(2,1)S(1)}, u32[]{:S(2)}, u32[]{:S(2)}) collective-permute-start(bf16[256,1024]{1,0:T(8,128)(2,1)S(1)} %get-tuple-element.11), channel_id=1, source_target_pairs={{0,2},{1,3},{2,4},{3,5},{4,6},{5,7},{6,8},{7,9},{8,10},{9,11},{10,... | collective-permute-start | bytes 1572872 | tf_op jit(solution)/shard_map/ppermute | solution.py:19
  46.2 29.8 %collective-permute-start.6 = (bf16[256,1024]{1,0:T(8,128)(2,1)S(1)}, bf16[256,1024]{1,0:T(8,128)(2,1)S(1)}, u32[]{:S(2)}, u32[]{:S(2)}) collective-permute-start(bf16[256,1024]{1,0:T(8,128)(2,1)S(1)} %get-tuple-element.4), channel_id=1, source_target_pairs={{0,2},{1,3},{2,4},{3,5},{4,6},{5,7},{6,8},{7,9},{8,10},{9,11},{10,... | collective-permute-start | bytes 1572872 | tf_op jit(solution)/shard_map/ppermute | solution.py:19
  49.6 27.8 %collective-permute-start.1 = (bf16[256,1024]{1,0:T(8,128)(2,1)}, bf16[256,1024]{1,0:T(8,128)(2,1)S(1)}, u32[]{:S(2)}, u32[]{:S(2)}) collective-permute-start(bf16[256,1024]{1,0:T(8,128)(2,1)} %collective-permute-done), channel_id=1, source_target_pairs={{0,1},{1,2},{2,3},{3,4},{4,5},{5,6},{6,7},{7,8},{8,9},{9,10},{10,1... | collective-permute-start | bytes 1572872 | tf_op jit(solution)/shard_map/ppermute | solution.py:19
  53.5 26.3 %collective-permute-start.5 = (bf16[256,1024]{1,0:T(8,128)(2,1)}, bf16[256,1024]{1,0:T(8,128)(2,1)S(1)}, u32[]{:S(2)}, u32[]{:S(2)}) collective-permute-start(bf16[256,1024]{1,0:T(8,128)(2,1)} %collective-permute-done.4), channel_id=1, source_target_pairs={{0,1},{1,2},{2,3},{3,4},{4,5},{5,6},{6,7},{7,8},{8,9},{9,10},{10,1... | collective-permute-start | bytes 1572872 | tf_op jit(solution)/shard_map/ppermute | solution.py:19
  56.2 23.6 %copy-start.6 = (bf16[2,1,1024,1024]{3,2,1,0:T(8,128)(2,1)S(1)}, bf16[2,1,1024,1024]{3,2,1,0:T(8,128)(2,1)}, u32[]{:S(2)}) copy-start(bf16[2,1,1024,1024]{3,2,1,0:T(8,128)(2,1)} %param.8) | copy-start | bytes 12582916
  64.8 16.9 %collective-permute-start.3 = (bf16[256,1024]{1,0:T(8,128)(2,1)S(1)}, bf16[256,1024]{1,0:T(8,128)(2,1)S(1)}, u32[]{:S(2)}, u32[]{:S(2)}) collective-permute-start(bf16[256,1024]{1,0:T(8,128)(2,1)S(1)} %collective-permute-done.2), channel_id=1, source_target_pairs={{0,1},{1,2},{2,3},{3,4},{4,5},{5,6},{6,7},{7,8},{8,9},{9,10},{10,1... | collective-permute-start | bytes 1572872 | tf_op jit(solution)/shard_map/ppermute | solution.py:19
  76.0 6.5 %collective-permute-start.7 = (bf16[256,1024]{1,0:T(8,128)(2,1)S(1)}, bf16[256,1024]{1,0:T(8,128)(2,1)S(1)}, u32[]{:S(2)}, u32[]{:S(2)}) collective-permute-start(bf16[256,1024]{1,0:T(8,128)(2,1)S(1)} %collective-permute-done.6), channel_id=1, source_target_pairs={{0,1},{1,2},{2,3},{3,4},{4,5},{5,6},{6,7},{7,8},{8,9},{9,10},{10,1... | collective-permute-start | bytes 1572872 | tf_op jit(solution)/shard_map/ppermute | solution.py:19
  81.7 2.2 %copy-start.7 = (bf16[2,1,1024,1024]{3,2,1,0:T(8,128)(2,1)S(1)}, bf16[2,1,1024,1024]{3,2,1,0:T(8,128)(2,1)}, u32[]{:S(2)}) copy-start(bf16[2,1,1024,1024]{3,2,1,0:T(8,128)(2,1)} %param.7) | copy-start | bytes 12582916
  81.7 3.5 %copy-start.8 = (f32[1024,1024]{1,0:T(8,128)S(1)}, f32[1024,1024]{1,0:T(8,128)}, u32[]{:S(2)}) copy-start(f32[1024,1024]{1,0:T(8,128)} %multiply_bitcast_fusion.2) | copy-start | bytes 12582916
  85.1 2.4 %copy-start = (f32[1,1024,1024]{2,1,0:T(8,128)S(1)}, f32[1,1024,1024]{2,1,0:T(8,128)}, u32[]{:S(2)}) copy-start(f32[1,1024,1024]{2,1,0:T(8,128)} %state_ref.1) | copy-start | bytes 12582916
  87.6 2.0 %copy-start.1 = (f32[1024,1024]{1,0:T(8,128)}, f32[1024,1024]{1,0:T(8,128)S(1)}, u32[]{:S(2)}) copy-start(f32[1024,1024]{1,0:T(8,128)S(1)} %multiply_multiply_fusion) | copy-start | bytes 12582916
  91.4 27.0 %all-to-all-start.1 = ((f32[32,1,2]{2,1,0:T(1,128)}), f32[32,1,2]{2,1,0:T(1,128)S(1)}, u32[]{:S(2)}, u32[]{:S(2)}) async-start(f32[32,1,2]{2,1,0:T(1,128)} %broadcast_in_dim.4), calls=%async_computation.1 | async-start | bytes 32768 | tf_op jit(solution)/shard_map/all_to_all | solution.py:28
  118.6 8.5 %copy-start.2 = (f32[2]{0:T(128)}, f32[2]{0:T(128)S(1)}, u32[]{:S(2)}) copy-start(f32[2]{0:T(128)S(1)} %compare_select_fusion) | copy-start | bytes 28

commit v17 on v16

--- a/solution.py
+++ b/solution.py
@@ -100,7 +100,7 @@
     )[0, 0]
     start_mean = start_sum / entries
     scale = jnp.sqrt(start_mean + 1e-06)
-    vector = masked / scale
+    vector = lax.optimization_barrier(masked / scale)
     rows = sec_size // CHUNKS
     pieces = [
         row_major((masked[c * rows:(c + 1) * rows] / scale).astype(jnp.bfloat16))
@@ -148,7 +148,7 @@
         lane == 0, means, jnp.sqrt(means - swapped * swapped * (2.0 - vector_mean) + 1e-06)
     )
     residual = image - coefficients[0] * vector
-    next_vector = residual / coefficients[1]
+    next_vector = residual * (1.0 / coefficients[1])
     return (next_vector[None], coefficients)
 
 

time: 128 us -> 128 us (level)
  waiting for transfers between devices: 28.2 us -> 30.9 us
  starting transfers between devices: 46.4 us -> 44.7 us
    div x0 -> x1, other arithmetic: none -> 4.81 us  [per_device(): vector = lax.optimization_barrier(masked / scale)]
    mul x1 -> x0, other arithmetic: 4.61 us -> none  [per_device(): masked = state[0] * live]
    all_to_all x2, waiting for transfers between devices: 7.09 us -> 9.67 us  [exchange_sum(): return jnp.sum(lax.all_to_all(spread, AXES, 0, 0, tiled=True), axis=0)]
    convert_element_type x1, other arithmetic: 2.76 us -> 0.6 us  [per_device(): (masked[c * rows:(c + 1) * rows] / scale).astype(jnp.bfloat16)]
  transfers between devices with their start and end apart: 10 -> 10, of which waited for: 4 -> 5; matrix products, arithmetic and copies ran while one was open for 17% -> 13% of each run, Pallas kernels for 0% -> 0%
where the time goes in v17:
time: 128 us; the launch traced here: 127 us
  starting transfers between devices  44.7 us (35%)
  waiting for transfers between devices  30.9 us (24%)
  matrix products  17.4 us (14%)
  other arithmetic  16.8 us (13%)
  local copies, waits for them, and re-layouts  7.13 us (6%)
  between operations  5.57 us (4%)
  Pallas kernels  4.77 us (4%)
    all_to_all x2, starting transfers between devices, exchange_sum(): return jnp.sum(lax.all_to_all(spread, AXES, 0, 0, tiled=True), axis=0)  26.6 us
    ppermute x8, waiting for transfers between devices, shift_up(): return lax.ppermute(block, AXES, route)  21.3 us
    ppermute x8, starting transfers between devices, shift_up(): return lax.ppermute(block, AXES, route)  18.1 us
    all_to_all x2, waiting for transfers between devices, exchange_sum(): return jnp.sum(lax.all_to_all(spread, AXES, 0, 0, tiled=True), axis=0)  9.67 us
    dot_general x1, matrix products, per_device(): jnp.dot(left_env[1, 0], part_one, preferred_element_type=jnp.float32)  9.3 us
    broadcast_in_dim x1, other arithmetic, per_device(): return (next_vector[None], coefficients)  7.58 us
    dot_general x4, matrix products, per_device(): jnp.dot(source, right_env[0, 0], preferred_element_type=jnp.float32)  5.73 us
    div x1, other arithmetic, per_device(): vector = lax.optimization_barrier(masked / scale)  4.81 us
  transfers between devices with their start and end apart: 10, of which 5 were waited for; matrix products, arithmetic and copies ran while one was open for 13% of the time, Pallas kernels for 0%

profile of v17, /device:TPU:0, one launch (start us, length us, event | category | flops | bytes accessed | tf_op | source)
XLA Modules:
  0.0 127.3 jit_solution(11541776206660272279)
XLA Ops:
  0.7 4.8 %shard_map.77 = f32[32,1,1]{2,1,0:T(1,128)} custom-call(s32[1]{0:T(128)} %bitcast.5.index_ref, s32[8]{0:T(128)} %left_ref.1, s32[10]{0:T(128)} %right_ref.1, f32[1,1024,1024]{2,1,0:T(8,128)} %state_ref.1), custom_call_target="tpu_custom_call" | custom-call | tf_op jit(solution)/shard_map/pallas_call | solution.py:58
  5.4 7.3 %all-to-all-start = ((f32[32,1,1]{2,1,0:T(1,128)}), f32[32,1,1]{2,1,0:T(1,128)S(1)}, u32[]{:S(2)}, u32[]{:S(2)}) async-start(f32[32,1,1]{2,1,0:T(1,128)} %shard_map.77), calls=%async_computation | async-start | bytes 32768 | tf_op jit(solution)/shard_map/all_to_all | solution.py:28
  17.2 2.6 %all-to-all-done = f32[32,1,1]{2,1,0:T(1,128)S(1)} async-done(((f32[32,1,1]{2,1,0:T(1,128)}), f32[32,1,1]{2,1,0:T(1,128)S(1)}, u32[]{:S(2)}, u32[]{:S(2)}) %all-to-all-start) | async-done | bytes 160 | tf_op jit(solution)/shard_map/all_to_all | solution.py:28
  21.1 4.8 %broadcast_divide_fusion = (f32[1024,1024]{1,0:T(8,128)}, f32[1024,1024]{1,0:T(8,128)S(1)}) fusion(f32[]{:T(128)S(6)} %sqrt.6, f32[1024]{0:T(1024)S(1)} %get-tuple-element.22, f32[1024]{0:T(1024)S(1)} %get-tuple-element.21, f32[1,1024,1024]{2,1,0:T(8,128)} %state_ref.1), kind=kLoop, calls=%fused_computation.34 | loop fusion | flops 3145728 | bytes 12591108 | tf_op jit(solution)/shard_map/div | solution.py:103
  26.6 3.3 %collective-permute-start = (bf16[256,1024]{1,0:T(8,128)(2,1)S(1)}, bf16[256,1024]{1,0:T(8,128)(2,1)}, u32[]{:S(2)}, u32[]{:S(2)}) collective-permute-start(bf16[256,1024]{1,0:T(8,128)(2,1)S(1)} %get-tuple-element.10), channel_id=1, source_target_pairs={{0,2},{1,3},{2,4},{3,5},{4,6},{5,7},{6,8},{7,9},{8,10},{9,11},{10,... | collective-permute-start | bytes 1572872 | tf_op jit(solution)/shard_map/ppermute | solution.py:19
  29.8 2.4 %collective-permute-start.4 = (bf16[256,1024]{1,0:T(8,128)(2,1)S(1)}, bf16[256,1024]{1,0:T(8,128)(2,1)}, u32[]{:S(2)}, u32[]{:S(2)}) collective-permute-start(bf16[256,1024]{1,0:T(8,128)(2,1)S(1)} %get-tuple-element.12), channel_id=1, source_target_pairs={{0,2},{1,3},{2,4},{3,5},{4,6},{5,7},{6,8},{7,9},{8,10},{9,11},{10,... | collective-permute-start | bytes 1572872 | tf_op jit(solution)/shard_map/ppermute | solution.py:19
  32.3 2.3 %collective-permute-start.2 = (bf16[256,1024]{1,0:T(8,128)(2,1)S(1)}, bf16[256,1024]{1,0:T(8,128)(2,1)S(1)}, u32[]{:S(2)}, u32[]{:S(2)}) collective-permute-start(bf16[256,1024]{1,0:T(8,128)(2,1)S(1)} %get-tuple-element.13), channel_id=1, source_target_pairs={{0,2},{1,3},{2,4},{3,5},{4,6},{5,7},{6,8},{7,9},{8,10},{9,11},{10,... | collective-permute-start | bytes 1572872 | tf_op jit(solution)/shard_map/ppermute | solution.py:19
  34.5 9.3 %multiply_bitcast_fusion.3 = f32[1024,1024]{1,0:T(8,128)} fusion(bf16[2,1,1024,1024]{3,2,1,0:T(8,128)(2,1)} %param.7, f32[]{:T(128)} %bitcast.8, bf16[256,1024]{1,0:T(8,128)(2,1)S(1)} %get-tuple-element.4, bf16[256,1024]{1,0:T(8,128)(2,1)S(1)} %get-tuple-element.12, bf16[256,1024]{1,0:T(8,128)(2,1)S(1)} %get-tuple-element.13, ...), kind=kOutput, calls=%fused_computation.7 | convolution fusion | flops 4305453056 | bytes 10486272 | tf_op jit(solution)/shard_map/dot_general | solution.py:125
  43.8 4.7 %collective-permute-start.6 = (bf16[256,1024]{1,0:T(8,128)(2,1)S(1)}, bf16[256,1024]{1,0:T(8,128)(2,1)S(1)}, u32[]{:S(2)}, u32[]{:S(2)}) collective-permute-start(bf16[256,1024]{1,0:T(8,128)(2,1)S(1)} %get-tuple-element.4), channel_id=1, source_target_pairs={{0,2},{1,3},{2,4},{3,5},{4,6},{5,7},{6,8},{7,9},{8,10},{9,11},{10,... | collective-permute-start | bytes 1572872 | tf_op jit(solution)/shard_map/ppermute | solution.py:19
  48.5 1.3 %collective-permute-start.1 = (bf16[256,1024]{1,0:T(8,128)(2,1)}, bf16[256,1024]{1,0:T(8,128)(2,1)S(1)}, u32[]{:S(2)}, u32[]{:S(2)}) collective-permute-start(bf16[256,1024]{1,0:T(8,128)(2,1)} %collective-permute-done), channel_id=1, source_target_pairs={{0,1},{1,2},{2,3},{3,4},{4,5},{5,6},{6,7},{7,8},{8,9},{9,10},{10,1... | collective-permute-start | bytes 1572872 | tf_op jit(solution)/shard_map/ppermute | solution.py:19
  49.9 2.7 %collective-permute-done.4 = bf16[256,1024]{1,0:T(8,128)(2,1)} collective-permute-done((bf16[256,1024]{1,0:T(8,128)(2,1)S(1)}, bf16[256,1024]{1,0:T(8,128)(2,1)}, u32[]{:S(2)}, u32[]{:S(2)}) %collective-permute-start.4) | collective-permute-done | bytes 524320 | tf_op jit(solution)/shard_map/ppermute | solution.py:19
  52.6 1.3 %collective-permute-start.5 = (bf16[256,1024]{1,0:T(8,128)(2,1)}, bf16[256,1024]{1,0:T(8,128)(2,1)S(1)}, u32[]{:S(2)}, u32[]{:S(2)}) collective-permute-start(bf16[256,1024]{1,0:T(8,128)(2,1)} %collective-permute-done.4), channel_id=1, source_target_pairs={{0,1},{1,2},{2,3},{3,4},{4,5},{5,6},{6,7},{7,8},{8,9},{9,10},{10,1... | collective-permute-start | bytes 1572872 | tf_op jit(solution)/shard_map/ppermute | solution.py:19
  55.1 8.6 %collective-permute-done.2 = bf16[256,1024]{1,0:T(8,128)(2,1)S(1)} collective-permute-done((bf16[256,1024]{1,0:T(8,128)(2,1)S(1)}, bf16[256,1024]{1,0:T(8,128)(2,1)S(1)}, u32[]{:S(2)}, u32[]{:S(2)}) %collective-permute-start.2) | collective-permute-done | bytes 524320 | tf_op jit(solution)/shard_map/ppermute | solution.py:19
  63.8 1.3 %collective-permute-start.3 = (bf16[256,1024]{1,0:T(8,128)(2,1)S(1)}, bf16[256,1024]{1,0:T(8,128)(2,1)S(1)}, u32[]{:S(2)}, u32[]{:S(2)}) collective-permute-start(bf16[256,1024]{1,0:T(8,128)(2,1)S(1)} %collective-permute-done.2), channel_id=1, source_target_pairs={{0,1},{1,2},{2,3},{3,4},{4,5},{5,6},{6,7},{7,8},{8,9},{9,10},{10,1... | collective-permute-start | bytes 1572872 | tf_op jit(solution)/shard_map/ppermute | solution.py:19
  65.1 9.9 %collective-permute-done.6 = bf16[256,1024]{1,0:T(8,128)(2,1)S(1)} collective-permute-done((bf16[256,1024]{1,0:T(8,128)(2,1)S(1)}, bf16[256,1024]{1,0:T(8,128)(2,1)S(1)}, u32[]{:S(2)}, u32[]{:S(2)}) %collective-permute-start.6) | collective-permute-done | bytes 524320 | tf_op jit(solution)/shard_map/ppermute | solution.py:19
  75.0 1.5 %collective-permute-start.7 = (bf16[256,1024]{1,0:T(8,128)(2,1)S(1)}, bf16[256,1024]{1,0:T(8,128)(2,1)S(1)}, u32[]{:S(2)}, u32[]{:S(2)}) collective-permute-start(bf16[256,1024]{1,0:T(8,128)(2,1)S(1)} %collective-permute-done.6), channel_id=1, source_target_pairs={{0,1},{1,2},{2,3},{3,4},{4,5},{5,6},{6,7},{7,8},{8,9},{9,10},{10,1... | collective-permute-start | bytes 1572872 | tf_op jit(solution)/shard_map/ppermute | solution.py:19
  76.5 2.5 %fusion.34 = bf16[256,1024]{1,0:T(8,128)(2,1)S(1)} fusion(bf16[2,1,1024,1024]{3,2,1,0:T(8,128)(2,1)} %param.8, bf16[256,1024]{1,0:T(8,128)(2,1)S(1)} %collective-permute-done.1, bf16[256,1024]{1,0:T(8,128)(2,1)} %collective-permute-done, f32[]{:T(128)S(6)} %select_n.79, f32[]{:T(128)S(6)} %select_n.71), kind=kOutput, calls=%fused_computation.43 | convolution fusion | flops 538705920 | bytes 3670024 | tf_op jit(solution)/shard_map/dot_general | solution.py:136
  79.0 1.8 %fusion.40 = bf16[256,1024]{1,0:T(8,128)(2,1)S(1)} fusion(bf16[2,1,1024,1024]{3,2,1,0:T(8,128)(2,1)S(1)} %copy-done.6, bf16[256,1024]{1,0:T(8,128)(2,1)S(1)} %collective-permute-done.5, bf16[256,1024]{1,0:T(8,128)(2,1)} %collective-permute-done.4, f32[]{:T(128)S(6)} %select_n.79, f32[]{:T(128)S(6)} %select_n.71), kind=kOutput, calls=%fused_computation.45 | convolution fusion | flops 538705920 | bytes 3670024 | tf_op jit(solution)/shard_map/dot_general | solution.py:136
  83.0 1.3 %copy-done.8 = f32[1024,1024]{1,0:T(8,128)S(1)} copy-done((f32[1024,1024]{1,0:T(8,128)S(1)}, f32[1024,1024]{1,0:T(8,128)}, u32[]{:S(2)}) %copy-start.8) | copy-done | bytes 4194328
  84.3 2.4 %multiply_multiply_fusion = f32[1024,1024]{1,0:T(8,128)S(1)} fusion(f32[1024,1024]{1,0:T(8,128)S(1)} %copy-done.8, bf16[256,1024]{1,0:T(8,128)(2,1)S(1)} %fusion.43, bf16[256,1024]{1,0:T(8,128)(2,1)S(1)} %fusion.40, bf16[256,1024]{1,0:T(8,128)(2,1)S(1)} %fusion.37, bf16[256,1024]{1,0:T(8,128)(2,1)S(1)} %fusion.34, ...), kind=kOutput, calls=%fused_computation.1 | convolution fusion | flops 2159017984 | bytes 12591104 | tf_op jit(solution)/shard_map/dot_general | solution.py:139
  86.7 1.9 %multiply_bitcast_fusion.2 = (f32[1,1024,1024]{2,1,0:T(8,128)S(1)}, f32[1,1024,1024]{2,1,0:T(8,128)S(1)}) fusion(f32[1024,1024]{1,0:T(8,128)S(1)} %copy-done, f32[1024,1024]{1,0:T(8,128)S(1)} %multiply_multiply_fusion), kind=kLoop, calls=%fused_computation.6 | loop fusion | flops 2097152 | bytes 16777216 | tf_op jit(solution)/shard_map/stack | solution.py:142
  91.7 19.3 %all-to-all-start.1 = ((f32[32,1,2]{2,1,0:T(1,128)}), f32[32,1,2]{2,1,0:T(1,128)S(1)}, u32[]{:S(2)}, u32[]{:S(2)}) async-start(f32[32,1,2]{2,1,0:T(1,128)} %broadcast_in_dim.4), calls=%async_computation.1 | async-start | bytes 32768 | tf_op jit(solution)/shard_map/all_to_all | solution.py:28
  111.1 7.1 %all-to-all-done.1 = f32[32,1,2]{2,1,0:T(1,128)S(1)} async-done(((f32[32,1,2]{2,1,0:T(1,128)}), f32[32,1,2]{2,1,0:T(1,128)S(1)}, u32[]{:S(2)}, u32[]{:S(2)}) %all-to-all-start.1) | async-done | bytes 288 | tf_op jit(solution)/shard_map/all_to_all | solution.py:28
  119.7 7.6 %multiply_bitcast_fusion = f32[1,1024,1024]{2,1,0:T(8,128)} fusion(f32[1024,1024]{1,0:T(8,128)} %copy-done.1, f32[1024,1024]{1,0:T(8,128)} %get-tuple-element.6, f32[]{:T(128)} %bitcast.17, f32[]{:T(128)} %bitcast.16), kind=kLoop, calls=%fused_computation.4 | loop fusion | flops 3145728 | bytes 12582920 | tf_op jit(solution)/shard_map/broadcast_in_dim | solution.py:152
  (39 shorter events, 9.8 us)
Async XLA Ops:
  0.6 14.1 %copy-start.5 = (s32[10]{0:T(128)S(1)}, s32[10]{0:T(128)}, u32[]{:S(2)}) copy-start(s32[10]{0:T(128)} %right_ref.1) | copy-start | bytes 124
  0.6 12.2 %copy-start.4 = (s32[8]{0:T(128)S(1)}, s32[8]{0:T(128)}, u32[]{:S(2)}) copy-start(s32[8]{0:T(128)} %left_ref.1) | copy-start | bytes 100
  0.7 15.9 %copy-start.3 = (f32[2,4,4]{2,1,0:T(4,128)S(1)}, f32[2,4,4]{2,1,0:T(4,128)}, u32[]{:S(2)}) copy-start(f32[2,4,4]{2,1,0:T(4,128)} %param.9) | copy-start | bytes 388
  5.4 14.4 %all-to-all-start = ((f32[32,1,1]{2,1,0:T(1,128)}), f32[32,1,1]{2,1,0:T(1,128)S(1)}, u32[]{:S(2)}, u32[]{:S(2)}) async-start(f32[32,1,1]{2,1,0:T(1,128)} %shard_map.77), calls=%async_computation | async-start | bytes 32768 | tf_op jit(solution)/shard_map/all_to_all | solution.py:28
  26.6 22.0 %collective-permute-start = (bf16[256,1024]{1,0:T(8,128)(2,1)S(1)}, bf16[256,1024]{1,0:T(8,128)(2,1)}, u32[]{:S(2)}, u32[]{:S(2)}) collective-permute-start(bf16[256,1024]{1,0:T(8,128)(2,1)S(1)} %get-tuple-element.10), channel_id=1, source_target_pairs={{0,2},{1,3},{2,4},{3,5},{4,6},{5,7},{6,8},{7,9},{8,10},{9,11},{10,... | collective-permute-start | bytes 1572872 | tf_op jit(solution)/shard_map/ppermute | solution.py:19
  29.8 22.7 %collective-permute-start.4 = (bf16[256,1024]{1,0:T(8,128)(2,1)S(1)}, bf16[256,1024]{1,0:T(8,128)(2,1)}, u32[]{:S(2)}, u32[]{:S(2)}) collective-permute-start(bf16[256,1024]{1,0:T(8,128)(2,1)S(1)} %get-tuple-element.12), channel_id=1, source_target_pairs={{0,2},{1,3},{2,4},{3,5},{4,6},{5,7},{6,8},{7,9},{8,10},{9,11},{10,... | collective-permute-start | bytes 1572872 | tf_op jit(solution)/shard_map/ppermute | solution.py:19
  32.3 31.5 %collective-permute-start.2 = (bf16[256,1024]{1,0:T(8,128)(2,1)S(1)}, bf16[256,1024]{1,0:T(8,128)(2,1)S(1)}, u32[]{:S(2)}, u32[]{:S(2)}) collective-permute-start(bf16[256,1024]{1,0:T(8,128)(2,1)S(1)} %get-tuple-element.13), channel_id=1, source_target_pairs={{0,2},{1,3},{2,4},{3,5},{4,6},{5,7},{6,8},{7,9},{8,10},{9,11},{10,... | collective-permute-start | bytes 1572872 | tf_op jit(solution)/shard_map/ppermute | solution.py:19
  43.8 31.2 %collective-permute-start.6 = (bf16[256,1024]{1,0:T(8,128)(2,1)S(1)}, bf16[256,1024]{1,0:T(8,128)(2,1)S(1)}, u32[]{:S(2)}, u32[]{:S(2)}) collective-permute-start(bf16[256,1024]{1,0:T(8,128)(2,1)S(1)} %get-tuple-element.4), channel_id=1, source_target_pairs={{0,2},{1,3},{2,4},{3,5},{4,6},{5,7},{6,8},{7,9},{8,10},{9,11},{10,... | collective-permute-start | bytes 1572872 | tf_op jit(solution)/shard_map/ppermute | solution.py:19
  48.5 28.0 %collective-permute-start.1 = (bf16[256,1024]{1,0:T(8,128)(2,1)}, bf16[256,1024]{1,0:T(8,128)(2,1)S(1)}, u32[]{:S(2)}, u32[]{:S(2)}) collective-permute-start(bf16[256,1024]{1,0:T(8,128)(2,1)} %collective-permute-done), channel_id=1, source_target_pairs={{0,1},{1,2},{2,3},{3,4},{4,5},{5,6},{6,7},{7,8},{8,9},{9,10},{10,1... | collective-permute-start | bytes 1572872 | tf_op jit(solution)/shard_map/ppermute | solution.py:19
  52.6 26.5 %collective-permute-start.5 = (bf16[256,1024]{1,0:T(8,128)(2,1)}, bf16[256,1024]{1,0:T(8,128)(2,1)S(1)}, u32[]{:S(2)}, u32[]{:S(2)}) collective-permute-start(bf16[256,1024]{1,0:T(8,128)(2,1)} %collective-permute-done.4), channel_id=1, source_target_pairs={{0,1},{1,2},{2,3},{3,4},{4,5},{5,6},{6,7},{7,8},{8,9},{9,10},{10,1... | collective-permute-start | bytes 1572872 | tf_op jit(solution)/shard_map/ppermute | solution.py:19
  55.1 23.9 %copy-start.6 = (bf16[2,1,1024,1024]{3,2,1,0:T(8,128)(2,1)S(1)}, bf16[2,1,1024,1024]{3,2,1,0:T(8,128)(2,1)}, u32[]{:S(2)}) copy-start(bf16[2,1,1024,1024]{3,2,1,0:T(8,128)(2,1)} %param.8) | copy-start | bytes 12582916
  63.8 17.1 %collective-permute-start.3 = (bf16[256,1024]{1,0:T(8,128)(2,1)S(1)}, bf16[256,1024]{1,0:T(8,128)(2,1)S(1)}, u32[]{:S(2)}, u32[]{:S(2)}) collective-permute-start(bf16[256,1024]{1,0:T(8,128)(2,1)S(1)} %collective-permute-done.2), channel_id=1, source_target_pairs={{0,1},{1,2},{2,3},{3,4},{4,5},{5,6},{6,7},{7,8},{8,9},{9,10},{10,1... | collective-permute-start | bytes 1572872 | tf_op jit(solution)/shard_map/ppermute | solution.py:19
  75.0 6.6 %collective-permute-start.7 = (bf16[256,1024]{1,0:T(8,128)(2,1)S(1)}, bf16[256,1024]{1,0:T(8,128)(2,1)S(1)}, u32[]{:S(2)}, u32[]{:S(2)}) collective-permute-start(bf16[256,1024]{1,0:T(8,128)(2,1)S(1)} %collective-permute-done.6), channel_id=1, source_target_pairs={{0,1},{1,2},{2,3},{3,4},{4,5},{5,6},{6,7},{7,8},{8,9},{9,10},{10,1... | collective-permute-start | bytes 1572872 | tf_op jit(solution)/shard_map/ppermute | solution.py:19
  80.8 2.2 %copy-start.7 = (bf16[2,1,1024,1024]{3,2,1,0:T(8,128)(2,1)S(1)}, bf16[2,1,1024,1024]{3,2,1,0:T(8,128)(2,1)}, u32[]{:S(2)}) copy-start(bf16[2,1,1024,1024]{3,2,1,0:T(8,128)(2,1)} %param.7) | copy-start | bytes 12582916
  80.9 3.5 %copy-start.8 = (f32[1024,1024]{1,0:T(8,128)S(1)}, f32[1024,1024]{1,0:T(8,128)}, u32[]{:S(2)}) copy-start(f32[1024,1024]{1,0:T(8,128)} %multiply_bitcast_fusion.3) | copy-start | bytes 12582916
  84.3 2.4 %copy-start = (f32[1024,1024]{1,0:T(8,128)S(1)}, f32[1024,1024]{1,0:T(8,128)}, u32[]{:S(2)}) copy-start(f32[1024,1024]{1,0:T(8,128)} %get-tuple-element.6) | copy-start | bytes 12582916
  86.7 3.2 %copy-start.1 = (f32[1024,1024]{1,0:T(8,128)}, f32[1024,1024]{1,0:T(8,128)S(1)}, u32[]{:S(2)}) copy-start(f32[1024,1024]{1,0:T(8,128)S(1)} %multiply_multiply_fusion) | copy-start | bytes 12582916
  91.7 26.5 %all-to-all-start.1 = ((f32[32,1,2]{2,1,0:T(1,128)}), f32[32,1,2]{2,1,0:T(1,128)S(1)}, u32[]{:S(2)}, u32[]{:S(2)}) async-start(f32[32,1,2]{2,1,0:T(1,128)} %broadcast_in_dim.4), calls=%async_computation.1 | async-start | bytes 32768 | tf_op jit(solution)/shard_map/all_to_all | solution.py:28
  118.3 9.0 %copy-start.2 = (f32[2]{0:T(128)}, f32[2]{0:T(128)S(1)}, u32[]{:S(2)}) copy-start(f32[2]{0:T(128)S(1)} %compare_select_fusion) | copy-start | bytes 28

commit v18 on v16

--- a/solution.py
+++ b/solution.py
@@ -40,11 +40,12 @@
     def _():
         acc_ref[...] = jnp.zeros_like(acc_ref)
 
-    x = state_ref[0]
-    row_ids = step * rows + lax.broadcasted_iota(jnp.int32, (rows, cols), 0)
-    col_ids = lax.broadcasted_iota(jnp.int32, (rows, cols), 1)
-    x = jnp.where((row_ids < row_limit) & (col_ids < col_limit), x, 0.0)
-    acc_ref[...] += jnp.sum((x * x).reshape(rows // 8, 8, cols), axis=0)
+    @pl.when(step * rows < row_limit)
+    def _():
+        x = state_ref[0]
+        col_ids = lax.broadcasted_iota(jnp.int32, (rows, cols), 1)
+        x = jnp.where(col_ids < col_limit, x, 0.0)
+        acc_ref[...] += jnp.sum((x * x).reshape(rows // 8, 8, cols), axis=0)
 
     @pl.when(step == pl.num_programs(0) - 1)
     def _():

time: 128 us -> 127 us (level)
  no operation moved by 1% of the time
where the time goes in v18:
time: 127 us
  starting transfers between devices  46.4 us (37%)
  waiting for transfers between devices  28.2 us (22%)
  other arithmetic  18 us (14%)
  matrix products  17.6 us (14%)
  local copies, waits for them, and re-layouts  7.05 us (6%)
  between operations  5.07 us (4%)
  Pallas kernels  4.47 us (4%)
    all_to_all x2, starting transfers between devices, exchange_sum(): return jnp.sum(lax.all_to_all(spread, AXES, 0, 0, tiled=True), axis=0)  27.2 us
    ppermute x8, waiting for transfers between devices, shift_up(): return lax.ppermute(block, AXES, route)  21.1 us
    ppermute x8, starting transfers between devices, shift_up(): return lax.ppermute(block, AXES, route)  19.2 us
    dot_general x1, matrix products, per_device(): jnp.dot(left_env[1, 0], part_one, preferred_element_type=jnp.float32)  9.38 us
    broadcast_in_dim x1, other arithmetic, per_device(): return (next_vector[None], coefficients)  7.81 us
    all_to_all x2, waiting for transfers between devices, exchange_sum(): return jnp.sum(lax.all_to_all(spread, AXES, 0, 0, tiled=True), axis=0)  7.09 us
    dot_general x4, matrix products, per_device(): jnp.dot(source, right_env[0, 0], preferred_element_type=jnp.float32)  5.79 us
    mul x1, other arithmetic, per_device(): masked = state[0] * live  4.61 us
  transfers between devices with their start and end apart: 10, of which 4 were waited for; matrix products, arithmetic and copies ran while one was open for 17% of the time, Pallas kernels for 0%

profile of v18, /device:TPU:0, one launch (start us, length us, event | category | flops | bytes accessed | tf_op | source)
XLA Modules:
  0.0 126.8 jit_solution(10837895734608072341)
XLA Ops:
  0.7 4.5 %shard_map.77 = f32[32,1,1]{2,1,0:T(1,128)} custom-call(s32[1]{0:T(128)} %bitcast.5.index_ref, s32[8]{0:T(128)} %left_ref.1, s32[10]{0:T(128)} %right_ref.1, f32[1,1024,1024]{2,1,0:T(8,128)} %state_ref.1), custom_call_target="tpu_custom_call" | custom-call | tf_op jit(solution)/shard_map/pallas_call | solution.py:59
  5.1 7.3 %all-to-all-start = ((f32[32,1,1]{2,1,0:T(1,128)}), f32[32,1,1]{2,1,0:T(1,128)S(1)}, u32[]{:S(2)}, u32[]{:S(2)}) async-start(f32[32,1,1]{2,1,0:T(1,128)} %shard_map.77), calls=%async_computation | async-start | bytes 32768 | tf_op jit(solution)/shard_map/all_to_all | solution.py:28
  16.6 4.6 %multiply_multiply_fusion.1 = f32[1024,1024]{1,0:T(8,128)} fusion(f32[1,1024,1024]{2,1,0:T(8,128)} %state_ref.1, f32[1024]{0:T(1024)S(1)} %get-tuple-element.20, f32[1024]{0:T(1024)S(1)} %get-tuple-element.19), kind=kLoop, calls=%fused_computation.2 | loop fusion | flops 2097152 | bytes 8396800 | tf_op jit(solution)/shard_map/mul | solution.py:98
  23.3 2.8 %fusion.49 = (bf16[256,1024]{1,0:T(8,128)(2,1)S(1)}, bf16[256,1024]{1,0:T(8,128)(2,1)S(1)}, bf16[256,1024]{1,0:T(8,128)(2,1)S(1)}, bf16[256,1024]{1,0:T(8,128)(2,1)S(1)}) fusion(f32[1024,1024]{1,0:T(8,128)} %multiply_multiply_fusion.1, f32[]{:T(128)S(6)} %sqrt.6), kind=kLoop, calls=%fused_computation.54 | loop fusion | flops 2097152 | bytes 6291460 | tf_op jit(solution)/shard_map/convert_element_type | solution.py:107
  26.0 4.5 %collective-permute-start = (bf16[256,1024]{1,0:T(8,128)(2,1)S(1)}, bf16[256,1024]{1,0:T(8,128)(2,1)}, u32[]{:S(2)}, u32[]{:S(2)}) collective-permute-start(bf16[256,1024]{1,0:T(8,128)(2,1)S(1)} %get-tuple-element.8), channel_id=1, source_target_pairs={{0,2},{1,3},{2,4},{3,5},{4,6},{5,7},{6,8},{7,9},{8,10},{9,11},{10,... | collective-permute-start | bytes 1572872 | tf_op jit(solution)/shard_map/ppermute | solution.py:19
  30.5 3.4 %collective-permute-start.4 = (bf16[256,1024]{1,0:T(8,128)(2,1)S(1)}, bf16[256,1024]{1,0:T(8,128)(2,1)}, u32[]{:S(2)}, u32[]{:S(2)}) collective-permute-start(bf16[256,1024]{1,0:T(8,128)(2,1)S(1)} %get-tuple-element.10), channel_id=1, source_target_pairs={{0,2},{1,3},{2,4},{3,5},{4,6},{5,7},{6,8},{7,9},{8,10},{9,11},{10,... | collective-permute-start | bytes 1572872 | tf_op jit(solution)/shard_map/ppermute | solution.py:19
  33.9 2.6 %collective-permute-start.2 = (bf16[256,1024]{1,0:T(8,128)(2,1)S(1)}, bf16[256,1024]{1,0:T(8,128)(2,1)S(1)}, u32[]{:S(2)}, u32[]{:S(2)}) collective-permute-start(bf16[256,1024]{1,0:T(8,128)(2,1)S(1)} %get-tuple-element.11), channel_id=1, source_target_pairs={{0,2},{1,3},{2,4},{3,5},{4,6},{5,7},{6,8},{7,9},{8,10},{9,11},{10,... | collective-permute-start | bytes 1572872 | tf_op jit(solution)/shard_map/ppermute | solution.py:19
  36.6 9.4 %multiply_bitcast_fusion.2 = f32[1024,1024]{1,0:T(8,128)} fusion(bf16[2,1,1024,1024]{3,2,1,0:T(8,128)(2,1)} %param.7, f32[]{:T(128)} %bitcast.8, bf16[256,1024]{1,0:T(8,128)(2,1)S(1)} %get-tuple-element.4, bf16[256,1024]{1,0:T(8,128)(2,1)S(1)} %get-tuple-element.10, bf16[256,1024]{1,0:T(8,128)(2,1)S(1)} %get-tuple-element.11, ...), kind=kOutput, calls=%fused_computation.7 | convolution fusion | flops 4305453056 | bytes 10486272 | tf_op jit(solution)/shard_map/dot_general | solution.py:126
  46.0 3.3 %collective-permute-start.6 = (bf16[256,1024]{1,0:T(8,128)(2,1)S(1)}, bf16[256,1024]{1,0:T(8,128)(2,1)S(1)}, u32[]{:S(2)}, u32[]{:S(2)}) collective-permute-start(bf16[256,1024]{1,0:T(8,128)(2,1)S(1)} %get-tuple-element.4), channel_id=1, source_target_pairs={{0,2},{1,3},{2,4},{3,5},{4,6},{5,7},{6,8},{7,9},{8,10},{9,11},{10,... | collective-permute-start | bytes 1572872 | tf_op jit(solution)/shard_map/ppermute | solution.py:19
  49.3 1.3 %collective-permute-start.1 = (bf16[256,1024]{1,0:T(8,128)(2,1)}, bf16[256,1024]{1,0:T(8,128)(2,1)S(1)}, u32[]{:S(2)}, u32[]{:S(2)}) collective-permute-start(bf16[256,1024]{1,0:T(8,128)(2,1)} %collective-permute-done), channel_id=1, source_target_pairs={{0,1},{1,2},{2,3},{3,4},{4,5},{5,6},{6,7},{7,8},{8,9},{9,10},{10,1... | collective-permute-start | bytes 1572872 | tf_op jit(solution)/shard_map/ppermute | solution.py:19
  50.6 2.6 %collective-permute-done.4 = bf16[256,1024]{1,0:T(8,128)(2,1)} collective-permute-done((bf16[256,1024]{1,0:T(8,128)(2,1)S(1)}, bf16[256,1024]{1,0:T(8,128)(2,1)}, u32[]{:S(2)}, u32[]{:S(2)}) %collective-permute-start.4) | collective-permute-done | bytes 524320 | tf_op jit(solution)/shard_map/ppermute | solution.py:19
  53.2 1.5 %collective-permute-start.5 = (bf16[256,1024]{1,0:T(8,128)(2,1)}, bf16[256,1024]{1,0:T(8,128)(2,1)S(1)}, u32[]{:S(2)}, u32[]{:S(2)}) collective-permute-start(bf16[256,1024]{1,0:T(8,128)(2,1)} %collective-permute-done.4), channel_id=1, source_target_pairs={{0,1},{1,2},{2,3},{3,4},{4,5},{5,6},{6,7},{7,8},{8,9},{9,10},{10,1... | collective-permute-start | bytes 1572872 | tf_op jit(solution)/shard_map/ppermute | solution.py:19
  55.9 8.5 %collective-permute-done.2 = bf16[256,1024]{1,0:T(8,128)(2,1)S(1)} collective-permute-done((bf16[256,1024]{1,0:T(8,128)(2,1)S(1)}, bf16[256,1024]{1,0:T(8,128)(2,1)S(1)}, u32[]{:S(2)}, u32[]{:S(2)}) %collective-permute-start.2) | collective-permute-done | bytes 524320 | tf_op jit(solution)/shard_map/ppermute | solution.py:19
  64.5 1.3 %collective-permute-start.3 = (bf16[256,1024]{1,0:T(8,128)(2,1)S(1)}, bf16[256,1024]{1,0:T(8,128)(2,1)S(1)}, u32[]{:S(2)}, u32[]{:S(2)}) collective-permute-start(bf16[256,1024]{1,0:T(8,128)(2,1)S(1)} %collective-permute-done.2), channel_id=1, source_target_pairs={{0,1},{1,2},{2,3},{3,4},{4,5},{5,6},{6,7},{7,8},{8,9},{9,10},{10,1... | collective-permute-start | bytes 1572872 | tf_op jit(solution)/shard_map/ppermute | solution.py:19
  65.8 9.9 %collective-permute-done.6 = bf16[256,1024]{1,0:T(8,128)(2,1)S(1)} collective-permute-done((bf16[256,1024]{1,0:T(8,128)(2,1)S(1)}, bf16[256,1024]{1,0:T(8,128)(2,1)S(1)}, u32[]{:S(2)}, u32[]{:S(2)}) %collective-permute-start.6) | collective-permute-done | bytes 524320 | tf_op jit(solution)/shard_map/ppermute | solution.py:19
  75.7 1.3 %collective-permute-start.7 = (bf16[256,1024]{1,0:T(8,128)(2,1)S(1)}, bf16[256,1024]{1,0:T(8,128)(2,1)S(1)}, u32[]{:S(2)}, u32[]{:S(2)}) collective-permute-start(bf16[256,1024]{1,0:T(8,128)(2,1)S(1)} %collective-permute-done.6), channel_id=1, source_target_pairs={{0,1},{1,2},{2,3},{3,4},{4,5},{5,6},{6,7},{7,8},{8,9},{9,10},{10,1... | collective-permute-start | bytes 1572872 | tf_op jit(solution)/shard_map/ppermute | solution.py:19
  77.0 2.5 %fusion.34 = bf16[256,1024]{1,0:T(8,128)(2,1)S(1)} fusion(bf16[2,1,1024,1024]{3,2,1,0:T(8,128)(2,1)} %param.8, bf16[256,1024]{1,0:T(8,128)(2,1)S(1)} %collective-permute-done.1, bf16[256,1024]{1,0:T(8,128)(2,1)} %collective-permute-done, f32[]{:T(128)S(6)} %select_n.79, f32[]{:T(128)S(6)} %select_n.71), kind=kOutput, calls=%fused_computation.43 | convolution fusion | flops 538705920 | bytes 3670024 | tf_op jit(solution)/shard_map/dot_general | solution.py:137
  79.5 1.8 %fusion.40 = bf16[256,1024]{1,0:T(8,128)(2,1)S(1)} fusion(bf16[2,1,1024,1024]{3,2,1,0:T(8,128)(2,1)S(1)} %copy-done.6, bf16[256,1024]{1,0:T(8,128)(2,1)S(1)} %collective-permute-done.5, bf16[256,1024]{1,0:T(8,128)(2,1)} %collective-permute-done.4, f32[]{:T(128)S(6)} %select_n.79, f32[]{:T(128)S(6)} %select_n.71), kind=kOutput, calls=%fused_computation.45 | convolution fusion | flops 538705920 | bytes 3670024 | tf_op jit(solution)/shard_map/dot_general | solution.py:137
  83.6 1.3 %copy-done.8 = f32[1024,1024]{1,0:T(8,128)S(1)} copy-done((f32[1024,1024]{1,0:T(8,128)S(1)}, f32[1024,1024]{1,0:T(8,128)}, u32[]{:S(2)}) %copy-start.8) | copy-done | bytes 4194328
  84.8 2.4 %multiply_multiply_fusion = f32[1024,1024]{1,0:T(8,128)S(1)} fusion(f32[1024,1024]{1,0:T(8,128)S(1)} %copy-done.8, bf16[256,1024]{1,0:T(8,128)(2,1)S(1)} %fusion.43, bf16[256,1024]{1,0:T(8,128)(2,1)S(1)} %fusion.40, bf16[256,1024]{1,0:T(8,128)(2,1)S(1)} %fusion.37, bf16[256,1024]{1,0:T(8,128)(2,1)S(1)} %fusion.34, ...), kind=kOutput, calls=%fused_computation.1 | convolution fusion | flops 2159017984 | bytes 12591104 | tf_op jit(solution)/shard_map/dot_general | solution.py:140
  89.3 1.2 maximum_reduce_fusion
  91.1 19.9 %all-to-all-start.1 = ((f32[32,1,2]{2,1,0:T(1,128)}), f32[32,1,2]{2,1,0:T(1,128)S(1)}, u32[]{:S(2)}, u32[]{:S(2)}) async-start(f32[32,1,2]{2,1,0:T(1,128)} %broadcast_in_dim.4), calls=%async_computation.1 | async-start | bytes 32768 | tf_op jit(solution)/shard_map/all_to_all | solution.py:28
  111.0 7.1 %all-to-all-done.1 = f32[32,1,2]{2,1,0:T(1,128)S(1)} async-done(((f32[32,1,2]{2,1,0:T(1,128)}), f32[32,1,2]{2,1,0:T(1,128)S(1)}, u32[]{:S(2)}, u32[]{:S(2)}) %all-to-all-start.1) | async-done | bytes 288 | tf_op jit(solution)/shard_map/all_to_all | solution.py:28
  119.0 7.8 %divide_bitcast_fusion = f32[1,1024,1024]{2,1,0:T(8,128)} fusion(f32[1024,1024]{1,0:T(8,128)} %copy-done.1, f32[]{:T(128)} %bitcast.17, f32[]{:T(128)} %bitcast.16, f32[]{:T(128)S(6)} %sqrt.6, f32[1024]{0:T(1024)S(1)} %get-tuple-element.20, f32[1024]{0:T(1024)S(1)} %get-tuple-element.19, f32[1,1024,1024]{2,1,0:T(8,128)} %state_ref.1), kind=kLoop, calls=%fused_computation.4 | loop fusion | flops 6291456 | bytes 12591116 | tf_op jit(solution)/shard_map/broadcast_in_dim | solution.py:153
  (39 shorter events, 8.9 us)
Async XLA Ops:
  0.6 13.9 %copy-start.5 = (s32[10]{0:T(128)S(1)}, s32[10]{0:T(128)}, u32[]{:S(2)}) copy-start(s32[10]{0:T(128)} %right_ref.1) | copy-start | bytes 124
  0.6 11.9 %copy-start.4 = (s32[8]{0:T(128)S(1)}, s32[8]{0:T(128)}, u32[]{:S(2)}) copy-start(s32[8]{0:T(128)} %left_ref.1) | copy-start | bytes 100
  0.7 15.9 %copy-start.3 = (f32[2,4,4]{2,1,0:T(4,128)S(1)}, f32[2,4,4]{2,1,0:T(4,128)}, u32[]{:S(2)}) copy-start(f32[2,4,4]{2,1,0:T(4,128)} %param.9) | copy-start | bytes 388
  5.1 16.7 %all-to-all-start = ((f32[32,1,1]{2,1,0:T(1,128)}), f32[32,1,1]{2,1,0:T(1,128)S(1)}, u32[]{:S(2)}, u32[]{:S(2)}) async-start(f32[32,1,1]{2,1,0:T(1,128)} %shard_map.77), calls=%async_computation | async-start | bytes 32768 | tf_op jit(solution)/shard_map/all_to_all | solution.py:28
  26.0 23.2 %collective-permute-start = (bf16[256,1024]{1,0:T(8,128)(2,1)S(1)}, bf16[256,1024]{1,0:T(8,128)(2,1)}, u32[]{:S(2)}, u32[]{:S(2)}) collective-permute-start(bf16[256,1024]{1,0:T(8,128)(2,1)S(1)} %get-tuple-element.8), channel_id=1, source_target_pairs={{0,2},{1,3},{2,4},{3,5},{4,6},{5,7},{6,8},{7,9},{8,10},{9,11},{10,... | collective-permute-start | bytes 1572872 | tf_op jit(solution)/shard_map/ppermute | solution.py:19
  30.5 22.7 %collective-permute-start.4 = (bf16[256,1024]{1,0:T(8,128)(2,1)S(1)}, bf16[256,1024]{1,0:T(8,128)(2,1)}, u32[]{:S(2)}, u32[]{:S(2)}) collective-permute-start(bf16[256,1024]{1,0:T(8,128)(2,1)S(1)} %get-tuple-element.10), channel_id=1, source_target_pairs={{0,2},{1,3},{2,4},{3,5},{4,6},{5,7},{6,8},{7,9},{8,10},{9,11},{10,... | collective-permute-start | bytes 1572872 | tf_op jit(solution)/shard_map/ppermute | solution.py:19
  33.9 30.5 %collective-permute-start.2 = (bf16[256,1024]{1,0:T(8,128)(2,1)S(1)}, bf16[256,1024]{1,0:T(8,128)(2,1)S(1)}, u32[]{:S(2)}, u32[]{:S(2)}) collective-permute-start(bf16[256,1024]{1,0:T(8,128)(2,1)S(1)} %get-tuple-element.11), channel_id=1, source_target_pairs={{0,2},{1,3},{2,4},{3,5},{4,6},{5,7},{6,8},{7,9},{8,10},{9,11},{10,... | collective-permute-start | bytes 1572872 | tf_op jit(solution)/shard_map/ppermute | solution.py:19
  46.0 29.8 %collective-permute-start.6 = (bf16[256,1024]{1,0:T(8,128)(2,1)S(1)}, bf16[256,1024]{1,0:T(8,128)(2,1)S(1)}, u32[]{:S(2)}, u32[]{:S(2)}) collective-permute-start(bf16[256,1024]{1,0:T(8,128)(2,1)S(1)} %get-tuple-element.4), channel_id=1, source_target_pairs={{0,2},{1,3},{2,4},{3,5},{4,6},{5,7},{6,8},{7,9},{8,10},{9,11},{10,... | collective-permute-start | bytes 1572872 | tf_op jit(solution)/shard_map/ppermute | solution.py:19
  49.3 27.8 %collective-permute-start.1 = (bf16[256,1024]{1,0:T(8,128)(2,1)}, bf16[256,1024]{1,0:T(8,128)(2,1)S(1)}, u32[]{:S(2)}, u32[]{:S(2)}) collective-permute-start(bf16[256,1024]{1,0:T(8,128)(2,1)} %collective-permute-done), channel_id=1, source_target_pairs={{0,1},{1,2},{2,3},{3,4},{4,5},{5,6},{6,7},{7,8},{8,9},{9,10},{10,1... | collective-permute-start | bytes 1572872 | tf_op jit(solution)/shard_map/ppermute | solution.py:19
  53.2 26.3 %collective-permute-start.5 = (bf16[256,1024]{1,0:T(8,128)(2,1)}, bf16[256,1024]{1,0:T(8,128)(2,1)S(1)}, u32[]{:S(2)}, u32[]{:S(2)}) collective-permute-start(bf16[256,1024]{1,0:T(8,128)(2,1)} %collective-permute-done.4), channel_id=1, source_target_pairs={{0,1},{1,2},{2,3},{3,4},{4,5},{5,6},{6,7},{7,8},{8,9},{9,10},{10,1... | collective-permute-start | bytes 1572872 | tf_op jit(solution)/shard_map/ppermute | solution.py:19
  55.9 23.6 %copy-start.6 = (bf16[2,1,1024,1024]{3,2,1,0:T(8,128)(2,1)S(1)}, bf16[2,1,1024,1024]{3,2,1,0:T(8,128)(2,1)}, u32[]{:S(2)}) copy-start(bf16[2,1,1024,1024]{3,2,1,0:T(8,128)(2,1)} %param.8) | copy-start | bytes 12582916
  64.5 16.9 %collective-permute-start.3 = (bf16[256,1024]{1,0:T(8,128)(2,1)S(1)}, bf16[256,1024]{1,0:T(8,128)(2,1)S(1)}, u32[]{:S(2)}, u32[]{:S(2)}) collective-permute-start(bf16[256,1024]{1,0:T(8,128)(2,1)S(1)} %collective-permute-done.2), channel_id=1, source_target_pairs={{0,1},{1,2},{2,3},{3,4},{4,5},{5,6},{6,7},{7,8},{8,9},{9,10},{10,1... | collective-permute-start | bytes 1572872 | tf_op jit(solution)/shard_map/ppermute | solution.py:19
  75.7 6.5 %collective-permute-start.7 = (bf16[256,1024]{1,0:T(8,128)(2,1)S(1)}, bf16[256,1024]{1,0:T(8,128)(2,1)S(1)}, u32[]{:S(2)}, u32[]{:S(2)}) collective-permute-start(bf16[256,1024]{1,0:T(8,128)(2,1)S(1)} %collective-permute-done.6), channel_id=1, source_target_pairs={{0,1},{1,2},{2,3},{3,4},{4,5},{5,6},{6,7},{7,8},{8,9},{9,10},{10,1... | collective-permute-start | bytes 1572872 | tf_op jit(solution)/shard_map/ppermute | solution.py:19
  81.4 2.2 %copy-start.7 = (bf16[2,1,1024,1024]{3,2,1,0:T(8,128)(2,1)S(1)}, bf16[2,1,1024,1024]{3,2,1,0:T(8,128)(2,1)}, u32[]{:S(2)}) copy-start(bf16[2,1,1024,1024]{3,2,1,0:T(8,128)(2,1)} %param.7) | copy-start | bytes 12582916
  81.4 3.5 %copy-start.8 = (f32[1024,1024]{1,0:T(8,128)S(1)}, f32[1024,1024]{1,0:T(8,128)}, u32[]{:S(2)}) copy-start(f32[1024,1024]{1,0:T(8,128)} %multiply_bitcast_fusion.2) | copy-start | bytes 12582916
  84.8 2.4 %copy-start = (f32[1,1024,1024]{2,1,0:T(8,128)S(1)}, f32[1,1024,1024]{2,1,0:T(8,128)}, u32[]{:S(2)}) copy-start(f32[1,1024,1024]{2,1,0:T(8,128)} %state_ref.1) | copy-start | bytes 12582916
  87.3 2.0 %copy-start.1 = (f32[1024,1024]{1,0:T(8,128)}, f32[1024,1024]{1,0:T(8,128)S(1)}, u32[]{:S(2)}) copy-start(f32[1024,1024]{1,0:T(8,128)S(1)} %multiply_multiply_fusion) | copy-start | bytes 12582916
  91.1 27.0 %all-to-all-start.1 = ((f32[32,1,2]{2,1,0:T(1,128)}), f32[32,1,2]{2,1,0:T(1,128)S(1)}, u32[]{:S(2)}, u32[]{:S(2)}) async-start(f32[32,1,2]{2,1,0:T(1,128)} %broadcast_in_dim.4), calls=%async_computation.1 | async-start | bytes 32768 | tf_op jit(solution)/shard_map/all_to_all | solution.py:28
  118.3 8.5 %copy-start.2 = (f32[2]{0:T(128)}, f32[2]{0:T(128)S(1)}, u32[]{:S(2)}) copy-start(f32[2]{0:T(128)S(1)} %compare_select_fusion) | copy-start | bytes 28

commit v19 on v18

--- a/solution.py
+++ b/solution.py
@@ -55,7 +55,7 @@
 def masked_square_sum(pairs, block_index, left_live, right_live, state):
     count = lax.axis_size(AXES)
     sec_size = state.shape[1]
-    rows = 256
+    rows = BLOCK // 2
     return pl.pallas_call(
         functools.partial(square_sum_kernel, pairs),
         grid_spec=pltpu.PrefetchScalarGridSpec(

time: 127 us -> 129 us (1.016)
  Pallas kernels: 4.47 us -> 6.2 us
    pallas_call x1, Pallas kernels: 4.47 us -> 6.2 us  [masked_square_sum(): pl.pallas_call(functools.partial(square_sum_kernel, pairs), grid_spec=plt...]
where the time goes in v19:
time: 129 us
  starting transfers between devices  46.4 us (36%)
  waiting for transfers between devices  28.2 us (22%)
  other arithmetic  18 us (14%)
  matrix products  17.6 us (14%)
  local copies, waits for them, and re-layouts  7.05 us (5%)
  Pallas kernels  6.2 us (5%)
  between operations  5.07 us (4%)
    all_to_all x2, starting transfers between devices, exchange_sum(): return jnp.sum(lax.all_to_all(spread, AXES, 0, 0, tiled=True), axis=0)  27.2 us
    ppermute x8, waiting for transfers between devices, shift_up(): return lax.ppermute(block, AXES, route)  21.1 us
    ppermute x8, starting transfers between devices, shift_up(): return lax.ppermute(block, AXES, route)  19.2 us
    dot_general x1, matrix products, per_device(): jnp.dot(left_env[1, 0], part_one, preferred_element_type=jnp.float32)  9.38 us
    broadcast_in_dim x1, other arithmetic, per_device(): return (next_vector[None], coefficients)  7.81 us
    all_to_all x2, waiting for transfers between devices, exchange_sum(): return jnp.sum(lax.all_to_all(spread, AXES, 0, 0, tiled=True), axis=0)  7.09 us
    pallas_call x1, Pallas kernels, masked_square_sum(): pl.pallas_call(functools.partial(square_sum_kernel, pairs), grid_spec=plt...  6.2 us
    dot_general x4, matrix products, per_device(): jnp.dot(source, right_env[0, 0], preferred_element_type=jnp.float32)  5.77 us
  transfers between devices with their start and end apart: 10, of which 4 were waited for; matrix products, arithmetic and copies ran while one was open for 17% of the time, Pallas kernels for 0%

profile of v19, /device:TPU:0, one launch (start us, length us, event | category | flops | bytes accessed | tf_op | source)
XLA Modules:
  0.0 128.5 jit_solution(8488983981990085499)
XLA Ops:
  0.7 6.2 %shard_map.77 = f32[32,1,1]{2,1,0:T(1,128)} custom-call(s32[1]{0:T(128)} %bitcast.5.index_ref, s32[8]{0:T(128)} %left_ref.1, s32[10]{0:T(128)} %right_ref.1, f32[1,1024,1024]{2,1,0:T(8,128)} %state_ref.1), custom_call_target="tpu_custom_call" | custom-call | tf_op jit(solution)/shard_map/pallas_call | solution.py:59
  6.9 7.3 %all-to-all-start = ((f32[32,1,1]{2,1,0:T(1,128)}), f32[32,1,1]{2,1,0:T(1,128)S(1)}, u32[]{:S(2)}, u32[]{:S(2)}) async-start(f32[32,1,1]{2,1,0:T(1,128)} %shard_map.77), calls=%async_computation | async-start | bytes 32768 | tf_op jit(solution)/shard_map/all_to_all | solution.py:28
  18.3 4.6 %multiply_multiply_fusion.1 = f32[1024,1024]{1,0:T(8,128)} fusion(f32[1,1024,1024]{2,1,0:T(8,128)} %state_ref.1, f32[1024]{0:T(1024)S(1)} %get-tuple-element.20, f32[1024]{0:T(1024)S(1)} %get-tuple-element.19), kind=kLoop, calls=%fused_computation.2 | loop fusion | flops 2097152 | bytes 8396800 | tf_op jit(solution)/shard_map/mul | solution.py:98
  25.0 2.8 %fusion.49 = (bf16[256,1024]{1,0:T(8,128)(2,1)S(1)}, bf16[256,1024]{1,0:T(8,128)(2,1)S(1)}, bf16[256,1024]{1,0:T(8,128)(2,1)S(1)}, bf16[256,1024]{1,0:T(8,128)(2,1)S(1)}) fusion(f32[1024,1024]{1,0:T(8,128)} %multiply_multiply_fusion.1, f32[]{:T(128)S(6)} %sqrt.6), kind=kLoop, calls=%fused_computation.54 | loop fusion | flops 2097152 | bytes 6291460 | tf_op jit(solution)/shard_map/convert_element_type | solution.py:107
  27.8 4.5 %collective-permute-start = (bf16[256,1024]{1,0:T(8,128)(2,1)S(1)}, bf16[256,1024]{1,0:T(8,128)(2,1)}, u32[]{:S(2)}, u32[]{:S(2)}) collective-permute-start(bf16[256,1024]{1,0:T(8,128)(2,1)S(1)} %get-tuple-element.8), channel_id=1, source_target_pairs={{0,2},{1,3},{2,4},{3,5},{4,6},{5,7},{6,8},{7,9},{8,10},{9,11},{10,... | collective-permute-start | bytes 1572872 | tf_op jit(solution)/shard_map/ppermute | solution.py:19
  32.3 3.4 %collective-permute-start.4 = (bf16[256,1024]{1,0:T(8,128)(2,1)S(1)}, bf16[256,1024]{1,0:T(8,128)(2,1)}, u32[]{:S(2)}, u32[]{:S(2)}) collective-permute-start(bf16[256,1024]{1,0:T(8,128)(2,1)S(1)} %get-tuple-element.10), channel_id=1, source_target_pairs={{0,2},{1,3},{2,4},{3,5},{4,6},{5,7},{6,8},{7,9},{8,10},{9,11},{10,... | collective-permute-start | bytes 1572872 | tf_op jit(solution)/shard_map/ppermute | solution.py:19
  35.7 2.6 %collective-permute-start.2 = (bf16[256,1024]{1,0:T(8,128)(2,1)S(1)}, bf16[256,1024]{1,0:T(8,128)(2,1)S(1)}, u32[]{:S(2)}, u32[]{:S(2)}) collective-permute-start(bf16[256,1024]{1,0:T(8,128)(2,1)S(1)} %get-tuple-element.11), channel_id=1, source_target_pairs={{0,2},{1,3},{2,4},{3,5},{4,6},{5,7},{6,8},{7,9},{8,10},{9,11},{10,... | collective-permute-start | bytes 1572872 | tf_op jit(solution)/shard_map/ppermute | solution.py:19
  38.3 9.4 %multiply_bitcast_fusion.2 = f32[1024,1024]{1,0:T(8,128)} fusion(bf16[2,1,1024,1024]{3,2,1,0:T(8,128)(2,1)} %param.7, f32[]{:T(128)} %bitcast.8, bf16[256,1024]{1,0:T(8,128)(2,1)S(1)} %get-tuple-element.4, bf16[256,1024]{1,0:T(8,128)(2,1)S(1)} %get-tuple-element.10, bf16[256,1024]{1,0:T(8,128)(2,1)S(1)} %get-tuple-element.11, ...), kind=kOutput, calls=%fused_computation.7 | convolution fusion | flops 4305453056 | bytes 10486272 | tf_op jit(solution)/shard_map/dot_general | solution.py:126
  47.7 3.3 %collective-permute-start.6 = (bf16[256,1024]{1,0:T(8,128)(2,1)S(1)}, bf16[256,1024]{1,0:T(8,128)(2,1)S(1)}, u32[]{:S(2)}, u32[]{:S(2)}) collective-permute-start(bf16[256,1024]{1,0:T(8,128)(2,1)S(1)} %get-tuple-element.4), channel_id=1, source_target_pairs={{0,2},{1,3},{2,4},{3,5},{4,6},{5,7},{6,8},{7,9},{8,10},{9,11},{10,... | collective-permute-start | bytes 1572872 | tf_op jit(solution)/shard_map/ppermute | solution.py:19
  51.0 1.3 %collective-permute-start.1 = (bf16[256,1024]{1,0:T(8,128)(2,1)}, bf16[256,1024]{1,0:T(8,128)(2,1)S(1)}, u32[]{:S(2)}, u32[]{:S(2)}) collective-permute-start(bf16[256,1024]{1,0:T(8,128)(2,1)} %collective-permute-done), channel_id=1, source_target_pairs={{0,1},{1,2},{2,3},{3,4},{4,5},{5,6},{6,7},{7,8},{8,9},{9,10},{10,1... | collective-permute-start | bytes 1572872 | tf_op jit(solution)/shard_map/ppermute | solution.py:19
  52.3 2.6 %collective-permute-done.4 = bf16[256,1024]{1,0:T(8,128)(2,1)} collective-permute-done((bf16[256,1024]{1,0:T(8,128)(2,1)S(1)}, bf16[256,1024]{1,0:T(8,128)(2,1)}, u32[]{:S(2)}, u32[]{:S(2)}) %collective-permute-start.4) | collective-permute-done | bytes 524320 | tf_op jit(solution)/shard_map/ppermute | solution.py:19
  55.0 1.5 %collective-permute-start.5 = (bf16[256,1024]{1,0:T(8,128)(2,1)}, bf16[256,1024]{1,0:T(8,128)(2,1)S(1)}, u32[]{:S(2)}, u32[]{:S(2)}) collective-permute-start(bf16[256,1024]{1,0:T(8,128)(2,1)} %collective-permute-done.4), channel_id=1, source_target_pairs={{0,1},{1,2},{2,3},{3,4},{4,5},{5,6},{6,7},{7,8},{8,9},{9,10},{10,1... | collective-permute-start | bytes 1572872 | tf_op jit(solution)/shard_map/ppermute | solution.py:19
  57.7 8.5 %collective-permute-done.2 = bf16[256,1024]{1,0:T(8,128)(2,1)S(1)} collective-permute-done((bf16[256,1024]{1,0:T(8,128)(2,1)S(1)}, bf16[256,1024]{1,0:T(8,128)(2,1)S(1)}, u32[]{:S(2)}, u32[]{:S(2)}) %collective-permute-start.2) | collective-permute-done | bytes 524320 | tf_op jit(solution)/shard_map/ppermute | solution.py:19
  66.2 1.3 %collective-permute-start.3 = (bf16[256,1024]{1,0:T(8,128)(2,1)S(1)}, bf16[256,1024]{1,0:T(8,128)(2,1)S(1)}, u32[]{:S(2)}, u32[]{:S(2)}) collective-permute-start(bf16[256,1024]{1,0:T(8,128)(2,1)S(1)} %collective-permute-done.2), channel_id=1, source_target_pairs={{0,1},{1,2},{2,3},{3,4},{4,5},{5,6},{6,7},{7,8},{8,9},{9,10},{10,1... | collective-permute-start | bytes 1572872 | tf_op jit(solution)/shard_map/ppermute | solution.py:19
  67.5 9.9 %collective-permute-done.6 = bf16[256,1024]{1,0:T(8,128)(2,1)S(1)} collective-permute-done((bf16[256,1024]{1,0:T(8,128)(2,1)S(1)}, bf16[256,1024]{1,0:T(8,128)(2,1)S(1)}, u32[]{:S(2)}, u32[]{:S(2)}) %collective-permute-start.6) | collective-permute-done | bytes 524320 | tf_op jit(solution)/shard_map/ppermute | solution.py:19
  77.4 1.3 %collective-permute-start.7 = (bf16[256,1024]{1,0:T(8,128)(2,1)S(1)}, bf16[256,1024]{1,0:T(8,128)(2,1)S(1)}, u32[]{:S(2)}, u32[]{:S(2)}) collective-permute-start(bf16[256,1024]{1,0:T(8,128)(2,1)S(1)} %collective-permute-done.6), channel_id=1, source_target_pairs={{0,1},{1,2},{2,3},{3,4},{4,5},{5,6},{6,7},{7,8},{8,9},{9,10},{10,1... | collective-permute-start | bytes 1572872 | tf_op jit(solution)/shard_map/ppermute | solution.py:19
  78.8 2.5 %fusion.34 = bf16[256,1024]{1,0:T(8,128)(2,1)S(1)} fusion(bf16[2,1,1024,1024]{3,2,1,0:T(8,128)(2,1)} %param.8, bf16[256,1024]{1,0:T(8,128)(2,1)S(1)} %collective-permute-done.1, bf16[256,1024]{1,0:T(8,128)(2,1)} %collective-permute-done, f32[]{:T(128)S(6)} %select_n.79, f32[]{:T(128)S(6)} %select_n.71), kind=kOutput, calls=%fused_computation.43 | convolution fusion | flops 538705920 | bytes 3670024 | tf_op jit(solution)/shard_map/dot_general | solution.py:137
  81.3 1.8 %fusion.40 = bf16[256,1024]{1,0:T(8,128)(2,1)S(1)} fusion(bf16[2,1,1024,1024]{3,2,1,0:T(8,128)(2,1)S(1)} %copy-done.6, bf16[256,1024]{1,0:T(8,128)(2,1)S(1)} %collective-permute-done.5, bf16[256,1024]{1,0:T(8,128)(2,1)} %collective-permute-done.4, f32[]{:T(128)S(6)} %select_n.79, f32[]{:T(128)S(6)} %select_n.71), kind=kOutput, calls=%fused_computation.45 | convolution fusion | flops 538705920 | bytes 3670024 | tf_op jit(solution)/shard_map/dot_general | solution.py:137
  85.3 1.3 copy-done.8
  86.5 2.4 %multiply_multiply_fusion = f32[1024,1024]{1,0:T(8,128)S(1)} fusion(f32[1024,1024]{1,0:T(8,128)S(1)} %copy-done.8, bf16[256,1024]{1,0:T(8,128)(2,1)S(1)} %fusion.43, bf16[256,1024]{1,0:T(8,128)(2,1)S(1)} %fusion.40, bf16[256,1024]{1,0:T(8,128)(2,1)S(1)} %fusion.37, bf16[256,1024]{1,0:T(8,128)(2,1)S(1)} %fusion.34, ...), kind=kOutput, calls=%fused_computation.1 | convolution fusion | flops 2159017984 | bytes 12591104 | tf_op jit(solution)/shard_map/dot_general | solution.py:140
  91.0 1.2 maximum_reduce_fusion
  92.8 19.9 %all-to-all-start.1 = ((f32[32,1,2]{2,1,0:T(1,128)}), f32[32,1,2]{2,1,0:T(1,128)S(1)}, u32[]{:S(2)}, u32[]{:S(2)}) async-start(f32[32,1,2]{2,1,0:T(1,128)} %broadcast_in_dim.4), calls=%async_computation.1 | async-start | bytes 32768 | tf_op jit(solution)/shard_map/all_to_all | solution.py:28
  112.8 7.1 %all-to-all-done.1 = f32[32,1,2]{2,1,0:T(1,128)S(1)} async-done(((f32[32,1,2]{2,1,0:T(1,128)}), f32[32,1,2]{2,1,0:T(1,128)S(1)}, u32[]{:S(2)}, u32[]{:S(2)}) %all-to-all-start.1) | async-done | bytes 288 | tf_op jit(solution)/shard_map/all_to_all | solution.py:28
  120.7 7.8 %divide_bitcast_fusion = f32[1,1024,1024]{2,1,0:T(8,128)} fusion(f32[1024,1024]{1,0:T(8,128)} %copy-done.1, f32[]{:T(128)} %bitcast.17, f32[]{:T(128)} %bitcast.16, f32[]{:T(128)S(6)} %sqrt.6, f32[1024]{0:T(1024)S(1)} %get-tuple-element.20, f32[1024]{0:T(1024)S(1)} %get-tuple-element.19, f32[1,1024,1024]{2,1,0:T(8,128)} %state_ref.1), kind=kLoop, calls=%fused_computation.4 | loop fusion | flops 6291456 | bytes 12591116 | tf_op jit(solution)/shard_map/broadcast_in_dim | solution.py:153
  (39 shorter events, 8.9 us)
Async XLA Ops:
  0.6 15.6 %copy-start.5 = (s32[10]{0:T(128)S(1)}, s32[10]{0:T(128)}, u32[]{:S(2)}) copy-start(s32[10]{0:T(128)} %right_ref.1) | copy-start | bytes 124
  0.6 13.6 %copy-start.4 = (s32[8]{0:T(128)S(1)}, s32[8]{0:T(128)}, u32[]{:S(2)}) copy-start(s32[8]{0:T(128)} %left_ref.1) | copy-start | bytes 100
  0.7 17.6 %copy-start.3 = (f32[2,4,4]{2,1,0:T(4,128)S(1)}, f32[2,4,4]{2,1,0:T(4,128)}, u32[]{:S(2)}) copy-start(f32[2,4,4]{2,1,0:T(4,128)} %param.9) | copy-start | bytes 388
  6.9 16.7 %all-to-all-start = ((f32[32,1,1]{2,1,0:T(1,128)}), f32[32,1,1]{2,1,0:T(1,128)S(1)}, u32[]{:S(2)}, u32[]{:S(2)}) async-start(f32[32,1,1]{2,1,0:T(1,128)} %shard_map.77), calls=%async_computation | async-start | bytes 32768 | tf_op jit(solution)/shard_map/all_to_all | solution.py:28
  27.8 23.2 %collective-permute-start = (bf16[256,1024]{1,0:T(8,128)(2,1)S(1)}, bf16[256,1024]{1,0:T(8,128)(2,1)}, u32[]{:S(2)}, u32[]{:S(2)}) collective-permute-start(bf16[256,1024]{1,0:T(8,128)(2,1)S(1)} %get-tuple-element.8), channel_id=1, source_target_pairs={{0,2},{1,3},{2,4},{3,5},{4,6},{5,7},{6,8},{7,9},{8,10},{9,11},{10,... | collective-permute-start | bytes 1572872 | tf_op jit(solution)/shard_map/ppermute | solution.py:19
  32.3 22.7 %collective-permute-start.4 = (bf16[256,1024]{1,0:T(8,128)(2,1)S(1)}, bf16[256,1024]{1,0:T(8,128)(2,1)}, u32[]{:S(2)}, u32[]{:S(2)}) collective-permute-start(bf16[256,1024]{1,0:T(8,128)(2,1)S(1)} %get-tuple-element.10), channel_id=1, source_target_pairs={{0,2},{1,3},{2,4},{3,5},{4,6},{5,7},{6,8},{7,9},{8,10},{9,11},{10,... | collective-permute-start | bytes 1572872 | tf_op jit(solution)/shard_map/ppermute | solution.py:19
  35.7 30.5 %collective-permute-start.2 = (bf16[256,1024]{1,0:T(8,128)(2,1)S(1)}, bf16[256,1024]{1,0:T(8,128)(2,1)S(1)}, u32[]{:S(2)}, u32[]{:S(2)}) collective-permute-start(bf16[256,1024]{1,0:T(8,128)(2,1)S(1)} %get-tuple-element.11), channel_id=1, source_target_pairs={{0,2},{1,3},{2,4},{3,5},{4,6},{5,7},{6,8},{7,9},{8,10},{9,11},{10,... | collective-permute-start | bytes 1572872 | tf_op jit(solution)/shard_map/ppermute | solution.py:19
  47.7 29.8 %collective-permute-start.6 = (bf16[256,1024]{1,0:T(8,128)(2,1)S(1)}, bf16[256,1024]{1,0:T(8,128)(2,1)S(1)}, u32[]{:S(2)}, u32[]{:S(2)}) collective-permute-start(bf16[256,1024]{1,0:T(8,128)(2,1)S(1)} %get-tuple-element.4), channel_id=1, source_target_pairs={{0,2},{1,3},{2,4},{3,5},{4,6},{5,7},{6,8},{7,9},{8,10},{9,11},{10,... | collective-permute-start | bytes 1572872 | tf_op jit(solution)/shard_map/ppermute | solution.py:19
  51.0 27.8 %collective-permute-start.1 = (bf16[256,1024]{1,0:T(8,128)(2,1)}, bf16[256,1024]{1,0:T(8,128)(2,1)S(1)}, u32[]{:S(2)}, u32[]{:S(2)}) collective-permute-start(bf16[256,1024]{1,0:T(8,128)(2,1)} %collective-permute-done), channel_id=1, source_target_pairs={{0,1},{1,2},{2,3},{3,4},{4,5},{5,6},{6,7},{7,8},{8,9},{9,10},{10,1... | collective-permute-start | bytes 1572872 | tf_op jit(solution)/shard_map/ppermute | solution.py:19
  55.0 26.3 %collective-permute-start.5 = (bf16[256,1024]{1,0:T(8,128)(2,1)}, bf16[256,1024]{1,0:T(8,128)(2,1)S(1)}, u32[]{:S(2)}, u32[]{:S(2)}) collective-permute-start(bf16[256,1024]{1,0:T(8,128)(2,1)} %collective-permute-done.4), channel_id=1, source_target_pairs={{0,1},{1,2},{2,3},{3,4},{4,5},{5,6},{6,7},{7,8},{8,9},{9,10},{10,1... | collective-permute-start | bytes 1572872 | tf_op jit(solution)/shard_map/ppermute | solution.py:19
  57.6 23.6 %copy-start.6 = (bf16[2,1,1024,1024]{3,2,1,0:T(8,128)(2,1)S(1)}, bf16[2,1,1024,1024]{3,2,1,0:T(8,128)(2,1)}, u32[]{:S(2)}) copy-start(bf16[2,1,1024,1024]{3,2,1,0:T(8,128)(2,1)} %param.8) | copy-start | bytes 12582916
  66.2 16.9 %collective-permute-start.3 = (bf16[256,1024]{1,0:T(8,128)(2,1)S(1)}, bf16[256,1024]{1,0:T(8,128)(2,1)S(1)}, u32[]{:S(2)}, u32[]{:S(2)}) collective-permute-start(bf16[256,1024]{1,0:T(8,128)(2,1)S(1)} %collective-permute-done.2), channel_id=1, source_target_pairs={{0,1},{1,2},{2,3},{3,4},{4,5},{5,6},{6,7},{7,8},{8,9},{9,10},{10,1... | collective-permute-start | bytes 1572872 | tf_op jit(solution)/shard_map/ppermute | solution.py:19
  77.4 6.4 %collective-permute-start.7 = (bf16[256,1024]{1,0:T(8,128)(2,1)S(1)}, bf16[256,1024]{1,0:T(8,128)(2,1)S(1)}, u32[]{:S(2)}, u32[]{:S(2)}) collective-permute-start(bf16[256,1024]{1,0:T(8,128)(2,1)S(1)} %collective-permute-done.6), channel_id=1, source_target_pairs={{0,1},{1,2},{2,3},{3,4},{4,5},{5,6},{6,7},{7,8},{8,9},{9,10},{10,1... | collective-permute-start | bytes 1572872 | tf_op jit(solution)/shard_map/ppermute | solution.py:19
  83.1 2.2 %copy-start.7 = (bf16[2,1,1024,1024]{3,2,1,0:T(8,128)(2,1)S(1)}, bf16[2,1,1024,1024]{3,2,1,0:T(8,128)(2,1)}, u32[]{:S(2)}) copy-start(bf16[2,1,1024,1024]{3,2,1,0:T(8,128)(2,1)} %param.7) | copy-start | bytes 12582916
  83.1 3.5 %copy-start.8 = (f32[1024,1024]{1,0:T(8,128)S(1)}, f32[1024,1024]{1,0:T(8,128)}, u32[]{:S(2)}) copy-start(f32[1024,1024]{1,0:T(8,128)} %multiply_bitcast_fusion.2) | copy-start | bytes 12582916
  86.5 2.4 %copy-start = (f32[1,1024,1024]{2,1,0:T(8,128)S(1)}, f32[1,1024,1024]{2,1,0:T(8,128)}, u32[]{:S(2)}) copy-start(f32[1,1024,1024]{2,1,0:T(8,128)} %state_ref.1) | copy-start | bytes 12582916
  89.0 2.0 %copy-start.1 = (f32[1024,1024]{1,0:T(8,128)}, f32[1024,1024]{1,0:T(8,128)S(1)}, u32[]{:S(2)}) copy-start(f32[1024,1024]{1,0:T(8,128)S(1)} %multiply_multiply_fusion) | copy-start | bytes 12582916
  92.8 27.1 %all-to-all-start.1 = ((f32[32,1,2]{2,1,0:T(1,128)}), f32[32,1,2]{2,1,0:T(1,128)S(1)}, u32[]{:S(2)}, u32[]{:S(2)}) async-start(f32[32,1,2]{2,1,0:T(1,128)} %broadcast_in_dim.4), calls=%async_computation.1 | async-start | bytes 32768 | tf_op jit(solution)/shard_map/all_to_all | solution.py:28
  120.0 8.5 %copy-start.2 = (f32[2]{0:T(128)}, f32[2]{0:T(128)S(1)}, u32[]{:S(2)}) copy-start(f32[2]{0:T(128)S(1)} %compare_select_fusion) | copy-start | bytes 28

commit v20 on v19

--- a/solution.py
+++ b/solution.py
@@ -43,8 +43,9 @@
     @pl.when(step * rows < row_limit)
     def _():
         x = state_ref[0]
+        row_ids = step * rows + lax.broadcasted_iota(jnp.int32, (rows, cols), 0)
         col_ids = lax.broadcasted_iota(jnp.int32, (rows, cols), 1)
-        x = jnp.where(col_ids < col_limit, x, 0.0)
+        x = jnp.where((row_ids < row_limit) & (col_ids < col_limit), x, 0.0)
         acc_ref[...] += jnp.sum((x * x).reshape(rows // 8, 8, cols), axis=0)
 
     @pl.when(step == pl.num_programs(0) - 1)
@@ -55,7 +56,7 @@
 def masked_square_sum(pairs, block_index, left_live, right_live, state):
     count = lax.axis_size(AXES)
     sec_size = state.shape[1]
-    rows = BLOCK // 2
+    rows = 2 * BLOCK
     return pl.pallas_call(
         functools.partial(square_sum_kernel, pairs),
         grid_spec=pltpu.PrefetchScalarGridSpec(

time: 129 us -> 127 us (0.984)
  Pallas kernels: 6.2 us -> 3.77 us
    pallas_call x1, Pallas kernels: 6.2 us -> 3.77 us  [masked_square_sum(): pl.pallas_call(functools.partial(square_sum_kernel, pairs), grid_spec=plt...]
where the time goes in v20:
time: 127 us; the launch traced here: 126 us
  starting transfers between devices  46.8 us (37%)
  waiting for transfers between devices  28.2 us (22%)
  other arithmetic  18 us (14%)
  matrix products  17.6 us (14%)
  local copies, waits for them, and re-layouts  7.05 us (6%)
  between operations  5.07 us (4%)
  Pallas kernels  3.77 us (3%)
    all_to_all x2, starting transfers between devices, exchange_sum(): return jnp.sum(lax.all_to_all(spread, AXES, 0, 0, tiled=True), axis=0)  27.4 us
    ppermute x8, waiting for transfers between devices, shift_up(): return lax.ppermute(block, AXES, route)  21.1 us
    ppermute x8, starting transfers between devices, shift_up(): return lax.ppermute(block, AXES, route)  19.4 us
    dot_general x1, matrix products, per_device(): jnp.dot(left_env[1, 0], part_one, preferred_element_type=jnp.float32)  9.38 us
    broadcast_in_dim x1, other arithmetic, per_device(): return (next_vector[None], coefficients)  7.81 us
    all_to_all x2, waiting for transfers between devices, exchange_sum(): return jnp.sum(lax.all_to_all(spread, AXES, 0, 0, tiled=True), axis=0)  7.09 us
    dot_general x4, matrix products, per_device(): jnp.dot(source, right_env[0, 0], preferred_element_type=jnp.float32)  5.79 us
    mul x1, other arithmetic, per_device(): masked = state[0] * live  4.61 us
  transfers between devices with their start and end apart: 10, of which 4 were waited for; matrix products, arithmetic and copies ran while one was open for 17% of the time, Pallas kernels for 0%

profile of v20, /device:TPU:0, one launch (start us, length us, event | category | flops | bytes accessed | tf_op | source)
XLA Modules:
  0.0 126.5 jit_solution(13857987165055150306)
XLA Ops:
  0.7 3.8 %shard_map.77 = f32[32,1,1]{2,1,0:T(1,128)} custom-call(s32[1]{0:T(128)} %bitcast.5.index_ref, s32[8]{0:T(128)} %left_ref.1, s32[10]{0:T(128)} %right_ref.1, f32[1,1024,1024]{2,1,0:T(8,128)} %state_ref.1), custom_call_target="tpu_custom_call" | custom-call | tf_op jit(solution)/shard_map/pallas_call | solution.py:60
  4.4 7.7 %all-to-all-start = ((f32[32,1,1]{2,1,0:T(1,128)}), f32[32,1,1]{2,1,0:T(1,128)S(1)}, u32[]{:S(2)}, u32[]{:S(2)}) async-start(f32[32,1,1]{2,1,0:T(1,128)} %shard_map.77), calls=%async_computation | async-start | bytes 32768 | tf_op jit(solution)/shard_map/all_to_all | solution.py:28
  16.2 4.6 %multiply_multiply_fusion.1 = f32[1024,1024]{1,0:T(8,128)} fusion(f32[1,1024,1024]{2,1,0:T(8,128)} %state_ref.1, f32[1024]{0:T(1024)S(1)} %get-tuple-element.20, f32[1024]{0:T(1024)S(1)} %get-tuple-element.19), kind=kLoop, calls=%fused_computation.2 | loop fusion | flops 2097152 | bytes 8396800 | tf_op jit(solution)/shard_map/mul | solution.py:99
  23.0 2.8 %fusion.49 = (bf16[256,1024]{1,0:T(8,128)(2,1)S(1)}, bf16[256,1024]{1,0:T(8,128)(2,1)S(1)}, bf16[256,1024]{1,0:T(8,128)(2,1)S(1)}, bf16[256,1024]{1,0:T(8,128)(2,1)S(1)}) fusion(f32[1024,1024]{1,0:T(8,128)} %multiply_multiply_fusion.1, f32[]{:T(128)S(6)} %sqrt.6), kind=kLoop, calls=%fused_computation.54 | loop fusion | flops 2097152 | bytes 6291460 | tf_op jit(solution)/shard_map/convert_element_type | solution.py:108
  25.7 4.5 %collective-permute-start = (bf16[256,1024]{1,0:T(8,128)(2,1)S(1)}, bf16[256,1024]{1,0:T(8,128)(2,1)}, u32[]{:S(2)}, u32[]{:S(2)}) collective-permute-start(bf16[256,1024]{1,0:T(8,128)(2,1)S(1)} %get-tuple-element.8), channel_id=1, source_target_pairs={{0,2},{1,3},{2,4},{3,5},{4,6},{5,7},{6,8},{7,9},{8,10},{9,11},{10,... | collective-permute-start | bytes 1572872 | tf_op jit(solution)/shard_map/ppermute | solution.py:19
  30.2 3.4 %collective-permute-start.4 = (bf16[256,1024]{1,0:T(8,128)(2,1)S(1)}, bf16[256,1024]{1,0:T(8,128)(2,1)}, u32[]{:S(2)}, u32[]{:S(2)}) collective-permute-start(bf16[256,1024]{1,0:T(8,128)(2,1)S(1)} %get-tuple-element.10), channel_id=1, source_target_pairs={{0,2},{1,3},{2,4},{3,5},{4,6},{5,7},{6,8},{7,9},{8,10},{9,11},{10,... | collective-permute-start | bytes 1572872 | tf_op jit(solution)/shard_map/ppermute | solution.py:19
  33.6 2.6 %collective-permute-start.2 = (bf16[256,1024]{1,0:T(8,128)(2,1)S(1)}, bf16[256,1024]{1,0:T(8,128)(2,1)S(1)}, u32[]{:S(2)}, u32[]{:S(2)}) collective-permute-start(bf16[256,1024]{1,0:T(8,128)(2,1)S(1)} %get-tuple-element.11), channel_id=1, source_target_pairs={{0,2},{1,3},{2,4},{3,5},{4,6},{5,7},{6,8},{7,9},{8,10},{9,11},{10,... | collective-permute-start | bytes 1572872 | tf_op jit(solution)/shard_map/ppermute | solution.py:19
  36.3 9.4 %multiply_bitcast_fusion.2 = f32[1024,1024]{1,0:T(8,128)} fusion(bf16[2,1,1024,1024]{3,2,1,0:T(8,128)(2,1)} %param.7, f32[]{:T(128)} %bitcast.8, bf16[256,1024]{1,0:T(8,128)(2,1)S(1)} %get-tuple-element.4, bf16[256,1024]{1,0:T(8,128)(2,1)S(1)} %get-tuple-element.10, bf16[256,1024]{1,0:T(8,128)(2,1)S(1)} %get-tuple-element.11, ...), kind=kOutput, calls=%fused_computation.7 | convolution fusion | flops 4305453056 | bytes 10486272 | tf_op jit(solution)/shard_map/dot_general | solution.py:127
  45.6 3.3 %collective-permute-start.6 = (bf16[256,1024]{1,0:T(8,128)(2,1)S(1)}, bf16[256,1024]{1,0:T(8,128)(2,1)S(1)}, u32[]{:S(2)}, u32[]{:S(2)}) collective-permute-start(bf16[256,1024]{1,0:T(8,128)(2,1)S(1)} %get-tuple-element.4), channel_id=1, source_target_pairs={{0,2},{1,3},{2,4},{3,5},{4,6},{5,7},{6,8},{7,9},{8,10},{9,11},{10,... | collective-permute-start | bytes 1572872 | tf_op jit(solution)/shard_map/ppermute | solution.py:19
  49.0 1.3 %collective-permute-start.1 = (bf16[256,1024]{1,0:T(8,128)(2,1)}, bf16[256,1024]{1,0:T(8,128)(2,1)S(1)}, u32[]{:S(2)}, u32[]{:S(2)}) collective-permute-start(bf16[256,1024]{1,0:T(8,128)(2,1)} %collective-permute-done), channel_id=1, source_target_pairs={{0,1},{1,2},{2,3},{3,4},{4,5},{5,6},{6,7},{7,8},{8,9},{9,10},{10,1... | collective-permute-start | bytes 1572872 | tf_op jit(solution)/shard_map/ppermute | solution.py:19
  50.3 2.6 %collective-permute-done.4 = bf16[256,1024]{1,0:T(8,128)(2,1)} collective-permute-done((bf16[256,1024]{1,0:T(8,128)(2,1)S(1)}, bf16[256,1024]{1,0:T(8,128)(2,1)}, u32[]{:S(2)}, u32[]{:S(2)}) %collective-permute-start.4) | collective-permute-done | bytes 524320 | tf_op jit(solution)/shard_map/ppermute | solution.py:19
  52.9 1.5 %collective-permute-start.5 = (bf16[256,1024]{1,0:T(8,128)(2,1)}, bf16[256,1024]{1,0:T(8,128)(2,1)S(1)}, u32[]{:S(2)}, u32[]{:S(2)}) collective-permute-start(bf16[256,1024]{1,0:T(8,128)(2,1)} %collective-permute-done.4), channel_id=1, source_target_pairs={{0,1},{1,2},{2,3},{3,4},{4,5},{5,6},{6,7},{7,8},{8,9},{9,10},{10,1... | collective-permute-start | bytes 1572872 | tf_op jit(solution)/shard_map/ppermute | solution.py:19
  55.6 8.5 %collective-permute-done.2 = bf16[256,1024]{1,0:T(8,128)(2,1)S(1)} collective-permute-done((bf16[256,1024]{1,0:T(8,128)(2,1)S(1)}, bf16[256,1024]{1,0:T(8,128)(2,1)S(1)}, u32[]{:S(2)}, u32[]{:S(2)}) %collective-permute-start.2) | collective-permute-done | bytes 524320 | tf_op jit(solution)/shard_map/ppermute | solution.py:19
  64.2 1.3 %collective-permute-start.3 = (bf16[256,1024]{1,0:T(8,128)(2,1)S(1)}, bf16[256,1024]{1,0:T(8,128)(2,1)S(1)}, u32[]{:S(2)}, u32[]{:S(2)}) collective-permute-start(bf16[256,1024]{1,0:T(8,128)(2,1)S(1)} %collective-permute-done.2), channel_id=1, source_target_pairs={{0,1},{1,2},{2,3},{3,4},{4,5},{5,6},{6,7},{7,8},{8,9},{9,10},{10,1... | collective-permute-start | bytes 1572872 | tf_op jit(solution)/shard_map/ppermute | solution.py:19
  65.5 9.9 %collective-permute-done.6 = bf16[256,1024]{1,0:T(8,128)(2,1)S(1)} collective-permute-done((bf16[256,1024]{1,0:T(8,128)(2,1)S(1)}, bf16[256,1024]{1,0:T(8,128)(2,1)S(1)}, u32[]{:S(2)}, u32[]{:S(2)}) %collective-permute-start.6) | collective-permute-done | bytes 524320 | tf_op jit(solution)/shard_map/ppermute | solution.py:19
  75.4 1.5 %collective-permute-start.7 = (bf16[256,1024]{1,0:T(8,128)(2,1)S(1)}, bf16[256,1024]{1,0:T(8,128)(2,1)S(1)}, u32[]{:S(2)}, u32[]{:S(2)}) collective-permute-start(bf16[256,1024]{1,0:T(8,128)(2,1)S(1)} %collective-permute-done.6), channel_id=1, source_target_pairs={{0,1},{1,2},{2,3},{3,4},{4,5},{5,6},{6,7},{7,8},{8,9},{9,10},{10,1... | collective-permute-start | bytes 1572872 | tf_op jit(solution)/shard_map/ppermute | solution.py:19
  76.9 2.5 %fusion.34 = bf16[256,1024]{1,0:T(8,128)(2,1)S(1)} fusion(bf16[2,1,1024,1024]{3,2,1,0:T(8,128)(2,1)} %param.8, bf16[256,1024]{1,0:T(8,128)(2,1)S(1)} %collective-permute-done.1, bf16[256,1024]{1,0:T(8,128)(2,1)} %collective-permute-done, f32[]{:T(128)S(6)} %select_n.79, f32[]{:T(128)S(6)} %select_n.71), kind=kOutput, calls=%fused_computation.43 | convolution fusion | flops 538705920 | bytes 3670024 | tf_op jit(solution)/shard_map/dot_general | solution.py:138
  79.4 1.8 %fusion.40 = bf16[256,1024]{1,0:T(8,128)(2,1)S(1)} fusion(bf16[2,1,1024,1024]{3,2,1,0:T(8,128)(2,1)S(1)} %copy-done.6, bf16[256,1024]{1,0:T(8,128)(2,1)S(1)} %collective-permute-done.5, bf16[256,1024]{1,0:T(8,128)(2,1)} %collective-permute-done.4, f32[]{:T(128)S(6)} %select_n.79, f32[]{:T(128)S(6)} %select_n.71), kind=kOutput, calls=%fused_computation.45 | convolution fusion | flops 538705920 | bytes 3670024 | tf_op jit(solution)/shard_map/dot_general | solution.py:138
  83.4 1.3 %copy-done.8 = f32[1024,1024]{1,0:T(8,128)S(1)} copy-done((f32[1024,1024]{1,0:T(8,128)S(1)}, f32[1024,1024]{1,0:T(8,128)}, u32[]{:S(2)}) %copy-start.8) | copy-done | bytes 4194328
  84.7 2.4 %multiply_multiply_fusion = f32[1024,1024]{1,0:T(8,128)S(1)} fusion(f32[1024,1024]{1,0:T(8,128)S(1)} %copy-done.8, bf16[256,1024]{1,0:T(8,128)(2,1)S(1)} %fusion.43, bf16[256,1024]{1,0:T(8,128)(2,1)S(1)} %fusion.40, bf16[256,1024]{1,0:T(8,128)(2,1)S(1)} %fusion.37, bf16[256,1024]{1,0:T(8,128)(2,1)S(1)} %fusion.34, ...), kind=kOutput, calls=%fused_computation.1 | convolution fusion | flops 2159017984 | bytes 12591104 | tf_op jit(solution)/shard_map/dot_general | solution.py:141
  89.2 1.2 maximum_reduce_fusion
  91.0 19.7 %all-to-all-start.1 = ((f32[32,1,2]{2,1,0:T(1,128)}), f32[32,1,2]{2,1,0:T(1,128)S(1)}, u32[]{:S(2)}, u32[]{:S(2)}) async-start(f32[32,1,2]{2,1,0:T(1,128)} %broadcast_in_dim.4), calls=%async_computation.1 | async-start | bytes 32768 | tf_op jit(solution)/shard_map/all_to_all | solution.py:28
  110.7 7.1 %all-to-all-done.1 = f32[32,1,2]{2,1,0:T(1,128)S(1)} async-done(((f32[32,1,2]{2,1,0:T(1,128)}), f32[32,1,2]{2,1,0:T(1,128)S(1)}, u32[]{:S(2)}, u32[]{:S(2)}) %all-to-all-start.1) | async-done | bytes 288 | tf_op jit(solution)/shard_map/all_to_all | solution.py:28
  118.6 7.8 %divide_bitcast_fusion = f32[1,1024,1024]{2,1,0:T(8,128)} fusion(f32[1024,1024]{1,0:T(8,128)} %copy-done.1, f32[]{:T(128)} %bitcast.17, f32[]{:T(128)} %bitcast.16, f32[]{:T(128)S(6)} %sqrt.6, f32[1024]{0:T(1024)S(1)} %get-tuple-element.20, f32[1024]{0:T(1024)S(1)} %get-tuple-element.19, f32[1,1024,1024]{2,1,0:T(8,128)} %state_ref.1), kind=kLoop, calls=%fused_computation.4 | loop fusion | flops 6291456 | bytes 12591116 | tf_op jit(solution)/shard_map/broadcast_in_dim | solution.py:154
  (39 shorter events, 8.9 us)
Async XLA Ops:
  0.6 13.6 %copy-start.5 = (s32[10]{0:T(128)S(1)}, s32[10]{0:T(128)}, u32[]{:S(2)}) copy-start(s32[10]{0:T(128)} %right_ref.1) | copy-start | bytes 124
  0.6 11.6 %copy-start.4 = (s32[8]{0:T(128)S(1)}, s32[8]{0:T(128)}, u32[]{:S(2)}) copy-start(s32[8]{0:T(128)} %left_ref.1) | copy-start | bytes 100
  0.7 15.6 %copy-start.3 = (f32[2,4,4]{2,1,0:T(4,128)S(1)}, f32[2,4,4]{2,1,0:T(4,128)}, u32[]{:S(2)}) copy-start(f32[2,4,4]{2,1,0:T(4,128)} %param.9) | copy-start | bytes 388
  4.4 17.1 %all-to-all-start = ((f32[32,1,1]{2,1,0:T(1,128)}), f32[32,1,1]{2,1,0:T(1,128)S(1)}, u32[]{:S(2)}, u32[]{:S(2)}) async-start(f32[32,1,1]{2,1,0:T(1,128)} %shard_map.77), calls=%async_computation | async-start | bytes 32768 | tf_op jit(solution)/shard_map/all_to_all | solution.py:28
  25.7 23.2 %collective-permute-start = (bf16[256,1024]{1,0:T(8,128)(2,1)S(1)}, bf16[256,1024]{1,0:T(8,128)(2,1)}, u32[]{:S(2)}, u32[]{:S(2)}) collective-permute-start(bf16[256,1024]{1,0:T(8,128)(2,1)S(1)} %get-tuple-element.8), channel_id=1, source_target_pairs={{0,2},{1,3},{2,4},{3,5},{4,6},{5,7},{6,8},{7,9},{8,10},{9,11},{10,... | collective-permute-start | bytes 1572872 | tf_op jit(solution)/shard_map/ppermute | solution.py:19
  30.2 22.7 %collective-permute-start.4 = (bf16[256,1024]{1,0:T(8,128)(2,1)S(1)}, bf16[256,1024]{1,0:T(8,128)(2,1)}, u32[]{:S(2)}, u32[]{:S(2)}) collective-permute-start(bf16[256,1024]{1,0:T(8,128)(2,1)S(1)} %get-tuple-element.10), channel_id=1, source_target_pairs={{0,2},{1,3},{2,4},{3,5},{4,6},{5,7},{6,8},{7,9},{8,10},{9,11},{10,... | collective-permute-start | bytes 1572872 | tf_op jit(solution)/shard_map/ppermute | solution.py:19
  33.6 30.5 %collective-permute-start.2 = (bf16[256,1024]{1,0:T(8,128)(2,1)S(1)}, bf16[256,1024]{1,0:T(8,128)(2,1)S(1)}, u32[]{:S(2)}, u32[]{:S(2)}) collective-permute-start(bf16[256,1024]{1,0:T(8,128)(2,1)S(1)} %get-tuple-element.11), channel_id=1, source_target_pairs={{0,2},{1,3},{2,4},{3,5},{4,6},{5,7},{6,8},{7,9},{8,10},{9,11},{10,... | collective-permute-start | bytes 1572872 | tf_op jit(solution)/shard_map/ppermute | solution.py:19
  45.6 29.8 %collective-permute-start.6 = (bf16[256,1024]{1,0:T(8,128)(2,1)S(1)}, bf16[256,1024]{1,0:T(8,128)(2,1)S(1)}, u32[]{:S(2)}, u32[]{:S(2)}) collective-permute-start(bf16[256,1024]{1,0:T(8,128)(2,1)S(1)} %get-tuple-element.4), channel_id=1, source_target_pairs={{0,2},{1,3},{2,4},{3,5},{4,6},{5,7},{6,8},{7,9},{8,10},{9,11},{10,... | collective-permute-start | bytes 1572872 | tf_op jit(solution)/shard_map/ppermute | solution.py:19
  49.0 27.9 %collective-permute-start.1 = (bf16[256,1024]{1,0:T(8,128)(2,1)}, bf16[256,1024]{1,0:T(8,128)(2,1)S(1)}, u32[]{:S(2)}, u32[]{:S(2)}) collective-permute-start(bf16[256,1024]{1,0:T(8,128)(2,1)} %collective-permute-done), channel_id=1, source_target_pairs={{0,1},{1,2},{2,3},{3,4},{4,5},{5,6},{6,7},{7,8},{8,9},{9,10},{10,1... | collective-permute-start | bytes 1572872 | tf_op jit(solution)/shard_map/ppermute | solution.py:19
  52.9 26.5 %collective-permute-start.5 = (bf16[256,1024]{1,0:T(8,128)(2,1)}, bf16[256,1024]{1,0:T(8,128)(2,1)S(1)}, u32[]{:S(2)}, u32[]{:S(2)}) collective-permute-start(bf16[256,1024]{1,0:T(8,128)(2,1)} %collective-permute-done.4), channel_id=1, source_target_pairs={{0,1},{1,2},{2,3},{3,4},{4,5},{5,6},{6,7},{7,8},{8,9},{9,10},{10,1... | collective-permute-start | bytes 1572872 | tf_op jit(solution)/shard_map/ppermute | solution.py:19
  55.6 23.8 %copy-start.6 = (bf16[2,1,1024,1024]{3,2,1,0:T(8,128)(2,1)S(1)}, bf16[2,1,1024,1024]{3,2,1,0:T(8,128)(2,1)}, u32[]{:S(2)}) copy-start(bf16[2,1,1024,1024]{3,2,1,0:T(8,128)(2,1)} %param.8) | copy-start | bytes 12582916
  64.2 17.1 %collective-permute-start.3 = (bf16[256,1024]{1,0:T(8,128)(2,1)S(1)}, bf16[256,1024]{1,0:T(8,128)(2,1)S(1)}, u32[]{:S(2)}, u32[]{:S(2)}) collective-permute-start(bf16[256,1024]{1,0:T(8,128)(2,1)S(1)} %collective-permute-done.2), channel_id=1, source_target_pairs={{0,1},{1,2},{2,3},{3,4},{4,5},{5,6},{6,7},{7,8},{8,9},{9,10},{10,1... | collective-permute-start | bytes 1572872 | tf_op jit(solution)/shard_map/ppermute | solution.py:19
  75.4 6.6 %collective-permute-start.7 = (bf16[256,1024]{1,0:T(8,128)(2,1)S(1)}, bf16[256,1024]{1,0:T(8,128)(2,1)S(1)}, u32[]{:S(2)}, u32[]{:S(2)}) collective-permute-start(bf16[256,1024]{1,0:T(8,128)(2,1)S(1)} %collective-permute-done.6), channel_id=1, source_target_pairs={{0,1},{1,2},{2,3},{3,4},{4,5},{5,6},{6,7},{7,8},{8,9},{9,10},{10,1... | collective-permute-start | bytes 1572872 | tf_op jit(solution)/shard_map/ppermute | solution.py:19
  81.2 2.2 %copy-start.7 = (bf16[2,1,1024,1024]{3,2,1,0:T(8,128)(2,1)S(1)}, bf16[2,1,1024,1024]{3,2,1,0:T(8,128)(2,1)}, u32[]{:S(2)}) copy-start(bf16[2,1,1024,1024]{3,2,1,0:T(8,128)(2,1)} %param.7) | copy-start | bytes 12582916
  81.2 3.5 %copy-start.8 = (f32[1024,1024]{1,0:T(8,128)S(1)}, f32[1024,1024]{1,0:T(8,128)}, u32[]{:S(2)}) copy-start(f32[1024,1024]{1,0:T(8,128)} %multiply_bitcast_fusion.2) | copy-start | bytes 12582916
  84.7 2.4 %copy-start = (f32[1,1024,1024]{2,1,0:T(8,128)S(1)}, f32[1,1024,1024]{2,1,0:T(8,128)}, u32[]{:S(2)}) copy-start(f32[1,1024,1024]{2,1,0:T(8,128)} %state_ref.1) | copy-start | bytes 12582916
  87.2 2.0 %copy-start.1 = (f32[1024,1024]{1,0:T(8,128)}, f32[1024,1024]{1,0:T(8,128)S(1)}, u32[]{:S(2)}) copy-start(f32[1024,1024]{1,0:T(8,128)S(1)} %multiply_multiply_fusion) | copy-start | bytes 12582916
  91.0 26.9 %all-to-all-start.1 = ((f32[32,1,2]{2,1,0:T(1,128)}), f32[32,1,2]{2,1,0:T(1,128)S(1)}, u32[]{:S(2)}, u32[]{:S(2)}) async-start(f32[32,1,2]{2,1,0:T(1,128)} %broadcast_in_dim.4), calls=%async_computation.1 | async-start | bytes 32768 | tf_op jit(solution)/shard_map/all_to_all | solution.py:28
  118.0 8.5 %copy-start.2 = (f32[2]{0:T(128)}, f32[2]{0:T(128)S(1)}, u32[]{:S(2)}) copy-start(f32[2]{0:T(128)S(1)} %compare_select_fusion) | copy-start | bytes 28

commit v21 on v20

--- a/solution.py
+++ b/solution.py
@@ -43,9 +43,9 @@
     @pl.when(step * rows < row_limit)
     def _():
         x = state_ref[0]
-        row_ids = step * rows + lax.broadcasted_iota(jnp.int32, (rows, cols), 0)
-        col_ids = lax.broadcasted_iota(jnp.int32, (rows, cols), 1)
-        x = jnp.where((row_ids < row_limit) & (col_ids < col_limit), x, 0.0)
+        row_live = step * rows + lax.broadcasted_iota(jnp.int32, (rows, 1), 0) < row_limit
+        col_live = lax.broadcasted_iota(jnp.int32, (1, cols), 1) < col_limit
+        x = jnp.where(row_live & col_live, x, 0.0)
         acc_ref[...] += jnp.sum((x * x).reshape(rows // 8, 8, cols), axis=0)
 
     @pl.when(step == pl.num_programs(0) - 1)

time: 127 us -> 127 us (level)
  no operation moved by 1% of the time
where the time goes in v21:
time: 127 us; the launch traced here: 126 us
  starting transfers between devices  46.4 us (37%)
  waiting for transfers between devices  28.2 us (22%)
  other arithmetic  18 us (14%)
  matrix products  17.6 us (14%)
  local copies, waits for them, and re-layouts  7.05 us (6%)
  between operations  5.07 us (4%)
  Pallas kernels  4.16 us (3%)
    all_to_all x2, starting transfers between devices, exchange_sum(): return jnp.sum(lax.all_to_all(spread, AXES, 0, 0, tiled=True), axis=0)  27 us
    ppermute x8, waiting for transfers between devices, shift_up(): return lax.ppermute(block, AXES, route)  21.1 us
    ppermute x8, starting transfers between devices, shift_up(): return lax.ppermute(block, AXES, route)  19.4 us
    dot_general x1, matrix products, per_device(): jnp.dot(left_env[1, 0], part_one, preferred_element_type=jnp.float32)  9.38 us
    broadcast_in_dim x1, other arithmetic, per_device(): return (next_vector[None], coefficients)  7.81 us
    all_to_all x2, waiting for transfers between devices, exchange_sum(): return jnp.sum(lax.all_to_all(spread, AXES, 0, 0, tiled=True), axis=0)  7.09 us
    dot_general x4, matrix products, per_device(): jnp.dot(source, right_env[0, 0], preferred_element_type=jnp.float32)  5.79 us
    mul x1, other arithmetic, per_device(): masked = state[0] * live  4.61 us
  transfers between devices with their start and end apart: 10, of which 4 were waited for; matrix products, arithmetic and copies ran while one was open for 17% of the time, Pallas kernels for 0%

profile of v21, /device:TPU:0, one launch (start us, length us, event | category | flops | bytes accessed | tf_op | source)
XLA Modules:
  0.0 126.5 jit_solution(13857987165055150306)
XLA Ops:
  0.7 4.2 %shard_map.77 = f32[32,1,1]{2,1,0:T(1,128)} custom-call(s32[1]{0:T(128)} %bitcast.5.index_ref, s32[8]{0:T(128)} %left_ref.1, s32[10]{0:T(128)} %right_ref.1, f32[1,1024,1024]{2,1,0:T(8,128)} %state_ref.1), custom_call_target="tpu_custom_call" | custom-call | tf_op jit(solution)/shard_map/pallas_call | solution.py:60
  4.8 7.3 %all-to-all-start = ((f32[32,1,1]{2,1,0:T(1,128)}), f32[32,1,1]{2,1,0:T(1,128)S(1)}, u32[]{:S(2)}, u32[]{:S(2)}) async-start(f32[32,1,1]{2,1,0:T(1,128)} %shard_map.77), calls=%async_computation | async-start | bytes 32768 | tf_op jit(solution)/shard_map/all_to_all | solution.py:28
  16.2 4.6 %multiply_multiply_fusion.1 = f32[1024,1024]{1,0:T(8,128)} fusion(f32[1,1024,1024]{2,1,0:T(8,128)} %state_ref.1, f32[1024]{0:T(1024)S(1)} %get-tuple-element.20, f32[1024]{0:T(1024)S(1)} %get-tuple-element.19), kind=kLoop, calls=%fused_computation.2 | loop fusion | flops 2097152 | bytes 8396800 | tf_op jit(solution)/shard_map/mul | solution.py:99
  23.0 2.8 %fusion.49 = (bf16[256,1024]{1,0:T(8,128)(2,1)S(1)}, bf16[256,1024]{1,0:T(8,128)(2,1)S(1)}, bf16[256,1024]{1,0:T(8,128)(2,1)S(1)}, bf16[256,1024]{1,0:T(8,128)(2,1)S(1)}) fusion(f32[1024,1024]{1,0:T(8,128)} %multiply_multiply_fusion.1, f32[]{:T(128)S(6)} %sqrt.6), kind=kLoop, calls=%fused_computation.54 | loop fusion | flops 2097152 | bytes 6291460 | tf_op jit(solution)/shard_map/convert_element_type | solution.py:108
  25.7 4.5 %collective-permute-start = (bf16[256,1024]{1,0:T(8,128)(2,1)S(1)}, bf16[256,1024]{1,0:T(8,128)(2,1)}, u32[]{:S(2)}, u32[]{:S(2)}) collective-permute-start(bf16[256,1024]{1,0:T(8,128)(2,1)S(1)} %get-tuple-element.8), channel_id=1, source_target_pairs={{0,2},{1,3},{2,4},{3,5},{4,6},{5,7},{6,8},{7,9},{8,10},{9,11},{10,... | collective-permute-start | bytes 1572872 | tf_op jit(solution)/shard_map/ppermute | solution.py:19
  30.2 3.4 %collective-permute-start.4 = (bf16[256,1024]{1,0:T(8,128)(2,1)S(1)}, bf16[256,1024]{1,0:T(8,128)(2,1)}, u32[]{:S(2)}, u32[]{:S(2)}) collective-permute-start(bf16[256,1024]{1,0:T(8,128)(2,1)S(1)} %get-tuple-element.10), channel_id=1, source_target_pairs={{0,2},{1,3},{2,4},{3,5},{4,6},{5,7},{6,8},{7,9},{8,10},{9,11},{10,... | collective-permute-start | bytes 1572872 | tf_op jit(solution)/shard_map/ppermute | solution.py:19
  33.6 2.6 %collective-permute-start.2 = (bf16[256,1024]{1,0:T(8,128)(2,1)S(1)}, bf16[256,1024]{1,0:T(8,128)(2,1)S(1)}, u32[]{:S(2)}, u32[]{:S(2)}) collective-permute-start(bf16[256,1024]{1,0:T(8,128)(2,1)S(1)} %get-tuple-element.11), channel_id=1, source_target_pairs={{0,2},{1,3},{2,4},{3,5},{4,6},{5,7},{6,8},{7,9},{8,10},{9,11},{10,... | collective-permute-start | bytes 1572872 | tf_op jit(solution)/shard_map/ppermute | solution.py:19
  36.3 9.4 %multiply_bitcast_fusion.2 = f32[1024,1024]{1,0:T(8,128)} fusion(bf16[2,1,1024,1024]{3,2,1,0:T(8,128)(2,1)} %param.7, f32[]{:T(128)} %bitcast.8, bf16[256,1024]{1,0:T(8,128)(2,1)S(1)} %get-tuple-element.4, bf16[256,1024]{1,0:T(8,128)(2,1)S(1)} %get-tuple-element.10, bf16[256,1024]{1,0:T(8,128)(2,1)S(1)} %get-tuple-element.11, ...), kind=kOutput, calls=%fused_computation.7 | convolution fusion | flops 4305453056 | bytes 10486272 | tf_op jit(solution)/shard_map/dot_general | solution.py:127
  45.6 3.3 %collective-permute-start.6 = (bf16[256,1024]{1,0:T(8,128)(2,1)S(1)}, bf16[256,1024]{1,0:T(8,128)(2,1)S(1)}, u32[]{:S(2)}, u32[]{:S(2)}) collective-permute-start(bf16[256,1024]{1,0:T(8,128)(2,1)S(1)} %get-tuple-element.4), channel_id=1, source_target_pairs={{0,2},{1,3},{2,4},{3,5},{4,6},{5,7},{6,8},{7,9},{8,10},{9,11},{10,... | collective-permute-start | bytes 1572872 | tf_op jit(solution)/shard_map/ppermute | solution.py:19
  49.0 1.3 %collective-permute-start.1 = (bf16[256,1024]{1,0:T(8,128)(2,1)}, bf16[256,1024]{1,0:T(8,128)(2,1)S(1)}, u32[]{:S(2)}, u32[]{:S(2)}) collective-permute-start(bf16[256,1024]{1,0:T(8,128)(2,1)} %collective-permute-done), channel_id=1, source_target_pairs={{0,1},{1,2},{2,3},{3,4},{4,5},{5,6},{6,7},{7,8},{8,9},{9,10},{10,1... | collective-permute-start | bytes 1572872 | tf_op jit(solution)/shard_map/ppermute | solution.py:19
  50.3 2.6 %collective-permute-done.4 = bf16[256,1024]{1,0:T(8,128)(2,1)} collective-permute-done((bf16[256,1024]{1,0:T(8,128)(2,1)S(1)}, bf16[256,1024]{1,0:T(8,128)(2,1)}, u32[]{:S(2)}, u32[]{:S(2)}) %collective-permute-start.4) | collective-permute-done | bytes 524320 | tf_op jit(solution)/shard_map/ppermute | solution.py:19
  52.9 1.5 %collective-permute-start.5 = (bf16[256,1024]{1,0:T(8,128)(2,1)}, bf16[256,1024]{1,0:T(8,128)(2,1)S(1)}, u32[]{:S(2)}, u32[]{:S(2)}) collective-permute-start(bf16[256,1024]{1,0:T(8,128)(2,1)} %collective-permute-done.4), channel_id=1, source_target_pairs={{0,1},{1,2},{2,3},{3,4},{4,5},{5,6},{6,7},{7,8},{8,9},{9,10},{10,1... | collective-permute-start | bytes 1572872 | tf_op jit(solution)/shard_map/ppermute | solution.py:19
  55.6 8.5 %collective-permute-done.2 = bf16[256,1024]{1,0:T(8,128)(2,1)S(1)} collective-permute-done((bf16[256,1024]{1,0:T(8,128)(2,1)S(1)}, bf16[256,1024]{1,0:T(8,128)(2,1)S(1)}, u32[]{:S(2)}, u32[]{:S(2)}) %collective-permute-start.2) | collective-permute-done | bytes 524320 | tf_op jit(solution)/shard_map/ppermute | solution.py:19
  64.2 1.3 %collective-permute-start.3 = (bf16[256,1024]{1,0:T(8,128)(2,1)S(1)}, bf16[256,1024]{1,0:T(8,128)(2,1)S(1)}, u32[]{:S(2)}, u32[]{:S(2)}) collective-permute-start(bf16[256,1024]{1,0:T(8,128)(2,1)S(1)} %collective-permute-done.2), channel_id=1, source_target_pairs={{0,1},{1,2},{2,3},{3,4},{4,5},{5,6},{6,7},{7,8},{8,9},{9,10},{10,1... | collective-permute-start | bytes 1572872 | tf_op jit(solution)/shard_map/ppermute | solution.py:19
  65.5 9.9 %collective-permute-done.6 = bf16[256,1024]{1,0:T(8,128)(2,1)S(1)} collective-permute-done((bf16[256,1024]{1,0:T(8,128)(2,1)S(1)}, bf16[256,1024]{1,0:T(8,128)(2,1)S(1)}, u32[]{:S(2)}, u32[]{:S(2)}) %collective-permute-start.6) | collective-permute-done | bytes 524320 | tf_op jit(solution)/shard_map/ppermute | solution.py:19
  75.4 1.5 %collective-permute-start.7 = (bf16[256,1024]{1,0:T(8,128)(2,1)S(1)}, bf16[256,1024]{1,0:T(8,128)(2,1)S(1)}, u32[]{:S(2)}, u32[]{:S(2)}) collective-permute-start(bf16[256,1024]{1,0:T(8,128)(2,1)S(1)} %collective-permute-done.6), channel_id=1, source_target_pairs={{0,1},{1,2},{2,3},{3,4},{4,5},{5,6},{6,7},{7,8},{8,9},{9,10},{10,1... | collective-permute-start | bytes 1572872 | tf_op jit(solution)/shard_map/ppermute | solution.py:19
  76.9 2.5 %fusion.34 = bf16[256,1024]{1,0:T(8,128)(2,1)S(1)} fusion(bf16[2,1,1024,1024]{3,2,1,0:T(8,128)(2,1)} %param.8, bf16[256,1024]{1,0:T(8,128)(2,1)S(1)} %collective-permute-done.1, bf16[256,1024]{1,0:T(8,128)(2,1)} %collective-permute-done, f32[]{:T(128)S(6)} %select_n.79, f32[]{:T(128)S(6)} %select_n.71), kind=kOutput, calls=%fused_computation.43 | convolution fusion | flops 538705920 | bytes 3670024 | tf_op jit(solution)/shard_map/dot_general | solution.py:138
  79.4 1.8 %fusion.40 = bf16[256,1024]{1,0:T(8,128)(2,1)S(1)} fusion(bf16[2,1,1024,1024]{3,2,1,0:T(8,128)(2,1)S(1)} %copy-done.6, bf16[256,1024]{1,0:T(8,128)(2,1)S(1)} %collective-permute-done.5, bf16[256,1024]{1,0:T(8,128)(2,1)} %collective-permute-done.4, f32[]{:T(128)S(6)} %select_n.79, f32[]{:T(128)S(6)} %select_n.71), kind=kOutput, calls=%fused_computation.45 | convolution fusion | flops 538705920 | bytes 3670024 | tf_op jit(solution)/shard_map/dot_general | solution.py:138
  83.4 1.3 %copy-done.8 = f32[1024,1024]{1,0:T(8,128)S(1)} copy-done((f32[1024,1024]{1,0:T(8,128)S(1)}, f32[1024,1024]{1,0:T(8,128)}, u32[]{:S(2)}) %copy-start.8) | copy-done | bytes 4194328
  84.7 2.4 %multiply_multiply_fusion = f32[1024,1024]{1,0:T(8,128)S(1)} fusion(f32[1024,1024]{1,0:T(8,128)S(1)} %copy-done.8, bf16[256,1024]{1,0:T(8,128)(2,1)S(1)} %fusion.43, bf16[256,1024]{1,0:T(8,128)(2,1)S(1)} %fusion.40, bf16[256,1024]{1,0:T(8,128)(2,1)S(1)} %fusion.37, bf16[256,1024]{1,0:T(8,128)(2,1)S(1)} %fusion.34, ...), kind=kOutput, calls=%fused_computation.1 | convolution fusion | flops 2159017984 | bytes 12591104 | tf_op jit(solution)/shard_map/dot_general | solution.py:141
  89.2 1.2 maximum_reduce_fusion
  91.0 19.7 %all-to-all-start.1 = ((f32[32,1,2]{2,1,0:T(1,128)}), f32[32,1,2]{2,1,0:T(1,128)S(1)}, u32[]{:S(2)}, u32[]{:S(2)}) async-start(f32[32,1,2]{2,1,0:T(1,128)} %broadcast_in_dim.4), calls=%async_computation.1 | async-start | bytes 32768 | tf_op jit(solution)/shard_map/all_to_all | solution.py:28
  110.7 7.1 %all-to-all-done.1 = f32[32,1,2]{2,1,0:T(1,128)S(1)} async-done(((f32[32,1,2]{2,1,0:T(1,128)}), f32[32,1,2]{2,1,0:T(1,128)S(1)}, u32[]{:S(2)}, u32[]{:S(2)}) %all-to-all-start.1) | async-done | bytes 288 | tf_op jit(solution)/shard_map/all_to_all | solution.py:28
  118.6 7.8 %divide_bitcast_fusion = f32[1,1024,1024]{2,1,0:T(8,128)} fusion(f32[1024,1024]{1,0:T(8,128)} %copy-done.1, f32[]{:T(128)} %bitcast.17, f32[]{:T(128)} %bitcast.16, f32[]{:T(128)S(6)} %sqrt.6, f32[1024]{0:T(1024)S(1)} %get-tuple-element.20, f32[1024]{0:T(1024)S(1)} %get-tuple-element.19, f32[1,1024,1024]{2,1,0:T(8,128)} %state_ref.1), kind=kLoop, calls=%fused_computation.4 | loop fusion | flops 6291456 | bytes 12591116 | tf_op jit(solution)/shard_map/broadcast_in_dim | solution.py:154
  (39 shorter events, 8.9 us)
Async XLA Ops:
  0.6 13.6 %copy-start.5 = (s32[10]{0:T(128)S(1)}, s32[10]{0:T(128)}, u32[]{:S(2)}) copy-start(s32[10]{0:T(128)} %right_ref.1) | copy-start | bytes 124
  0.6 11.6 %copy-start.4 = (s32[8]{0:T(128)S(1)}, s32[8]{0:T(128)}, u32[]{:S(2)}) copy-start(s32[8]{0:T(128)} %left_ref.1) | copy-start | bytes 100
  0.7 15.6 %copy-start.3 = (f32[2,4,4]{2,1,0:T(4,128)S(1)}, f32[2,4,4]{2,1,0:T(4,128)}, u32[]{:S(2)}) copy-start(f32[2,4,4]{2,1,0:T(4,128)} %param.9) | copy-start | bytes 388
  4.8 16.7 %all-to-all-start = ((f32[32,1,1]{2,1,0:T(1,128)}), f32[32,1,1]{2,1,0:T(1,128)S(1)}, u32[]{:S(2)}, u32[]{:S(2)}) async-start(f32[32,1,1]{2,1,0:T(1,128)} %shard_map.77), calls=%async_computation | async-start | bytes 32768 | tf_op jit(solution)/shard_map/all_to_all | solution.py:28
  25.7 23.2 %collective-permute-start = (bf16[256,1024]{1,0:T(8,128)(2,1)S(1)}, bf16[256,1024]{1,0:T(8,128)(2,1)}, u32[]{:S(2)}, u32[]{:S(2)}) collective-permute-start(bf16[256,1024]{1,0:T(8,128)(2,1)S(1)} %get-tuple-element.8), channel_id=1, source_target_pairs={{0,2},{1,3},{2,4},{3,5},{4,6},{5,7},{6,8},{7,9},{8,10},{9,11},{10,... | collective-permute-start | bytes 1572872 | tf_op jit(solution)/shard_map/ppermute | solution.py:19
  30.2 22.7 %collective-permute-start.4 = (bf16[256,1024]{1,0:T(8,128)(2,1)S(1)}, bf16[256,1024]{1,0:T(8,128)(2,1)}, u32[]{:S(2)}, u32[]{:S(2)}) collective-permute-start(bf16[256,1024]{1,0:T(8,128)(2,1)S(1)} %get-tuple-element.10), channel_id=1, source_target_pairs={{0,2},{1,3},{2,4},{3,5},{4,6},{5,7},{6,8},{7,9},{8,10},{9,11},{10,... | collective-permute-start | bytes 1572872 | tf_op jit(solution)/shard_map/ppermute | solution.py:19
  33.6 30.5 %collective-permute-start.2 = (bf16[256,1024]{1,0:T(8,128)(2,1)S(1)}, bf16[256,1024]{1,0:T(8,128)(2,1)S(1)}, u32[]{:S(2)}, u32[]{:S(2)}) collective-permute-start(bf16[256,1024]{1,0:T(8,128)(2,1)S(1)} %get-tuple-element.11), channel_id=1, source_target_pairs={{0,2},{1,3},{2,4},{3,5},{4,6},{5,7},{6,8},{7,9},{8,10},{9,11},{10,... | collective-permute-start | bytes 1572872 | tf_op jit(solution)/shard_map/ppermute | solution.py:19
  45.6 29.8 %collective-permute-start.6 = (bf16[256,1024]{1,0:T(8,128)(2,1)S(1)}, bf16[256,1024]{1,0:T(8,128)(2,1)S(1)}, u32[]{:S(2)}, u32[]{:S(2)}) collective-permute-start(bf16[256,1024]{1,0:T(8,128)(2,1)S(1)} %get-tuple-element.4), channel_id=1, source_target_pairs={{0,2},{1,3},{2,4},{3,5},{4,6},{5,7},{6,8},{7,9},{8,10},{9,11},{10,... | collective-permute-start | bytes 1572872 | tf_op jit(solution)/shard_map/ppermute | solution.py:19
  49.0 27.9 %collective-permute-start.1 = (bf16[256,1024]{1,0:T(8,128)(2,1)}, bf16[256,1024]{1,0:T(8,128)(2,1)S(1)}, u32[]{:S(2)}, u32[]{:S(2)}) collective-permute-start(bf16[256,1024]{1,0:T(8,128)(2,1)} %collective-permute-done), channel_id=1, source_target_pairs={{0,1},{1,2},{2,3},{3,4},{4,5},{5,6},{6,7},{7,8},{8,9},{9,10},{10,1... | collective-permute-start | bytes 1572872 | tf_op jit(solution)/shard_map/ppermute | solution.py:19
  52.9 26.5 %collective-permute-start.5 = (bf16[256,1024]{1,0:T(8,128)(2,1)}, bf16[256,1024]{1,0:T(8,128)(2,1)S(1)}, u32[]{:S(2)}, u32[]{:S(2)}) collective-permute-start(bf16[256,1024]{1,0:T(8,128)(2,1)} %collective-permute-done.4), channel_id=1, source_target_pairs={{0,1},{1,2},{2,3},{3,4},{4,5},{5,6},{6,7},{7,8},{8,9},{9,10},{10,1... | collective-permute-start | bytes 1572872 | tf_op jit(solution)/shard_map/ppermute | solution.py:19
  55.6 23.8 %copy-start.6 = (bf16[2,1,1024,1024]{3,2,1,0:T(8,128)(2,1)S(1)}, bf16[2,1,1024,1024]{3,2,1,0:T(8,128)(2,1)}, u32[]{:S(2)}) copy-start(bf16[2,1,1024,1024]{3,2,1,0:T(8,128)(2,1)} %param.8) | copy-start | bytes 12582916
  64.2 17.1 %collective-permute-start.3 = (bf16[256,1024]{1,0:T(8,128)(2,1)S(1)}, bf16[256,1024]{1,0:T(8,128)(2,1)S(1)}, u32[]{:S(2)}, u32[]{:S(2)}) collective-permute-start(bf16[256,1024]{1,0:T(8,128)(2,1)S(1)} %collective-permute-done.2), channel_id=1, source_target_pairs={{0,1},{1,2},{2,3},{3,4},{4,5},{5,6},{6,7},{7,8},{8,9},{9,10},{10,1... | collective-permute-start | bytes 1572872 | tf_op jit(solution)/shard_map/ppermute | solution.py:19
  75.4 6.6 %collective-permute-start.7 = (bf16[256,1024]{1,0:T(8,128)(2,1)S(1)}, bf16[256,1024]{1,0:T(8,128)(2,1)S(1)}, u32[]{:S(2)}, u32[]{:S(2)}) collective-permute-start(bf16[256,1024]{1,0:T(8,128)(2,1)S(1)} %collective-permute-done.6), channel_id=1, source_target_pairs={{0,1},{1,2},{2,3},{3,4},{4,5},{5,6},{6,7},{7,8},{8,9},{9,10},{10,1... | collective-permute-start | bytes 1572872 | tf_op jit(solution)/shard_map/ppermute | solution.py:19
  81.2 2.2 %copy-start.7 = (bf16[2,1,1024,1024]{3,2,1,0:T(8,128)(2,1)S(1)}, bf16[2,1,1024,1024]{3,2,1,0:T(8,128)(2,1)}, u32[]{:S(2)}) copy-start(bf16[2,1,1024,1024]{3,2,1,0:T(8,128)(2,1)} %param.7) | copy-start | bytes 12582916
  81.2 3.5 %copy-start.8 = (f32[1024,1024]{1,0:T(8,128)S(1)}, f32[1024,1024]{1,0:T(8,128)}, u32[]{:S(2)}) copy-start(f32[1024,1024]{1,0:T(8,128)} %multiply_bitcast_fusion.2) | copy-start | bytes 12582916
  84.7 2.4 %copy-start = (f32[1,1024,1024]{2,1,0:T(8,128)S(1)}, f32[1,1024,1024]{2,1,0:T(8,128)}, u32[]{:S(2)}) copy-start(f32[1,1024,1024]{2,1,0:T(8,128)} %state_ref.1) | copy-start | bytes 12582916
  87.2 2.0 %copy-start.1 = (f32[1024,1024]{1,0:T(8,128)}, f32[1024,1024]{1,0:T(8,128)S(1)}, u32[]{:S(2)}) copy-start(f32[1024,1024]{1,0:T(8,128)S(1)} %multiply_multiply_fusion) | copy-start | bytes 12582916
  91.0 26.9 %all-to-all-start.1 = ((f32[32,1,2]{2,1,0:T(1,128)}), f32[32,1,2]{2,1,0:T(1,128)S(1)}, u32[]{:S(2)}, u32[]{:S(2)}) async-start(f32[32,1,2]{2,1,0:T(1,128)} %broadcast_in_dim.4), calls=%async_computation.1 | async-start | bytes 32768 | tf_op jit(solution)/shard_map/all_to_all | solution.py:28
  118.0 8.5 %copy-start.2 = (f32[2]{0:T(128)}, f32[2]{0:T(128)S(1)}, u32[]{:S(2)}) copy-start(f32[2]{0:T(128)S(1)} %compare_select_fusion) | copy-start | bytes 28

commit v22 on v21

--- a/solution.py
+++ b/solution.py
@@ -56,7 +56,7 @@
 def masked_square_sum(pairs, block_index, left_live, right_live, state):
     count = lax.axis_size(AXES)
     sec_size = state.shape[1]
-    rows = 2 * BLOCK
+    rows = 4 * BLOCK
     return pl.pallas_call(
         functools.partial(square_sum_kernel, pairs),
         grid_spec=pltpu.PrefetchScalarGridSpec(

time: 127 us -> 127 us (level)
  no operation moved by 1% of the time
where the time goes in v22:
time: 127 us
  starting transfers between devices  46.4 us (37%)
  waiting for transfers between devices  28.2 us (22%)
  other arithmetic  18 us (14%)
  matrix products  17.6 us (14%)
  local copies, waits for them, and re-layouts  7.05 us (6%)
  between operations  5.07 us (4%)
  Pallas kernels  4.49 us (4%)
    all_to_all x2, starting transfers between devices, exchange_sum(): return jnp.sum(lax.all_to_all(spread, AXES, 0, 0, tiled=True), axis=0)  27 us
    ppermute x8, waiting for transfers between devices, shift_up(): return lax.ppermute(block, AXES, route)  21.1 us
    ppermute x8, starting transfers between devices, shift_up(): return lax.ppermute(block, AXES, route)  19.4 us
    dot_general x1, matrix products, per_device(): jnp.dot(left_env[1, 0], part_one, preferred_element_type=jnp.float32)  9.38 us
    broadcast_in_dim x1, other arithmetic, per_device(): return (next_vector[None], coefficients)  7.81 us
    all_to_all x2, waiting for transfers between devices, exchange_sum(): return jnp.sum(lax.all_to_all(spread, AXES, 0, 0, tiled=True), axis=0)  7.09 us
    dot_general x4, matrix products, per_device(): jnp.dot(source, right_env[0, 0], preferred_element_type=jnp.float32)  5.79 us
    mul x1, other arithmetic, per_device(): masked = state[0] * live  4.61 us
  transfers between devices with their start and end apart: 10, of which 4 were waited for; matrix products, arithmetic and copies ran while one was open for 17% of the time, Pallas kernels for 0%

profile of v22, /device:TPU:0, one launch (start us, length us, event | category | flops | bytes accessed | tf_op | source)
XLA Modules:
  0.0 126.8 jit_solution(5891079142021765353)
XLA Ops:
  0.7 4.5 %shard_map.77 = f32[32,1,1]{2,1,0:T(1,128)} custom-call(s32[1]{0:T(128)} %bitcast.5.index_ref, s32[8]{0:T(128)} %left_ref.1, s32[10]{0:T(128)} %right_ref.1, f32[1,1024,1024]{2,1,0:T(8,128)} %state_ref.1), custom_call_target="tpu_custom_call" | custom-call | tf_op jit(solution)/shard_map/pallas_call | solution.py:60
  5.2 7.3 %all-to-all-start = ((f32[32,1,1]{2,1,0:T(1,128)}), f32[32,1,1]{2,1,0:T(1,128)S(1)}, u32[]{:S(2)}, u32[]{:S(2)}) async-start(f32[32,1,1]{2,1,0:T(1,128)} %shard_map.77), calls=%async_computation | async-start | bytes 32768 | tf_op jit(solution)/shard_map/all_to_all | solution.py:28
  16.6 4.6 %multiply_multiply_fusion.1 = f32[1024,1024]{1,0:T(8,128)} fusion(f32[1,1024,1024]{2,1,0:T(8,128)} %state_ref.1, f32[1024]{0:T(1024)S(1)} %get-tuple-element.20, f32[1024]{0:T(1024)S(1)} %get-tuple-element.19), kind=kLoop, calls=%fused_computation.2 | loop fusion | flops 2097152 | bytes 8396800 | tf_op jit(solution)/shard_map/mul | solution.py:99
  23.3 2.8 %fusion.49 = (bf16[256,1024]{1,0:T(8,128)(2,1)S(1)}, bf16[256,1024]{1,0:T(8,128)(2,1)S(1)}, bf16[256,1024]{1,0:T(8,128)(2,1)S(1)}, bf16[256,1024]{1,0:T(8,128)(2,1)S(1)}) fusion(f32[1024,1024]{1,0:T(8,128)} %multiply_multiply_fusion.1, f32[]{:T(128)S(6)} %sqrt.6), kind=kLoop, calls=%fused_computation.54 | loop fusion | flops 2097152 | bytes 6291460 | tf_op jit(solution)/shard_map/convert_element_type | solution.py:108
  26.1 4.5 %collective-permute-start = (bf16[256,1024]{1,0:T(8,128)(2,1)S(1)}, bf16[256,1024]{1,0:T(8,128)(2,1)}, u32[]{:S(2)}, u32[]{:S(2)}) collective-permute-start(bf16[256,1024]{1,0:T(8,128)(2,1)S(1)} %get-tuple-element.8), channel_id=1, source_target_pairs={{0,2},{1,3},{2,4},{3,5},{4,6},{5,7},{6,8},{7,9},{8,10},{9,11},{10,... | collective-permute-start | bytes 1572872 | tf_op jit(solution)/shard_map/ppermute | solution.py:19
  30.5 3.4 %collective-permute-start.4 = (bf16[256,1024]{1,0:T(8,128)(2,1)S(1)}, bf16[256,1024]{1,0:T(8,128)(2,1)}, u32[]{:S(2)}, u32[]{:S(2)}) collective-permute-start(bf16[256,1024]{1,0:T(8,128)(2,1)S(1)} %get-tuple-element.10), channel_id=1, source_target_pairs={{0,2},{1,3},{2,4},{3,5},{4,6},{5,7},{6,8},{7,9},{8,10},{9,11},{10,... | collective-permute-start | bytes 1572872 | tf_op jit(solution)/shard_map/ppermute | solution.py:19
  33.9 2.6 %collective-permute-start.2 = (bf16[256,1024]{1,0:T(8,128)(2,1)S(1)}, bf16[256,1024]{1,0:T(8,128)(2,1)S(1)}, u32[]{:S(2)}, u32[]{:S(2)}) collective-permute-start(bf16[256,1024]{1,0:T(8,128)(2,1)S(1)} %get-tuple-element.11), channel_id=1, source_target_pairs={{0,2},{1,3},{2,4},{3,5},{4,6},{5,7},{6,8},{7,9},{8,10},{9,11},{10,... | collective-permute-start | bytes 1572872 | tf_op jit(solution)/shard_map/ppermute | solution.py:19
  36.6 9.4 %multiply_bitcast_fusion.2 = f32[1024,1024]{1,0:T(8,128)} fusion(bf16[2,1,1024,1024]{3,2,1,0:T(8,128)(2,1)} %param.7, f32[]{:T(128)} %bitcast.8, bf16[256,1024]{1,0:T(8,128)(2,1)S(1)} %get-tuple-element.4, bf16[256,1024]{1,0:T(8,128)(2,1)S(1)} %get-tuple-element.10, bf16[256,1024]{1,0:T(8,128)(2,1)S(1)} %get-tuple-element.11, ...), kind=kOutput, calls=%fused_computation.7 | convolution fusion | flops 4305453056 | bytes 10486272 | tf_op jit(solution)/shard_map/dot_general | solution.py:127
  46.0 3.3 %collective-permute-start.6 = (bf16[256,1024]{1,0:T(8,128)(2,1)S(1)}, bf16[256,1024]{1,0:T(8,128)(2,1)S(1)}, u32[]{:S(2)}, u32[]{:S(2)}) collective-permute-start(bf16[256,1024]{1,0:T(8,128)(2,1)S(1)} %get-tuple-element.4), channel_id=1, source_target_pairs={{0,2},{1,3},{2,4},{3,5},{4,6},{5,7},{6,8},{7,9},{8,10},{9,11},{10,... | collective-permute-start | bytes 1572872 | tf_op jit(solution)/shard_map/ppermute | solution.py:19
  49.3 1.3 %collective-permute-start.1 = (bf16[256,1024]{1,0:T(8,128)(2,1)}, bf16[256,1024]{1,0:T(8,128)(2,1)S(1)}, u32[]{:S(2)}, u32[]{:S(2)}) collective-permute-start(bf16[256,1024]{1,0:T(8,128)(2,1)} %collective-permute-done), channel_id=1, source_target_pairs={{0,1},{1,2},{2,3},{3,4},{4,5},{5,6},{6,7},{7,8},{8,9},{9,10},{10,1... | collective-permute-start | bytes 1572872 | tf_op jit(solution)/shard_map/ppermute | solution.py:19
  50.6 2.6 %collective-permute-done.4 = bf16[256,1024]{1,0:T(8,128)(2,1)} collective-permute-done((bf16[256,1024]{1,0:T(8,128)(2,1)S(1)}, bf16[256,1024]{1,0:T(8,128)(2,1)}, u32[]{:S(2)}, u32[]{:S(2)}) %collective-permute-start.4) | collective-permute-done | bytes 524320 | tf_op jit(solution)/shard_map/ppermute | solution.py:19
  53.2 1.5 %collective-permute-start.5 = (bf16[256,1024]{1,0:T(8,128)(2,1)}, bf16[256,1024]{1,0:T(8,128)(2,1)S(1)}, u32[]{:S(2)}, u32[]{:S(2)}) collective-permute-start(bf16[256,1024]{1,0:T(8,128)(2,1)} %collective-permute-done.4), channel_id=1, source_target_pairs={{0,1},{1,2},{2,3},{3,4},{4,5},{5,6},{6,7},{7,8},{8,9},{9,10},{10,1... | collective-permute-start | bytes 1572872 | tf_op jit(solution)/shard_map/ppermute | solution.py:19
  55.9 8.5 %collective-permute-done.2 = bf16[256,1024]{1,0:T(8,128)(2,1)S(1)} collective-permute-done((bf16[256,1024]{1,0:T(8,128)(2,1)S(1)}, bf16[256,1024]{1,0:T(8,128)(2,1)S(1)}, u32[]{:S(2)}, u32[]{:S(2)}) %collective-permute-start.2) | collective-permute-done | bytes 524320 | tf_op jit(solution)/shard_map/ppermute | solution.py:19
  64.5 1.3 %collective-permute-start.3 = (bf16[256,1024]{1,0:T(8,128)(2,1)S(1)}, bf16[256,1024]{1,0:T(8,128)(2,1)S(1)}, u32[]{:S(2)}, u32[]{:S(2)}) collective-permute-start(bf16[256,1024]{1,0:T(8,128)(2,1)S(1)} %collective-permute-done.2), channel_id=1, source_target_pairs={{0,1},{1,2},{2,3},{3,4},{4,5},{5,6},{6,7},{7,8},{8,9},{9,10},{10,1... | collective-permute-start | bytes 1572872 | tf_op jit(solution)/shard_map/ppermute | solution.py:19
  65.8 9.9 %collective-permute-done.6 = bf16[256,1024]{1,0:T(8,128)(2,1)S(1)} collective-permute-done((bf16[256,1024]{1,0:T(8,128)(2,1)S(1)}, bf16[256,1024]{1,0:T(8,128)(2,1)S(1)}, u32[]{:S(2)}, u32[]{:S(2)}) %collective-permute-start.6) | collective-permute-done | bytes 524320 | tf_op jit(solution)/shard_map/ppermute | solution.py:19
  75.7 1.5 %collective-permute-start.7 = (bf16[256,1024]{1,0:T(8,128)(2,1)S(1)}, bf16[256,1024]{1,0:T(8,128)(2,1)S(1)}, u32[]{:S(2)}, u32[]{:S(2)}) collective-permute-start(bf16[256,1024]{1,0:T(8,128)(2,1)S(1)} %collective-permute-done.6), channel_id=1, source_target_pairs={{0,1},{1,2},{2,3},{3,4},{4,5},{5,6},{6,7},{7,8},{8,9},{9,10},{10,1... | collective-permute-start | bytes 1572872 | tf_op jit(solution)/shard_map/ppermute | solution.py:19
  77.2 2.5 %fusion.34 = bf16[256,1024]{1,0:T(8,128)(2,1)S(1)} fusion(bf16[2,1,1024,1024]{3,2,1,0:T(8,128)(2,1)} %param.8, bf16[256,1024]{1,0:T(8,128)(2,1)S(1)} %collective-permute-done.1, bf16[256,1024]{1,0:T(8,128)(2,1)} %collective-permute-done, f32[]{:T(128)S(6)} %select_n.79, f32[]{:T(128)S(6)} %select_n.71), kind=kOutput, calls=%fused_computation.43 | convolution fusion | flops 538705920 | bytes 3670024 | tf_op jit(solution)/shard_map/dot_general | solution.py:138
  79.7 1.8 %fusion.40 = bf16[256,1024]{1,0:T(8,128)(2,1)S(1)} fusion(bf16[2,1,1024,1024]{3,2,1,0:T(8,128)(2,1)S(1)} %copy-done.6, bf16[256,1024]{1,0:T(8,128)(2,1)S(1)} %collective-permute-done.5, bf16[256,1024]{1,0:T(8,128)(2,1)} %collective-permute-done.4, f32[]{:T(128)S(6)} %select_n.79, f32[]{:T(128)S(6)} %select_n.71), kind=kOutput, calls=%fused_computation.45 | convolution fusion | flops 538705920 | bytes 3670024 | tf_op jit(solution)/shard_map/dot_general | solution.py:138
  83.7 1.3 %copy-done.8 = f32[1024,1024]{1,0:T(8,128)S(1)} copy-done((f32[1024,1024]{1,0:T(8,128)S(1)}, f32[1024,1024]{1,0:T(8,128)}, u32[]{:S(2)}) %copy-start.8) | copy-done | bytes 4194328
  85.0 2.4 %multiply_multiply_fusion = f32[1024,1024]{1,0:T(8,128)S(1)} fusion(f32[1024,1024]{1,0:T(8,128)S(1)} %copy-done.8, bf16[256,1024]{1,0:T(8,128)(2,1)S(1)} %fusion.43, bf16[256,1024]{1,0:T(8,128)(2,1)S(1)} %fusion.40, bf16[256,1024]{1,0:T(8,128)(2,1)S(1)} %fusion.37, bf16[256,1024]{1,0:T(8,128)(2,1)S(1)} %fusion.34, ...), kind=kOutput, calls=%fused_computation.1 | convolution fusion | flops 2159017984 | bytes 12591104 | tf_op jit(solution)/shard_map/dot_general | solution.py:141
  89.5 1.2 maximum_reduce_fusion
  91.3 19.7 %all-to-all-start.1 = ((f32[32,1,2]{2,1,0:T(1,128)}), f32[32,1,2]{2,1,0:T(1,128)S(1)}, u32[]{:S(2)}, u32[]{:S(2)}) async-start(f32[32,1,2]{2,1,0:T(1,128)} %broadcast_in_dim.4), calls=%async_computation.1 | async-start | bytes 32768 | tf_op jit(solution)/shard_map/all_to_all | solution.py:28
  111.0 7.1 %all-to-all-done.1 = f32[32,1,2]{2,1,0:T(1,128)S(1)} async-done(((f32[32,1,2]{2,1,0:T(1,128)}), f32[32,1,2]{2,1,0:T(1,128)S(1)}, u32[]{:S(2)}, u32[]{:S(2)}) %all-to-all-start.1) | async-done | bytes 288 | tf_op jit(solution)/shard_map/all_to_all | solution.py:28
  119.0 7.8 %divide_bitcast_fusion = f32[1,1024,1024]{2,1,0:T(8,128)} fusion(f32[1024,1024]{1,0:T(8,128)} %copy-done.1, f32[]{:T(128)} %bitcast.17, f32[]{:T(128)} %bitcast.16, f32[]{:T(128)S(6)} %sqrt.6, f32[1024]{0:T(1024)S(1)} %get-tuple-element.20, f32[1024]{0:T(1024)S(1)} %get-tuple-element.19, f32[1,1024,1024]{2,1,0:T(8,128)} %state_ref.1), kind=kLoop, calls=%fused_computation.4 | loop fusion | flops 6291456 | bytes 12591116 | tf_op jit(solution)/shard_map/broadcast_in_dim | solution.py:154
  (39 shorter events, 8.9 us)
Async XLA Ops:
  0.6 13.9 %copy-start.5 = (s32[10]{0:T(128)S(1)}, s32[10]{0:T(128)}, u32[]{:S(2)}) copy-start(s32[10]{0:T(128)} %right_ref.1) | copy-start | bytes 124
  0.6 11.9 %copy-start.4 = (s32[8]{0:T(128)S(1)}, s32[8]{0:T(128)}, u32[]{:S(2)}) copy-start(s32[8]{0:T(128)} %left_ref.1) | copy-start | bytes 100
  0.7 15.9 %copy-start.3 = (f32[2,4,4]{2,1,0:T(4,128)S(1)}, f32[2,4,4]{2,1,0:T(4,128)}, u32[]{:S(2)}) copy-start(f32[2,4,4]{2,1,0:T(4,128)} %param.9) | copy-start | bytes 388
  5.2 16.7 %all-to-all-start = ((f32[32,1,1]{2,1,0:T(1,128)}), f32[32,1,1]{2,1,0:T(1,128)S(1)}, u32[]{:S(2)}, u32[]{:S(2)}) async-start(f32[32,1,1]{2,1,0:T(1,128)} %shard_map.77), calls=%async_computation | async-start | bytes 32768 | tf_op jit(solution)/shard_map/all_to_all | solution.py:28
  26.1 23.2 %collective-permute-start = (bf16[256,1024]{1,0:T(8,128)(2,1)S(1)}, bf16[256,1024]{1,0:T(8,128)(2,1)}, u32[]{:S(2)}, u32[]{:S(2)}) collective-permute-start(bf16[256,1024]{1,0:T(8,128)(2,1)S(1)} %get-tuple-element.8), channel_id=1, source_target_pairs={{0,2},{1,3},{2,4},{3,5},{4,6},{5,7},{6,8},{7,9},{8,10},{9,11},{10,... | collective-permute-start | bytes 1572872 | tf_op jit(solution)/shard_map/ppermute | solution.py:19
  30.5 22.7 %collective-permute-start.4 = (bf16[256,1024]{1,0:T(8,128)(2,1)S(1)}, bf16[256,1024]{1,0:T(8,128)(2,1)}, u32[]{:S(2)}, u32[]{:S(2)}) collective-permute-start(bf16[256,1024]{1,0:T(8,128)(2,1)S(1)} %get-tuple-element.10), channel_id=1, source_target_pairs={{0,2},{1,3},{2,4},{3,5},{4,6},{5,7},{6,8},{7,9},{8,10},{9,11},{10,... | collective-permute-start | bytes 1572872 | tf_op jit(solution)/shard_map/ppermute | solution.py:19
  33.9 30.5 %collective-permute-start.2 = (bf16[256,1024]{1,0:T(8,128)(2,1)S(1)}, bf16[256,1024]{1,0:T(8,128)(2,1)S(1)}, u32[]{:S(2)}, u32[]{:S(2)}) collective-permute-start(bf16[256,1024]{1,0:T(8,128)(2,1)S(1)} %get-tuple-element.11), channel_id=1, source_target_pairs={{0,2},{1,3},{2,4},{3,5},{4,6},{5,7},{6,8},{7,9},{8,10},{9,11},{10,... | collective-permute-start | bytes 1572872 | tf_op jit(solution)/shard_map/ppermute | solution.py:19
  46.0 29.8 %collective-permute-start.6 = (bf16[256,1024]{1,0:T(8,128)(2,1)S(1)}, bf16[256,1024]{1,0:T(8,128)(2,1)S(1)}, u32[]{:S(2)}, u32[]{:S(2)}) collective-permute-start(bf16[256,1024]{1,0:T(8,128)(2,1)S(1)} %get-tuple-element.4), channel_id=1, source_target_pairs={{0,2},{1,3},{2,4},{3,5},{4,6},{5,7},{6,8},{7,9},{8,10},{9,11},{10,... | collective-permute-start | bytes 1572872 | tf_op jit(solution)/shard_map/ppermute | solution.py:19
  49.3 27.9 %collective-permute-start.1 = (bf16[256,1024]{1,0:T(8,128)(2,1)}, bf16[256,1024]{1,0:T(8,128)(2,1)S(1)}, u32[]{:S(2)}, u32[]{:S(2)}) collective-permute-start(bf16[256,1024]{1,0:T(8,128)(2,1)} %collective-permute-done), channel_id=1, source_target_pairs={{0,1},{1,2},{2,3},{3,4},{4,5},{5,6},{6,7},{7,8},{8,9},{9,10},{10,1... | collective-permute-start | bytes 1572872 | tf_op jit(solution)/shard_map/ppermute | solution.py:19
  53.2 26.5 %collective-permute-start.5 = (bf16[256,1024]{1,0:T(8,128)(2,1)}, bf16[256,1024]{1,0:T(8,128)(2,1)S(1)}, u32[]{:S(2)}, u32[]{:S(2)}) collective-permute-start(bf16[256,1024]{1,0:T(8,128)(2,1)} %collective-permute-done.4), channel_id=1, source_target_pairs={{0,1},{1,2},{2,3},{3,4},{4,5},{5,6},{6,7},{7,8},{8,9},{9,10},{10,1... | collective-permute-start | bytes 1572872 | tf_op jit(solution)/shard_map/ppermute | solution.py:19
  55.9 23.8 %copy-start.6 = (bf16[2,1,1024,1024]{3,2,1,0:T(8,128)(2,1)S(1)}, bf16[2,1,1024,1024]{3,2,1,0:T(8,128)(2,1)}, u32[]{:S(2)}) copy-start(bf16[2,1,1024,1024]{3,2,1,0:T(8,128)(2,1)} %param.8) | copy-start | bytes 12582916
  64.5 17.1 %collective-permute-start.3 = (bf16[256,1024]{1,0:T(8,128)(2,1)S(1)}, bf16[256,1024]{1,0:T(8,128)(2,1)S(1)}, u32[]{:S(2)}, u32[]{:S(2)}) collective-permute-start(bf16[256,1024]{1,0:T(8,128)(2,1)S(1)} %collective-permute-done.2), channel_id=1, source_target_pairs={{0,1},{1,2},{2,3},{3,4},{4,5},{5,6},{6,7},{7,8},{8,9},{9,10},{10,1... | collective-permute-start | bytes 1572872 | tf_op jit(solution)/shard_map/ppermute | solution.py:19
  75.7 6.6 %collective-permute-start.7 = (bf16[256,1024]{1,0:T(8,128)(2,1)S(1)}, bf16[256,1024]{1,0:T(8,128)(2,1)S(1)}, u32[]{:S(2)}, u32[]{:S(2)}) collective-permute-start(bf16[256,1024]{1,0:T(8,128)(2,1)S(1)} %collective-permute-done.6), channel_id=1, source_target_pairs={{0,1},{1,2},{2,3},{3,4},{4,5},{5,6},{6,7},{7,8},{8,9},{9,10},{10,1... | collective-permute-start | bytes 1572872 | tf_op jit(solution)/shard_map/ppermute | solution.py:19
  81.6 2.2 %copy-start.7 = (bf16[2,1,1024,1024]{3,2,1,0:T(8,128)(2,1)S(1)}, bf16[2,1,1024,1024]{3,2,1,0:T(8,128)(2,1)}, u32[]{:S(2)}) copy-start(bf16[2,1,1024,1024]{3,2,1,0:T(8,128)(2,1)} %param.7) | copy-start | bytes 12582916
  81.6 3.5 %copy-start.8 = (f32[1024,1024]{1,0:T(8,128)S(1)}, f32[1024,1024]{1,0:T(8,128)}, u32[]{:S(2)}) copy-start(f32[1024,1024]{1,0:T(8,128)} %multiply_bitcast_fusion.2) | copy-start | bytes 12582916
  85.0 2.4 %copy-start = (f32[1,1024,1024]{2,1,0:T(8,128)S(1)}, f32[1,1024,1024]{2,1,0:T(8,128)}, u32[]{:S(2)}) copy-start(f32[1,1024,1024]{2,1,0:T(8,128)} %state_ref.1) | copy-start | bytes 12582916
  87.5 2.0 %copy-start.1 = (f32[1024,1024]{1,0:T(8,128)}, f32[1024,1024]{1,0:T(8,128)S(1)}, u32[]{:S(2)}) copy-start(f32[1024,1024]{1,0:T(8,128)S(1)} %multiply_multiply_fusion) | copy-start | bytes 12582916
  91.3 26.9 %all-to-all-start.1 = ((f32[32,1,2]{2,1,0:T(1,128)}), f32[32,1,2]{2,1,0:T(1,128)S(1)}, u32[]{:S(2)}, u32[]{:S(2)}) async-start(f32[32,1,2]{2,1,0:T(1,128)} %broadcast_in_dim.4), calls=%async_computation.1 | async-start | bytes 32768 | tf_op jit(solution)/shard_map/all_to_all | solution.py:28
  118.3 8.5 %copy-start.2 = (f32[2]{0:T(128)}, f32[2]{0:T(128)S(1)}, u32[]{:S(2)}) copy-start(f32[2]{0:T(128)S(1)} %compare_select_fusion) | copy-start | bytes 28

commit v23 on v21

--- a/solution.py
+++ b/solution.py
@@ -126,7 +126,7 @@
     diag_weight = table_entry(site_ops[1], own_pair, own_pair)
     image_one = diag_weight * jnp.dot(left_env[1, 0], part_one, preferred_element_type=jnp.float32)
 
-    image_one, pieces[-1] = lax.optimization_barrier((image_one, pieces[-1]))
+    image_one, pieces[-2] = lax.optimization_barrier((image_one, pieces[-2]))
     parts = []
     for c in range(CHUNKS):
         far_two = shift_up(pieces[c], 2)

time: 127 us -> 127 us (level)
  no operation moved by 1% of the time
where the time goes in v23:
time: 127 us; the launch traced here: 126 us
  starting transfers between devices  46.8 us (37%)
  waiting for transfers between devices  28.2 us (22%)
  other arithmetic  18 us (14%)
  matrix products  17.6 us (14%)
  local copies, waits for them, and re-layouts  7.05 us (6%)
  between operations  5.07 us (4%)
  Pallas kernels  3.77 us (3%)
    all_to_all x2, starting transfers between devices, exchange_sum(): return jnp.sum(lax.all_to_all(spread, AXES, 0, 0, tiled=True), axis=0)  27.4 us
    ppermute x8, waiting for transfers between devices, shift_up(): return lax.ppermute(block, AXES, route)  21.1 us
    ppermute x8, starting transfers between devices, shift_up(): return lax.ppermute(block, AXES, route)  19.4 us
    dot_general x1, matrix products, per_device(): jnp.dot(left_env[1, 0], part_one, preferred_element_type=jnp.float32)  9.38 us
    broadcast_in_dim x1, other arithmetic, per_device(): return (next_vector[None], coefficients)  7.81 us
    all_to_all x2, waiting for transfers between devices, exchange_sum(): return jnp.sum(lax.all_to_all(spread, AXES, 0, 0, tiled=True), axis=0)  7.09 us
    dot_general x4, matrix products, per_device(): jnp.dot(source, right_env[0, 0], preferred_element_type=jnp.float32)  5.79 us
    mul x1, other arithmetic, per_device(): masked = state[0] * live  4.61 us
  transfers between devices with their start and end apart: 10, of which 4 were waited for; matrix products, arithmetic and copies ran while one was open for 17% of the time, Pallas kernels for 0%

profile of v23, /device:TPU:0, one launch (start us, length us, event | category | flops | bytes accessed | tf_op | source)
XLA Modules:
  0.0 126.5 jit_solution(11457413459168568730)
XLA Ops:
  0.7 3.8 %shard_map.77 = f32[32,1,1]{2,1,0:T(1,128)} custom-call(s32[1]{0:T(128)} %bitcast.5.index_ref, s32[8]{0:T(128)} %left_ref.1, s32[10]{0:T(128)} %right_ref.1, f32[1,1024,1024]{2,1,0:T(8,128)} %state_ref.1), custom_call_target="tpu_custom_call" | custom-call | tf_op jit(solution)/shard_map/pallas_call | solution.py:60
  4.4 7.7 %all-to-all-start = ((f32[32,1,1]{2,1,0:T(1,128)}), f32[32,1,1]{2,1,0:T(1,128)S(1)}, u32[]{:S(2)}, u32[]{:S(2)}) async-start(f32[32,1,1]{2,1,0:T(1,128)} %shard_map.77), calls=%async_computation | async-start | bytes 32768 | tf_op jit(solution)/shard_map/all_to_all | solution.py:28
  16.2 4.6 %multiply_multiply_fusion.1 = f32[1024,1024]{1,0:T(8,128)} fusion(f32[1,1024,1024]{2,1,0:T(8,128)} %state_ref.1, f32[1024]{0:T(1024)S(1)} %get-tuple-element.20, f32[1024]{0:T(1024)S(1)} %get-tuple-element.19), kind=kLoop, calls=%fused_computation.2 | loop fusion | flops 2097152 | bytes 8396800 | tf_op jit(solution)/shard_map/mul | solution.py:99
  23.0 2.8 %fusion.49 = (bf16[256,1024]{1,0:T(8,128)(2,1)S(1)}, bf16[256,1024]{1,0:T(8,128)(2,1)S(1)}, bf16[256,1024]{1,0:T(8,128)(2,1)S(1)}, bf16[256,1024]{1,0:T(8,128)(2,1)S(1)}) fusion(f32[1024,1024]{1,0:T(8,128)} %multiply_multiply_fusion.1, f32[]{:T(128)S(6)} %sqrt.6), kind=kLoop, calls=%fused_computation.54 | loop fusion | flops 2097152 | bytes 6291460 | tf_op jit(solution)/shard_map/convert_element_type | solution.py:108
  25.7 4.5 %collective-permute-start = (bf16[256,1024]{1,0:T(8,128)(2,1)S(1)}, bf16[256,1024]{1,0:T(8,128)(2,1)}, u32[]{:S(2)}, u32[]{:S(2)}) collective-permute-start(bf16[256,1024]{1,0:T(8,128)(2,1)S(1)} %get-tuple-element.8), channel_id=1, source_target_pairs={{0,2},{1,3},{2,4},{3,5},{4,6},{5,7},{6,8},{7,9},{8,10},{9,11},{10,... | collective-permute-start | bytes 1572872 | tf_op jit(solution)/shard_map/ppermute | solution.py:19
  30.2 3.4 %collective-permute-start.6 = (bf16[256,1024]{1,0:T(8,128)(2,1)S(1)}, bf16[256,1024]{1,0:T(8,128)(2,1)}, u32[]{:S(2)}, u32[]{:S(2)}) collective-permute-start(bf16[256,1024]{1,0:T(8,128)(2,1)S(1)} %get-tuple-element.9), channel_id=1, source_target_pairs={{0,2},{1,3},{2,4},{3,5},{4,6},{5,7},{6,8},{7,9},{8,10},{9,11},{10,... | collective-permute-start | bytes 1572872 | tf_op jit(solution)/shard_map/ppermute | solution.py:19
  33.6 2.6 %collective-permute-start.2 = (bf16[256,1024]{1,0:T(8,128)(2,1)S(1)}, bf16[256,1024]{1,0:T(8,128)(2,1)S(1)}, u32[]{:S(2)}, u32[]{:S(2)}) collective-permute-start(bf16[256,1024]{1,0:T(8,128)(2,1)S(1)} %get-tuple-element.11), channel_id=1, source_target_pairs={{0,2},{1,3},{2,4},{3,5},{4,6},{5,7},{6,8},{7,9},{8,10},{9,11},{10,... | collective-permute-start | bytes 1572872 | tf_op jit(solution)/shard_map/ppermute | solution.py:19
  36.3 9.4 %multiply_bitcast_fusion.2 = f32[1024,1024]{1,0:T(8,128)} fusion(bf16[2,1,1024,1024]{3,2,1,0:T(8,128)(2,1)} %param.7, f32[]{:T(128)} %bitcast.8, bf16[256,1024]{1,0:T(8,128)(2,1)S(1)} %get-tuple-element.9, bf16[256,1024]{1,0:T(8,128)(2,1)S(1)} %get-tuple-element.4, bf16[256,1024]{1,0:T(8,128)(2,1)S(1)} %get-tuple-element.11, ...), kind=kOutput, calls=%fused_computation.7 | convolution fusion | flops 4305453056 | bytes 10486272 | tf_op jit(solution)/shard_map/dot_general | solution.py:127
  45.6 3.3 %collective-permute-start.4 = (bf16[256,1024]{1,0:T(8,128)(2,1)S(1)}, bf16[256,1024]{1,0:T(8,128)(2,1)S(1)}, u32[]{:S(2)}, u32[]{:S(2)}) collective-permute-start(bf16[256,1024]{1,0:T(8,128)(2,1)S(1)} %get-tuple-element.4), channel_id=1, source_target_pairs={{0,2},{1,3},{2,4},{3,5},{4,6},{5,7},{6,8},{7,9},{8,10},{9,11},{10,... | collective-permute-start | bytes 1572872 | tf_op jit(solution)/shard_map/ppermute | solution.py:19
  49.0 1.3 %collective-permute-start.1 = (bf16[256,1024]{1,0:T(8,128)(2,1)}, bf16[256,1024]{1,0:T(8,128)(2,1)S(1)}, u32[]{:S(2)}, u32[]{:S(2)}) collective-permute-start(bf16[256,1024]{1,0:T(8,128)(2,1)} %collective-permute-done), channel_id=1, source_target_pairs={{0,1},{1,2},{2,3},{3,4},{4,5},{5,6},{6,7},{7,8},{8,9},{9,10},{10,1... | collective-permute-start | bytes 1572872 | tf_op jit(solution)/shard_map/ppermute | solution.py:19
  50.3 2.6 %collective-permute-done.6 = bf16[256,1024]{1,0:T(8,128)(2,1)} collective-permute-done((bf16[256,1024]{1,0:T(8,128)(2,1)S(1)}, bf16[256,1024]{1,0:T(8,128)(2,1)}, u32[]{:S(2)}, u32[]{:S(2)}) %collective-permute-start.6) | collective-permute-done | bytes 524320 | tf_op jit(solution)/shard_map/ppermute | solution.py:19
  52.9 1.5 %collective-permute-start.7 = (bf16[256,1024]{1,0:T(8,128)(2,1)}, bf16[256,1024]{1,0:T(8,128)(2,1)S(1)}, u32[]{:S(2)}, u32[]{:S(2)}) collective-permute-start(bf16[256,1024]{1,0:T(8,128)(2,1)} %collective-permute-done.6), channel_id=1, source_target_pairs={{0,1},{1,2},{2,3},{3,4},{4,5},{5,6},{6,7},{7,8},{8,9},{9,10},{10,1... | collective-permute-start | bytes 1572872 | tf_op jit(solution)/shard_map/ppermute | solution.py:19
  55.6 8.5 %collective-permute-done.2 = bf16[256,1024]{1,0:T(8,128)(2,1)S(1)} collective-permute-done((bf16[256,1024]{1,0:T(8,128)(2,1)S(1)}, bf16[256,1024]{1,0:T(8,128)(2,1)S(1)}, u32[]{:S(2)}, u32[]{:S(2)}) %collective-permute-start.2) | collective-permute-done | bytes 524320 | tf_op jit(solution)/shard_map/ppermute | solution.py:19
  64.2 1.3 %collective-permute-start.3 = (bf16[256,1024]{1,0:T(8,128)(2,1)S(1)}, bf16[256,1024]{1,0:T(8,128)(2,1)S(1)}, u32[]{:S(2)}, u32[]{:S(2)}) collective-permute-start(bf16[256,1024]{1,0:T(8,128)(2,1)S(1)} %collective-permute-done.2), channel_id=1, source_target_pairs={{0,1},{1,2},{2,3},{3,4},{4,5},{5,6},{6,7},{7,8},{8,9},{9,10},{10,1... | collective-permute-start | bytes 1572872 | tf_op jit(solution)/shard_map/ppermute | solution.py:19
  65.5 9.9 %collective-permute-done.4 = bf16[256,1024]{1,0:T(8,128)(2,1)S(1)} collective-permute-done((bf16[256,1024]{1,0:T(8,128)(2,1)S(1)}, bf16[256,1024]{1,0:T(8,128)(2,1)S(1)}, u32[]{:S(2)}, u32[]{:S(2)}) %collective-permute-start.4) | collective-permute-done | bytes 524320 | tf_op jit(solution)/shard_map/ppermute | solution.py:19
  75.4 1.5 %collective-permute-start.5 = (bf16[256,1024]{1,0:T(8,128)(2,1)S(1)}, bf16[256,1024]{1,0:T(8,128)(2,1)S(1)}, u32[]{:S(2)}, u32[]{:S(2)}) collective-permute-start(bf16[256,1024]{1,0:T(8,128)(2,1)S(1)} %collective-permute-done.4), channel_id=1, source_target_pairs={{0,1},{1,2},{2,3},{3,4},{4,5},{5,6},{6,7},{7,8},{8,9},{9,10},{10,1... | collective-permute-start | bytes 1572872 | tf_op jit(solution)/shard_map/ppermute | solution.py:19
  76.9 2.5 %fusion.34 = bf16[256,1024]{1,0:T(8,128)(2,1)S(1)} fusion(bf16[2,1,1024,1024]{3,2,1,0:T(8,128)(2,1)} %param.8, bf16[256,1024]{1,0:T(8,128)(2,1)S(1)} %collective-permute-done.1, bf16[256,1024]{1,0:T(8,128)(2,1)} %collective-permute-done, f32[]{:T(128)S(6)} %select_n.79, f32[]{:T(128)S(6)} %select_n.71), kind=kOutput, calls=%fused_computation.43 | convolution fusion | flops 538705920 | bytes 3670024 | tf_op jit(solution)/shard_map/dot_general | solution.py:138
  79.4 1.8 %fusion.43 = bf16[256,1024]{1,0:T(8,128)(2,1)S(1)} fusion(bf16[2,1,1024,1024]{3,2,1,0:T(8,128)(2,1)S(1)} %copy-done.6, bf16[256,1024]{1,0:T(8,128)(2,1)S(1)} %collective-permute-done.7, bf16[256,1024]{1,0:T(8,128)(2,1)} %collective-permute-done.6, f32[]{:T(128)S(6)} %select_n.79, f32[]{:T(128)S(6)} %select_n.71), kind=kOutput, calls=%fused_computation.46 | convolution fusion | flops 538705920 | bytes 3670024 | tf_op jit(solution)/shard_map/dot_general | solution.py:138
  83.4 1.3 %copy-done.8 = f32[1024,1024]{1,0:T(8,128)S(1)} copy-done((f32[1024,1024]{1,0:T(8,128)S(1)}, f32[1024,1024]{1,0:T(8,128)}, u32[]{:S(2)}) %copy-start.8) | copy-done | bytes 4194328
  84.7 2.4 %multiply_multiply_fusion = f32[1024,1024]{1,0:T(8,128)S(1)} fusion(f32[1024,1024]{1,0:T(8,128)S(1)} %copy-done.8, bf16[256,1024]{1,0:T(8,128)(2,1)S(1)} %fusion.43, bf16[256,1024]{1,0:T(8,128)(2,1)S(1)} %fusion.40, bf16[256,1024]{1,0:T(8,128)(2,1)S(1)} %fusion.37, bf16[256,1024]{1,0:T(8,128)(2,1)S(1)} %fusion.34, ...), kind=kOutput, calls=%fused_computation.1 | convolution fusion | flops 2159017984 | bytes 12591104 | tf_op jit(solution)/shard_map/dot_general | solution.py:141
  89.2 1.2 maximum_reduce_fusion
  91.0 19.7 %all-to-all-start.1 = ((f32[32,1,2]{2,1,0:T(1,128)}), f32[32,1,2]{2,1,0:T(1,128)S(1)}, u32[]{:S(2)}, u32[]{:S(2)}) async-start(f32[32,1,2]{2,1,0:T(1,128)} %broadcast_in_dim.4), calls=%async_computation.1 | async-start | bytes 32768 | tf_op jit(solution)/shard_map/all_to_all | solution.py:28
  110.7 7.1 %all-to-all-done.1 = f32[32,1,2]{2,1,0:T(1,128)S(1)} async-done(((f32[32,1,2]{2,1,0:T(1,128)}), f32[32,1,2]{2,1,0:T(1,128)S(1)}, u32[]{:S(2)}, u32[]{:S(2)}) %all-to-all-start.1) | async-done | bytes 288 | tf_op jit(solution)/shard_map/all_to_all | solution.py:28
  118.6 7.8 %divide_bitcast_fusion = f32[1,1024,1024]{2,1,0:T(8,128)} fusion(f32[1024,1024]{1,0:T(8,128)} %copy-done.1, f32[]{:T(128)} %bitcast.17, f32[]{:T(128)} %bitcast.16, f32[]{:T(128)S(6)} %sqrt.6, f32[1024]{0:T(1024)S(1)} %get-tuple-element.20, f32[1024]{0:T(1024)S(1)} %get-tuple-element.19, f32[1,1024,1024]{2,1,0:T(8,128)} %state_ref.1), kind=kLoop, calls=%fused_computation.4 | loop fusion | flops 6291456 | bytes 12591116 | tf_op jit(solution)/shard_map/broadcast_in_dim | solution.py:154
  (39 shorter events, 8.9 us)
Async XLA Ops:
  0.6 13.6 %copy-start.5 = (s32[10]{0:T(128)S(1)}, s32[10]{0:T(128)}, u32[]{:S(2)}) copy-start(s32[10]{0:T(128)} %right_ref.1) | copy-start | bytes 124
  0.6 11.6 %copy-start.4 = (s32[8]{0:T(128)S(1)}, s32[8]{0:T(128)}, u32[]{:S(2)}) copy-start(s32[8]{0:T(128)} %left_ref.1) | copy-start | bytes 100
  0.7 15.6 %copy-start.3 = (f32[2,4,4]{2,1,0:T(4,128)S(1)}, f32[2,4,4]{2,1,0:T(4,128)}, u32[]{:S(2)}) copy-start(f32[2,4,4]{2,1,0:T(4,128)} %param.9) | copy-start | bytes 388
  4.4 17.1 %all-to-all-start = ((f32[32,1,1]{2,1,0:T(1,128)}), f32[32,1,1]{2,1,0:T(1,128)S(1)}, u32[]{:S(2)}, u32[]{:S(2)}) async-start(f32[32,1,1]{2,1,0:T(1,128)} %shard_map.77), calls=%async_computation | async-start | bytes 32768 | tf_op jit(solution)/shard_map/all_to_all | solution.py:28
  25.7 23.2 %collective-permute-start = (bf16[256,1024]{1,0:T(8,128)(2,1)S(1)}, bf16[256,1024]{1,0:T(8,128)(2,1)}, u32[]{:S(2)}, u32[]{:S(2)}) collective-permute-start(bf16[256,1024]{1,0:T(8,128)(2,1)S(1)} %get-tuple-element.8), channel_id=1, source_target_pairs={{0,2},{1,3},{2,4},{3,5},{4,6},{5,7},{6,8},{7,9},{8,10},{9,11},{10,... | collective-permute-start | bytes 1572872 | tf_op jit(solution)/shard_map/ppermute | solution.py:19
  30.2 22.7 %collective-permute-start.6 = (bf16[256,1024]{1,0:T(8,128)(2,1)S(1)}, bf16[256,1024]{1,0:T(8,128)(2,1)}, u32[]{:S(2)}, u32[]{:S(2)}) collective-permute-start(bf16[256,1024]{1,0:T(8,128)(2,1)S(1)} %get-tuple-element.9), channel_id=1, source_target_pairs={{0,2},{1,3},{2,4},{3,5},{4,6},{5,7},{6,8},{7,9},{8,10},{9,11},{10,... | collective-permute-start | bytes 1572872 | tf_op jit(solution)/shard_map/ppermute | solution.py:19
  33.6 30.5 %collective-permute-start.2 = (bf16[256,1024]{1,0:T(8,128)(2,1)S(1)}, bf16[256,1024]{1,0:T(8,128)(2,1)S(1)}, u32[]{:S(2)}, u32[]{:S(2)}) collective-permute-start(bf16[256,1024]{1,0:T(8,128)(2,1)S(1)} %get-tuple-element.11), channel_id=1, source_target_pairs={{0,2},{1,3},{2,4},{3,5},{4,6},{5,7},{6,8},{7,9},{8,10},{9,11},{10,... | collective-permute-start | bytes 1572872 | tf_op jit(solution)/shard_map/ppermute | solution.py:19
  45.6 29.8 %collective-permute-start.4 = (bf16[256,1024]{1,0:T(8,128)(2,1)S(1)}, bf16[256,1024]{1,0:T(8,128)(2,1)S(1)}, u32[]{:S(2)}, u32[]{:S(2)}) collective-permute-start(bf16[256,1024]{1,0:T(8,128)(2,1)S(1)} %get-tuple-element.4), channel_id=1, source_target_pairs={{0,2},{1,3},{2,4},{3,5},{4,6},{5,7},{6,8},{7,9},{8,10},{9,11},{10,... | collective-permute-start | bytes 1572872 | tf_op jit(solution)/shard_map/ppermute | solution.py:19
  49.0 27.9 %collective-permute-start.1 = (bf16[256,1024]{1,0:T(8,128)(2,1)}, bf16[256,1024]{1,0:T(8,128)(2,1)S(1)}, u32[]{:S(2)}, u32[]{:S(2)}) collective-permute-start(bf16[256,1024]{1,0:T(8,128)(2,1)} %collective-permute-done), channel_id=1, source_target_pairs={{0,1},{1,2},{2,3},{3,4},{4,5},{5,6},{6,7},{7,8},{8,9},{9,10},{10,1... | collective-permute-start | bytes 1572872 | tf_op jit(solution)/shard_map/ppermute | solution.py:19
  52.9 26.5 %collective-permute-start.7 = (bf16[256,1024]{1,0:T(8,128)(2,1)}, bf16[256,1024]{1,0:T(8,128)(2,1)S(1)}, u32[]{:S(2)}, u32[]{:S(2)}) collective-permute-start(bf16[256,1024]{1,0:T(8,128)(2,1)} %collective-permute-done.6), channel_id=1, source_target_pairs={{0,1},{1,2},{2,3},{3,4},{4,5},{5,6},{6,7},{7,8},{8,9},{9,10},{10,1... | collective-permute-start | bytes 1572872 | tf_op jit(solution)/shard_map/ppermute | solution.py:19
  55.6 23.8 %copy-start.6 = (bf16[2,1,1024,1024]{3,2,1,0:T(8,128)(2,1)S(1)}, bf16[2,1,1024,1024]{3,2,1,0:T(8,128)(2,1)}, u32[]{:S(2)}) copy-start(bf16[2,1,1024,1024]{3,2,1,0:T(8,128)(2,1)} %param.8) | copy-start | bytes 12582916
  64.2 17.1 %collective-permute-start.3 = (bf16[256,1024]{1,0:T(8,128)(2,1)S(1)}, bf16[256,1024]{1,0:T(8,128)(2,1)S(1)}, u32[]{:S(2)}, u32[]{:S(2)}) collective-permute-start(bf16[256,1024]{1,0:T(8,128)(2,1)S(1)} %collective-permute-done.2), channel_id=1, source_target_pairs={{0,1},{1,2},{2,3},{3,4},{4,5},{5,6},{6,7},{7,8},{8,9},{9,10},{10,1... | collective-permute-start | bytes 1572872 | tf_op jit(solution)/shard_map/ppermute | solution.py:19
  75.4 6.6 %collective-permute-start.5 = (bf16[256,1024]{1,0:T(8,128)(2,1)S(1)}, bf16[256,1024]{1,0:T(8,128)(2,1)S(1)}, u32[]{:S(2)}, u32[]{:S(2)}) collective-permute-start(bf16[256,1024]{1,0:T(8,128)(2,1)S(1)} %collective-permute-done.4), channel_id=1, source_target_pairs={{0,1},{1,2},{2,3},{3,4},{4,5},{5,6},{6,7},{7,8},{8,9},{9,10},{10,1... | collective-permute-start | bytes 1572872 | tf_op jit(solution)/shard_map/ppermute | solution.py:19
  81.2 2.2 %copy-start.7 = (bf16[2,1,1024,1024]{3,2,1,0:T(8,128)(2,1)S(1)}, bf16[2,1,1024,1024]{3,2,1,0:T(8,128)(2,1)}, u32[]{:S(2)}) copy-start(bf16[2,1,1024,1024]{3,2,1,0:T(8,128)(2,1)} %param.7) | copy-start | bytes 12582916
  81.2 3.5 %copy-start.8 = (f32[1024,1024]{1,0:T(8,128)S(1)}, f32[1024,1024]{1,0:T(8,128)}, u32[]{:S(2)}) copy-start(f32[1024,1024]{1,0:T(8,128)} %multiply_bitcast_fusion.2) | copy-start | bytes 12582916
  84.7 2.4 %copy-start = (f32[1,1024,1024]{2,1,0:T(8,128)S(1)}, f32[1,1024,1024]{2,1,0:T(8,128)}, u32[]{:S(2)}) copy-start(f32[1,1024,1024]{2,1,0:T(8,128)} %state_ref.1) | copy-start | bytes 12582916
  87.2 2.0 %copy-start.1 = (f32[1024,1024]{1,0:T(8,128)}, f32[1024,1024]{1,0:T(8,128)S(1)}, u32[]{:S(2)}) copy-start(f32[1024,1024]{1,0:T(8,128)S(1)} %multiply_multiply_fusion) | copy-start | bytes 12582916
  91.0 26.9 %all-to-all-start.1 = ((f32[32,1,2]{2,1,0:T(1,128)}), f32[32,1,2]{2,1,0:T(1,128)S(1)}, u32[]{:S(2)}, u32[]{:S(2)}) async-start(f32[32,1,2]{2,1,0:T(1,128)} %broadcast_in_dim.4), calls=%async_computation.1 | async-start | bytes 32768 | tf_op jit(solution)/shard_map/all_to_all | solution.py:28
  118.0 8.5 %copy-start.2 = (f32[2]{0:T(128)}, f32[2]{0:T(128)S(1)}, u32[]{:S(2)}) copy-start(f32[2]{0:T(128)S(1)} %compare_select_fusion) | copy-start | bytes 28
